TPU v7x, 32 devices: a whole 2x2x4 slice. The times are simulated.
32 devices in a mesh: groups: 2 (over y), ctx: 8 (over z, x), tp: 2 (over core).
Axes of the slice: x: 2, y: 2, z: 4, core: 2. Of those that a mesh axis runs over, the one named last changes fastest.
Arguments:
- tokens: bfloat16 [4096, 2688], P(('groups', 'ctx', 'tp')), parts along dimension 0, may hold values from -6 to 6
- output_gradient: bfloat16 [4096, 2688], P(('groups', 'ctx', 'tp')), parts along dimension 0, may hold values from -6 to 6
- document_index: int32 [4096], P(('groups', 'ctx')), parts along dimension 0, may hold values from 0 to 3, never falling along the last dimension, each value on 1 to 1024 neighbouring positions
- real_token_count: int32 [16], P(('groups', 'ctx')), parts along dimension 0, may hold values from 64 to 256, as said below
- input_norm_gain: float32 [2688], replicated, may hold values from 0.1 to 1.9
- query_norm_gain: float32 [128], replicated, may hold values from 0.1 to 1.9
- key_norm_gain: float32 [128], replicated, may hold values from 0.1 to 1.9
- output_norm_gain: float32 [2688], replicated, may hold values from 0.1 to 1.9
- query_projection: bfloat16 [2688, 512], P(None, 'tp'), may hold values from -0.125 to 0.125
- key_projection: bfloat16 [2688, 256], P(None, 'tp'), may hold values from -0.125 to 0.125
- value_projection: bfloat16 [2688, 256], P(None, 'tp'), may hold values from -0.125 to 0.125
- output_projection: bfloat16 [512, 2688], P('tp'), may hold values from -0.25 to 0.25
- adapter_down_maps: bfloat16 [2688, 48], replicated, may hold values from -0.125 to 0.125
- adapter_query_up: bfloat16 [16, 512], P(None, 'tp'), may hold values from -0.375 to 0.375
- adapter_key_up: bfloat16 [16, 256], P(None, 'tp'), may hold values from -0.375 to 0.375
- adapter_value_up: bfloat16 [16, 256], P(None, 'tp'), may hold values from -0.375 to 0.375
- adapter_output_down: bfloat16 [512, 16], P('tp'), may hold values from -0.25 to 0.25
- adapter_output_up: bfloat16 [16, 2688], replicated, may hold values from -0.375 to 0.375
Outputs:
- layer_out: bfloat16 [4096, 2688], P(('groups', 'ctx', 'tp')), parts along dimension 0
- grad_in: bfloat16 [4096, 2688], P(('groups', 'ctx', 'tp')), parts along dimension 0
- grad_down: float32 [5376, 48], P(('groups', 'tp')), parts along dimension 0
- query_up_gradient: float32 [32, 512], P('groups', 'tp'), parts along dimension 0
- key_up_gradient: float32 [32, 256], P('groups', 'tp'), parts along dimension 0
- value_up_gradient: float32 [32, 256], P('groups', 'tp'), parts along dimension 0
- grad_down_out: float32 [1024, 16], P(('groups', 'tp')), parts along dimension 0
- output_up_gradient: float32 [32, 2688], P('groups', 'tp'), parts along dimension 0
There are 2 independent parts, one for each index of `groups`. A program takes and returns all parts, laid end to end along the dimension named above; an argument that names none is the same for every part. Nothing has to cross between parts.
Inputs may be any that keep to these rules, and one draw needn't show every extreme that they name: `document_index`: document numbers never fall along the tokens; a document has 1 to 1024 tokens and one has exactly that many. `real_token_count`: the real tokens of a block come first and the rest is padding; some block is full and some holds 64 real tokens.
All inputs are finite; a program needn't handle non-finite values.
Results may differ from a plain program's by a relative error of at most 0.034.
Values may be sent and summed in bfloat16 or wider, within the bound.
No kernel may reach another device: no remote copies, remote signals or barrier semaphores. Data moves between devices by JAX's collectives and lax.ppermute only.
A program may use at most 64 MiB of HBM per device.

v0:
```python
import jax
import jax.numpy as jnp
from jax import lax
from jax.sharding import PartitionSpec as P

WINDOW = 1024


epsilon = 1e-06
adapter_scale = 2.0
score_scale = 168.0 ** (-0.5)


def passed_along(value, axis, steps):
    count = lax.axis_size(axis)
    leading, last = (max(0, -steps), min(count, count - steps))
    return lax.ppermute(value, axis, [(source, source + steps) for source in range(leading, last)])


def norm_rows(source, gain_vec):
    inverse = lax.rsqrt(jnp.mean(source * source, axis=-1, keepdims=True) + epsilon)
    return source * inverse * gain_vec


def norm_back(source, gain_vec, incoming):
    inverse = lax.rsqrt(jnp.mean(source * source, axis=-1, keepdims=True) + epsilon)
    scaled = source * inverse
    upward = incoming * gain_vec
    return inverse * (upward - scaled * jnp.mean(upward * scaled, axis=-1, keepdims=True))


def matrix_product(first_op, second_op):
    return jnp.dot(first_op, second_op, preferred_element_type=jnp.float32)


def multiply_by_transpose(first_op, second_op):
    return lax.dot_general(
        first_op, second_op, (((1,), (1,)), ((), ())), preferred_element_type=jnp.float32
    )


def transpose_multiply(first_op, second_op):
    return lax.dot_general(
        first_op, second_op, (((0,), (0,)), ((), ())), preferred_element_type=jnp.float32
    )


def window_mask(query_segs, key_codes):
    query_count = query_segs.shape[0]
    key_total = key_codes.shape[0]
    distance = (key_total - query_count + jnp.arange(query_count))[:, None] - jnp.arange(key_total)[
        None, :
    ]
    same_doc = key_codes[None, :] == query_segs[:, None] + 1
    return (distance == 0) | (distance > 0) & (distance < WINDOW) & same_doc


def on_device(
    tokens,
    output_gradient,
    document_index,
    real_token_count,
    input_norm_gain,
    query_norm_gain,
    key_norm_gain,
    output_norm_gain,
    query_projection,
    key_projection,
    value_projection,
    output_projection,
    adapter_down_maps,
    adapter_query_up,
    adapter_key_up,
    adapter_value_up,
    adapter_output_down,
    adapter_output_up,
):
    row_count, model_width = tokens.shape
    shard_len = document_index.shape[0]
    head_dim = key_projection.shape[1]
    adapter_product = adapter_key_up.shape[0]
    heads_here = query_projection.shape[1] // head_dim
    ctx_size = lax.axis_size("ctx")
    tp_index = lax.axis_index("tp")
    slice_width = model_width // lax.axis_size("tp")
    reach_shards = WINDOW // shard_len
    send_count = min(reach_shards, ctx_size - 1)
    tok_float = tokens.astype(jnp.float32)
    normed_rows = norm_rows(tok_float, input_norm_gain).astype(jnp.bfloat16)
    normalized_input = lax.all_gather(normed_rows, "tp", axis=0, tiled=True)
    middle_list = matrix_product(normalized_input, adapter_down_maps).astype(jnp.bfloat16)
    middle_query = middle_list[:, :adapter_product]
    middle_key = middle_list[:, adapter_product : 2 * adapter_product]
    middle_value = middle_list[:, 2 * adapter_product :]
    query_before_norm = matrix_product(
        normalized_input, query_projection
    ) + adapter_scale * matrix_product(middle_query, adapter_query_up)
    key_before_norm = matrix_product(
        normalized_input, key_projection
    ) + adapter_scale * matrix_product(middle_key, adapter_key_up)
    value_before_norm = matrix_product(
        normalized_input, value_projection
    ) + adapter_scale * matrix_product(middle_value, adapter_value_up)
    query_heads = query_before_norm.reshape(shard_len, heads_here, head_dim)
    query_normed = norm_rows(query_heads, query_norm_gain).astype(jnp.bfloat16)
    key_normed = norm_rows(key_before_norm, key_norm_gain).astype(jnp.bfloat16)
    value_cast = value_before_norm.astype(jnp.bfloat16)
    positions = jnp.arange(shard_len)
    is_valid = positions < real_token_count[0]
    valid_rows = is_valid.astype(jnp.float32)
    local_codes = jnp.where(is_valid, document_index + 1, 0)
    local_pair = jnp.concatenate([key_normed, value_cast], axis=1)
    received = []
    for hop_index in range(1, send_count + 1):
        received.append(passed_along((local_pair, local_codes), "ctx", hop_index))
    missing = reach_shards - send_count
    blank_pair = jnp.zeros_like(local_pair)
    blank_codes = jnp.zeros_like(local_codes)
    earlier = [(blank_pair, blank_codes)] * missing + list(reversed(received))
    key_pairs = jnp.concatenate([entry[0] for entry in earlier] + [local_pair], axis=0)
    key_codes_all = jnp.concatenate([entry[1] for entry in earlier] + [local_codes], axis=0)
    keys_all = key_pairs[:, :head_dim]
    values_all = key_pairs[:, head_dim:]
    allowed = window_mask(document_index, key_codes_all)
    scores = (
        jnp.einsum("thd,sd->hts", query_normed, keys_all, preferred_element_type=jnp.float32)
        * score_scale
    )
    weights = jnp.where(allowed[None], jnp.exp(scores), 0.0)
    attn_probs = weights / jnp.sum(weights, axis=-1, keepdims=True)
    probs_cast = attn_probs.astype(jnp.bfloat16)
    attention_result = jnp.einsum(
        "hts,sd->thd", probs_cast, values_all, preferred_element_type=jnp.float32
    )
    attention_result = (
        (attention_result * valid_rows[:, None, None])
        .astype(jnp.bfloat16)
        .reshape(shard_len, heads_here * head_dim)
    )
    part_out = matrix_product(attention_result, output_projection)
    partial_middle = matrix_product(attention_result, adapter_output_down)
    output_total, mid_sum = (
        lax.psum_scatter(
            part_out.astype(jnp.bfloat16), "tp", scatter_dimension=0, tiled=True
        ).astype(jnp.float32),
        lax.psum_scatter(
            partial_middle.astype(jnp.bfloat16), "tp", scatter_dimension=0, tiled=True
        ).astype(jnp.float32),
    )
    middle_output = mid_sum.astype(jnp.bfloat16)
    apply_prenorm = output_total + adapter_scale * matrix_product(middle_output, adapter_output_up)
    layer_out = norm_rows(apply_prenorm, output_norm_gain).astype(jnp.bfloat16)
    prenorm_gradient = norm_back(
        apply_prenorm, output_norm_gain, output_gradient.astype(jnp.float32)
    ).astype(jnp.bfloat16)
    middle_output_gradient = (
        adapter_scale * multiply_by_transpose(prenorm_gradient, adapter_output_up)
    ).astype(jnp.bfloat16)
    complete_gradient, middle_complete_gradient, middle_complete = (
        lax.all_gather(prenorm_gradient, "tp", axis=0, tiled=True),
        lax.all_gather(middle_output_gradient, "tp", axis=0, tiled=True),
        lax.all_gather(middle_output, "tp", axis=0, tiled=True),
    )
    gradient_portion = lax.dynamic_slice_in_dim(
        complete_gradient, tp_index * slice_width, slice_width, 1
    )
    output_up_contribution = adapter_scale * transpose_multiply(middle_complete, gradient_portion)
    attention_gradient = multiply_by_transpose(
        complete_gradient, output_projection
    ) + multiply_by_transpose(middle_complete_gradient, adapter_output_down)
    attention_gradient = (attention_gradient * valid_rows[:, None]).astype(jnp.bfloat16)
    down_out_term = transpose_multiply(attention_result, middle_complete_gradient)
    grad_heads = attention_gradient.reshape(shard_len, heads_here, head_dim)
    grad_probs = jnp.einsum(
        "thd,sd->hts", grad_heads, values_all, preferred_element_type=jnp.float32
    )
    inner_sum = jnp.sum(attn_probs * grad_probs, axis=-1, keepdims=True)
    grad_scores = (attn_probs * (grad_probs - inner_sum) * score_scale).astype(jnp.bfloat16)
    grad_query = jnp.einsum(
        "hts,sd->thd", grad_scores, keys_all, preferred_element_type=jnp.float32
    )
    grad_keys = jnp.einsum(
        "hts,thd->sd", grad_scores, query_normed, preferred_element_type=jnp.float32
    )
    grad_values = jnp.einsum(
        "hts,thd->sd", probs_cast, grad_heads, preferred_element_type=jnp.float32
    )
    grad_pairs = jnp.concatenate([grad_keys, grad_values], axis=1)
    own_grads = grad_pairs[reach_shards * shard_len :]
    for hop_index in range(1, send_count + 1):
        own_grads = own_grads + passed_along(
            grad_pairs[
                (reach_shards - hop_index) * shard_len : (reach_shards - hop_index + 1) * shard_len
            ].astype(jnp.bfloat16),
            "ctx",
            -hop_index,
        ).astype(jnp.float32)
    query_prenorm_gradient = (
        norm_back(query_heads, query_norm_gain, grad_query)
        .reshape(shard_len, heads_here * head_dim)
        .astype(jnp.bfloat16)
    )
    key_prenorm_gradient = norm_back(
        key_before_norm, key_norm_gain, own_grads[:, :head_dim]
    ).astype(jnp.bfloat16)
    value_prenorm_gradient = own_grads[:, head_dim:].astype(jnp.bfloat16)
    query_up_contribution = adapter_scale * transpose_multiply(middle_query, query_prenorm_gradient)
    key_up_contribution = adapter_scale * transpose_multiply(middle_key, key_prenorm_gradient)
    value_up_contribution = adapter_scale * transpose_multiply(middle_value, value_prenorm_gradient)
    middle_gradients = jnp.concatenate(
        [
            adapter_scale * multiply_by_transpose(query_prenorm_gradient, adapter_query_up),
            adapter_scale * multiply_by_transpose(key_prenorm_gradient, adapter_key_up),
            adapter_scale * multiply_by_transpose(value_prenorm_gradient, adapter_value_up),
        ],
        axis=1,
    ).astype(jnp.bfloat16)
    grad_normed = (
        multiply_by_transpose(query_prenorm_gradient, query_projection)
        + multiply_by_transpose(key_prenorm_gradient, key_projection)
        + multiply_by_transpose(value_prenorm_gradient, value_projection)
        + multiply_by_transpose(middle_gradients, adapter_down_maps)
    )
    grad_normed_rows = lax.psum_scatter(
        grad_normed.astype(jnp.bfloat16), "tp", scatter_dimension=0, tiled=True
    ).astype(jnp.float32)
    grad_in = norm_back(tok_float, input_norm_gain, grad_normed_rows).astype(jnp.bfloat16)
    down_term = lax.psum_scatter(
        transpose_multiply(normalized_input, middle_gradients).astype(jnp.bfloat16),
        "tp",
        scatter_dimension=0,
        tiled=True,
    )
    adapter_totals = (
        lax.psum(down_term, "ctx").astype(jnp.float32),
        lax.psum(query_up_contribution.astype(jnp.bfloat16), "ctx").astype(jnp.float32),
        lax.psum(key_up_contribution.astype(jnp.bfloat16), "ctx").astype(jnp.float32),
        lax.psum(value_up_contribution.astype(jnp.bfloat16), "ctx").astype(jnp.float32),
        lax.psum(down_out_term.astype(jnp.bfloat16), "ctx").astype(jnp.float32),
        lax.psum(output_up_contribution.astype(jnp.bfloat16), "ctx").astype(jnp.float32),
    )
    return (
        layer_out,
        grad_in,
        adapter_totals[0],
        adapter_totals[1],
        adapter_totals[2],
        adapter_totals[3],
        adapter_totals[4],
        adapter_totals[5],
    )


def solution(mesh):
    in_specs = (
        P(("groups", "ctx", "tp"), None),
        P(("groups", "ctx", "tp"), None),
        P(("groups", "ctx")),
        P(("groups", "ctx")),
        P(),
        P(),
        P(),
        P(),
        P(None, "tp"),
        P(None, "tp"),
        P(None, "tp"),
        P("tp", None),
        P(),
        P(None, "tp"),
        P(None, "tp"),
        P(None, "tp"),
        P("tp", None),
        P(),
    )
    out_specs = (
        P(("groups", "ctx", "tp"), None),
        P(("groups", "ctx", "tp"), None),
        P(("groups", "tp"), None),
        P("groups", "tp"),
        P("groups", "tp"),
        P("groups", "tp"),
        P(("groups", "tp"), None),
        P("groups", "tp"),
    )
    return jax.shard_map(
        on_device, mesh=mesh, in_specs=in_specs, out_specs=out_specs, check_vma=False
    )
```

profile of v0, /device:TPU:0, one launch (start us, length us, event | category | flops | bytes accessed | tf_op | source)
XLA Modules:
  0.0 319.8 jit_solution(16461796081767223556)
XLA Ops:
  9.2 2.2 fusion.21
  12.2 5.9 %collective-permute-start.4 = (s32[256]{0:T(256)S(1)}, s32[256]{0:T(256)S(1)}, u32[]{:S(2)}, u32[]{:S(2)}) collective-permute-start(s32[256]{0:T(256)S(1)} %get-tuple-element.19), channel_id=1, source_target_pairs={{0,8},{2,10},{4,12},{6,14},{1,9},{3,11},{5,13},{7,15},{16,24},{18,... | collective-permute-start | bytes 3080 | tf_op jit(solution)/shard_map/ppermute | solution.py:17
  18.1 4.4 %collective-permute-start.5 = (s32[256]{0:T(256)S(1)}, s32[256]{0:T(256)S(1)}, u32[]{:S(2)}, u32[]{:S(2)}) collective-permute-start(s32[256]{0:T(256)S(1)} %get-tuple-element.19), channel_id=1, source_target_pairs={{0,6},{2,8},{4,10},{6,12},{8,14},{1,7},{3,9},{5,11},{7,13},{9,15},... | collective-permute-start | bytes 3080 | tf_op jit(solution)/shard_map/ppermute | solution.py:17
  23.8 3.1 collective-permute-start.7
  33.5 3.9 %collective-permute-start = (bf16[256,256]{0,1:T(8,128)(2,1)S(1)}, bf16[256,256]{0,1:T(8,128)(2,1)S(1)}, u32[]{:S(2)}, u32[]{:S(2)}) collective-permute-start(bf16[256,256]{0,1:T(8,128)(2,1)S(1)} %pad_maximum_fusion.1), channel_id=1, source_target_pairs={{0,8},{2,10},{4,12},{6,14},{1,9},{3,11},{5,13},{7,15},{16,24},{18,... | collective-permute-start | bytes 393224 | tf_op jit(solution)/shard_map/ppermute | solution.py:17
  40.5 2.8 collective-permute-start.3
  47.9 3.4 %fusion.31 = f32[2,256,1280]{1,2,0:T(8,128)} fusion(pred[256,1280]{0,1:T(8,128)(4,1)S(1)} %copy-done.21, bf16[1280,256]{0,1:T(8,128)(2,1)} %constant_dynamic-update-slice_fusion, f32[256,256]{0,1:T(8,128)S(1)} %get-tuple-element.24, f32[128]{0:T(128)S(1)} %copy-done.43, f32[256,2]{0,1:T(2,128)S(1)} %add_rsqrt_fusion), kind=kOutput, calls=%fused_computation.49 | convolution fusion | flops 169936640 | bytes 3541504 | tf_op jit(solution)/shard_map/div | solution.py:130
  51.3 2.2 fusion.46
  54.5 3.0 convolution_convert_fusion
  57.6 8.8 %reduce-scatter.13.cloned.1.call-done = bf16[128,16]{1,0:T(8,128)(2,1)} async-done(((bf16[256,16]{1,0:T(8,128)(2,1)}), bf16[128,16]{1,0:T(8,128)(2,1)}) %reduce-scatter.13.cloned.1.call-update) | async-done | bytes 4112
  66.4 12.3 %reduce-scatter.9.cloned.1.call-done = bf16[128,2688]{1,0:T(8,128)(2,1)} async-done(((bf16[256,2688]{1,0:T(8,128)(2,1)}), bf16[128,2688]{1,0:T(8,128)(2,1)}) %reduce-scatter.9.cloned.1.call-update) | async-done | bytes 688144 | tf_op jit(solution)/shard_map/reduce_scatter | solution.py:143
  89.1 4.0 %all-gather.5.cloned.1.call-done = bf16[256,2688]{1,0:T(8,128)(2,1)} async-done(((bf16[128,2688]{1,0:T(8,128)(2,1)}), bf16[256,2688]{1,0:T(8,128)(2,1)}) %all-gather.5.cloned.1.call-update) | async-done | bytes 1376272 | tf_op jit(solution)/shard_map/all_gather | solution.py:160
  93.1 2.3 fusion.45
  95.4 3.2 convolution_bitcast_fusion
  99.3 5.7 %multiply_reduce_fusion.3 = (f32[256,2]{0,1:T(2,128)S(1)}, f32[256,2,128]{0,2,1:T(8,128)}) fusion(f32[256,256]{0,1:T(8,128)} %copy-done.18, f32[256,2]{0,1:T(2,128)S(1)} %copy-done.37, f32[128]{0:T(128)S(1)} %copy-done.44, f32[2,256,1280]{1,2,0:T(8,128)} %fusion.31, f32[2,256,1280]{1,2,0:T(8,128)} %convolution_bitcast_fusion, ...), kind=kOutput, calls=%fused_computation.99 | convolution fusion | flops 171312384 | bytes 11342336 | tf_op jit(solution)/shard_map/hts,sd->thd/dot_general | solution.py:179
  105.0 5.7 %convolution_bitcast_fusion.2 = f32[1280,128]{0,1:T(8,128)} fusion(f32[2,256,1280]{1,2,0:T(8,128)} %fusion.31, f32[2,256,1280]{1,2,0:T(8,128)} %convolution_bitcast_fusion, f32[256,256]{0,1:T(8,128)} %copy-done.18, f32[128]{0:T(128)S(1)} %copy-done.44, f32[256,2]{0,1:T(2,128)S(1)} %copy-done.37), kind=kOutput, calls=%fused_computation.19 | convolution fusion | flops 171247360 | bytes 6162944 | tf_op jit(solution)/shard_map/hts,thd->sd/dot_general | solution.py:182
  112.7 2.1 fusion.83
  123.7 10.1 %collective-permute-done.11 = bf16[256,256]{0,1:T(8,128)(2,1)S(1)} collective-permute-done((bf16[256,256]{0,1:T(8,128)(2,1)S(1)}, bf16[256,256]{0,1:T(8,128)(2,1)S(1)}, u32[]{:S(2)}, u32[]{:S(2)}) %collective-permute-start.11) | collective-permute-done | bytes 131104 | tf_op jit(solution)/shard_map/ppermute | solution.py:17
  139.8 3.9 %convolution_add_fusion.1 = f32[256,2688]{1,0:T(8,128)} fusion(f32[256,2688]{1,0:T(8,128)} %fusion.83, bf16[256,128]{0,1:T(8,128)(2,1)S(1)} %multiply_convert_fusion.4, bf16[2688,128]{1,0:T(8,128)(2,1)S(1)} %copy-done.8), kind=kOutput, calls=%fused_computation.2 | convolution fusion | flops 176848896 | bytes 6258688 | tf_op jit(solution)/shard_map/dot_general | solution.py:37
  145.9 3.6 %reduce-scatter.15.cloned.1.call-done = bf16[1344,48]{1,0:T(8,128)(2,1)} async-done(((bf16[2688,48]{1,0:T(8,128)(2,1)}), bf16[1344,48]{1,0:T(8,128)(2,1)}) %reduce-scatter.15.cloned.1.call-update) | async-done | bytes 129040
  151.4 4.3 %fusion.2 = bf16[256,2688]{1,0:T(8,128)(2,1)} fusion(f32[256,2688]{1,0:T(8,128)} %fusion.63, f32[256,2688]{1,0:T(8,128)} %convolution_add_fusion.1, bf16[2688,128]{1,0:T(8,128)(2,1)S(1)} %copy-done.12, f32[256,256]{0,1:T(8,128)S(1)} %copy-done.5), kind=kOutput, calls=%fused_computation.5 | convolution fusion | flops 178225152 | bytes 7634944 | tf_op jit(solution)/shard_map/dot_general | solution.py:37
  155.7 70.0 %all-reduce.6.cloned.1.call-done = (bf16[16,256]{1,0:T(8,128)(2,1)}, bf16[16,128]{1,0:T(8,128)(2,1)}, bf16[16,128]{1,0:T(8,128)(2,1)}, bf16[256,16]{0,1:T(8,128)(2,1)}, bf16[16,1344]{1,0:T(8,128)(2,1)}) async-done(((bf16[16,256]{1,0:T(8,128)(2,1)}, bf16[16,128]{1,0:T(8,128)(2,1)}, bf16[16,128]{1,0:T(8,128)(2,1)}, bf16[256,16]{0,1:T(8,128)(2,1)}, bf16[16,1344]{1,0:T(8,128)(2,1)}), ...) | async-done | bytes 67600 | tf_op jit(solution)/shard_map/psum | solution.py:236
  232.3 67.5 %all-reduce.4.cloned.1.call-done = bf16[1344,48]{0,1:T(8,128)(2,1)} async-done(((bf16[1344,48]{0,1:T(8,128)(2,1)}), bf16[1344,48]{0,1:T(8,128)(2,1)}) %all-reduce.4.cloned.1.call-update) | async-done | bytes 129040 | tf_op jit(solution)/shard_map/psum | solution.py:235
  301.4 8.7 %reduce-scatter.11.cloned.1.call-done = bf16[128,2688]{1,0:T(8,128)(2,1)} async-done(((bf16[256,2688]{1,0:T(8,128)(2,1)}), bf16[128,2688]{1,0:T(8,128)(2,1)}) %reduce-scatter.11.cloned.1.call-update) | async-done | bytes 688144 | tf_op jit(solution)/shard_map/reduce_scatter | solution.py:224
  (195 shorter events, 61.1 us)
Async XLA Ops:
  7.2 36.4 %copy-start = (bf16[2688,256]{1,0:T(8,128)(2,1)S(1)}, bf16[2688,256]{1,0:T(8,128)(2,1)}, u32[]{:S(2)}) copy-start(bf16[2688,256]{1,0:T(8,128)(2,1)} %param.26) | copy-start | bytes 4128772
  7.2 22.3 %all-gather.3.cloned.1.call-start = ((), (), s32[]{:S(2)}) async-start(), calls=%async_computation.4 | async-start | bytes 2064384 | tf_op jit(solution)/shard_map/all_gather | solution.py:90
  11.4 55.0 %reduce-scatter.13.cloned.1.call-start = ((), (), s32[]{:S(2)}) async-start(), calls=%async_computation.9 | async-start | bytes 98304
  12.2 14.8 %collective-permute-start.4 = (s32[256]{0:T(256)S(1)}, s32[256]{0:T(256)S(1)}, u32[]{:S(2)}, u32[]{:S(2)}) collective-permute-start(s32[256]{0:T(256)S(1)} %get-tuple-element.19), channel_id=1, source_target_pairs={{0,8},{2,10},{4,12},{6,14},{1,9},{3,11},{5,13},{7,15},{16,24},{18,... | collective-permute-start | bytes 3080 | tf_op jit(solution)/shard_map/ppermute | solution.py:17
  18.1 8.9 %collective-permute-start.5 = (s32[256]{0:T(256)S(1)}, s32[256]{0:T(256)S(1)}, u32[]{:S(2)}, u32[]{:S(2)}) collective-permute-start(s32[256]{0:T(256)S(1)} %get-tuple-element.19), channel_id=1, source_target_pairs={{0,6},{2,8},{4,10},{6,12},{8,14},{1,7},{3,9},{5,11},{7,13},{9,15},... | collective-permute-start | bytes 3080 | tf_op jit(solution)/shard_map/ppermute | solution.py:17
  22.5 4.5 %collective-permute-start.6 = (s32[256]{0:T(256)S(1)}, s32[256]{0:T(256)S(1)}, u32[]{:S(2)}, u32[]{:S(2)}) collective-permute-start(s32[256]{0:T(256)S(1)} %get-tuple-element.19), channel_id=1, source_target_pairs={{0,4},{2,6},{4,8},{6,10},{8,12},{10,14},{1,5},{3,7},{5,9},{7,11},{... | collective-permute-start | bytes 3080 | tf_op jit(solution)/shard_map/ppermute | solution.py:17
  23.8 4.4 %collective-permute-start.7 = (s32[256]{0:T(256)S(1)}, s32[256]{0:T(256)S(1)}, u32[]{:S(2)}, u32[]{:S(2)}) collective-permute-start(s32[256]{0:T(256)S(1)} %get-tuple-element.19), channel_id=1, source_target_pairs={{0,2},{2,4},{4,6},{6,8},{8,10},{10,12},{12,14},{1,3},{3,5},{5,7},{... | collective-permute-start | bytes 3080 | tf_op jit(solution)/shard_map/ppermute | solution.py:17
  33.5 10.9 %collective-permute-start = (bf16[256,256]{0,1:T(8,128)(2,1)S(1)}, bf16[256,256]{0,1:T(8,128)(2,1)S(1)}, u32[]{:S(2)}, u32[]{:S(2)}) collective-permute-start(bf16[256,256]{0,1:T(8,128)(2,1)S(1)} %pad_maximum_fusion.1), channel_id=1, source_target_pairs={{0,8},{2,10},{4,12},{6,14},{1,9},{3,11},{5,13},{7,15},{16,24},{18,... | collective-permute-start | bytes 393224 | tf_op jit(solution)/shard_map/ppermute | solution.py:17
  37.4 7.7 %collective-permute-start.1 = (bf16[256,256]{0,1:T(8,128)(2,1)S(1)}, bf16[256,256]{0,1:T(8,128)(2,1)S(1)}, u32[]{:S(2)}, u32[]{:S(2)}) collective-permute-start(bf16[256,256]{0,1:T(8,128)(2,1)S(1)} %pad_maximum_fusion.1), channel_id=1, source_target_pairs={{0,6},{2,8},{4,10},{6,12},{8,14},{1,7},{3,9},{5,11},{7,13},{9,15},... | collective-permute-start | bytes 393224 | tf_op jit(solution)/shard_map/ppermute | solution.py:17
  38.7 7.1 %collective-permute-start.2 = (bf16[256,256]{0,1:T(8,128)(2,1)S(1)}, bf16[256,256]{0,1:T(8,128)(2,1)S(1)}, u32[]{:S(2)}, u32[]{:S(2)}) collective-permute-start(bf16[256,256]{0,1:T(8,128)(2,1)S(1)} %pad_maximum_fusion.1), channel_id=1, source_target_pairs={{0,4},{2,6},{4,8},{6,10},{8,12},{10,14},{1,5},{3,7},{5,9},{7,11},{... | collective-permute-start | bytes 393224 | tf_op jit(solution)/shard_map/ppermute | solution.py:17
  40.5 5.9 %collective-permute-start.3 = (bf16[256,256]{0,1:T(8,128)(2,1)S(1)}, bf16[256,256]{0,1:T(8,128)(2,1)S(1)}, u32[]{:S(2)}, u32[]{:S(2)}) collective-permute-start(bf16[256,256]{0,1:T(8,128)(2,1)S(1)} %pad_maximum_fusion.1), channel_id=1, source_target_pairs={{0,2},{2,4},{4,6},{6,8},{8,10},{10,12},{12,14},{1,3},{3,5},{5,7},{... | collective-permute-start | bytes 393224 | tf_op jit(solution)/shard_map/ppermute | solution.py:17
  54.4 24.2 %reduce-scatter.9.cloned.1.call-start = ((), (), s32[]{:S(2)}) async-start(), calls=%async_computation.5 | async-start | bytes 2064384 | tf_op jit(solution)/shard_map/reduce_scatter | solution.py:143
  57.5 35.6 %all-gather.5.cloned.1.call-start = ((), (), s32[]{:S(2)}) async-start(), calls=%async_computation.6 | async-start | bytes 2064384 | tf_op jit(solution)/shard_map/all_gather | solution.py:160
  82.2 67.3 %reduce-scatter.15.cloned.1.call-start = ((), (), s32[]{:S(2)}) async-start(), calls=%async_computation.10 | async-start | bytes 1032192
  115.0 8.7 %collective-permute-start.10 = (bf16[256,256]{0,1:T(8,128)(2,1)S(1)}, bf16[256,256]{0,1:T(8,128)(2,1)S(1)}, u32[]{:S(2)}, u32[]{:S(2)}) collective-permute-start(bf16[256,256]{0,1:T(8,128)(2,1)S(1)} %get-tuple-element.17), channel_id=1, source_target_pairs={{6,0},{8,2},{10,4},{12,6},{14,8},{7,1},{9,3},{11,5},{13,7},{15,9},... | collective-permute-start | bytes 393224 | tf_op jit(solution)/shard_map/ppermute | solution.py:17
  116.4 17.4 %collective-permute-start.11 = (bf16[256,256]{0,1:T(8,128)(2,1)S(1)}, bf16[256,256]{0,1:T(8,128)(2,1)S(1)}, u32[]{:S(2)}, u32[]{:S(2)}) collective-permute-start(bf16[256,256]{0,1:T(8,128)(2,1)S(1)} %get-tuple-element.16), channel_id=1, source_target_pairs={{8,0},{10,2},{12,4},{14,6},{9,1},{11,3},{13,5},{15,7},{24,16},{26,... | collective-permute-start | bytes 393224 | tf_op jit(solution)/shard_map/ppermute | solution.py:17
  117.7 16.1 %collective-permute-start.8 = (bf16[256,256]{0,1:T(8,128)(2,1)S(1)}, bf16[256,256]{0,1:T(8,128)(2,1)S(1)}, u32[]{:S(2)}, u32[]{:S(2)}) collective-permute-start(bf16[256,256]{0,1:T(8,128)(2,1)S(1)} %get-tuple-element.15), channel_id=1, source_target_pairs={{2,0},{4,2},{6,4},{8,6},{10,8},{12,10},{14,12},{3,1},{5,3},{7,5},{... | collective-permute-start | bytes 393224 | tf_op jit(solution)/shard_map/ppermute | solution.py:17
  119.0 14.8 %collective-permute-start.9 = (bf16[256,256]{0,1:T(8,128)(2,1)S(1)}, bf16[256,256]{0,1:T(8,128)(2,1)S(1)}, u32[]{:S(2)}, u32[]{:S(2)}) collective-permute-start(bf16[256,256]{0,1:T(8,128)(2,1)S(1)} %get-tuple-element.18), channel_id=1, source_target_pairs={{4,0},{6,2},{8,4},{10,6},{12,8},{14,10},{5,1},{7,3},{9,5},{11,7},{... | collective-permute-start | bytes 393224 | tf_op jit(solution)/shard_map/ppermute | solution.py:17
  139.0 86.7 %all-reduce.6.cloned.1.call-start = ((), (), s32[]{:S(2)}) async-start(), calls=%async_computation.11 | async-start | bytes 139264 | tf_op jit(solution)/shard_map/psum | solution.py:236
  143.7 156.0 %all-reduce.4.cloned.1.call-start = ((), (), s32[]{:S(2)}) async-start(), calls=%async_computation.8 | async-start | bytes 270336 | tf_op jit(solution)/shard_map/psum | solution.py:235
  151.3 158.8 %reduce-scatter.11.cloned.1.call-start = ((), (), s32[]{:S(2)}) async-start(), calls=%async_computation.7 | async-start | bytes 2064384 | tf_op jit(solution)/shard_map/reduce_scatter | solution.py:224
  155.6 154.5 %copy-start.2 = (bf16[128,2688]{1,0:T(8,128)(2,1)S(1)}, bf16[128,2688]{1,0:T(8,128)(2,1)}, u32[]{:S(2)}) copy-start(bf16[128,2688]{1,0:T(8,128)(2,1)} %param.18) | copy-start | bytes 2064388
  155.6 154.5 %copy-start.22 = (f32[2688]{0:T(1024)S(1)}, f32[2688]{0:T(1024)}, u32[]{:S(2)}) copy-start(f32[2688]{0:T(1024)} %param.22) | copy-start | bytes 32260
  155.6 154.5 %copy-start.39 = (f32[128]{0:T(128)S(1)}, f32[128]{0:T(128)}, u32[]{:S(2)}) copy-start(f32[128]{0:T(128)} %copy-done.38) | copy-start | bytes 1540
  (41 other events, 289.0 us)
Sparse Core Ops, SparseCore 0:
  11.5 12.2 all-gather.2
  54.6 11.7 reduce-scatter.12
  68.6 9.9 reduce-scatter.8
  82.3 10.7 all-gather.4
  139.1 10.3 reduce-scatter.14
  154.5 71.0 all-reduce.5
  230.0 69.7 all-reduce.3
  302.0 8.0 reduce-scatter.10
where the time goes:
time: 321 us; the launch traced here: 320 us
  waiting for transfers between devices  188 us (59%)
  matrix products  51.8 us (16%)
  starting transfers between devices  30.5 us (10%)
  other arithmetic  20.1 us (6%)
  between operations  15.6 us (5%)
  local copies, waits for them, and re-layouts  9.76 us (3%)
  blocking collectives  3.64 us (1%)
    psum x1, waiting for transfers between devices, on_device(): lax.psum(query_up_contribution.astype(jnp.bfloat16), 'ctx')  70 us
    psum x1, waiting for transfers between devices, on_device(): lax.psum(down_term, 'ctx').astype(jnp.float32)  67.5 us
    ppermute x12, starting transfers between devices, passed_along(): lax.ppermute(value, axis, [(source, source + steps) for source in range(l...  30.2 us
    dot_general x10, matrix products, multiply_by_transpose(): lax.dot_general(first_op, second_op, (((1,), (1,)), ((), ())), preferred_...  16.7 us
    ppermute x12, waiting for transfers between devices, passed_along(): lax.ppermute(value, axis, [(source, source + steps) for source in range(l...  13.4 us
    unnamed x10, waiting for transfers between devices  12.5 us
    reduce_scatter x1, waiting for transfers between devices, on_device(): lax.psum_scatter(part_out.astype(jnp.bfloat16), 'tp', scatter_dimension=0...  12.3 us
    unnamed x102, local copies, waits for them, and re-layouts  9.72 us
  transfers between devices with their start and end apart: 20, of which 10 were waited for; matrix products, arithmetic and copies ran while one was open for 10% of the time, Pallas kernels for 0%

commit v1 on v0

--- a/solution.py
+++ b/solution.py
@@ -53,6 +53,22 @@
     ]
     same_doc = key_codes[None, :] == query_segs[:, None] + 1
     return (distance == 0) | (distance > 0) & (distance < WINDOW) & same_doc
+
+
+def ctx_sum(parts):
+    count = lax.axis_size("ctx")
+    if count & (count - 1):
+        return [lax.psum(p.astype(jnp.bfloat16), "ctx").astype(jnp.float32) for p in parts]
+    flat = jnp.concatenate([p.astype(jnp.float32).reshape(-1) for p in parts])
+    step = 1
+    while step < count:
+        flat = flat + lax.ppermute(flat, "ctx", [(i, i ^ step) for i in range(count)])
+        step *= 2
+    results, offset = [], 0
+    for p in parts:
+        results.append(flat[offset : offset + p.size].reshape(p.shape))
+        offset += p.size
+    return results
 
 
 def on_device(
@@ -231,13 +247,15 @@
         scatter_dimension=0,
         tiled=True,
     )
-    adapter_totals = (
-        lax.psum(down_term, "ctx").astype(jnp.float32),
-        lax.psum(query_up_contribution.astype(jnp.bfloat16), "ctx").astype(jnp.float32),
-        lax.psum(key_up_contribution.astype(jnp.bfloat16), "ctx").astype(jnp.float32),
-        lax.psum(value_up_contribution.astype(jnp.bfloat16), "ctx").astype(jnp.float32),
-        lax.psum(down_out_term.astype(jnp.bfloat16), "ctx").astype(jnp.float32),
-        lax.psum(output_up_contribution.astype(jnp.bfloat16), "ctx").astype(jnp.float32),
+    adapter_totals = ctx_sum(
+        [
+            down_term,
+            query_up_contribution,
+            key_up_contribution,
+            value_up_contribution,
+            down_out_term,
+            output_up_contribution,
+        ]
     )
     return (
         layer_out,

time: 321 us -> 217 us (0.68)
  waiting for transfers between devices: 188 us -> 84 us
  starting transfers between devices: 30.5 us -> 38.4 us
  matrix products: 51.8 us -> 44.4 us
  other arithmetic: 20.1 us -> 13.2 us
  local copies, waits for them, and re-layouts: 9.76 us -> 16.5 us
    psum x2 -> x0, waiting for transfers between devices: 138 us -> none  [the longest x1 70 us: on_device(): lax.psum(query_up_contribution.astype(jnp.bfloat16), 'ctx')]
    ppermute x0 -> x3, waiting for transfers between devices: none -> 34.7 us  [ctx_sum(): lax.ppermute(flat, 'ctx', [(i, i ^ step) for i in range(count)])]
    reduce_scatter x1, waiting for transfers between devices: 8.71 us -> 0.01 us  [on_device(): lax.psum_scatter(grad_normed.astype(jnp.bfloat16), 'tp', scatter_dimensio...]
    convert_element_type x6 -> x0, other arithmetic: 8.22 us -> none  [the longest x1 1.63 us: on_device(): lax.psum(down_term, 'ctx').astype(jnp.float32)]
    ppermute x0 -> x3, starting transfers between devices: none -> 6.31 us  [ctx_sum(): lax.ppermute(flat, 'ctx', [(i, i ^ step) for i in range(count)])]
    dot_general x10, matrix products: 16.7 us -> 11.3 us  [multiply_by_transpose(): lax.dot_general(first_op, second_op, (((1,), (1,)), ((), ())), preferred_...]
    unnamed x10 -> x8, waiting for transfers between devices: 12.5 us -> 17.1 us
    reshape x0 -> x5, local copies, waits for them, and re-layouts: none -> 3.63 us  [the longest x4 2.91 us: ctx_sum(): flat = jnp.concatenate([p.astype(jnp.float32).reshape(-1) for p in parts])]
  transfers between devices with their start and end apart: 20 -> 21, of which waited for: 10 -> 11; matrix products, arithmetic and copies ran while one was open for 10% -> 10% of each run, Pallas kernels for 0% -> 0%
where the time goes in v1:
time: 217 us; the launch traced here: 216 us
  waiting for transfers between devices  84 us (39%)
  matrix products  44.4 us (20%)
  starting transfers between devices  38.4 us (18%)
  local copies, waits for them, and re-layouts  16.5 us (8%)
  between operations  15.8 us (7%)
  other arithmetic  13.2 us (6%)
  blocking collectives  3.7 us (2%)
    ppermute x3, waiting for transfers between devices, ctx_sum(): lax.ppermute(flat, 'ctx', [(i, i ^ step) for i in range(count)])  34.7 us
    ppermute x12, starting transfers between devices, passed_along(): lax.ppermute(value, axis, [(source, source + steps) for source in range(l...  31.9 us
    unnamed x8, waiting for transfers between devices  17.1 us
    ppermute x12, waiting for transfers between devices, passed_along(): lax.ppermute(value, axis, [(source, source + steps) for source in range(l...  16.1 us
    reduce_scatter x1, waiting for transfers between devices, on_device(): lax.psum_scatter(part_out.astype(jnp.bfloat16), 'tp', scatter_dimension=0...  12.3 us
    unnamed x110, local copies, waits for them, and re-layouts  11.3 us
    dot_general x10, matrix products, multiply_by_transpose(): lax.dot_general(first_op, second_op, (((1,), (1,)), ((), ())), preferred_...  11.3 us
    dot_general x10, matrix products, matrix_product(): return jnp.dot(first_op, second_op, preferred_element_type=jnp.float32)  9.22 us
  transfers between devices with their start and end apart: 21, of which 11 were waited for; matrix products, arithmetic and copies ran while one was open for 10% of the time, Pallas kernels for 0%

profile of v1, /device:TPU:0, one launch (start us, length us, event | category | flops | bytes accessed | tf_op | source)
XLA Modules:
  0.0 216.0 jit_solution(17175077400922098512)
XLA Ops:
  8.7 2.2 %fusion.20 = bf16[128,2688]{1,0:T(8,128)(2,1)} fusion(bf16[128,2688]{1,0:T(8,128)(2,1)} %param.18, f32[2688]{0:T(1024)} %param.22, f32[128]{0:T(128)S(1)} %add_rsqrt_fusion.3), kind=kLoop, calls=%fused_computation.32 | loop fusion | flops 1376256 | bytes 1387520 | tf_op jit(solution)/shard_map/convert_element_type | solution.py:105
  11.7 4.8 %collective-permute-start.7 = (s32[256]{0:T(256)S(1)}, s32[256]{0:T(256)S(1)}, u32[]{:S(2)}, u32[]{:S(2)}) collective-permute-start(s32[256]{0:T(256)S(1)} %get-tuple-element.34), channel_id=1, source_target_pairs={{0,2},{2,4},{4,6},{6,8},{8,10},{10,12},{12,14},{1,3},{3,5},{5,7},{... | collective-permute-start | bytes 3080 | tf_op jit(solution)/shard_map/ppermute | solution.py:17
  16.5 3.5 %collective-permute-start.6 = (s32[256]{0:T(256)S(1)}, s32[256]{0:T(256)S(1)}, u32[]{:S(2)}, u32[]{:S(2)}) collective-permute-start(s32[256]{0:T(256)S(1)} %get-tuple-element.34), channel_id=1, source_target_pairs={{0,4},{2,6},{4,8},{6,10},{8,12},{10,14},{1,5},{3,7},{5,9},{7,11},{... | collective-permute-start | bytes 3080 | tf_op jit(solution)/shard_map/ppermute | solution.py:17
  20.0 4.5 %collective-permute-start.5 = (s32[256]{0:T(256)S(1)}, s32[256]{0:T(256)S(1)}, u32[]{:S(2)}, u32[]{:S(2)}) collective-permute-start(s32[256]{0:T(256)S(1)} %get-tuple-element.34), channel_id=1, source_target_pairs={{0,6},{2,8},{4,10},{6,12},{8,14},{1,7},{3,9},{5,11},{7,13},{9,15},... | collective-permute-start | bytes 3080 | tf_op jit(solution)/shard_map/ppermute | solution.py:17
  33.0 2.7 %collective-permute-start.3 = (bf16[256,256]{0,1:T(8,128)(2,1)S(1)}, bf16[256,256]{0,1:T(8,128)(2,1)S(1)}, u32[]{:S(2)}, u32[]{:S(2)}) collective-permute-start(bf16[256,256]{0,1:T(8,128)(2,1)S(1)} %pad_maximum_fusion.1), channel_id=1, source_target_pairs={{0,2},{2,4},{4,6},{6,8},{8,10},{10,12},{12,14},{1,3},{3,5},{5,7},{... | collective-permute-start | bytes 393224 | tf_op jit(solution)/shard_map/ppermute | solution.py:17
  35.8 2.8 %collective-permute-start.2 = (bf16[256,256]{0,1:T(8,128)(2,1)S(1)}, bf16[256,256]{0,1:T(8,128)(2,1)S(1)}, u32[]{:S(2)}, u32[]{:S(2)}) collective-permute-start(bf16[256,256]{0,1:T(8,128)(2,1)S(1)} %pad_maximum_fusion.1), channel_id=1, source_target_pairs={{0,4},{2,6},{4,8},{6,10},{8,12},{10,14},{1,5},{3,7},{5,9},{7,11},{... | collective-permute-start | bytes 393224 | tf_op jit(solution)/shard_map/ppermute | solution.py:17
  38.6 4.8 %collective-permute-start.1 = (bf16[256,256]{0,1:T(8,128)(2,1)S(1)}, bf16[256,256]{0,1:T(8,128)(2,1)S(1)}, u32[]{:S(2)}, u32[]{:S(2)}) collective-permute-start(bf16[256,256]{0,1:T(8,128)(2,1)S(1)} %pad_maximum_fusion.1), channel_id=1, source_target_pairs={{0,6},{2,8},{4,10},{6,12},{8,14},{1,7},{3,9},{5,11},{7,13},{9,15},... | collective-permute-start | bytes 393224 | tf_op jit(solution)/shard_map/ppermute | solution.py:17
  50.8 3.4 %fusion.30 = f32[2,256,1280]{1,2,0:T(8,128)} fusion(pred[256,1280]{0,1:T(8,128)(4,1)S(1)} %copy-done.22, bf16[1280,256]{0,1:T(8,128)(2,1)} %constant_dynamic-update-slice_fusion, f32[256,256]{0,1:T(8,128)S(1)} %get-tuple-element.39, f32[128]{0:T(128)S(1)} %copy-done.44, f32[256,2]{0,1:T(2,128)S(1)} %add_rsqrt_fusion), kind=kOutput, calls=%fused_computation.48 | convolution fusion | flops 169936640 | bytes 3541504 | tf_op jit(solution)/shard_map/div | solution.py:146
  54.2 2.2 %fusion.45 = bf16[128,2,256]{2,0,1:T(8,128)(2,1)S(1)} fusion(f32[2,256,1280]{1,2,0:T(8,128)} %fusion.30, bf16[1280,256]{0,1:T(8,128)(2,1)} %constant_dynamic-update-slice_fusion, f32[256]{0:T(256)S(1)} %fusion.71), kind=kOutput, calls=%fused_computation.64 | convolution fusion | flops 168558592 | bytes 3081216 | tf_op jit(solution)/shard_map/hts,sd->thd/dot_general | solution.py:148
  57.4 3.0 %convolution_convert_fusion = bf16[256,2688]{1,0:T(8,128)(2,1)} fusion(bf16[256,256]{0,1:T(8,128)(2,1)S(1)} %bitcast.105, bf16[256,2688]{1,0:T(8,128)(2,1)} %param.29), kind=kOutput, calls=%fused_computation.4 | convolution fusion | flops 353009664 | bytes 2883584 | tf_op jit(solution)/shard_map/dot_general | solution.py:33
  60.5 11.8 %reduce-scatter.13.cloned.1.call-done = bf16[128,16]{1,0:T(8,128)(2,1)} async-done(((bf16[256,16]{1,0:T(8,128)(2,1)}), bf16[128,16]{1,0:T(8,128)(2,1)}) %reduce-scatter.13.cloned.1.call-update) | async-done | bytes 4112
  72.3 12.3 %reduce-scatter.9.cloned.1.call-done = bf16[128,2688]{1,0:T(8,128)(2,1)} async-done(((bf16[256,2688]{1,0:T(8,128)(2,1)}), bf16[128,2688]{1,0:T(8,128)(2,1)}) %reduce-scatter.9.cloned.1.call-update) | async-done | bytes 688144 | tf_op jit(solution)/shard_map/reduce_scatter | solution.py:159
  95.2 3.8 %all-gather.5.cloned.1.call-done = bf16[256,2688]{1,0:T(8,128)(2,1)} async-done(((bf16[128,2688]{1,0:T(8,128)(2,1)}), bf16[256,2688]{1,0:T(8,128)(2,1)}) %all-gather.5.cloned.1.call-update) | async-done | bytes 1376272 | tf_op jit(solution)/shard_map/all_gather | solution.py:176
  99.0 2.5 %fusion.44 = bf16[256,256]{0,1:T(8,128)(2,1)S(1)} fusion(f32[256,256]{0,1:T(8,128)S(1)} %fusion.84, bf16[256,2688]{1,0:T(8,128)(2,1)} %all-gather.5.cloned.1.call-done, bf16[256,2688]{1,0:T(8,128)(2,1)} %param.29, f32[256]{0:T(256)S(1)} %fusion.71), kind=kOutput, calls=%fused_computation.63 | convolution fusion | flops 352518144 | bytes 3146752 | tf_op jit(solution)/shard_map/dot_general | solution.py:37
  102.1 3.0 %convolution_bitcast_fusion = f32[2,256,1280]{1,2,0:T(8,128)} fusion(bf16[256,2,128]{0,2,1:T(8,128)(2,1)S(1)} %bitcast.111, bf16[1280,256]{0,1:T(8,128)(2,1)} %constant_dynamic-update-slice_fusion), kind=kOutput, calls=%fused_computation.13 | convolution fusion | flops 167772160 | bytes 3080192 | tf_op jit(solution)/shard_map/thd,sd->hts/dot_general | solution.py:190
  105.2 5.7 %multiply_reduce_fusion.3 = (f32[256,2]{0,1:T(2,128)S(1)}, f32[256,2,128]{0,2,1:T(8,128)}) fusion(f32[256,256]{0,1:T(8,128)} %copy-done.18, f32[256,2]{0,1:T(2,128)S(1)} %add_rsqrt_fusion, f32[128]{0:T(128)S(1)} %copy-done.45, f32[2,256,1280]{1,2,0:T(8,128)} %fusion.30, f32[2,256,1280]{1,2,0:T(8,128)} %convolution_bitcast_fusion, ...), kind=kOutput, calls=%fused_computation.99 | convolution fusion | flops 171312384 | bytes 11342336 | tf_op jit(solution)/shard_map/hts,sd->thd/dot_general | solution.py:195
  110.8 5.7 %convolution_bitcast_fusion.2 = f32[1280,128]{0,1:T(8,128)} fusion(f32[2,256,1280]{1,2,0:T(8,128)} %fusion.30, f32[2,256,1280]{1,2,0:T(8,128)} %convolution_bitcast_fusion, f32[256,256]{0,1:T(8,128)} %copy-done.18, f32[128]{0:T(128)S(1)} %copy-done.45, f32[256,2]{0,1:T(2,128)S(1)} %add_rsqrt_fusion), kind=kOutput, calls=%fused_computation.19 | convolution fusion | flops 171247360 | bytes 6162944 | tf_op jit(solution)/shard_map/hts,thd->sd/dot_general | solution.py:198
  132.9 11.2 %collective-permute-done.11 = bf16[256,256]{0,1:T(8,128)(2,1)S(1)} collective-permute-done((bf16[256,256]{0,1:T(8,128)(2,1)S(1)}, bf16[256,256]{0,1:T(8,128)(2,1)S(1)}, u32[]{:S(2)}, u32[]{:S(2)}) %collective-permute-start.11) | collective-permute-done | bytes 131104 | tf_op jit(solution)/shard_map/ppermute | solution.py:17
  148.4 2.4 %convolution_add_fusion.1 = f32[256,2688]{1,0:T(8,128)S(1)} fusion(f32[256,2688]{1,0:T(8,128)} %fusion.85, bf16[256,128]{0,1:T(8,128)(2,1)S(1)} %multiply_convert_fusion.4, bf16[2688,128]{1,0:T(8,128)(2,1)S(1)} %copy-done.8), kind=kOutput, calls=%fused_computation.2 | convolution fusion | flops 176848896 | bytes 6258688 | tf_op jit(solution)/shard_map/dot_general | solution.py:37
  153.7 5.1 %reduce-scatter.15.cloned.1.call-done = bf16[1344,48]{1,0:T(8,128)(2,1)} async-done(((bf16[2688,48]{1,0:T(8,128)(2,1)}), bf16[1344,48]{1,0:T(8,128)(2,1)}) %reduce-scatter.15.cloned.1.call-update) | async-done | bytes 129040
  162.8 9.6 %collective-permute-done.12 = f32[98304]{0:T(1024)S(1)} collective-permute-done((f32[98304]{0:T(1024)S(1)}, f32[98304]{0:T(1024)S(1)}, u32[]{:S(2)}, u32[]{:S(2)}) %collective-permute-start.12) | collective-permute-done | bytes 393248 | tf_op jit(solution)/shard_map/ppermute | solution.py:65
  174.2 8.8 %collective-permute-done.13 = f32[98304]{0:T(1024)S(1)} collective-permute-done((f32[98304]{0:T(1024)S(1)}, f32[98304]{0:T(1024)S(1)}, u32[]{:S(2)}, u32[]{:S(2)}) %collective-permute-start.13) | collective-permute-done | bytes 393248 | tf_op jit(solution)/shard_map/ppermute | solution.py:65
  183.1 2.7 %collective-permute-start.14 = (f32[98304]{0:T(1024)S(1)}, f32[98304]{0:T(1024)S(1)}, u32[]{:S(2)}, u32[]{:S(2)}) collective-permute-start(f32[98304]{0:T(1024)S(1)} %add.135), channel_id=1, source_target_pairs={{0,8},{2,10},{4,12},{6,14},{8,0},{10,2},{12,4},{14,6},{1,9},{3,11}... | collective-permute-start | bytes 1179656 | tf_op jit(solution)/shard_map/ppermute | solution.py:65
  185.8 16.3 %collective-permute-done.14 = f32[98304]{0:T(1024)S(1)} collective-permute-done((f32[98304]{0:T(1024)S(1)}, f32[98304]{0:T(1024)S(1)}, u32[]{:S(2)}, u32[]{:S(2)}) %collective-permute-start.14) | collective-permute-done | bytes 393248 | tf_op jit(solution)/shard_map/ppermute | solution.py:65
  (213 shorter events, 65.4 us)
Async XLA Ops:
  7.2 37.8 %copy-start = (bf16[2688,256]{1,0:T(8,128)(2,1)S(1)}, bf16[2688,256]{1,0:T(8,128)(2,1)}, u32[]{:S(2)}) copy-start(bf16[2688,256]{1,0:T(8,128)(2,1)} %param.26) | copy-start | bytes 4128772
  7.2 21.9 %all-gather.3.cloned.1.call-start = ((), (), s32[]{:S(2)}) async-start(), calls=%async_computation.4 | async-start | bytes 2064384 | tf_op jit(solution)/shard_map/all_gather | solution.py:106
  10.9 61.4 %reduce-scatter.13.cloned.1.call-start = ((), (), s32[]{:S(2)}) async-start(), calls=%async_computation.8 | async-start | bytes 98304
  11.7 16.1 %collective-permute-start.7 = (s32[256]{0:T(256)S(1)}, s32[256]{0:T(256)S(1)}, u32[]{:S(2)}, u32[]{:S(2)}) collective-permute-start(s32[256]{0:T(256)S(1)} %get-tuple-element.34), channel_id=1, source_target_pairs={{0,2},{2,4},{4,6},{6,8},{8,10},{10,12},{12,14},{1,3},{3,5},{5,7},{... | collective-permute-start | bytes 3080 | tf_op jit(solution)/shard_map/ppermute | solution.py:17
  16.5 11.2 %collective-permute-start.6 = (s32[256]{0:T(256)S(1)}, s32[256]{0:T(256)S(1)}, u32[]{:S(2)}, u32[]{:S(2)}) collective-permute-start(s32[256]{0:T(256)S(1)} %get-tuple-element.34), channel_id=1, source_target_pairs={{0,4},{2,6},{4,8},{6,10},{8,12},{10,14},{1,5},{3,7},{5,9},{7,11},{... | collective-permute-start | bytes 3080 | tf_op jit(solution)/shard_map/ppermute | solution.py:17
  20.0 7.7 %collective-permute-start.5 = (s32[256]{0:T(256)S(1)}, s32[256]{0:T(256)S(1)}, u32[]{:S(2)}, u32[]{:S(2)}) collective-permute-start(s32[256]{0:T(256)S(1)} %get-tuple-element.34), channel_id=1, source_target_pairs={{0,6},{2,8},{4,10},{6,12},{8,14},{1,7},{3,9},{5,11},{7,13},{9,15},... | collective-permute-start | bytes 3080 | tf_op jit(solution)/shard_map/ppermute | solution.py:17
  24.5 3.2 %collective-permute-start.4 = (s32[256]{0:T(256)S(1)}, s32[256]{0:T(256)S(1)}, u32[]{:S(2)}, u32[]{:S(2)}) collective-permute-start(s32[256]{0:T(256)S(1)} %get-tuple-element.34), channel_id=1, source_target_pairs={{0,8},{2,10},{4,12},{6,14},{1,9},{3,11},{5,13},{7,15},{16,24},{18,... | collective-permute-start | bytes 3080 | tf_op jit(solution)/shard_map/ppermute | solution.py:17
  33.0 16.4 %collective-permute-start.3 = (bf16[256,256]{0,1:T(8,128)(2,1)S(1)}, bf16[256,256]{0,1:T(8,128)(2,1)S(1)}, u32[]{:S(2)}, u32[]{:S(2)}) collective-permute-start(bf16[256,256]{0,1:T(8,128)(2,1)S(1)} %pad_maximum_fusion.1), channel_id=1, source_target_pairs={{0,2},{2,4},{4,6},{6,8},{8,10},{10,12},{12,14},{1,3},{3,5},{5,7},{... | collective-permute-start | bytes 393224 | tf_op jit(solution)/shard_map/ppermute | solution.py:17
  35.8 12.9 %collective-permute-start.2 = (bf16[256,256]{0,1:T(8,128)(2,1)S(1)}, bf16[256,256]{0,1:T(8,128)(2,1)S(1)}, u32[]{:S(2)}, u32[]{:S(2)}) collective-permute-start(bf16[256,256]{0,1:T(8,128)(2,1)S(1)} %pad_maximum_fusion.1), channel_id=1, source_target_pairs={{0,4},{2,6},{4,8},{6,10},{8,12},{10,14},{1,5},{3,7},{5,9},{7,11},{... | collective-permute-start | bytes 393224 | tf_op jit(solution)/shard_map/ppermute | solution.py:17
  38.6 9.4 %collective-permute-start.1 = (bf16[256,256]{0,1:T(8,128)(2,1)S(1)}, bf16[256,256]{0,1:T(8,128)(2,1)S(1)}, u32[]{:S(2)}, u32[]{:S(2)}) collective-permute-start(bf16[256,256]{0,1:T(8,128)(2,1)S(1)} %pad_maximum_fusion.1), channel_id=1, source_target_pairs={{0,6},{2,8},{4,10},{6,12},{8,14},{1,7},{3,9},{5,11},{7,13},{9,15},... | collective-permute-start | bytes 393224 | tf_op jit(solution)/shard_map/ppermute | solution.py:17
  43.4 3.9 %collective-permute-start = (bf16[256,256]{0,1:T(8,128)(2,1)S(1)}, bf16[256,256]{0,1:T(8,128)(2,1)S(1)}, u32[]{:S(2)}, u32[]{:S(2)}) collective-permute-start(bf16[256,256]{0,1:T(8,128)(2,1)S(1)} %pad_maximum_fusion.1), channel_id=1, source_target_pairs={{0,8},{2,10},{4,12},{6,14},{1,9},{3,11},{5,13},{7,15},{16,24},{18,... | collective-permute-start | bytes 393224 | tf_op jit(solution)/shard_map/ppermute | solution.py:17
  57.3 27.3 %reduce-scatter.9.cloned.1.call-start = ((), (), s32[]{:S(2)}) async-start(), calls=%async_computation.5 | async-start | bytes 2064384 | tf_op jit(solution)/shard_map/reduce_scatter | solution.py:159
  60.4 25.8 %copy-start.9 = (bf16[128,2688]{1,0:T(8,128)(2,1)S(1)}, bf16[128,2688]{1,0:T(8,128)(2,1)}, u32[]{:S(2)}) copy-start(bf16[128,2688]{1,0:T(8,128)(2,1)} %param.19) | copy-start | bytes 2064388
  60.4 25.8 %copy-start.28 = (f32[2688]{0:T(1024)S(1)}, f32[2688]{0:T(1024)}, u32[]{:S(2)}) copy-start(f32[2688]{0:T(1024)} %param.25) | copy-start | bytes 32260
  60.4 38.6 %all-gather.5.cloned.1.call-start = ((), (), s32[]{:S(2)}) async-start(), calls=%async_computation.6 | async-start | bytes 2064384 | tf_op jit(solution)/shard_map/all_gather | solution.py:176
  88.1 70.7 %reduce-scatter.15.cloned.1.call-start = ((), (), s32[]{:S(2)}) async-start(), calls=%async_computation.9 | async-start | bytes 1032192
  125.2 7.7 %collective-permute-start.8 = (bf16[256,256]{0,1:T(8,128)(2,1)S(1)}, bf16[256,256]{0,1:T(8,128)(2,1)S(1)}, u32[]{:S(2)}, u32[]{:S(2)}) collective-permute-start(bf16[256,256]{0,1:T(8,128)(2,1)S(1)} %get-tuple-element.26), channel_id=1, source_target_pairs={{2,0},{4,2},{6,4},{8,6},{10,8},{12,10},{14,12},{3,1},{5,3},{7,5},{... | collective-permute-start | bytes 393224 | tf_op jit(solution)/shard_map/ppermute | solution.py:17
  126.6 17.4 %collective-permute-start.11 = (bf16[256,256]{0,1:T(8,128)(2,1)S(1)}, bf16[256,256]{0,1:T(8,128)(2,1)S(1)}, u32[]{:S(2)}, u32[]{:S(2)}) collective-permute-start(bf16[256,256]{0,1:T(8,128)(2,1)S(1)} %get-tuple-element.27), channel_id=1, source_target_pairs={{8,0},{10,2},{12,4},{14,6},{9,1},{11,3},{13,5},{15,7},{24,16},{26,... | collective-permute-start | bytes 393224 | tf_op jit(solution)/shard_map/ppermute | solution.py:17
  127.9 16.2 %collective-permute-start.10 = (bf16[256,256]{0,1:T(8,128)(2,1)S(1)}, bf16[256,256]{0,1:T(8,128)(2,1)S(1)}, u32[]{:S(2)}, u32[]{:S(2)}) collective-permute-start(bf16[256,256]{0,1:T(8,128)(2,1)S(1)} %get-tuple-element.28), channel_id=1, source_target_pairs={{6,0},{8,2},{10,4},{12,6},{14,8},{7,1},{9,3},{11,5},{13,7},{15,9},... | collective-permute-start | bytes 393224 | tf_op jit(solution)/shard_map/ppermute | solution.py:17
  129.2 14.9 %collective-permute-start.9 = (bf16[256,256]{0,1:T(8,128)(2,1)S(1)}, bf16[256,256]{0,1:T(8,128)(2,1)S(1)}, u32[]{:S(2)}, u32[]{:S(2)}) collective-permute-start(bf16[256,256]{0,1:T(8,128)(2,1)S(1)} %get-tuple-element.29), channel_id=1, source_target_pairs={{4,0},{6,2},{8,4},{10,6},{12,8},{14,10},{5,1},{7,3},{9,5},{11,7},{... | collective-permute-start | bytes 393224 | tf_op jit(solution)/shard_map/ppermute | solution.py:17
  148.3 57.9 %reduce-scatter.11.cloned.1.call-start = ((), (), s32[]{:S(2)}) async-start(), calls=%async_computation.7 | async-start | bytes 2064384 | tf_op jit(solution)/shard_map/reduce_scatter | solution.py:240
  161.0 11.4 %collective-permute-start.12 = (f32[98304]{0:T(1024)S(1)}, f32[98304]{0:T(1024)S(1)}, u32[]{:S(2)}, u32[]{:S(2)}) collective-permute-start(f32[98304]{0:T(1024)S(1)} %constant_dynamic-update-slice_fusion.11), channel_id=1, source_target_pairs={{0,2},{2,0},{4,6},{6,4},{8,10},{10,8},{12,14},{14,12},{1,3},{3,1},... | collective-permute-start | bytes 1179656 | tf_op jit(solution)/shard_map/ppermute | solution.py:65
  172.4 10.6 %collective-permute-start.13 = (f32[98304]{0:T(1024)S(1)}, f32[98304]{0:T(1024)S(1)}, u32[]{:S(2)}, u32[]{:S(2)}) collective-permute-start(f32[98304]{0:T(1024)S(1)} %add.134), channel_id=1, source_target_pairs={{0,4},{2,6},{4,0},{6,2},{8,12},{10,14},{12,8},{14,10},{1,5},{3,7},... | collective-permute-start | bytes 1179656 | tf_op jit(solution)/shard_map/ppermute | solution.py:65
  183.1 19.1 %collective-permute-start.14 = (f32[98304]{0:T(1024)S(1)}, f32[98304]{0:T(1024)S(1)}, u32[]{:S(2)}, u32[]{:S(2)}) collective-permute-start(f32[98304]{0:T(1024)S(1)} %add.135), channel_id=1, source_target_pairs={{0,8},{2,10},{4,12},{6,14},{8,0},{10,2},{12,4},{14,6},{1,9},{3,11}... | collective-permute-start | bytes 1179656 | tf_op jit(solution)/shard_map/ppermute | solution.py:65
  (43 other events, 349.1 us)
Sparse Core Ops, SparseCore 0:
  11.0 12.2 all-gather.2
  57.5 14.8 reduce-scatter.12
  74.6 9.9 reduce-scatter.8
  88.2 10.7 all-gather.4
  148.4 10.3 reduce-scatter.14
  161.1 9.9 reduce-scatter.10

commit v2 on v1

--- a/solution.py
+++ b/solution.py
@@ -53,6 +53,17 @@
     ]
     same_doc = key_codes[None, :] == query_segs[:, None] + 1
     return (distance == 0) | (distance > 0) & (distance < WINDOW) & same_doc
+
+
+def tp_sum_scatter(value):
+    if lax.axis_size("tp") != 2:
+        return lax.psum_scatter(value, "tp", scatter_dimension=0, tiled=True).astype(jnp.float32)
+    half = value.shape[0] // 2
+    tp_index = lax.axis_index("tp")
+    mine = lax.dynamic_slice_in_dim(value, tp_index * half, half, 0)
+    theirs = lax.dynamic_slice_in_dim(value, (1 - tp_index) * half, half, 0)
+    received = lax.ppermute(theirs, "tp", [(0, 1), (1, 0)])
+    return mine.astype(jnp.float32) + received.astype(jnp.float32)
 
 
 def ctx_sum(parts):
@@ -155,14 +166,8 @@
     )
     part_out = matrix_product(attention_result, output_projection)
     partial_middle = matrix_product(attention_result, adapter_output_down)
-    output_total, mid_sum = (
-        lax.psum_scatter(
-            part_out.astype(jnp.bfloat16), "tp", scatter_dimension=0, tiled=True
-        ).astype(jnp.float32),
-        lax.psum_scatter(
-            partial_middle.astype(jnp.bfloat16), "tp", scatter_dimension=0, tiled=True
-        ).astype(jnp.float32),
-    )
+    output_total = tp_sum_scatter(part_out.astype(jnp.bfloat16))
+    mid_sum = tp_sum_scatter(partial_middle.astype(jnp.bfloat16))
     middle_output = mid_sum.astype(jnp.bfloat16)
     apply_prenorm = output_total + adapter_scale * matrix_product(middle_output, adapter_output_up)
     layer_out = norm_rows(apply_prenorm, output_norm_gain).astype(jnp.bfloat16)
@@ -237,9 +242,7 @@
         + multiply_by_transpose(value_prenorm_gradient, value_projection)
         + multiply_by_transpose(middle_gradients, adapter_down_maps)
     )
-    grad_normed_rows = lax.psum_scatter(
-        grad_normed.astype(jnp.bfloat16), "tp", scatter_dimension=0, tiled=True
-    ).astype(jnp.float32)
+    grad_normed_rows = tp_sum_scatter(grad_normed.astype(jnp.bfloat16))
     grad_in = norm_back(tok_float, input_norm_gain, grad_normed_rows).astype(jnp.bfloat16)
     down_term = lax.psum_scatter(
         transpose_multiply(normalized_input, middle_gradients).astype(jnp.bfloat16),

time: 217 us -> 206 us (0.949)
  waiting for transfers between devices: 84 us -> 65.6 us
  local copies, waits for them, and re-layouts: 16.5 us -> 23.6 us
    reduce_scatter x2 -> x0, waiting for transfers between devices: 12.3 us -> none  [the longest x1 12.3 us: on_device(): lax.psum_scatter(part_out.astype(jnp.bfloat16), 'tp', scatter_dimension=0...]
    unnamed x8 -> x4, waiting for transfers between devices: 17.1 us -> 6.28 us
    all_gather x1, waiting for transfers between devices: 3.78 us -> 10.8 us  [on_device(): lax.all_gather(prenorm_gradient, 'tp', axis=0, tiled=True)]
    ppermute x3, waiting for transfers between devices: 34.7 us -> 30.7 us  [ctx_sum(): lax.ppermute(flat, 'ctx', [(i, i ^ step) for i in range(count)])]
    reshape x4, local copies, waits for them, and re-layouts: 2.91 us -> 5.69 us  [ctx_sum(): flat = jnp.concatenate([p.astype(jnp.float32).reshape(-1) for p in parts])]
    unnamed x110 -> x100, local copies, waits for them, and re-layouts: 11.3 us -> 12.8 us
  transfers between devices with their start and end apart: 21 -> 21, of which waited for: 11 -> 11; matrix products, arithmetic and copies ran while one was open for 10% -> 12% of each run, Pallas kernels for 0% -> 0%
where the time goes in v2:
time: 206 us; the launch traced here: 205 us
  waiting for transfers between devices  65.6 us (32%)
  matrix products  43.7 us (21%)
  starting transfers between devices  38.9 us (19%)
  local copies, waits for them, and re-layouts  23.6 us (11%)
  between operations  15.3 us (7%)
  other arithmetic  14.2 us (7%)
  blocking collectives  3.75 us (2%)
    ppermute x12, starting transfers between devices, passed_along(): lax.ppermute(value, axis, [(source, source + steps) for source in range(l...  31.9 us
    ppermute x3, waiting for transfers between devices, ctx_sum(): lax.ppermute(flat, 'ctx', [(i, i ^ step) for i in range(count)])  30.7 us
    ppermute x12, waiting for transfers between devices, passed_along(): lax.ppermute(value, axis, [(source, source + steps) for source in range(l...  16 us
    unnamed x100, local copies, waits for them, and re-layouts  12.8 us
    dot_general x10, matrix products, multiply_by_transpose(): lax.dot_general(first_op, second_op, (((1,), (1,)), ((), ())), preferred_...  11.8 us
    all_gather x1, waiting for transfers between devices, on_device(): lax.all_gather(prenorm_gradient, 'tp', axis=0, tiled=True)  10.8 us
    dot_general x10, matrix products, matrix_product(): return jnp.dot(first_op, second_op, preferred_element_type=jnp.float32)  7.06 us
    ppermute x3, starting transfers between devices, ctx_sum(): lax.ppermute(flat, 'ctx', [(i, i ^ step) for i in range(count)])  6.37 us
  transfers between devices with their start and end apart: 21, of which 11 were waited for; matrix products, arithmetic and copies ran while one was open for 12% of the time, Pallas kernels for 0%

profile of v2, /device:TPU:0, one launch (start us, length us, event | category | flops | bytes accessed | tf_op | source)
XLA Modules:
  0.0 205.1 jit_solution(14682252645972573811)
XLA Ops:
  9.2 2.2 %fusion.19 = bf16[128,2688]{1,0:T(8,128)(2,1)} fusion(bf16[128,2688]{1,0:T(8,128)(2,1)} %param.18, f32[2688]{0:T(1024)} %param.22, f32[128]{0:T(128)S(1)} %add_rsqrt_fusion.3), kind=kLoop, calls=%fused_computation.31 | loop fusion | flops 1376256 | bytes 1387520 | tf_op jit(solution)/shard_map/convert_element_type | solution.py:116
  12.2 4.8 %collective-permute-start.7 = (s32[256]{0:T(256)S(1)}, s32[256]{0:T(256)S(1)}, u32[]{:S(2)}, u32[]{:S(2)}) collective-permute-start(s32[256]{0:T(256)S(1)} %get-tuple-element.34), channel_id=1, source_target_pairs={{0,2},{2,4},{4,6},{6,8},{8,10},{10,12},{12,14},{1,3},{3,5},{5,7},{... | collective-permute-start | bytes 3080 | tf_op jit(solution)/shard_map/ppermute | solution.py:17
  17.0 3.5 %collective-permute-start.6 = (s32[256]{0:T(256)S(1)}, s32[256]{0:T(256)S(1)}, u32[]{:S(2)}, u32[]{:S(2)}) collective-permute-start(s32[256]{0:T(256)S(1)} %get-tuple-element.34), channel_id=1, source_target_pairs={{0,4},{2,6},{4,8},{6,10},{8,12},{10,14},{1,5},{3,7},{5,9},{7,11},{... | collective-permute-start | bytes 3080 | tf_op jit(solution)/shard_map/ppermute | solution.py:17
  20.5 4.5 %collective-permute-start.5 = (s32[256]{0:T(256)S(1)}, s32[256]{0:T(256)S(1)}, u32[]{:S(2)}, u32[]{:S(2)}) collective-permute-start(s32[256]{0:T(256)S(1)} %get-tuple-element.34), channel_id=1, source_target_pairs={{0,6},{2,8},{4,10},{6,12},{8,14},{1,7},{3,9},{5,11},{7,13},{9,15},... | collective-permute-start | bytes 3080 | tf_op jit(solution)/shard_map/ppermute | solution.py:17
  33.5 2.7 %collective-permute-start.3 = (bf16[256,256]{0,1:T(8,128)(2,1)S(1)}, bf16[256,256]{0,1:T(8,128)(2,1)S(1)}, u32[]{:S(2)}, u32[]{:S(2)}) collective-permute-start(bf16[256,256]{0,1:T(8,128)(2,1)S(1)} %pad_maximum_fusion.1), channel_id=1, source_target_pairs={{0,2},{2,4},{4,6},{6,8},{8,10},{10,12},{12,14},{1,3},{3,5},{5,7},{... | collective-permute-start | bytes 393224 | tf_op jit(solution)/shard_map/ppermute | solution.py:17
  36.3 2.8 %collective-permute-start.2 = (bf16[256,256]{0,1:T(8,128)(2,1)S(1)}, bf16[256,256]{0,1:T(8,128)(2,1)S(1)}, u32[]{:S(2)}, u32[]{:S(2)}) collective-permute-start(bf16[256,256]{0,1:T(8,128)(2,1)S(1)} %pad_maximum_fusion.1), channel_id=1, source_target_pairs={{0,4},{2,6},{4,8},{6,10},{8,12},{10,14},{1,5},{3,7},{5,9},{7,11},{... | collective-permute-start | bytes 393224 | tf_op jit(solution)/shard_map/ppermute | solution.py:17
  39.1 4.8 %collective-permute-start.1 = (bf16[256,256]{0,1:T(8,128)(2,1)S(1)}, bf16[256,256]{0,1:T(8,128)(2,1)S(1)}, u32[]{:S(2)}, u32[]{:S(2)}) collective-permute-start(bf16[256,256]{0,1:T(8,128)(2,1)S(1)} %pad_maximum_fusion.1), channel_id=1, source_target_pairs={{0,6},{2,8},{4,10},{6,12},{8,14},{1,7},{3,9},{5,11},{7,13},{9,15},... | collective-permute-start | bytes 393224 | tf_op jit(solution)/shard_map/ppermute | solution.py:17
  51.3 3.4 %fusion.29 = f32[2,256,1280]{1,2,0:T(8,128)} fusion(pred[256,1280]{0,1:T(8,128)(4,1)S(1)} %copy-done.21, bf16[1280,256]{0,1:T(8,128)(2,1)} %constant_dynamic-update-slice_fusion, f32[256,256]{0,1:T(8,128)S(1)} %get-tuple-element.39, f32[128]{0:T(128)S(1)} %copy-done.41, f32[256,2]{0,1:T(2,128)S(1)} %add_rsqrt_fusion), kind=kOutput, calls=%fused_computation.48 | convolution fusion | flops 169936640 | bytes 3541504 | tf_op jit(solution)/shard_map/div | solution.py:157
  54.7 2.3 %fusion.44 = bf16[128,2,256]{2,0,1:T(8,128)(2,1)S(1)} fusion(f32[2,256,1280]{1,2,0:T(8,128)} %fusion.29, bf16[1280,256]{0,1:T(8,128)(2,1)} %constant_dynamic-update-slice_fusion, f32[256]{0:T(256)S(1)} %fusion.71), kind=kOutput, calls=%fused_computation.64 | convolution fusion | flops 168558592 | bytes 3081216 | tf_op jit(solution)/shard_map/hts,sd->thd/dot_general | solution.py:159
  72.1 10.8 %all-gather.5.cloned.1.call-done = bf16[256,2688]{1,0:T(8,128)(2,1)} async-done(((bf16[128,2688]{1,0:T(8,128)(2,1)}), bf16[256,2688]{1,0:T(8,128)(2,1)}) %all-gather.5.cloned.1.call-update) | async-done | bytes 1376272 | tf_op jit(solution)/shard_map/all_gather | solution.py:181
  82.8 2.5 %fusion.43 = bf16[256,256]{0,1:T(8,128)(2,1)S(1)} fusion(f32[256,256]{0,1:T(8,128)S(1)} %fusion.83, bf16[256,2688]{1,0:T(8,128)(2,1)} %all-gather.5.cloned.1.call-done, bf16[256,2688]{1,0:T(8,128)(2,1)} %param.29, f32[256]{0:T(256)S(1)} %fusion.71), kind=kOutput, calls=%fused_computation.63 | convolution fusion | flops 352518144 | bytes 3146752 | tf_op jit(solution)/shard_map/dot_general | solution.py:37
  86.0 3.0 %convolution_bitcast_fusion = f32[2,256,1280]{1,2,0:T(8,128)} fusion(bf16[256,2,128]{0,2,1:T(8,128)(2,1)S(1)} %bitcast.110, bf16[1280,256]{0,1:T(8,128)(2,1)} %constant_dynamic-update-slice_fusion), kind=kOutput, calls=%fused_computation.12 | convolution fusion | flops 167772160 | bytes 3080192 | tf_op jit(solution)/shard_map/thd,sd->hts/dot_general | solution.py:195
  89.0 5.7 %multiply_reduce_fusion.3 = (f32[256,2]{0,1:T(2,128)S(1)}, f32[256,2,128]{0,2,1:T(8,128)}) fusion(f32[256,256]{0,1:T(8,128)} %copy-done.18, f32[256,2]{0,1:T(2,128)S(1)} %add_rsqrt_fusion, f32[128]{0:T(128)S(1)} %copy-done.41, f32[2,256,1280]{1,2,0:T(8,128)} %fusion.29, f32[2,256,1280]{1,2,0:T(8,128)} %convolution_bitcast_fusion, ...), kind=kOutput, calls=%fused_computation.99 | convolution fusion | flops 171312384 | bytes 11342336 | tf_op jit(solution)/shard_map/hts,sd->thd/dot_general | solution.py:200
  94.6 5.7 %convolution_bitcast_fusion.2 = f32[1280,128]{0,1:T(8,128)} fusion(f32[2,256,1280]{1,2,0:T(8,128)} %fusion.29, f32[2,256,1280]{1,2,0:T(8,128)} %convolution_bitcast_fusion, f32[256,256]{0,1:T(8,128)} %copy-done.18, f32[128]{0:T(128)S(1)} %copy-done.41, f32[256,2]{0,1:T(2,128)S(1)} %add_rsqrt_fusion), kind=kOutput, calls=%fused_computation.18 | convolution fusion | flops 171247360 | bytes 6162944 | tf_op jit(solution)/shard_map/hts,thd->sd/dot_general | solution.py:203
  116.7 11.1 %collective-permute-done.13 = bf16[256,256]{0,1:T(8,128)(2,1)S(1)} collective-permute-done((bf16[256,256]{0,1:T(8,128)(2,1)S(1)}, bf16[256,256]{0,1:T(8,128)(2,1)S(1)}, u32[]{:S(2)}, u32[]{:S(2)}) %collective-permute-start.13) | collective-permute-done | bytes 131104 | tf_op jit(solution)/shard_map/ppermute | solution.py:17
  133.8 2.5 %convolution_add_fusion.1 = f32[256,2688]{1,0:T(8,128)S(1)} fusion(f32[256,2688]{1,0:T(8,128)} %fusion.84, bf16[256,128]{0,1:T(8,128)(2,1)S(1)} %multiply_convert_fusion.4, bf16[2688,128]{1,0:T(8,128)(2,1)S(1)} %copy-done.11), kind=kOutput, calls=%fused_computation.2 | convolution fusion | flops 176848896 | bytes 6258688 | tf_op jit(solution)/shard_map/dot_general | solution.py:37
  138.1 6.2 %reduce-scatter.4.cloned.1.call-done = bf16[1344,48]{1,0:T(8,128)(2,1)} async-done(((bf16[2688,48]{1,0:T(8,128)(2,1)}), bf16[1344,48]{1,0:T(8,128)(2,1)}) %reduce-scatter.4.cloned.1.call-update) | async-done | bytes 129040
  146.5 2.3 %reshape.229 = f32[64512]{0:T(1024)} reshape(f32[1344,48]{1,0:T(8,128)} %copy.54) | data formatting | bytes 516096 | tf_op jit(solution)/shard_map/reshape | solution.py:73
  153.3 2.3 %collective-permute-start.15 = (f32[98304]{0:T(1024)S(1)}, f32[98304]{0:T(1024)S(1)}, u32[]{:S(2)}, u32[]{:S(2)}) collective-permute-start(f32[98304]{0:T(1024)S(1)} %constant_dynamic-update-slice_fusion.11), channel_id=1, source_target_pairs={{0,2},{2,0},{4,6},{6,4},{8,10},{10,8},{12,14},{14,12},{1,3},{3,1},... | collective-permute-start | bytes 1179656 | tf_op jit(solution)/shard_map/ppermute | solution.py:76
  155.7 9.3 %collective-permute-done.15 = f32[98304]{0:T(1024)S(1)} collective-permute-done((f32[98304]{0:T(1024)S(1)}, f32[98304]{0:T(1024)S(1)}, u32[]{:S(2)}, u32[]{:S(2)}) %collective-permute-start.15) | collective-permute-done | bytes 393248 | tf_op jit(solution)/shard_map/ppermute | solution.py:76
  168.1 7.4 %collective-permute-done.16 = f32[98304]{0:T(1024)S(1)} collective-permute-done((f32[98304]{0:T(1024)S(1)}, f32[98304]{0:T(1024)S(1)}, u32[]{:S(2)}, u32[]{:S(2)}) %collective-permute-start.16) | collective-permute-done | bytes 393248 | tf_op jit(solution)/shard_map/ppermute | solution.py:76
  175.6 2.5 %collective-permute-start.17 = (f32[98304]{0:T(1024)S(1)}, f32[98304]{0:T(1024)S(1)}, u32[]{:S(2)}, u32[]{:S(2)}) collective-permute-start(f32[98304]{0:T(1024)S(1)} %add.153), channel_id=1, source_target_pairs={{0,8},{2,10},{4,12},{6,14},{8,0},{10,2},{12,4},{14,6},{1,9},{3,11}... | collective-permute-start | bytes 1179656 | tf_op jit(solution)/shard_map/ppermute | solution.py:76
  178.1 2.4 %fusion.23 = bf16[128,2688]{1,0:T(8,128)(2,1)} fusion(bf16[128,2688]{1,0:T(8,128)(2,1)S(1)} %copy-done.2, bf16[128,2688]{1,0:T(8,128)(2,1)} %collective-permute-done.14, f32[128]{0:T(128)S(1)} %broadcast_multiply_fusion.2, f32[2688]{0:T(1024)S(1)} %copy-done.24, f32[128]{0:T(128)S(1)} %copy-done.39, bf16[256,2688]{1,0:T(8,128)(2,1)S(1)} %fusion.2, ...), kind=kLoop, calls=%fused_computation.35 | loop fusion | flops 3440640 | bytes 2764292 | tf_op jit(solution)/shard_map/convert_element_type | solution.py:246
  180.5 14.0 %collective-permute-done.17 = f32[98304]{0:T(1024)S(1)} collective-permute-done((f32[98304]{0:T(1024)S(1)}, f32[98304]{0:T(1024)S(1)}, u32[]{:S(2)}, u32[]{:S(2)}) %collective-permute-start.17) | collective-permute-done | bytes 393248 | tf_op jit(solution)/shard_map/ppermute | solution.py:76
  (204 shorter events, 71.1 us)
Async XLA Ops:
  7.2 38.4 %copy-start = (bf16[2688,256]{1,0:T(8,128)(2,1)S(1)}, bf16[2688,256]{1,0:T(8,128)(2,1)}, u32[]{:S(2)}) copy-start(bf16[2688,256]{1,0:T(8,128)(2,1)} %param.26) | copy-start | bytes 4128772
  7.2 22.4 %all-gather.3.cloned.1.call-start = ((), (), s32[]{:S(2)}) async-start(), calls=%async_computation.1 | async-start | bytes 2064384 | tf_op jit(solution)/shard_map/all_gather | solution.py:117
  11.4 20.5 %copy-start.34 = (bf16[16,128]{1,0:T(8,128)(2,1)S(1)}, bf16[16,128]{1,0:T(8,128)(2,1)}, u32[]{:S(2)}) copy-start(bf16[16,128]{1,0:T(8,128)(2,1)} %param.32) | copy-start | bytes 12292
  11.4 20.7 %copy-start.10 = (bf16[2688,128]{1,0:T(8,128)(2,1)S(1)}, bf16[2688,128]{1,0:T(8,128)(2,1)}, u32[]{:S(2)}) copy-start(bf16[2688,128]{1,0:T(8,128)(2,1)} %param.27) | copy-start | bytes 2064388
  11.4 71.4 %all-gather.5.cloned.1.call-start = ((), (), s32[]{:S(2)}) async-start(), calls=%async_computation.2 | async-start | bytes 2064384 | tf_op jit(solution)/shard_map/all_gather | solution.py:181
  12.2 16.1 %collective-permute-start.7 = (s32[256]{0:T(256)S(1)}, s32[256]{0:T(256)S(1)}, u32[]{:S(2)}, u32[]{:S(2)}) collective-permute-start(s32[256]{0:T(256)S(1)} %get-tuple-element.34), channel_id=1, source_target_pairs={{0,2},{2,4},{4,6},{6,8},{8,10},{10,12},{12,14},{1,3},{3,5},{5,7},{... | collective-permute-start | bytes 3080 | tf_op jit(solution)/shard_map/ppermute | solution.py:17
  17.0 11.2 %collective-permute-start.6 = (s32[256]{0:T(256)S(1)}, s32[256]{0:T(256)S(1)}, u32[]{:S(2)}, u32[]{:S(2)}) collective-permute-start(s32[256]{0:T(256)S(1)} %get-tuple-element.34), channel_id=1, source_target_pairs={{0,4},{2,6},{4,8},{6,10},{8,12},{10,14},{1,5},{3,7},{5,9},{7,11},{... | collective-permute-start | bytes 3080 | tf_op jit(solution)/shard_map/ppermute | solution.py:17
  20.5 7.7 %collective-permute-start.5 = (s32[256]{0:T(256)S(1)}, s32[256]{0:T(256)S(1)}, u32[]{:S(2)}, u32[]{:S(2)}) collective-permute-start(s32[256]{0:T(256)S(1)} %get-tuple-element.34), channel_id=1, source_target_pairs={{0,6},{2,8},{4,10},{6,12},{8,14},{1,7},{3,9},{5,11},{7,13},{9,15},... | collective-permute-start | bytes 3080 | tf_op jit(solution)/shard_map/ppermute | solution.py:17
  25.0 3.2 %collective-permute-start.4 = (s32[256]{0:T(256)S(1)}, s32[256]{0:T(256)S(1)}, u32[]{:S(2)}, u32[]{:S(2)}) collective-permute-start(s32[256]{0:T(256)S(1)} %get-tuple-element.34), channel_id=1, source_target_pairs={{0,8},{2,10},{4,12},{6,14},{1,9},{3,11},{5,13},{7,15},{16,24},{18,... | collective-permute-start | bytes 3080 | tf_op jit(solution)/shard_map/ppermute | solution.py:17
  33.5 16.4 %collective-permute-start.3 = (bf16[256,256]{0,1:T(8,128)(2,1)S(1)}, bf16[256,256]{0,1:T(8,128)(2,1)S(1)}, u32[]{:S(2)}, u32[]{:S(2)}) collective-permute-start(bf16[256,256]{0,1:T(8,128)(2,1)S(1)} %pad_maximum_fusion.1), channel_id=1, source_target_pairs={{0,2},{2,4},{4,6},{6,8},{8,10},{10,12},{12,14},{1,3},{3,5},{5,7},{... | collective-permute-start | bytes 393224 | tf_op jit(solution)/shard_map/ppermute | solution.py:17
  36.3 12.9 %collective-permute-start.2 = (bf16[256,256]{0,1:T(8,128)(2,1)S(1)}, bf16[256,256]{0,1:T(8,128)(2,1)S(1)}, u32[]{:S(2)}, u32[]{:S(2)}) collective-permute-start(bf16[256,256]{0,1:T(8,128)(2,1)S(1)} %pad_maximum_fusion.1), channel_id=1, source_target_pairs={{0,4},{2,6},{4,8},{6,10},{8,12},{10,14},{1,5},{3,7},{5,9},{7,11},{... | collective-permute-start | bytes 393224 | tf_op jit(solution)/shard_map/ppermute | solution.py:17
  39.1 9.4 %collective-permute-start.1 = (bf16[256,256]{0,1:T(8,128)(2,1)S(1)}, bf16[256,256]{0,1:T(8,128)(2,1)S(1)}, u32[]{:S(2)}, u32[]{:S(2)}) collective-permute-start(bf16[256,256]{0,1:T(8,128)(2,1)S(1)} %pad_maximum_fusion.1), channel_id=1, source_target_pairs={{0,6},{2,8},{4,10},{6,12},{8,14},{1,7},{3,9},{5,11},{7,13},{9,15},... | collective-permute-start | bytes 393224 | tf_op jit(solution)/shard_map/ppermute | solution.py:17
  43.9 3.9 %collective-permute-start = (bf16[256,256]{0,1:T(8,128)(2,1)S(1)}, bf16[256,256]{0,1:T(8,128)(2,1)S(1)}, u32[]{:S(2)}, u32[]{:S(2)}) collective-permute-start(bf16[256,256]{0,1:T(8,128)(2,1)S(1)} %pad_maximum_fusion.1), channel_id=1, source_target_pairs={{0,8},{2,10},{4,12},{6,14},{1,9},{3,11},{5,13},{7,15},{16,24},{18,... | collective-permute-start | bytes 393224 | tf_op jit(solution)/shard_map/ppermute | solution.py:17
  59.6 2.5 %collective-permute-start.8 = (bf16[128,2688]{1,0:T(8,128)(2,1)}, bf16[128,2688]{1,0:T(8,128)(2,1)}, u32[]{:S(2)}, u32[]{:S(2)}) collective-permute-start(bf16[128,2688]{1,0:T(8,128)(2,1)} %constant_dynamic-slice_fusion.2), channel_id=1, source_target_pairs={{0,1},{1,0},{2,3},{3,2},{4,5},{5,4},{6,7},{7,6},{8,9},{9,8},{10,11... | collective-permute-start | bytes 2064392 | tf_op jit(solution)/shard_map/ppermute | solution.py:65
  59.7 2.0 collective-permute-start.9
  65.8 78.5 %reduce-scatter.4.cloned.1.call-start = ((), (), s32[]{:S(2)}) async-start(), calls=%async_computation.3 | async-start | bytes 1032192
  109.0 7.7 %collective-permute-start.10 = (bf16[256,256]{0,1:T(8,128)(2,1)S(1)}, bf16[256,256]{0,1:T(8,128)(2,1)S(1)}, u32[]{:S(2)}, u32[]{:S(2)}) collective-permute-start(bf16[256,256]{0,1:T(8,128)(2,1)S(1)} %get-tuple-element.26), channel_id=1, source_target_pairs={{2,0},{4,2},{6,4},{8,6},{10,8},{12,10},{14,12},{3,1},{5,3},{7,5},{... | collective-permute-start | bytes 393224 | tf_op jit(solution)/shard_map/ppermute | solution.py:17
  110.4 17.4 %collective-permute-start.13 = (bf16[256,256]{0,1:T(8,128)(2,1)S(1)}, bf16[256,256]{0,1:T(8,128)(2,1)S(1)}, u32[]{:S(2)}, u32[]{:S(2)}) collective-permute-start(bf16[256,256]{0,1:T(8,128)(2,1)S(1)} %get-tuple-element.27), channel_id=1, source_target_pairs={{8,0},{10,2},{12,4},{14,6},{9,1},{11,3},{13,5},{15,7},{24,16},{26,... | collective-permute-start | bytes 393224 | tf_op jit(solution)/shard_map/ppermute | solution.py:17
  111.7 16.1 %collective-permute-start.12 = (bf16[256,256]{0,1:T(8,128)(2,1)S(1)}, bf16[256,256]{0,1:T(8,128)(2,1)S(1)}, u32[]{:S(2)}, u32[]{:S(2)}) collective-permute-start(bf16[256,256]{0,1:T(8,128)(2,1)S(1)} %get-tuple-element.28), channel_id=1, source_target_pairs={{6,0},{8,2},{10,4},{12,6},{14,8},{7,1},{9,3},{11,5},{13,7},{15,9},... | collective-permute-start | bytes 393224 | tf_op jit(solution)/shard_map/ppermute | solution.py:17
  113.0 14.8 %collective-permute-start.11 = (bf16[256,256]{0,1:T(8,128)(2,1)S(1)}, bf16[256,256]{0,1:T(8,128)(2,1)S(1)}, u32[]{:S(2)}, u32[]{:S(2)}) collective-permute-start(bf16[256,256]{0,1:T(8,128)(2,1)S(1)} %get-tuple-element.29), channel_id=1, source_target_pairs={{4,0},{6,2},{8,4},{10,6},{12,8},{14,10},{5,1},{7,3},{9,5},{11,7},{... | collective-permute-start | bytes 393224 | tf_op jit(solution)/shard_map/ppermute | solution.py:17
  138.1 28.4 %collective-permute-start.14 = (bf16[128,2688]{1,0:T(8,128)(2,1)}, bf16[128,2688]{1,0:T(8,128)(2,1)}, u32[]{:S(2)}, u32[]{:S(2)}) collective-permute-start(bf16[128,2688]{1,0:T(8,128)(2,1)} %constant_dynamic-slice_fusion), channel_id=1, source_target_pairs={{0,1},{1,0},{2,3},{3,2},{4,5},{5,4},{6,7},{7,6},{8,9},{9,8},{10,11... | collective-permute-start | bytes 2064392 | tf_op jit(solution)/shard_map/ppermute | solution.py:65
  153.3 11.6 %collective-permute-start.15 = (f32[98304]{0:T(1024)S(1)}, f32[98304]{0:T(1024)S(1)}, u32[]{:S(2)}, u32[]{:S(2)}) collective-permute-start(f32[98304]{0:T(1024)S(1)} %constant_dynamic-update-slice_fusion.11), channel_id=1, source_target_pairs={{0,2},{2,0},{4,6},{6,4},{8,10},{10,8},{12,14},{14,12},{1,3},{3,1},... | collective-permute-start | bytes 1179656 | tf_op jit(solution)/shard_map/ppermute | solution.py:76
  165.0 10.5 %collective-permute-start.16 = (f32[98304]{0:T(1024)S(1)}, f32[98304]{0:T(1024)S(1)}, u32[]{:S(2)}, u32[]{:S(2)}) collective-permute-start(f32[98304]{0:T(1024)S(1)} %add.152), channel_id=1, source_target_pairs={{0,4},{2,6},{4,0},{6,2},{8,12},{10,14},{12,8},{14,10},{1,5},{3,7},... | collective-permute-start | bytes 1179656 | tf_op jit(solution)/shard_map/ppermute | solution.py:76
  175.6 18.9 %collective-permute-start.17 = (f32[98304]{0:T(1024)S(1)}, f32[98304]{0:T(1024)S(1)}, u32[]{:S(2)}, u32[]{:S(2)}) collective-permute-start(f32[98304]{0:T(1024)S(1)} %add.153), channel_id=1, source_target_pairs={{0,8},{2,10},{4,12},{6,14},{8,0},{10,2},{12,4},{14,6},{1,9},{3,11}... | collective-permute-start | bytes 1179656 | tf_op jit(solution)/shard_map/ppermute | solution.py:76
  (39 other events, 322.4 us)
Sparse Core Ops, SparseCore 0:
  11.5 12.2 all-gather.2
  65.9 16.8 all-gather.4
  133.9 10.3 reduce-scatter.3

commit v3 on v2

--- a/solution.py
+++ b/solution.py
@@ -64,6 +64,16 @@
     theirs = lax.dynamic_slice_in_dim(value, (1 - tp_index) * half, half, 0)
     received = lax.ppermute(theirs, "tp", [(0, 1), (1, 0)])
     return mine.astype(jnp.float32) + received.astype(jnp.float32)
+
+
+def tp_gather(value):
+    if lax.axis_size("tp") != 2:
+        return lax.all_gather(value, "tp", axis=0, tiled=True)
+    received = lax.ppermute(value, "tp", [(0, 1), (1, 0)])
+    first = lax.axis_index("tp") == 0
+    return jnp.concatenate(
+        [jnp.where(first, value, received), jnp.where(first, received, value)], axis=0
+    )
 
 
 def ctx_sum(parts):
@@ -177,11 +187,10 @@
     middle_output_gradient = (
         adapter_scale * multiply_by_transpose(prenorm_gradient, adapter_output_up)
     ).astype(jnp.bfloat16)
-    complete_gradient, middle_complete_gradient, middle_complete = (
-        lax.all_gather(prenorm_gradient, "tp", axis=0, tiled=True),
-        lax.all_gather(middle_output_gradient, "tp", axis=0, tiled=True),
-        lax.all_gather(middle_output, "tp", axis=0, tiled=True),
-    )
+    complete_gradient = tp_gather(prenorm_gradient)
+    middle_pair = tp_gather(jnp.concatenate([middle_output_gradient, middle_output], axis=1))
+    middle_complete_gradient = middle_pair[:, :adapter_product]
+    middle_complete = middle_pair[:, adapter_product:]
     gradient_portion = lax.dynamic_slice_in_dim(
         complete_gradient, tp_index * slice_width, slice_width, 1
     )
@@ -244,11 +253,8 @@
     )
     grad_normed_rows = tp_sum_scatter(grad_normed.astype(jnp.bfloat16))
     grad_in = norm_back(tok_float, input_norm_gain, grad_normed_rows).astype(jnp.bfloat16)
-    down_term = lax.psum_scatter(
-        transpose_multiply(normalized_input, middle_gradients).astype(jnp.bfloat16),
-        "tp",
-        scatter_dimension=0,
-        tiled=True,
+    down_term = tp_sum_scatter(
+        transpose_multiply(normalized_input, middle_gradients).astype(jnp.bfloat16)
     )
     adapter_totals = ctx_sum(
         [

time: 206 us -> 194 us (0.942)
  waiting for transfers between devices: 65.6 us -> 57.1 us
  matrix products: 43.7 us -> 39.3 us
  blocking collectives: 3.75 us -> 0 us
  starting transfers between devices: 38.9 us -> 41.1 us
    all_gather x1 -> x0, waiting for transfers between devices: 10.8 us -> none  [on_device(): lax.all_gather(prenorm_gradient, 'tp', axis=0, tiled=True)]
    unnamed x4 -> x1, waiting for transfers between devices: 6.28 us -> 0.02 us
    dot_general x10, matrix products: 11.8 us -> 5.89 us  [multiply_by_transpose(): lax.dot_general(first_op, second_op, (((1,), (1,)), ((), ())), preferred_...]
    ppermute x12, waiting for transfers between devices: 16 us -> 21.2 us  [passed_along(): lax.ppermute(value, axis, [(source, source + steps) for source in range(l...]
    all_gather x2 -> x0, blocking collectives: 3.75 us -> none  [the longest x1 1.93 us: on_device(): lax.all_gather(middle_output, 'tp', axis=0, tiled=True)]
    ppermute x3, waiting for transfers between devices: 30.7 us -> 33.5 us  [ctx_sum(): lax.ppermute(flat, 'ctx', [(i, i ^ step) for i in range(count)])]
    unnamed x100 -> x114, local copies, waits for them, and re-layouts: 12.8 us -> 12.6 us
    reshape x4 -> x3, local copies, waits for them, and re-layouts: 5.69 us -> 5.48 us  [ctx_sum(): flat = jnp.concatenate([p.astype(jnp.float32).reshape(-1) for p in parts])]
  transfers between devices with their start and end apart: 21 -> 22, of which waited for: 11 -> 10; matrix products, arithmetic and copies ran while one was open for 12% -> 12% of each run, Pallas kernels for 0% -> 0%
where the time goes in v3:
time: 194 us; the launch traced here: 193 us
  waiting for transfers between devices  57.1 us (29%)
  starting transfers between devices  41.1 us (21%)
  matrix products  39.3 us (20%)
  local copies, waits for them, and re-layouts  24.4 us (13%)
  between operations  15.7 us (8%)
  other arithmetic  15.5 us (8%)
    ppermute x3, waiting for transfers between devices, ctx_sum(): lax.ppermute(flat, 'ctx', [(i, i ^ step) for i in range(count)])  33.5 us
    ppermute x12, starting transfers between devices, passed_along(): lax.ppermute(value, axis, [(source, source + steps) for source in range(l...  31.9 us
    ppermute x12, waiting for transfers between devices, passed_along(): lax.ppermute(value, axis, [(source, source + steps) for source in range(l...  21.2 us
    unnamed x114, local copies, waits for them, and re-layouts  12.6 us
    ppermute x3, starting transfers between devices, ctx_sum(): lax.ppermute(flat, 'ctx', [(i, i ^ step) for i in range(count)])  7.99 us
    dot_general x10, matrix products, matrix_product(): return jnp.dot(first_op, second_op, preferred_element_type=jnp.float32)  6.89 us
    dot_general x10, matrix products, multiply_by_transpose(): lax.dot_general(first_op, second_op, (((1,), (1,)), ((), ())), preferred_...  5.89 us
    dot_general x6, matrix products, transpose_multiply(): lax.dot_general(first_op, second_op, (((0,), (0,)), ((), ())), preferred_...  5.81 us
  transfers between devices with their start and end apart: 22, of which 10 were waited for; matrix products, arithmetic and copies ran while one was open for 12% of the time, Pallas kernels for 0%

profile of v3, /device:TPU:0, one launch (start us, length us, event | category | flops | bytes accessed | tf_op | source)
XLA Modules:
  0.0 193.1 jit_solution(5258034468710784232)
XLA Ops:
  9.2 2.2 %fusion.20 = bf16[128,2688]{1,0:T(8,128)(2,1)} fusion(bf16[128,2688]{1,0:T(8,128)(2,1)} %param.18, f32[2688]{0:T(1024)} %param.22, f32[128]{0:T(128)S(1)} %add_rsqrt_fusion.3), kind=kLoop, calls=%fused_computation.35 | loop fusion | flops 1376256 | bytes 1387520 | tf_op jit(solution)/shard_map/convert_element_type | solution.py:126
  12.2 4.8 %collective-permute-start.7 = (s32[256]{0:T(256)S(1)}, s32[256]{0:T(256)S(1)}, u32[]{:S(2)}, u32[]{:S(2)}) collective-permute-start(s32[256]{0:T(256)S(1)} %get-tuple-element.30), channel_id=1, source_target_pairs={{0,2},{2,4},{4,6},{6,8},{8,10},{10,12},{12,14},{1,3},{3,5},{5,7},{... | collective-permute-start | bytes 3080 | tf_op jit(solution)/shard_map/ppermute | solution.py:17
  17.0 3.5 %collective-permute-start.6 = (s32[256]{0:T(256)S(1)}, s32[256]{0:T(256)S(1)}, u32[]{:S(2)}, u32[]{:S(2)}) collective-permute-start(s32[256]{0:T(256)S(1)} %get-tuple-element.30), channel_id=1, source_target_pairs={{0,4},{2,6},{4,8},{6,10},{8,12},{10,14},{1,5},{3,7},{5,9},{7,11},{... | collective-permute-start | bytes 3080 | tf_op jit(solution)/shard_map/ppermute | solution.py:17
  20.5 4.5 %collective-permute-start.5 = (s32[256]{0:T(256)S(1)}, s32[256]{0:T(256)S(1)}, u32[]{:S(2)}, u32[]{:S(2)}) collective-permute-start(s32[256]{0:T(256)S(1)} %get-tuple-element.30), channel_id=1, source_target_pairs={{0,6},{2,8},{4,10},{6,12},{8,14},{1,7},{3,9},{5,11},{7,13},{9,15},... | collective-permute-start | bytes 3080 | tf_op jit(solution)/shard_map/ppermute | solution.py:17
  25.0 1.9 %collective-permute-start.4 = (s32[256]{0:T(256)S(1)}, s32[256]{0:T(256)S(1)}, u32[]{:S(2)}, u32[]{:S(2)}) collective-permute-start(s32[256]{0:T(256)S(1)} %get-tuple-element.30), channel_id=1, source_target_pairs={{0,8},{2,10},{4,12},{6,14},{1,9},{3,11},{5,13},{7,15},{16,24},{18,... | collective-permute-start | bytes 3080 | tf_op jit(solution)/shard_map/ppermute | solution.py:17
  29.6 2.0 %convolution_convert_fusion.2 = bf16[256,48]{0,1:T(8,128)(2,1)S(1)} fusion(bf16[256,2688]{1,0:T(8,128)(2,1)} %all-gather.2.cloned.1.call-done, bf16[2688,48]{0,1:T(8,128)(2,1)} %param.30), kind=kOutput, calls=%fused_computation.74 | convolution fusion | flops 66072576 | bytes 1658880 | tf_op jit(solution)/shard_map/dot_general | solution.py:33
  33.6 2.7 %collective-permute-start.3 = (bf16[256,256]{0,1:T(8,128)(2,1)S(1)}, bf16[256,256]{0,1:T(8,128)(2,1)S(1)}, u32[]{:S(2)}, u32[]{:S(2)}) collective-permute-start(bf16[256,256]{0,1:T(8,128)(2,1)S(1)} %pad_maximum_fusion.9), channel_id=1, source_target_pairs={{0,2},{2,4},{4,6},{6,8},{8,10},{10,12},{12,14},{1,3},{3,5},{5,7},{... | collective-permute-start | bytes 393224 | tf_op jit(solution)/shard_map/ppermute | solution.py:17
  36.3 2.8 %collective-permute-start.2 = (bf16[256,256]{0,1:T(8,128)(2,1)S(1)}, bf16[256,256]{0,1:T(8,128)(2,1)S(1)}, u32[]{:S(2)}, u32[]{:S(2)}) collective-permute-start(bf16[256,256]{0,1:T(8,128)(2,1)S(1)} %pad_maximum_fusion.9), channel_id=1, source_target_pairs={{0,4},{2,6},{4,8},{6,10},{8,12},{10,14},{1,5},{3,7},{5,9},{7,11},{... | collective-permute-start | bytes 393224 | tf_op jit(solution)/shard_map/ppermute | solution.py:17
  39.2 4.8 %collective-permute-start.1 = (bf16[256,256]{0,1:T(8,128)(2,1)S(1)}, bf16[256,256]{0,1:T(8,128)(2,1)S(1)}, u32[]{:S(2)}, u32[]{:S(2)}) collective-permute-start(bf16[256,256]{0,1:T(8,128)(2,1)S(1)} %pad_maximum_fusion.9), channel_id=1, source_target_pairs={{0,6},{2,8},{4,10},{6,12},{8,14},{1,7},{3,9},{5,11},{7,13},{9,15},... | collective-permute-start | bytes 393224 | tf_op jit(solution)/shard_map/ppermute | solution.py:17
  51.3 3.4 %fusion.30 = f32[2,256,1280]{1,2,0:T(8,128)} fusion(pred[256,1280]{0,1:T(8,128)(4,1)S(1)} %copy-done.25, bf16[1280,256]{0,1:T(8,128)(2,1)} %constant_dynamic-update-slice_fusion, f32[256,256]{0,1:T(8,128)S(1)} %get-tuple-element.35, f32[128]{0:T(128)S(1)} %copy-done.48, f32[256,2]{0,1:T(2,128)S(1)} %add_rsqrt_fusion), kind=kOutput, calls=%fused_computation.52 | convolution fusion | flops 169936640 | bytes 3541504 | tf_op jit(solution)/shard_map/div | solution.py:167
  54.7 2.3 %fusion.45 = bf16[128,2,256]{2,0,1:T(8,128)(2,1)S(1)} fusion(f32[2,256,1280]{1,2,0:T(8,128)} %fusion.30, bf16[1280,256]{0,1:T(8,128)(2,1)} %constant_dynamic-update-slice_fusion, f32[256]{0:T(256)S(1)} %fusion.76), kind=kOutput, calls=%fused_computation.67 | convolution fusion | flops 168558592 | bytes 3081216 | tf_op jit(solution)/shard_map/hts,sd->thd/dot_general | solution.py:169
  75.3 3.0 %convolution_bitcast_fusion = f32[2,256,1280]{1,2,0:T(8,128)} fusion(bf16[256,2,128]{0,2,1:T(8,128)(2,1)S(1)} %bitcast.105, bf16[1280,256]{0,1:T(8,128)(2,1)} %constant_dynamic-update-slice_fusion), kind=kOutput, calls=%fused_computation.12 | convolution fusion | flops 167772160 | bytes 3080192 | tf_op jit(solution)/shard_map/thd,sd->hts/dot_general | solution.py:204
  78.3 5.7 %multiply_reduce_fusion.3 = (f32[256,2]{0,1:T(2,128)S(1)}, f32[256,2,128]{0,2,1:T(8,128)}) fusion(f32[256,256]{0,1:T(8,128)} %copy-done.18, f32[256,2]{0,1:T(2,128)S(1)} %copy-done.40, f32[128]{0:T(128)S(1)} %copy-done.49, f32[2,256,1280]{1,2,0:T(8,128)} %fusion.30, f32[2,256,1280]{1,2,0:T(8,128)} %convolution_bitcast_fusion, ...), kind=kOutput, calls=%fused_computation.106 | convolution fusion | flops 171312384 | bytes 11342336 | tf_op jit(solution)/shard_map/hts,sd->thd/dot_general | solution.py:209
  83.9 5.8 %convolution_bitcast_fusion.2 = f32[1280,128]{0,1:T(8,128)} fusion(f32[2,256,1280]{1,2,0:T(8,128)} %fusion.30, f32[2,256,1280]{1,2,0:T(8,128)} %convolution_bitcast_fusion, f32[256,256]{0,1:T(8,128)} %copy-done.18, f32[128]{0:T(128)S(1)} %copy-done.49, f32[256,2]{0,1:T(2,128)S(1)} %copy-done.40), kind=kOutput, calls=%fused_computation.18 | convolution fusion | flops 171247360 | bytes 6162944 | tf_op jit(solution)/shard_map/hts,thd->sd/dot_general | solution.py:212
  92.3 2.1 %fusion.94 = f32[256,2688]{1,0:T(8,128)} fusion(bf16[256,256]{0,1:T(8,128)(2,1)S(1)} %bitcast.102, bf16[2688,256]{1,0:T(8,128)(2,1)S(1)} %copy-done), kind=kOutput, calls=%fused_computation.179 | convolution fusion | flops 352321536 | bytes 4259840 | tf_op jit(solution)/shard_map/dot_general | solution.py:37
  105.4 2.1 %collective-permute-done.12 = bf16[256,256]{0,1:T(8,128)(2,1)S(1)} collective-permute-done((bf16[256,256]{0,1:T(8,128)(2,1)S(1)}, bf16[256,256]{0,1:T(8,128)(2,1)S(1)}, u32[]{:S(2)}, u32[]{:S(2)}) %collective-permute-start.12) | collective-permute-done | bytes 131104 | tf_op jit(solution)/shard_map/ppermute | solution.py:17
  107.5 16.3 %collective-permute-done.15 = bf16[256,256]{0,1:T(8,128)(2,1)S(1)} collective-permute-done((bf16[256,256]{0,1:T(8,128)(2,1)S(1)}, bf16[256,256]{0,1:T(8,128)(2,1)S(1)}, u32[]{:S(2)}, u32[]{:S(2)}) %collective-permute-start.15) | collective-permute-done | bytes 131104 | tf_op jit(solution)/shard_map/ppermute | solution.py:17
  129.8 2.3 %reshape.217 = f32[64512]{0:T(1024)} reshape(f32[1344,48]{1,0:T(8,128)} %copy.42) | data formatting | bytes 516096 | tf_op jit(solution)/shard_map/reshape | solution.py:83
  136.6 4.3 %collective-permute-start.18 = (f32[98304]{0:T(1024)S(1)}, f32[98304]{0:T(1024)S(1)}, u32[]{:S(2)}, u32[]{:S(2)}) collective-permute-start(f32[98304]{0:T(1024)S(1)} %constant_dynamic-update-slice_fusion.11), channel_id=1, source_target_pairs={{0,2},{2,0},{4,6},{6,4},{8,10},{10,8},{12,14},{14,12},{1,3},{3,1},... | collective-permute-start | bytes 1179656 | tf_op jit(solution)/shard_map/ppermute | solution.py:86
  140.8 9.8 %collective-permute-done.18 = f32[98304]{0:T(1024)S(1)} collective-permute-done((f32[98304]{0:T(1024)S(1)}, f32[98304]{0:T(1024)S(1)}, u32[]{:S(2)}, u32[]{:S(2)}) %collective-permute-start.18) | collective-permute-done | bytes 393248 | tf_op jit(solution)/shard_map/ppermute | solution.py:86
  150.6 2.9 %collective-permute-start.19 = (f32[98304]{0:T(1024)S(1)}, f32[98304]{0:T(1024)S(1)}, u32[]{:S(2)}, u32[]{:S(2)}) collective-permute-start(f32[98304]{0:T(1024)S(1)} %add.159), channel_id=1, source_target_pairs={{0,4},{2,6},{4,0},{6,2},{8,12},{10,14},{12,8},{14,10},{1,5},{3,7},... | collective-permute-start | bytes 1179656 | tf_op jit(solution)/shard_map/ppermute | solution.py:86
  155.2 7.4 %collective-permute-done.19 = f32[98304]{0:T(1024)S(1)} collective-permute-done((f32[98304]{0:T(1024)S(1)}, f32[98304]{0:T(1024)S(1)}, u32[]{:S(2)}, u32[]{:S(2)}) %collective-permute-start.19) | collective-permute-done | bytes 393248 | tf_op jit(solution)/shard_map/ppermute | solution.py:86
  163.4 2.4 %fusion.24 = bf16[128,2688]{1,0:T(8,128)(2,1)} fusion(bf16[128,2688]{1,0:T(8,128)(2,1)S(1)} %copy-done.3, bf16[128,2688]{1,0:T(8,128)(2,1)} %collective-permute-done.16, f32[128]{0:T(128)S(1)} %broadcast_multiply_fusion.2, f32[2688]{0:T(1024)S(1)} %copy-done.28, f32[128]{0:T(128)S(1)} %copy-done.44, bf16[256,2688]{1,0:T(8,128)(2,1)S(1)} %fusion.2, ...), kind=kLoop, calls=%fused_computation.39 | loop fusion | flops 3440640 | bytes 2764292 | tf_op jit(solution)/shard_map/convert_element_type | solution.py:255
  165.8 16.4 %collective-permute-done.20 = f32[98304]{0:T(1024)S(1)} collective-permute-done((f32[98304]{0:T(1024)S(1)}, f32[98304]{0:T(1024)S(1)}, u32[]{:S(2)}, u32[]{:S(2)}) %collective-permute-start.20) | collective-permute-done | bytes 393248 | tf_op jit(solution)/shard_map/ppermute | solution.py:86
  (221 shorter events, 62.0 us)
Async XLA Ops:
  7.2 38.4 %copy-start = (bf16[2688,256]{1,0:T(8,128)(2,1)S(1)}, bf16[2688,256]{1,0:T(8,128)(2,1)}, u32[]{:S(2)}) copy-start(bf16[2688,256]{1,0:T(8,128)(2,1)} %param.26) | copy-start | bytes 4128772
  7.2 22.4 %all-gather.2.cloned.1.call-start = ((), (), s32[]{:S(2)}) async-start(), calls=%async_computation | async-start | bytes 2064384 | tf_op jit(solution)/shard_map/all_gather | solution.py:127
  12.2 16.1 %collective-permute-start.7 = (s32[256]{0:T(256)S(1)}, s32[256]{0:T(256)S(1)}, u32[]{:S(2)}, u32[]{:S(2)}) collective-permute-start(s32[256]{0:T(256)S(1)} %get-tuple-element.30), channel_id=1, source_target_pairs={{0,2},{2,4},{4,6},{6,8},{8,10},{10,12},{12,14},{1,3},{3,5},{5,7},{... | collective-permute-start | bytes 3080 | tf_op jit(solution)/shard_map/ppermute | solution.py:17
  17.0 11.2 %collective-permute-start.6 = (s32[256]{0:T(256)S(1)}, s32[256]{0:T(256)S(1)}, u32[]{:S(2)}, u32[]{:S(2)}) collective-permute-start(s32[256]{0:T(256)S(1)} %get-tuple-element.30), channel_id=1, source_target_pairs={{0,4},{2,6},{4,8},{6,10},{8,12},{10,14},{1,5},{3,7},{5,9},{7,11},{... | collective-permute-start | bytes 3080 | tf_op jit(solution)/shard_map/ppermute | solution.py:17
  20.5 7.7 %collective-permute-start.5 = (s32[256]{0:T(256)S(1)}, s32[256]{0:T(256)S(1)}, u32[]{:S(2)}, u32[]{:S(2)}) collective-permute-start(s32[256]{0:T(256)S(1)} %get-tuple-element.30), channel_id=1, source_target_pairs={{0,6},{2,8},{4,10},{6,12},{8,14},{1,7},{3,9},{5,11},{7,13},{9,15},... | collective-permute-start | bytes 3080 | tf_op jit(solution)/shard_map/ppermute | solution.py:17
  25.0 3.2 %collective-permute-start.4 = (s32[256]{0:T(256)S(1)}, s32[256]{0:T(256)S(1)}, u32[]{:S(2)}, u32[]{:S(2)}) collective-permute-start(s32[256]{0:T(256)S(1)} %get-tuple-element.30), channel_id=1, source_target_pairs={{0,8},{2,10},{4,12},{6,14},{1,9},{3,11},{5,13},{7,15},{16,24},{18,... | collective-permute-start | bytes 3080 | tf_op jit(solution)/shard_map/ppermute | solution.py:17
  27.0 27.7 %copy-start.45 = (f32[256]{0:T(256)}, f32[256]{0:T(256)S(1)}, u32[]{:S(2)}) copy-start(f32[256]{0:T(256)S(1)} %fusion.76) | copy-start | bytes 3076
  33.6 16.4 %collective-permute-start.3 = (bf16[256,256]{0,1:T(8,128)(2,1)S(1)}, bf16[256,256]{0,1:T(8,128)(2,1)S(1)}, u32[]{:S(2)}, u32[]{:S(2)}) collective-permute-start(bf16[256,256]{0,1:T(8,128)(2,1)S(1)} %pad_maximum_fusion.9), channel_id=1, source_target_pairs={{0,2},{2,4},{4,6},{6,8},{8,10},{10,12},{12,14},{1,3},{3,5},{5,7},{... | collective-permute-start | bytes 393224 | tf_op jit(solution)/shard_map/ppermute | solution.py:17
  36.3 12.9 %collective-permute-start.2 = (bf16[256,256]{0,1:T(8,128)(2,1)S(1)}, bf16[256,256]{0,1:T(8,128)(2,1)S(1)}, u32[]{:S(2)}, u32[]{:S(2)}) collective-permute-start(bf16[256,256]{0,1:T(8,128)(2,1)S(1)} %pad_maximum_fusion.9), channel_id=1, source_target_pairs={{0,4},{2,6},{4,8},{6,10},{8,12},{10,14},{1,5},{3,7},{5,9},{7,11},{... | collective-permute-start | bytes 393224 | tf_op jit(solution)/shard_map/ppermute | solution.py:17
  39.2 9.4 %collective-permute-start.1 = (bf16[256,256]{0,1:T(8,128)(2,1)S(1)}, bf16[256,256]{0,1:T(8,128)(2,1)S(1)}, u32[]{:S(2)}, u32[]{:S(2)}) collective-permute-start(bf16[256,256]{0,1:T(8,128)(2,1)S(1)} %pad_maximum_fusion.9), channel_id=1, source_target_pairs={{0,6},{2,8},{4,10},{6,12},{8,14},{1,7},{3,9},{5,11},{7,13},{9,15},... | collective-permute-start | bytes 393224 | tf_op jit(solution)/shard_map/ppermute | solution.py:17
  44.0 3.9 %collective-permute-start = (bf16[256,256]{0,1:T(8,128)(2,1)S(1)}, bf16[256,256]{0,1:T(8,128)(2,1)S(1)}, u32[]{:S(2)}, u32[]{:S(2)}) collective-permute-start(bf16[256,256]{0,1:T(8,128)(2,1)S(1)} %pad_maximum_fusion.9), channel_id=1, source_target_pairs={{0,8},{2,10},{4,12},{6,14},{1,9},{3,11},{5,13},{7,15},{16,24},{18,... | collective-permute-start | bytes 393224 | tf_op jit(solution)/shard_map/ppermute | solution.py:17
  59.6 2.4 %collective-permute-start.8 = (bf16[128,2688]{1,0:T(8,128)(2,1)}, bf16[128,2688]{1,0:T(8,128)(2,1)S(1)}, u32[]{:S(2)}, u32[]{:S(2)}) collective-permute-start(bf16[128,2688]{1,0:T(8,128)(2,1)} %constant_dynamic-slice_fusion.3), channel_id=1, source_target_pairs={{0,1},{1,0},{2,3},{3,2},{4,5},{5,4},{6,7},{7,6},{8,9},{9,8},{10,11... | collective-permute-start | bytes 2064392 | tf_op jit(solution)/shard_map/ppermute | solution.py:65
  59.8 2.0 %collective-permute-start.9 = (bf16[128,16]{0,1:T(8,128)(2,1)S(1)}, bf16[128,16]{0,1:T(8,128)(2,1)S(1)}, u32[]{:S(2)}, u32[]{:S(2)}) collective-permute-start(bf16[128,16]{0,1:T(8,128)(2,1)S(1)} %constant_dynamic-slice_fusion.2), channel_id=1, source_target_pairs={{0,1},{1,0},{2,3},{3,2},{4,5},{5,4},{6,7},{7,6},{8,9},{9,8},{10,11... | collective-permute-start | bytes 12296 | tf_op jit(solution)/shard_map/ppermute | solution.py:65
  65.6 1.2 collective-permute-start.11
  65.8 5.3 %collective-permute-start.10 = (bf16[128,2688]{1,0:T(8,128)(2,1)S(1)}, bf16[128,2688]{1,0:T(8,128)(2,1)}, u32[]{:S(2)}, u32[]{:S(2)}) collective-permute-start(bf16[128,2688]{1,0:T(8,128)(2,1)S(1)} %get-tuple-element.16), channel_id=1, source_target_pairs={{0,1},{1,0},{2,3},{3,2},{4,5},{5,4},{6,7},{7,6},{8,9},{9,8},{10,11... | collective-permute-start | bytes 2064392 | tf_op jit(solution)/shard_map/ppermute | solution.py:72
  99.7 7.7 %collective-permute-start.12 = (bf16[256,256]{0,1:T(8,128)(2,1)S(1)}, bf16[256,256]{0,1:T(8,128)(2,1)S(1)}, u32[]{:S(2)}, u32[]{:S(2)}) collective-permute-start(bf16[256,256]{0,1:T(8,128)(2,1)S(1)} %get-tuple-element.20), channel_id=1, source_target_pairs={{2,0},{4,2},{6,4},{8,6},{10,8},{12,10},{14,12},{3,1},{5,3},{7,5},{... | collective-permute-start | bytes 393224 | tf_op jit(solution)/shard_map/ppermute | solution.py:17
  101.2 22.6 %collective-permute-start.15 = (bf16[256,256]{0,1:T(8,128)(2,1)S(1)}, bf16[256,256]{0,1:T(8,128)(2,1)S(1)}, u32[]{:S(2)}, u32[]{:S(2)}) collective-permute-start(bf16[256,256]{0,1:T(8,128)(2,1)S(1)} %get-tuple-element.21), channel_id=1, source_target_pairs={{8,0},{10,2},{12,4},{14,6},{9,1},{11,3},{13,5},{15,7},{24,16},{26,... | collective-permute-start | bytes 393224 | tf_op jit(solution)/shard_map/ppermute | solution.py:17
  102.5 21.3 %collective-permute-start.14 = (bf16[256,256]{0,1:T(8,128)(2,1)S(1)}, bf16[256,256]{0,1:T(8,128)(2,1)S(1)}, u32[]{:S(2)}, u32[]{:S(2)}) collective-permute-start(bf16[256,256]{0,1:T(8,128)(2,1)S(1)} %get-tuple-element.22), channel_id=1, source_target_pairs={{6,0},{8,2},{10,4},{12,6},{14,8},{7,1},{9,3},{11,5},{13,7},{15,9},... | collective-permute-start | bytes 393224 | tf_op jit(solution)/shard_map/ppermute | solution.py:17
  103.8 20.0 %collective-permute-start.13 = (bf16[256,256]{0,1:T(8,128)(2,1)S(1)}, bf16[256,256]{0,1:T(8,128)(2,1)S(1)}, u32[]{:S(2)}, u32[]{:S(2)}) collective-permute-start(bf16[256,256]{0,1:T(8,128)(2,1)S(1)} %get-tuple-element.23), channel_id=1, source_target_pairs={{4,0},{6,2},{8,4},{10,6},{12,8},{14,10},{5,1},{7,3},{9,5},{11,7},{... | collective-permute-start | bytes 393224 | tf_op jit(solution)/shard_map/ppermute | solution.py:17
  125.5 3.0 %collective-permute-start.17 = (bf16[1344,48]{0,1:T(8,128)(2,1)S(1)}, bf16[1344,48]{0,1:T(8,128)(2,1)S(1)}, u32[]{:S(2)}, u32[]{:S(2)}) collective-permute-start(bf16[1344,48]{0,1:T(8,128)(2,1)S(1)} %constant_dynamic-slice_fusion), channel_id=1, source_target_pairs={{0,1},{1,0},{2,3},{3,2},{4,5},{5,4},{6,7},{7,6},{8,9},{9,8},{10,11... | collective-permute-start | bytes 387080 | tf_op jit(solution)/shard_map/ppermute | solution.py:65
  128.5 25.1 %collective-permute-start.16 = (bf16[128,2688]{1,0:T(8,128)(2,1)}, bf16[128,2688]{1,0:T(8,128)(2,1)}, u32[]{:S(2)}, u32[]{:S(2)}) collective-permute-start(bf16[128,2688]{1,0:T(8,128)(2,1)} %constant_dynamic-slice_fusion.1), channel_id=1, source_target_pairs={{0,1},{1,0},{2,3},{3,2},{4,5},{5,4},{6,7},{7,6},{8,9},{9,8},{10,11... | collective-permute-start | bytes 2064392 | tf_op jit(solution)/shard_map/ppermute | solution.py:65
  136.6 14.0 %collective-permute-start.18 = (f32[98304]{0:T(1024)S(1)}, f32[98304]{0:T(1024)S(1)}, u32[]{:S(2)}, u32[]{:S(2)}) collective-permute-start(f32[98304]{0:T(1024)S(1)} %constant_dynamic-update-slice_fusion.11), channel_id=1, source_target_pairs={{0,2},{2,0},{4,6},{6,4},{8,10},{10,8},{12,14},{14,12},{1,3},{3,1},... | collective-permute-start | bytes 1179656 | tf_op jit(solution)/shard_map/ppermute | solution.py:86
  150.6 11.9 %collective-permute-start.19 = (f32[98304]{0:T(1024)S(1)}, f32[98304]{0:T(1024)S(1)}, u32[]{:S(2)}, u32[]{:S(2)}) collective-permute-start(f32[98304]{0:T(1024)S(1)} %add.159), channel_id=1, source_target_pairs={{0,4},{2,6},{4,0},{6,2},{8,12},{10,14},{12,8},{14,10},{1,5},{3,7},... | collective-permute-start | bytes 1179656 | tf_op jit(solution)/shard_map/ppermute | solution.py:86
  162.6 19.6 %collective-permute-start.20 = (f32[98304]{0:T(1024)S(1)}, f32[98304]{0:T(1024)S(1)}, u32[]{:S(2)}, u32[]{:S(2)}) collective-permute-start(f32[98304]{0:T(1024)S(1)} %add.160), channel_id=1, source_target_pairs={{0,8},{2,10},{4,12},{6,14},{8,0},{10,2},{12,4},{14,6},{1,9},{3,11}... | collective-permute-start | bytes 1179656 | tf_op jit(solution)/shard_map/ppermute | solution.py:86
  (48 other events, 422.8 us)
Sparse Core Ops, SparseCore 0:
  11.6 12.2 all-gather.1

commit v4 on v3

--- a/solution.py
+++ b/solution.py
@@ -83,7 +83,9 @@
     flat = jnp.concatenate([p.astype(jnp.float32).reshape(-1) for p in parts])
     step = 1
     while step < count:
-        flat = flat + lax.ppermute(flat, "ctx", [(i, i ^ step) for i in range(count)])
+        sent = flat.astype(jnp.bfloat16)
+        received = lax.ppermute(sent, "ctx", [(i, i ^ step) for i in range(count)])
+        flat = sent.astype(jnp.float32) + received.astype(jnp.float32)
         step *= 2
     results, offset = [], 0
     for p in parts:

time: 194 us -> 161 us (0.83)
  waiting for transfers between devices: 57.1 us -> 41.8 us
  local copies, waits for them, and re-layouts: 24.4 us -> 13.7 us
  starting transfers between devices: 41.1 us -> 31.6 us
  matrix products: 39.3 us -> 43.5 us
  other arithmetic: 15.5 us -> 13.3 us
    ppermute x3, waiting for transfers between devices: 33.5 us -> 16.5 us  [ctx_sum(): received = lax.ppermute(sent, 'ctx', [(i, i ^ step) for i in range(count)])]
    ppermute x3, starting transfers between devices: 7.99 us -> 0.21 us  [ctx_sum(): received = lax.ppermute(sent, 'ctx', [(i, i ^ step) for i in range(count)])]
    dot_general x10, matrix products: 5.89 us -> 11.6 us  [multiply_by_transpose(): lax.dot_general(first_op, second_op, (((1,), (1,)), ((), ())), preferred_...]
    unnamed x114 -> x122, local copies, waits for them, and re-layouts: 12.6 us -> 7.16 us
    reshape x3, local copies, waits for them, and re-layouts: 5.48 us -> 2.68 us  [ctx_sum(): flat = jnp.concatenate([p.astype(jnp.float32).reshape(-1) for p in parts])]
  transfers between devices with their start and end apart: 22 -> 22, of which waited for: 10 -> 11; matrix products, arithmetic and copies ran while one was open for 12% -> 10% of each run, Pallas kernels for 0% -> 0%
where the time goes in v4:
time: 161 us; the launch traced here: 160 us
  matrix products  43.5 us (27%)
  waiting for transfers between devices  41.8 us (26%)
  starting transfers between devices  31.6 us (20%)
  between operations  15.8 us (10%)
  local copies, waits for them, and re-layouts  13.7 us (9%)
  other arithmetic  13.3 us (8%)
    ppermute x12, starting transfers between devices, passed_along(): lax.ppermute(value, axis, [(source, source + steps) for source in range(l...  30.1 us
    ppermute x12, waiting for transfers between devices, passed_along(): lax.ppermute(value, axis, [(source, source + steps) for source in range(l...  23 us
    ppermute x3, waiting for transfers between devices, ctx_sum(): received = lax.ppermute(sent, 'ctx', [(i, i ^ step) for i in range(count)])  16.5 us
    dot_general x10, matrix products, multiply_by_transpose(): lax.dot_general(first_op, second_op, (((1,), (1,)), ((), ())), preferred_...  11.6 us
    unnamed x122, local copies, waits for them, and re-layouts  7.16 us
    dot_general x10, matrix products, matrix_product(): return jnp.dot(first_op, second_op, preferred_element_type=jnp.float32)  6.9 us
    dot_general x1, matrix products, on_device(): jnp.einsum('hts,thd->sd', grad_scores, query_normed, preferred_element_ty...  5.71 us
    dot_general x1, matrix products, on_device(): jnp.einsum('hts,sd->thd', grad_scores, keys_all, preferred_element_type=j...  5.65 us
  transfers between devices with their start and end apart: 22, of which 11 were waited for; matrix products, arithmetic and copies ran while one was open for 10% of the time, Pallas kernels for 0%

profile of v4, /device:TPU:0, one launch (start us, length us, event | category | flops | bytes accessed | tf_op | source)
XLA Modules:
  0.0 159.7 jit_solution(2829705394573438584)
XLA Ops:
  8.7 2.2 %fusion.21 = bf16[128,2688]{1,0:T(8,128)(2,1)} fusion(bf16[128,2688]{1,0:T(8,128)(2,1)} %param.18, f32[2688]{0:T(1024)} %param.22, f32[128]{0:T(128)S(1)} %add_rsqrt_fusion.3), kind=kLoop, calls=%fused_computation.36 | loop fusion | flops 1376256 | bytes 1387520 | tf_op jit(solution)/shard_map/convert_element_type | solution.py:128
  11.6 5.9 %collective-permute-start.4 = (s32[256]{0:T(256)S(1)}, s32[256]{0:T(256)S(1)}, u32[]{:S(2)}, u32[]{:S(2)}) collective-permute-start(s32[256]{0:T(256)S(1)} %get-tuple-element.30), channel_id=1, source_target_pairs={{0,8},{2,10},{4,12},{6,14},{1,9},{3,11},{5,13},{7,15},{16,24},{18,... | collective-permute-start | bytes 3080 | tf_op jit(solution)/shard_map/ppermute | solution.py:17
  17.6 4.4 %collective-permute-start.5 = (s32[256]{0:T(256)S(1)}, s32[256]{0:T(256)S(1)}, u32[]{:S(2)}, u32[]{:S(2)}) collective-permute-start(s32[256]{0:T(256)S(1)} %get-tuple-element.30), channel_id=1, source_target_pairs={{0,6},{2,8},{4,10},{6,12},{8,14},{1,7},{3,9},{5,11},{7,13},{9,15},... | collective-permute-start | bytes 3080 | tf_op jit(solution)/shard_map/ppermute | solution.py:17
  23.3 3.1 %collective-permute-start.7 = (s32[256]{0:T(256)S(1)}, s32[256]{0:T(256)S(1)}, u32[]{:S(2)}, u32[]{:S(2)}) collective-permute-start(s32[256]{0:T(256)S(1)} %get-tuple-element.30), channel_id=1, source_target_pairs={{0,2},{2,4},{4,6},{6,8},{8,10},{10,12},{12,14},{1,3},{3,5},{5,7},{... | collective-permute-start | bytes 3080 | tf_op jit(solution)/shard_map/ppermute | solution.py:17
  29.0 2.0 %convolution_convert_fusion.2 = bf16[256,48]{0,1:T(8,128)(2,1)S(1)} fusion(bf16[256,2688]{1,0:T(8,128)(2,1)} %all-gather.2.cloned.1.call-done, bf16[2688,48]{0,1:T(8,128)(2,1)} %param.30), kind=kOutput, calls=%fused_computation.75 | convolution fusion | flops 66072576 | bytes 1658880 | tf_op jit(solution)/shard_map/dot_general | solution.py:33
  32.9 3.9 %collective-permute-start = (bf16[256,256]{0,1:T(8,128)(2,1)S(1)}, bf16[256,256]{0,1:T(8,128)(2,1)S(1)}, u32[]{:S(2)}, u32[]{:S(2)}) collective-permute-start(bf16[256,256]{0,1:T(8,128)(2,1)S(1)} %pad_maximum_fusion.9), channel_id=1, source_target_pairs={{0,8},{2,10},{4,12},{6,14},{1,9},{3,11},{5,13},{7,15},{16,24},{18,... | collective-permute-start | bytes 393224 | tf_op jit(solution)/shard_map/ppermute | solution.py:17
  38.2 1.8 %collective-permute-start.2 = (bf16[256,256]{0,1:T(8,128)(2,1)S(1)}, bf16[256,256]{0,1:T(8,128)(2,1)S(1)}, u32[]{:S(2)}, u32[]{:S(2)}) collective-permute-start(bf16[256,256]{0,1:T(8,128)(2,1)S(1)} %pad_maximum_fusion.9), channel_id=1, source_target_pairs={{0,4},{2,6},{4,8},{6,10},{8,12},{10,14},{1,5},{3,7},{5,9},{7,11},{... | collective-permute-start | bytes 393224 | tf_op jit(solution)/shard_map/ppermute | solution.py:17
  40.0 2.8 %collective-permute-start.3 = (bf16[256,256]{0,1:T(8,128)(2,1)S(1)}, bf16[256,256]{0,1:T(8,128)(2,1)S(1)}, u32[]{:S(2)}, u32[]{:S(2)}) collective-permute-start(bf16[256,256]{0,1:T(8,128)(2,1)S(1)} %pad_maximum_fusion.9), channel_id=1, source_target_pairs={{0,2},{2,4},{4,6},{6,8},{8,10},{10,12},{12,14},{1,3},{3,5},{5,7},{... | collective-permute-start | bytes 393224 | tf_op jit(solution)/shard_map/ppermute | solution.py:17
  47.3 3.4 %fusion.31 = f32[2,256,1280]{1,2,0:T(8,128)} fusion(pred[256,1280]{0,1:T(8,128)(4,1)S(1)} %copy-done.26, bf16[1280,256]{0,1:T(8,128)(2,1)} %constant_dynamic-update-slice_fusion, f32[256,256]{0,1:T(8,128)S(1)} %get-tuple-element.35, f32[128]{0:T(128)S(1)} %copy-done.52, f32[256,2]{0,1:T(2,128)S(1)} %add_rsqrt_fusion), kind=kOutput, calls=%fused_computation.53 | convolution fusion | flops 169936640 | bytes 3541504 | tf_op jit(solution)/shard_map/div | solution.py:169
  50.7 2.3 %fusion.46 = bf16[128,2,256]{2,0,1:T(8,128)(2,1)S(1)} fusion(f32[2,256,1280]{1,2,0:T(8,128)} %fusion.31, bf16[1280,256]{0,1:T(8,128)(2,1)} %constant_dynamic-update-slice_fusion, f32[256]{0:T(256)S(1)} %fusion.80), kind=kOutput, calls=%fused_computation.68 | convolution fusion | flops 168558592 | bytes 3081216 | tf_op jit(solution)/shard_map/hts,sd->thd/dot_general | solution.py:171
  68.1 3.2 %convolution_bitcast_fusion = f32[2,256,1280]{1,2,0:T(8,128)} fusion(bf16[256,2,128]{0,2,1:T(8,128)(2,1)S(1)} %bitcast.104, bf16[1280,256]{0,1:T(8,128)(2,1)} %constant_dynamic-update-slice_fusion), kind=kOutput, calls=%fused_computation.12 | convolution fusion | flops 167772160 | bytes 3080192 | tf_op jit(solution)/shard_map/thd,sd->hts/dot_general | solution.py:206
  71.9 5.6 %multiply_reduce_fusion.3 = (f32[256,2]{0,1:T(2,128)S(1)}, f32[256,2,128]{0,2,1:T(8,128)}) fusion(f32[256,256]{0,1:T(8,128)} %copy-done.19, f32[256,2]{0,1:T(2,128)S(1)} %copy-done.44, f32[128]{0:T(128)S(1)} %copy-done.53, f32[2,256,1280]{1,2,0:T(8,128)} %fusion.31, f32[2,256,1280]{1,2,0:T(8,128)} %convolution_bitcast_fusion, ...), kind=kOutput, calls=%fused_computation.114 | convolution fusion | flops 171312384 | bytes 11342336 | tf_op jit(solution)/shard_map/hts,sd->thd/dot_general | solution.py:211
  77.5 5.7 %convolution_bitcast_fusion.2 = f32[1280,128]{0,1:T(8,128)} fusion(f32[2,256,1280]{1,2,0:T(8,128)} %fusion.31, f32[2,256,1280]{1,2,0:T(8,128)} %convolution_bitcast_fusion, f32[256,256]{0,1:T(8,128)} %copy-done.19, f32[128]{0:T(128)S(1)} %copy-done.53, f32[256,2]{0,1:T(2,128)S(1)} %copy-done.44), kind=kOutput, calls=%fused_computation.18 | convolution fusion | flops 171247360 | bytes 6162944 | tf_op jit(solution)/shard_map/hts,thd->sd/dot_general | solution.py:214
  85.8 2.1 %fusion.97 = f32[256,2688]{1,0:T(8,128)} fusion(bf16[256,256]{0,1:T(8,128)(2,1)S(1)} %bitcast.102, bf16[2688,256]{1,0:T(8,128)(2,1)S(1)} %copy-done), kind=kOutput, calls=%fused_computation.186 | convolution fusion | flops 352321536 | bytes 4259840 | tf_op jit(solution)/shard_map/dot_general | solution.py:37
  97.5 2.0 %collective-permute-done.12 = bf16[256,256]{0,1:T(8,128)(2,1)S(1)} collective-permute-done((bf16[256,256]{0,1:T(8,128)(2,1)S(1)}, bf16[256,256]{0,1:T(8,128)(2,1)S(1)}, u32[]{:S(2)}, u32[]{:S(2)}) %collective-permute-start.12) | collective-permute-done | bytes 131104 | tf_op jit(solution)/shard_map/ppermute | solution.py:17
  99.5 4.4 %collective-permute-done.13 = bf16[256,256]{0,1:T(8,128)(2,1)S(1)} collective-permute-done((bf16[256,256]{0,1:T(8,128)(2,1)S(1)}, bf16[256,256]{0,1:T(8,128)(2,1)S(1)}, u32[]{:S(2)}, u32[]{:S(2)}) %collective-permute-start.13) | collective-permute-done | bytes 131104 | tf_op jit(solution)/shard_map/ppermute | solution.py:17
  103.9 4.2 %collective-permute-done.14 = bf16[256,256]{0,1:T(8,128)(2,1)S(1)} collective-permute-done((bf16[256,256]{0,1:T(8,128)(2,1)S(1)}, bf16[256,256]{0,1:T(8,128)(2,1)S(1)}, u32[]{:S(2)}, u32[]{:S(2)}) %collective-permute-start.14) | collective-permute-done | bytes 131104 | tf_op jit(solution)/shard_map/ppermute | solution.py:17
  108.1 11.2 %collective-permute-done.15 = bf16[256,256]{0,1:T(8,128)(2,1)S(1)} collective-permute-done((bf16[256,256]{0,1:T(8,128)(2,1)S(1)}, bf16[256,256]{0,1:T(8,128)(2,1)S(1)}, u32[]{:S(2)}, u32[]{:S(2)}) %collective-permute-start.15) | collective-permute-done | bytes 131104 | tf_op jit(solution)/shard_map/ppermute | solution.py:17
  121.4 2.1 %convolution_add_fusion.1 = f32[256,2688]{1,0:T(8,128)} fusion(f32[256,2688]{1,0:T(8,128)S(1)} %copy-done.2, bf16[256,128]{0,1:T(8,128)(2,1)S(1)} %multiply_convert_fusion.4, bf16[2688,128]{1,0:T(8,128)(2,1)S(1)} %copy-done.9), kind=kOutput, calls=%fused_computation.2 | convolution fusion | flops 176848896 | bytes 6258688 | tf_op jit(solution)/shard_map/dot_general | solution.py:37
  123.5 2.1 %fusion.70 = f32[256,2688]{1,0:T(8,128)} fusion(bf16[2688,48]{0,1:T(8,128)(2,1)S(1)} %copy-done.20, bf16[256,16]{0,1:T(8,128)(2,1)S(1)} %fusion.52, bf16[256,16]{0,1:T(8,128)(2,1)S(1)} %fusion.51, bf16[256,16]{0,1:T(8,128)(2,1)S(1)} %fusion.50), kind=kOutput, calls=%fused_computation.134 | convolution fusion | flops 66134016 | bytes 3035136 | tf_op jit(solution)/shard_map/dot_general | solution.py:37
  126.8 3.2 %fusion.2 = bf16[256,2688]{1,0:T(8,128)(2,1)S(1)} fusion(f32[256,2688]{1,0:T(8,128)} %fusion.70, f32[256,2688]{1,0:T(8,128)} %convolution_add_fusion.1, bf16[2688,128]{1,0:T(8,128)(2,1)S(1)} %copy-done.12, f32[256,256]{0,1:T(8,128)S(1)} %copy-done.7), kind=kOutput, calls=%fused_computation.5 | convolution fusion | flops 178225152 | bytes 7634944 | tf_op jit(solution)/shard_map/dot_general | solution.py:37
  130.0 3.3 %collective-permute-done.18 = bf16[98304]{0:T(1024)(128)(2,1)S(1)} collective-permute-done((bf16[98304]{0:T(1024)(128)(2,1)S(1)}, bf16[98304]{0:T(1024)(128)(2,1)S(1)}, u32[]{:S(2)}, u32[]{:S(2)}) %collective-permute-start.18) | collective-permute-done | bytes 196640 | tf_op jit(solution)/shard_map/ppermute | solution.py:87
  133.6 5.5 %collective-permute-done.19 = bf16[98304]{0:T(1024)(128)(2,1)S(1)} collective-permute-done((bf16[98304]{0:T(1024)(128)(2,1)S(1)}, bf16[98304]{0:T(1024)(128)(2,1)S(1)}, u32[]{:S(2)}, u32[]{:S(2)}) %collective-permute-start.19) | collective-permute-done | bytes 196640 | tf_op jit(solution)/shard_map/ppermute | solution.py:87
  141.1 7.7 %collective-permute-done.20 = bf16[98304]{0:T(1024)(128)(2,1)S(1)} collective-permute-done((bf16[98304]{0:T(1024)(128)(2,1)S(1)}, bf16[98304]{0:T(1024)(128)(2,1)S(1)}, u32[]{:S(2)}, u32[]{:S(2)}) %collective-permute-start.20) | collective-permute-done | bytes 196640 | tf_op jit(solution)/shard_map/ppermute | solution.py:87
  (230 shorter events, 49.8 us)
Async XLA Ops:
  7.2 35.9 %copy-start = (bf16[2688,256]{1,0:T(8,128)(2,1)S(1)}, bf16[2688,256]{1,0:T(8,128)(2,1)}, u32[]{:S(2)}) copy-start(bf16[2688,256]{1,0:T(8,128)(2,1)} %param.26) | copy-start | bytes 4128772
  7.2 21.8 %all-gather.2.cloned.1.call-start = ((), (), s32[]{:S(2)}) async-start(), calls=%async_computation | async-start | bytes 2064384 | tf_op jit(solution)/shard_map/all_gather | solution.py:129
  11.6 14.8 %collective-permute-start.4 = (s32[256]{0:T(256)S(1)}, s32[256]{0:T(256)S(1)}, u32[]{:S(2)}, u32[]{:S(2)}) collective-permute-start(s32[256]{0:T(256)S(1)} %get-tuple-element.30), channel_id=1, source_target_pairs={{0,8},{2,10},{4,12},{6,14},{1,9},{3,11},{5,13},{7,15},{16,24},{18,... | collective-permute-start | bytes 3080 | tf_op jit(solution)/shard_map/ppermute | solution.py:17
  17.6 8.9 %collective-permute-start.5 = (s32[256]{0:T(256)S(1)}, s32[256]{0:T(256)S(1)}, u32[]{:S(2)}, u32[]{:S(2)}) collective-permute-start(s32[256]{0:T(256)S(1)} %get-tuple-element.30), channel_id=1, source_target_pairs={{0,6},{2,8},{4,10},{6,12},{8,14},{1,7},{3,9},{5,11},{7,13},{9,15},... | collective-permute-start | bytes 3080 | tf_op jit(solution)/shard_map/ppermute | solution.py:17
  22.0 4.5 %collective-permute-start.6 = (s32[256]{0:T(256)S(1)}, s32[256]{0:T(256)S(1)}, u32[]{:S(2)}, u32[]{:S(2)}) collective-permute-start(s32[256]{0:T(256)S(1)} %get-tuple-element.30), channel_id=1, source_target_pairs={{0,4},{2,6},{4,8},{6,10},{8,12},{10,14},{1,5},{3,7},{5,9},{7,11},{... | collective-permute-start | bytes 3080 | tf_op jit(solution)/shard_map/ppermute | solution.py:17
  23.3 4.4 %collective-permute-start.7 = (s32[256]{0:T(256)S(1)}, s32[256]{0:T(256)S(1)}, u32[]{:S(2)}, u32[]{:S(2)}) collective-permute-start(s32[256]{0:T(256)S(1)} %get-tuple-element.30), channel_id=1, source_target_pairs={{0,2},{2,4},{4,6},{6,8},{8,10},{10,12},{12,14},{1,3},{3,5},{5,7},{... | collective-permute-start | bytes 3080 | tf_op jit(solution)/shard_map/ppermute | solution.py:17
  32.9 10.9 %collective-permute-start = (bf16[256,256]{0,1:T(8,128)(2,1)S(1)}, bf16[256,256]{0,1:T(8,128)(2,1)S(1)}, u32[]{:S(2)}, u32[]{:S(2)}) collective-permute-start(bf16[256,256]{0,1:T(8,128)(2,1)S(1)} %pad_maximum_fusion.9), channel_id=1, source_target_pairs={{0,8},{2,10},{4,12},{6,14},{1,9},{3,11},{5,13},{7,15},{16,24},{18,... | collective-permute-start | bytes 393224 | tf_op jit(solution)/shard_map/ppermute | solution.py:17
  36.8 7.7 %collective-permute-start.1 = (bf16[256,256]{0,1:T(8,128)(2,1)S(1)}, bf16[256,256]{0,1:T(8,128)(2,1)S(1)}, u32[]{:S(2)}, u32[]{:S(2)}) collective-permute-start(bf16[256,256]{0,1:T(8,128)(2,1)S(1)} %pad_maximum_fusion.9), channel_id=1, source_target_pairs={{0,6},{2,8},{4,10},{6,12},{8,14},{1,7},{3,9},{5,11},{7,13},{9,15},... | collective-permute-start | bytes 393224 | tf_op jit(solution)/shard_map/ppermute | solution.py:17
  38.2 7.1 %collective-permute-start.2 = (bf16[256,256]{0,1:T(8,128)(2,1)S(1)}, bf16[256,256]{0,1:T(8,128)(2,1)S(1)}, u32[]{:S(2)}, u32[]{:S(2)}) collective-permute-start(bf16[256,256]{0,1:T(8,128)(2,1)S(1)} %pad_maximum_fusion.9), channel_id=1, source_target_pairs={{0,4},{2,6},{4,8},{6,10},{8,12},{10,14},{1,5},{3,7},{5,9},{7,11},{... | collective-permute-start | bytes 393224 | tf_op jit(solution)/shard_map/ppermute | solution.py:17
  40.0 5.9 %collective-permute-start.3 = (bf16[256,256]{0,1:T(8,128)(2,1)S(1)}, bf16[256,256]{0,1:T(8,128)(2,1)S(1)}, u32[]{:S(2)}, u32[]{:S(2)}) collective-permute-start(bf16[256,256]{0,1:T(8,128)(2,1)S(1)} %pad_maximum_fusion.9), channel_id=1, source_target_pairs={{0,2},{2,4},{4,6},{6,8},{8,10},{10,12},{12,14},{1,3},{3,5},{5,7},{... | collective-permute-start | bytes 393224 | tf_op jit(solution)/shard_map/ppermute | solution.py:17
  55.6 2.4 %collective-permute-start.8 = (bf16[128,2688]{1,0:T(8,128)(2,1)}, bf16[128,2688]{1,0:T(8,128)(2,1)S(1)}, u32[]{:S(2)}, u32[]{:S(2)}) collective-permute-start(bf16[128,2688]{1,0:T(8,128)(2,1)} %constant_dynamic-slice_fusion.3), channel_id=1, source_target_pairs={{0,1},{1,0},{2,3},{3,2},{4,5},{5,4},{6,7},{7,6},{8,9},{9,8},{10,11... | collective-permute-start | bytes 2064392 | tf_op jit(solution)/shard_map/ppermute | solution.py:65
  55.7 2.0 %collective-permute-start.9 = (bf16[128,16]{0,1:T(8,128)(2,1)S(1)}, bf16[128,16]{0,1:T(8,128)(2,1)S(1)}, u32[]{:S(2)}, u32[]{:S(2)}) collective-permute-start(bf16[128,16]{0,1:T(8,128)(2,1)S(1)} %constant_dynamic-slice_fusion.2), channel_id=1, source_target_pairs={{0,1},{1,0},{2,3},{3,2},{4,5},{5,4},{6,7},{7,6},{8,9},{9,8},{10,11... | collective-permute-start | bytes 12296 | tf_op jit(solution)/shard_map/ppermute | solution.py:65
  61.5 1.2 collective-permute-start.11
  61.7 3.9 %collective-permute-start.10 = (bf16[128,2688]{1,0:T(8,128)(2,1)S(1)}, bf16[128,2688]{1,0:T(8,128)(2,1)}, u32[]{:S(2)}, u32[]{:S(2)}) collective-permute-start(bf16[128,2688]{1,0:T(8,128)(2,1)S(1)} %get-tuple-element.16), channel_id=1, source_target_pairs={{0,1},{1,0},{2,3},{3,2},{4,5},{5,4},{6,7},{7,6},{8,9},{9,8},{10,11... | collective-permute-start | bytes 2064392 | tf_op jit(solution)/shard_map/ppermute | solution.py:72
  90.5 28.8 %copy-start.13 = (f32[1280,128]{0,1:T(8,128)S(1)}, f32[1280,128]{0,1:T(8,128)}, u32[]{:S(2)}) copy-start(f32[1280,128]{0,1:T(8,128)} %convolution_bitcast_fusion.2) | copy-start | bytes 1966084
  91.8 7.7 %collective-permute-start.12 = (bf16[256,256]{0,1:T(8,128)(2,1)S(1)}, bf16[256,256]{0,1:T(8,128)(2,1)S(1)}, u32[]{:S(2)}, u32[]{:S(2)}) collective-permute-start(bf16[256,256]{0,1:T(8,128)(2,1)S(1)} %get-tuple-element.20), channel_id=1, source_target_pairs={{2,0},{4,2},{6,4},{8,6},{10,8},{12,10},{14,12},{3,1},{5,3},{7,5},{... | collective-permute-start | bytes 393224 | tf_op jit(solution)/shard_map/ppermute | solution.py:17
  93.2 10.7 %collective-permute-start.13 = (bf16[256,256]{0,1:T(8,128)(2,1)S(1)}, bf16[256,256]{0,1:T(8,128)(2,1)S(1)}, u32[]{:S(2)}, u32[]{:S(2)}) collective-permute-start(bf16[256,256]{0,1:T(8,128)(2,1)S(1)} %get-tuple-element.23), channel_id=1, source_target_pairs={{4,0},{6,2},{8,4},{10,6},{12,8},{14,10},{5,1},{7,3},{9,5},{11,7},{... | collective-permute-start | bytes 393224 | tf_op jit(solution)/shard_map/ppermute | solution.py:17
  94.5 13.6 %collective-permute-start.14 = (bf16[256,256]{0,1:T(8,128)(2,1)S(1)}, bf16[256,256]{0,1:T(8,128)(2,1)S(1)}, u32[]{:S(2)}, u32[]{:S(2)}) collective-permute-start(bf16[256,256]{0,1:T(8,128)(2,1)S(1)} %get-tuple-element.22), channel_id=1, source_target_pairs={{6,0},{8,2},{10,4},{12,6},{14,8},{7,1},{9,3},{11,5},{13,7},{15,9},... | collective-permute-start | bytes 393224 | tf_op jit(solution)/shard_map/ppermute | solution.py:17
  95.8 23.5 %collective-permute-start.15 = (bf16[256,256]{0,1:T(8,128)(2,1)S(1)}, bf16[256,256]{0,1:T(8,128)(2,1)S(1)}, u32[]{:S(2)}, u32[]{:S(2)}) collective-permute-start(bf16[256,256]{0,1:T(8,128)(2,1)S(1)} %get-tuple-element.21), channel_id=1, source_target_pairs={{8,0},{10,2},{12,4},{14,6},{9,1},{11,3},{13,5},{15,7},{24,16},{26,... | collective-permute-start | bytes 393224 | tf_op jit(solution)/shard_map/ppermute | solution.py:17
  120.5 5.1 %collective-permute-start.17 = (bf16[1344,48]{0,1:T(8,128)(2,1)S(1)}, bf16[1344,48]{0,1:T(8,128)(2,1)S(1)}, u32[]{:S(2)}, u32[]{:S(2)}) collective-permute-start(bf16[1344,48]{0,1:T(8,128)(2,1)S(1)} %constant_dynamic-slice_fusion), channel_id=1, source_target_pairs={{0,1},{1,0},{2,3},{3,2},{4,5},{5,4},{6,7},{7,6},{8,9},{9,8},{10,11... | collective-permute-start | bytes 387080 | tf_op jit(solution)/shard_map/ppermute | solution.py:65
  126.7 6.6 %collective-permute-start.18 = (bf16[98304]{0:T(1024)(128)(2,1)S(1)}, bf16[98304]{0:T(1024)(128)(2,1)S(1)}, u32[]{:S(2)}, u32[]{:S(2)}) collective-permute-start(bf16[98304]{0:T(1024)(128)(2,1)S(1)} %constant_dynamic-update-slice_fusion.11), channel_id=1, source_target_pairs={{0,2},{2,0},{4,6},{6,4},{8,10},{10,8},{12,14},{14,12},{1,3},{3,1},... | collective-permute-start | bytes 589832 | tf_op jit(solution)/shard_map/ppermute | solution.py:87
  133.4 5.7 %collective-permute-start.19 = (bf16[98304]{0:T(1024)(128)(2,1)S(1)}, bf16[98304]{0:T(1024)(128)(2,1)S(1)}, u32[]{:S(2)}, u32[]{:S(2)}) collective-permute-start(bf16[98304]{0:T(1024)(128)(2,1)S(1)} %add_convert_fusion.1), channel_id=1, source_target_pairs={{0,4},{2,6},{4,0},{6,2},{8,12},{10,14},{12,8},{14,10},{1,5},{3,7},... | collective-permute-start | bytes 589832 | tf_op jit(solution)/shard_map/ppermute | solution.py:87
  133.5 5.7 %collective-permute-start.16 = (bf16[128,2688]{1,0:T(8,128)(2,1)S(1)}, bf16[128,2688]{1,0:T(8,128)(2,1)S(1)}, u32[]{:S(2)}, u32[]{:S(2)}) collective-permute-start(bf16[128,2688]{1,0:T(8,128)(2,1)S(1)} %constant_dynamic-slice_fusion.1), channel_id=1, source_target_pairs={{0,1},{1,0},{2,3},{3,2},{4,5},{5,4},{6,7},{7,6},{8,9},{9,8},{10,11... | collective-permute-start | bytes 2064392 | tf_op jit(solution)/shard_map/ppermute | solution.py:65
  139.2 9.6 %collective-permute-start.20 = (bf16[98304]{0:T(1024)(128)(2,1)S(1)}, bf16[98304]{0:T(1024)(128)(2,1)S(1)}, u32[]{:S(2)}, u32[]{:S(2)}) collective-permute-start(bf16[98304]{0:T(1024)(128)(2,1)S(1)} %add_convert_fusion), channel_id=1, source_target_pairs={{0,8},{2,10},{4,12},{6,14},{8,0},{10,2},{12,4},{14,6},{1,9},{3,11}... | collective-permute-start | bytes 589832 | tf_op jit(solution)/shard_map/ppermute | solution.py:87
  (52 other events, 354.6 us)
Sparse Core Ops, SparseCore 0:
  11.0 12.2 all-gather.1

commit v5 on v4

--- a/solution.py
+++ b/solution.py
@@ -149,9 +149,15 @@
     valid_rows = is_valid.astype(jnp.float32)
     local_codes = jnp.where(is_valid, document_index + 1, 0)
     local_pair = jnp.concatenate([key_normed, value_cast], axis=1)
+    code_rows = jnp.zeros((16, local_pair.shape[1]), jnp.bfloat16)
+    code_rows = code_rows.at[0, :shard_len].set(local_codes.astype(jnp.bfloat16))
+    payload = jnp.concatenate([local_pair, code_rows], axis=0)
     received = []
     for hop_index in range(1, send_count + 1):
-        received.append(passed_along((local_pair, local_codes), "ctx", hop_index))
+        arrived = passed_along(payload, "ctx", hop_index)
+        received.append(
+            (arrived[:shard_len], arrived[shard_len, :shard_len].astype(jnp.int32))
+        )
     missing = reach_shards - send_count
     blank_pair = jnp.zeros_like(local_pair)
     blank_codes = jnp.zeros_like(local_codes)

time: 161 us -> 170 us (1.056)
  waiting for transfers between devices: 41.8 us -> 55.9 us
  starting transfers between devices: 31.6 us -> 27 us
    all_gather x1, waiting for transfers between devices: 0.01 us -> 11.5 us  [on_device(): normalized_input = lax.all_gather(normed_rows, 'tp', axis=0, tiled=True)]
    ppermute x12 -> x8, starting transfers between devices: 30.1 us -> 18.8 us  [passed_along(): lax.ppermute(value, axis, [(source, source + steps) for source in range(l...]
    ppermute x3, starting transfers between devices: 0.21 us -> 6.95 us  [ctx_sum(): received = lax.ppermute(sent, 'ctx', [(i, i ^ step) for i in range(count)])]
    ppermute x12 -> x8, waiting for transfers between devices: 23 us -> 27 us  [passed_along(): lax.ppermute(value, axis, [(source, source + steps) for source in range(l...]
    unnamed x122 -> x120, local copies, waits for them, and re-layouts: 7.16 us -> 7.73 us
  transfers between devices with their start and end apart: 22 -> 18, of which waited for: 11 -> 10; matrix products, arithmetic and copies ran while one was open for 10% -> 9% of each run, Pallas kernels for 0% -> 0%
where the time goes in v5:
time: 170 us
  waiting for transfers between devices  55.9 us (33%)
  matrix products  43.5 us (26%)
  starting transfers between devices  27 us (16%)
  between operations  15.8 us (9%)
  local copies, waits for them, and re-layouts  14.3 us (8%)
  other arithmetic  13.1 us (8%)
    ppermute x8, waiting for transfers between devices, passed_along(): lax.ppermute(value, axis, [(source, source + steps) for source in range(l...  27 us
    ppermute x8, starting transfers between devices, passed_along(): lax.ppermute(value, axis, [(source, source + steps) for source in range(l...  18.8 us
    ppermute x3, waiting for transfers between devices, ctx_sum(): received = lax.ppermute(sent, 'ctx', [(i, i ^ step) for i in range(count)])  15 us
    dot_general x10, matrix products, multiply_by_transpose(): lax.dot_general(first_op, second_op, (((1,), (1,)), ((), ())), preferred_...  11.6 us
    all_gather x1, waiting for transfers between devices, on_device(): normalized_input = lax.all_gather(normed_rows, 'tp', axis=0, tiled=True)  11.5 us
    unnamed x120, local copies, waits for them, and re-layouts  7.73 us
    ppermute x3, starting transfers between devices, ctx_sum(): received = lax.ppermute(sent, 'ctx', [(i, i ^ step) for i in range(count)])  6.95 us
    dot_general x10, matrix products, matrix_product(): return jnp.dot(first_op, second_op, preferred_element_type=jnp.float32)  6.88 us
  transfers between devices with their start and end apart: 18, of which 10 were waited for; matrix products, arithmetic and copies ran while one was open for 9% of the time, Pallas kernels for 0%

profile of v5, /device:TPU:0, one launch (start us, length us, event | category | flops | bytes accessed | tf_op | source)
XLA Modules:
  0.0 169.5 jit_solution(985383785272335674)
XLA Ops:
  9.2 2.2 %fusion.21 = bf16[128,2688]{1,0:T(8,128)(2,1)} fusion(bf16[128,2688]{1,0:T(8,128)(2,1)} %param.20, f32[2688]{0:T(1024)} %param.24, f32[128]{0:T(128)S(1)} %add_rsqrt_fusion.3), kind=kLoop, calls=%fused_computation.36 | loop fusion | flops 1376256 | bytes 1387520 | tf_op jit(solution)/shard_map/convert_element_type | solution.py:128
  12.3 11.5 %all-gather.2.cloned.1.call-done = bf16[256,2688]{1,0:T(8,128)(2,1)} async-done(((bf16[128,2688]{1,0:T(8,128)(2,1)}), bf16[256,2688]{1,0:T(8,128)(2,1)}) %all-gather.2.cloned.1.call-update) | async-done | bytes 1376272 | tf_op jit(solution)/shard_map/all_gather | solution.py:129
  23.8 2.0 %convolution_convert_fusion.2 = bf16[256,48]{0,1:T(8,128)(2,1)S(1)} fusion(bf16[256,2688]{1,0:T(8,128)(2,1)} %all-gather.2.cloned.1.call-done, bf16[2688,48]{0,1:T(8,128)(2,1)} %param.32), kind=kOutput, calls=%fused_computation.75 | convolution fusion | flops 66072576 | bytes 1658880 | tf_op jit(solution)/shard_map/dot_general | solution.py:33
  27.8 4.6 %collective-permute-start = (bf16[272,256]{0,1:T(8,128)(2,1)S(1)}, bf16[272,256]{0,1:T(8,128)(2,1)S(1)}, u32[]{:S(2)}, u32[]{:S(2)}) collective-permute-start(bf16[272,256]{0,1:T(8,128)(2,1)S(1)} %fusion.71), channel_id=1, source_target_pairs={{0,8},{2,10},{4,12},{6,14},{1,9},{3,11},{5,13},{7,15},{16,24},{18,... | collective-permute-start | bytes 417800 | tf_op jit(solution)/shard_map/ppermute | solution.py:17
  32.4 4.3 %collective-permute-start.1 = (bf16[272,256]{0,1:T(8,128)(2,1)S(1)}, bf16[272,256]{0,1:T(8,128)(2,1)S(1)}, u32[]{:S(2)}, u32[]{:S(2)}) collective-permute-start(bf16[272,256]{0,1:T(8,128)(2,1)S(1)} %fusion.71), channel_id=1, source_target_pairs={{0,6},{2,8},{4,10},{6,12},{8,14},{1,7},{3,9},{5,11},{7,13},{9,15},... | collective-permute-start | bytes 417800 | tf_op jit(solution)/shard_map/ppermute | solution.py:17
  38.0 3.1 %collective-permute-start.3 = (bf16[272,256]{0,1:T(8,128)(2,1)S(1)}, bf16[272,256]{0,1:T(8,128)(2,1)S(1)}, u32[]{:S(2)}, u32[]{:S(2)}) collective-permute-start(bf16[272,256]{0,1:T(8,128)(2,1)S(1)} %fusion.71), channel_id=1, source_target_pairs={{0,2},{2,4},{4,6},{6,8},{8,10},{10,12},{12,14},{1,3},{3,5},{5,7},{... | collective-permute-start | bytes 417800 | tf_op jit(solution)/shard_map/ppermute | solution.py:17
  43.5 1.9 %collective-permute-done.2 = bf16[272,256]{0,1:T(8,128)(2,1)S(1)} collective-permute-done((bf16[272,256]{0,1:T(8,128)(2,1)S(1)}, bf16[272,256]{0,1:T(8,128)(2,1)S(1)}, u32[]{:S(2)}, u32[]{:S(2)}) %collective-permute-start.2) | collective-permute-done | bytes 139296 | tf_op jit(solution)/shard_map/ppermute | solution.py:17
  48.6 3.4 %fusion.31 = f32[2,256,1280]{1,2,0:T(8,128)} fusion(pred[256,1280]{0,1:T(8,128)(4,1)S(1)} %fusion.35, bf16[1280,256]{0,1:T(8,128)(2,1)} %maximum_dynamic-update-slice_fusion, f32[256,256]{0,1:T(8,128)S(1)} %get-tuple-element.47, f32[128]{0:T(128)S(1)} %copy-done.51, f32[256,2]{0,1:T(2,128)S(1)} %add_rsqrt_fusion), kind=kOutput, calls=%fused_computation.53 | convolution fusion | flops 169936640 | bytes 3541504 | tf_op jit(solution)/shard_map/div | solution.py:175
  52.0 2.3 %fusion.46 = bf16[128,2,256]{2,0,1:T(8,128)(2,1)S(1)} fusion(f32[2,256,1280]{1,2,0:T(8,128)} %fusion.31, bf16[1280,256]{0,1:T(8,128)(2,1)} %maximum_dynamic-update-slice_fusion, f32[256]{0:T(256)S(1)} %fusion.82), kind=kOutput, calls=%fused_computation.68 | convolution fusion | flops 168558592 | bytes 3081216 | tf_op jit(solution)/shard_map/hts,sd->thd/dot_general | solution.py:177
  59.3 1.6 multiply_reduce_fusion.2
  69.4 3.2 %convolution_bitcast_fusion = f32[2,256,1280]{1,2,0:T(8,128)} fusion(bf16[256,2,128]{0,2,1:T(8,128)(2,1)S(1)} %bitcast.105, bf16[1280,256]{0,1:T(8,128)(2,1)} %maximum_dynamic-update-slice_fusion), kind=kOutput, calls=%fused_computation.12 | convolution fusion | flops 167772160 | bytes 3080192 | tf_op jit(solution)/shard_map/thd,sd->hts/dot_general | solution.py:212
  73.3 5.7 %multiply_reduce_fusion.3 = (f32[256,2]{0,1:T(2,128)S(1)}, f32[256,2,128]{0,2,1:T(8,128)}) fusion(f32[256,256]{0,1:T(8,128)} %copy-done.19, f32[256,2]{0,1:T(2,128)S(1)} %copy-done.43, f32[128]{0:T(128)S(1)} %copy-done.52, f32[2,256,1280]{1,2,0:T(8,128)} %fusion.31, f32[2,256,1280]{1,2,0:T(8,128)} %convolution_bitcast_fusion, ...), kind=kOutput, calls=%fused_computation.116 | convolution fusion | flops 171312384 | bytes 11342336 | tf_op jit(solution)/shard_map/hts,sd->thd/dot_general | solution.py:217
  78.9 5.7 %convolution_bitcast_fusion.2 = f32[1280,128]{0,1:T(8,128)} fusion(f32[2,256,1280]{1,2,0:T(8,128)} %fusion.31, f32[2,256,1280]{1,2,0:T(8,128)} %convolution_bitcast_fusion, f32[256,256]{0,1:T(8,128)} %copy-done.19, f32[128]{0:T(128)S(1)} %copy-done.52, f32[256,2]{0,1:T(2,128)S(1)} %copy-done.43), kind=kOutput, calls=%fused_computation.18 | convolution fusion | flops 171247360 | bytes 6162944 | tf_op jit(solution)/shard_map/hts,thd->sd/dot_general | solution.py:220
  87.2 2.1 %fusion.100 = f32[256,2688]{1,0:T(8,128)} fusion(bf16[256,256]{0,1:T(8,128)(2,1)S(1)} %bitcast.103, bf16[2688,256]{1,0:T(8,128)(2,1)S(1)} %copy-done), kind=kOutput, calls=%fused_computation.193 | convolution fusion | flops 352321536 | bytes 4259840 | tf_op jit(solution)/shard_map/dot_general | solution.py:37
  90.4 1.5 reshape.265
  98.9 17.6 %collective-permute-done.10 = bf16[256,256]{0,1:T(8,128)(2,1)S(1)} collective-permute-done((bf16[256,256]{0,1:T(8,128)(2,1)S(1)}, bf16[256,256]{0,1:T(8,128)(2,1)S(1)}, u32[]{:S(2)}, u32[]{:S(2)}) %collective-permute-start.10) | collective-permute-done | bytes 131104 | tf_op jit(solution)/shard_map/ppermute | solution.py:17
  116.6 7.4 %collective-permute-done.11 = bf16[256,256]{0,1:T(8,128)(2,1)S(1)} collective-permute-done((bf16[256,256]{0,1:T(8,128)(2,1)S(1)}, bf16[256,256]{0,1:T(8,128)(2,1)S(1)}, u32[]{:S(2)}, u32[]{:S(2)}) %collective-permute-start.11) | collective-permute-done | bytes 131104 | tf_op jit(solution)/shard_map/ppermute | solution.py:17
  126.0 2.1 %convolution_add_fusion.1 = f32[256,2688]{1,0:T(8,128)} fusion(f32[256,2688]{1,0:T(8,128)S(1)} %copy-done.2, bf16[256,128]{0,1:T(8,128)(2,1)S(1)} %multiply_convert_fusion.4, bf16[2688,128]{1,0:T(8,128)(2,1)S(1)} %copy-done.9), kind=kOutput, calls=%fused_computation.2 | convolution fusion | flops 176848896 | bytes 6258688 | tf_op jit(solution)/shard_map/dot_general | solution.py:37
  128.2 2.1 %fusion.72 = f32[256,2688]{1,0:T(8,128)} fusion(bf16[2688,48]{0,1:T(8,128)(2,1)S(1)} %copy-done.20, bf16[256,16]{0,1:T(8,128)(2,1)S(1)} %fusion.52, bf16[256,16]{0,1:T(8,128)(2,1)S(1)} %fusion.51, bf16[256,16]{0,1:T(8,128)(2,1)S(1)} %fusion.50), kind=kOutput, calls=%fused_computation.140 | convolution fusion | flops 66134016 | bytes 3035136 | tf_op jit(solution)/shard_map/dot_general | solution.py:37
  131.5 3.2 %fusion.2 = bf16[256,2688]{1,0:T(8,128)(2,1)S(1)} fusion(f32[256,2688]{1,0:T(8,128)} %fusion.72, f32[256,2688]{1,0:T(8,128)} %convolution_add_fusion.1, bf16[2688,128]{1,0:T(8,128)(2,1)S(1)} %copy-done.12, f32[256,256]{0,1:T(8,128)S(1)} %copy-done.7), kind=kOutput, calls=%fused_computation.5 | convolution fusion | flops 178225152 | bytes 7634944 | tf_op jit(solution)/shard_map/dot_general | solution.py:37
  134.7 3.3 %collective-permute-done.14 = bf16[98304]{0:T(1024)(128)(2,1)S(1)} collective-permute-done((bf16[98304]{0:T(1024)(128)(2,1)S(1)}, bf16[98304]{0:T(1024)(128)(2,1)S(1)}, u32[]{:S(2)}, u32[]{:S(2)}) %collective-permute-start.14) | collective-permute-done | bytes 196640 | tf_op jit(solution)/shard_map/ppermute | solution.py:87
  138.1 6.1 %collective-permute-start.15 = (bf16[98304]{0:T(1024)(128)(2,1)S(1)}, bf16[98304]{0:T(1024)(128)(2,1)S(1)}, u32[]{:S(2)}, u32[]{:S(2)}) collective-permute-start(bf16[98304]{0:T(1024)(128)(2,1)S(1)} %add_convert_fusion.1), channel_id=1, source_target_pairs={{0,4},{2,6},{4,0},{6,2},{8,12},{10,14},{12,8},{14,10},{1,5},{3,7},... | collective-permute-start | bytes 589832 | tf_op jit(solution)/shard_map/ppermute | solution.py:87
  144.3 3.9 %collective-permute-done.15 = bf16[98304]{0:T(1024)(128)(2,1)S(1)} collective-permute-done((bf16[98304]{0:T(1024)(128)(2,1)S(1)}, bf16[98304]{0:T(1024)(128)(2,1)S(1)}, u32[]{:S(2)}, u32[]{:S(2)}) %collective-permute-start.15) | collective-permute-done | bytes 196640 | tf_op jit(solution)/shard_map/ppermute | solution.py:87
  150.9 7.8 %collective-permute-done.16 = bf16[98304]{0:T(1024)(128)(2,1)S(1)} collective-permute-done((bf16[98304]{0:T(1024)(128)(2,1)S(1)}, bf16[98304]{0:T(1024)(128)(2,1)S(1)}, u32[]{:S(2)}, u32[]{:S(2)}) %collective-permute-start.16) | collective-permute-done | bytes 196640 | tf_op jit(solution)/shard_map/ppermute | solution.py:87
  (225 shorter events, 45.1 us)
Async XLA Ops:
  7.2 34.2 %copy-start = (bf16[2688,256]{1,0:T(8,128)(2,1)S(1)}, bf16[2688,256]{1,0:T(8,128)(2,1)}, u32[]{:S(2)}) copy-start(bf16[2688,256]{1,0:T(8,128)(2,1)} %param.28) | copy-start | bytes 4128772
  7.2 16.6 %all-gather.2.cloned.1.call-start = ((), (), s32[]{:S(2)}) async-start(), calls=%async_computation | async-start | bytes 2064384 | tf_op jit(solution)/shard_map/all_gather | solution.py:129
  12.3 39.7 %copy-start.49 = (f32[256]{0:T(256)}, f32[256]{0:T(256)S(1)}, u32[]{:S(2)}) copy-start(f32[256]{0:T(256)S(1)} %fusion.82) | copy-start | bytes 3076
  27.8 14.3 %collective-permute-start = (bf16[272,256]{0,1:T(8,128)(2,1)S(1)}, bf16[272,256]{0,1:T(8,128)(2,1)S(1)}, u32[]{:S(2)}, u32[]{:S(2)}) collective-permute-start(bf16[272,256]{0,1:T(8,128)(2,1)S(1)} %fusion.71), channel_id=1, source_target_pairs={{0,8},{2,10},{4,12},{6,14},{1,9},{3,11},{5,13},{7,15},{16,24},{18,... | collective-permute-start | bytes 417800 | tf_op jit(solution)/shard_map/ppermute | solution.py:17
  32.4 10.4 %collective-permute-start.1 = (bf16[272,256]{0,1:T(8,128)(2,1)S(1)}, bf16[272,256]{0,1:T(8,128)(2,1)S(1)}, u32[]{:S(2)}, u32[]{:S(2)}) collective-permute-start(bf16[272,256]{0,1:T(8,128)(2,1)S(1)} %fusion.71), channel_id=1, source_target_pairs={{0,6},{2,8},{4,10},{6,12},{8,14},{1,7},{3,9},{5,11},{7,13},{9,15},... | collective-permute-start | bytes 417800 | tf_op jit(solution)/shard_map/ppermute | solution.py:17
  36.7 8.8 %collective-permute-start.2 = (bf16[272,256]{0,1:T(8,128)(2,1)S(1)}, bf16[272,256]{0,1:T(8,128)(2,1)S(1)}, u32[]{:S(2)}, u32[]{:S(2)}) collective-permute-start(bf16[272,256]{0,1:T(8,128)(2,1)S(1)} %fusion.71), channel_id=1, source_target_pairs={{0,4},{2,6},{4,8},{6,10},{8,12},{10,14},{1,5},{3,7},{5,9},{7,11},{... | collective-permute-start | bytes 417800 | tf_op jit(solution)/shard_map/ppermute | solution.py:17
  38.0 8.1 %collective-permute-start.3 = (bf16[272,256]{0,1:T(8,128)(2,1)S(1)}, bf16[272,256]{0,1:T(8,128)(2,1)S(1)}, u32[]{:S(2)}, u32[]{:S(2)}) collective-permute-start(bf16[272,256]{0,1:T(8,128)(2,1)S(1)} %fusion.71), channel_id=1, source_target_pairs={{0,2},{2,4},{4,6},{6,8},{8,10},{10,12},{12,14},{1,3},{3,5},{5,7},{... | collective-permute-start | bytes 417800 | tf_op jit(solution)/shard_map/ppermute | solution.py:17
  56.9 2.4 %collective-permute-start.4 = (bf16[128,2688]{1,0:T(8,128)(2,1)}, bf16[128,2688]{1,0:T(8,128)(2,1)S(1)}, u32[]{:S(2)}, u32[]{:S(2)}) collective-permute-start(bf16[128,2688]{1,0:T(8,128)(2,1)} %constant_dynamic-slice_fusion.3), channel_id=1, source_target_pairs={{0,1},{1,0},{2,3},{3,2},{4,5},{5,4},{6,7},{7,6},{8,9},{9,8},{10,11... | collective-permute-start | bytes 2064392 | tf_op jit(solution)/shard_map/ppermute | solution.py:65
  57.1 2.0 %collective-permute-start.5 = (bf16[128,16]{0,1:T(8,128)(2,1)S(1)}, bf16[128,16]{0,1:T(8,128)(2,1)S(1)}, u32[]{:S(2)}, u32[]{:S(2)}) collective-permute-start(bf16[128,16]{0,1:T(8,128)(2,1)S(1)} %constant_dynamic-slice_fusion.2), channel_id=1, source_target_pairs={{0,1},{1,0},{2,3},{3,2},{4,5},{5,4},{6,7},{7,6},{8,9},{9,8},{10,11... | collective-permute-start | bytes 12296 | tf_op jit(solution)/shard_map/ppermute | solution.py:65
  62.8 1.2 collective-permute-start.7
  63.1 3.9 %collective-permute-start.6 = (bf16[128,2688]{1,0:T(8,128)(2,1)S(1)}, bf16[128,2688]{1,0:T(8,128)(2,1)}, u32[]{:S(2)}, u32[]{:S(2)}) collective-permute-start(bf16[128,2688]{1,0:T(8,128)(2,1)S(1)} %get-tuple-element.28), channel_id=1, source_target_pairs={{0,1},{1,0},{2,3},{3,2},{4,5},{5,4},{6,7},{7,6},{8,9},{9,8},{10,11... | collective-permute-start | bytes 2064392 | tf_op jit(solution)/shard_map/ppermute | solution.py:72
  91.9 32.1 %copy-start.13 = (f32[1280,128]{0,1:T(8,128)S(1)}, f32[1280,128]{0,1:T(8,128)}, u32[]{:S(2)}) copy-start(f32[1280,128]{0,1:T(8,128)} %convolution_bitcast_fusion.2) | copy-start | bytes 1966084
  93.2 30.9 %copy-start.15 = (f32[256,128]{0,1:T(8,128)S(1)}, f32[256,128]{0,1:T(8,128)}, u32[]{:S(2)}) copy-start(f32[256,128]{0,1:T(8,128)} %copy-done.14) | copy-start | bytes 393220
  93.2 30.9 %copy-start.37 = (f32[256]{0:T(256)S(1)}, f32[256]{0:T(256)}, u32[]{:S(2)}) copy-start(f32[256]{0:T(256)} %copy-done.36) | copy-start | bytes 3076
  93.2 31.1 %copy-start.39 = (bf16[16,128]{1,0:T(8,128)(2,1)S(1)}, bf16[16,128]{1,0:T(8,128)(2,1)}, u32[]{:S(2)}) copy-start(bf16[16,128]{1,0:T(8,128)(2,1)} %param.35) | copy-start | bytes 12292
  93.2 23.3 %collective-permute-start.10 = (bf16[256,256]{0,1:T(8,128)(2,1)S(1)}, bf16[256,256]{0,1:T(8,128)(2,1)S(1)}, u32[]{:S(2)}, u32[]{:S(2)}) collective-permute-start(bf16[256,256]{0,1:T(8,128)(2,1)S(1)} %get-tuple-element.34), channel_id=1, source_target_pairs={{6,0},{8,2},{10,4},{12,6},{14,8},{7,1},{9,3},{11,5},{13,7},{15,9},... | collective-permute-start | bytes 393224 | tf_op jit(solution)/shard_map/ppermute | solution.py:17
  94.7 29.4 %collective-permute-start.11 = (bf16[256,256]{0,1:T(8,128)(2,1)S(1)}, bf16[256,256]{0,1:T(8,128)(2,1)S(1)}, u32[]{:S(2)}, u32[]{:S(2)}) collective-permute-start(bf16[256,256]{0,1:T(8,128)(2,1)S(1)} %get-tuple-element.33), channel_id=1, source_target_pairs={{8,0},{10,2},{12,4},{14,6},{9,1},{11,3},{13,5},{15,7},{24,16},{26,... | collective-permute-start | bytes 393224 | tf_op jit(solution)/shard_map/ppermute | solution.py:17
  96.0 28.1 %collective-permute-start.8 = (bf16[256,256]{0,1:T(8,128)(2,1)S(1)}, bf16[256,256]{0,1:T(8,128)(2,1)S(1)}, u32[]{:S(2)}, u32[]{:S(2)}) collective-permute-start(bf16[256,256]{0,1:T(8,128)(2,1)S(1)} %get-tuple-element.32), channel_id=1, source_target_pairs={{2,0},{4,2},{6,4},{8,6},{10,8},{12,10},{14,12},{3,1},{5,3},{7,5},{... | collective-permute-start | bytes 393224 | tf_op jit(solution)/shard_map/ppermute | solution.py:17
  97.3 26.8 %collective-permute-start.9 = (bf16[256,256]{0,1:T(8,128)(2,1)S(1)}, bf16[256,256]{0,1:T(8,128)(2,1)S(1)}, u32[]{:S(2)}, u32[]{:S(2)}) collective-permute-start(bf16[256,256]{0,1:T(8,128)(2,1)S(1)} %get-tuple-element.35), channel_id=1, source_target_pairs={{4,0},{6,2},{8,4},{10,6},{12,8},{14,10},{5,1},{7,3},{9,5},{11,7},{... | collective-permute-start | bytes 393224 | tf_op jit(solution)/shard_map/ppermute | solution.py:17
  125.2 5.1 %collective-permute-start.13 = (bf16[1344,48]{0,1:T(8,128)(2,1)S(1)}, bf16[1344,48]{0,1:T(8,128)(2,1)S(1)}, u32[]{:S(2)}, u32[]{:S(2)}) collective-permute-start(bf16[1344,48]{0,1:T(8,128)(2,1)S(1)} %constant_dynamic-slice_fusion), channel_id=1, source_target_pairs={{0,1},{1,0},{2,3},{3,2},{4,5},{5,4},{6,7},{7,6},{8,9},{9,8},{10,11... | collective-permute-start | bytes 387080 | tf_op jit(solution)/shard_map/ppermute | solution.py:65
  131.4 6.6 %collective-permute-start.14 = (bf16[98304]{0:T(1024)(128)(2,1)S(1)}, bf16[98304]{0:T(1024)(128)(2,1)S(1)}, u32[]{:S(2)}, u32[]{:S(2)}) collective-permute-start(bf16[98304]{0:T(1024)(128)(2,1)S(1)} %constant_dynamic-update-slice_fusion.6), channel_id=1, source_target_pairs={{0,2},{2,0},{4,6},{6,4},{8,10},{10,8},{12,14},{14,12},{1,3},{3,1},... | collective-permute-start | bytes 589832 | tf_op jit(solution)/shard_map/ppermute | solution.py:87
  138.1 10.2 %collective-permute-start.15 = (bf16[98304]{0:T(1024)(128)(2,1)S(1)}, bf16[98304]{0:T(1024)(128)(2,1)S(1)}, u32[]{:S(2)}, u32[]{:S(2)}) collective-permute-start(bf16[98304]{0:T(1024)(128)(2,1)S(1)} %add_convert_fusion.1), channel_id=1, source_target_pairs={{0,4},{2,6},{4,0},{6,2},{8,12},{10,14},{12,8},{14,10},{1,5},{3,7},... | collective-permute-start | bytes 589832 | tf_op jit(solution)/shard_map/ppermute | solution.py:87
  144.3 4.8 %collective-permute-start.12 = (bf16[128,2688]{1,0:T(8,128)(2,1)S(1)}, bf16[128,2688]{1,0:T(8,128)(2,1)S(1)}, u32[]{:S(2)}, u32[]{:S(2)}) collective-permute-start(bf16[128,2688]{1,0:T(8,128)(2,1)S(1)} %constant_dynamic-slice_fusion.1), channel_id=1, source_target_pairs={{0,1},{1,0},{2,3},{3,2},{4,5},{5,4},{6,7},{7,6},{8,9},{9,8},{10,11... | collective-permute-start | bytes 2064392 | tf_op jit(solution)/shard_map/ppermute | solution.py:65
  148.3 10.3 %collective-permute-start.16 = (bf16[98304]{0:T(1024)(128)(2,1)S(1)}, bf16[98304]{0:T(1024)(128)(2,1)S(1)}, u32[]{:S(2)}, u32[]{:S(2)}) collective-permute-start(bf16[98304]{0:T(1024)(128)(2,1)S(1)} %add_convert_fusion), channel_id=1, source_target_pairs={{0,8},{2,10},{4,12},{6,14},{8,0},{10,2},{12,4},{14,6},{1,9},{3,11}... | collective-permute-start | bytes 589832 | tf_op jit(solution)/shard_map/ppermute | solution.py:87
  (47 other events, 252.3 us)
Sparse Core Ops, SparseCore 0:
  11.6 12.2 all-gather.1

commit v6 on v5

--- a/solution.py
+++ b/solution.py
@@ -126,7 +126,7 @@
     send_count = min(reach_shards, ctx_size - 1)
     tok_float = tokens.astype(jnp.float32)
     normed_rows = norm_rows(tok_float, input_norm_gain).astype(jnp.bfloat16)
-    normalized_input = lax.all_gather(normed_rows, "tp", axis=0, tiled=True)
+    normalized_input = tp_gather(normed_rows)
     middle_list = matrix_product(normalized_input, adapter_down_maps).astype(jnp.bfloat16)
     middle_query = middle_list[:, :adapter_product]
     middle_key = middle_list[:, adapter_product : 2 * adapter_product]

time: 170 us -> 140 us (0.82)
  between operations: 15.8 us -> 2.32 us
  waiting for transfers between devices: 55.9 us -> 49.3 us
  matrix products: 43.5 us -> 37 us
    all_gather x1 -> x0, waiting for transfers between devices: 11.5 us -> none  [on_device(): normalized_input = lax.all_gather(normed_rows, 'tp', axis=0, tiled=True)]
    ppermute x8, waiting for transfers between devices: 27 us -> 31.7 us  [passed_along(): lax.ppermute(value, axis, [(source, source + steps) for source in range(l...]
    ppermute x3, starting transfers between devices: 6.95 us -> 3.86 us  [ctx_sum(): received = lax.ppermute(sent, 'ctx', [(i, i ^ step) for i in range(count)])]
    unnamed x120 -> x124, local copies, waits for them, and re-layouts: 7.73 us -> 6.11 us
  transfers between devices with their start and end apart: 18 -> 18, of which waited for: 10 -> 11; matrix products, arithmetic and copies ran while one was open for 9% -> 9% of each run, Pallas kernels for 0% -> 0%
where the time goes in v6:
time: 140 us; the launch traced here: 139 us
  waiting for transfers between devices  49.3 us (35%)
  matrix products  37 us (26%)
  starting transfers between devices  25.8 us (18%)
  local copies, waits for them, and re-layouts  12.7 us (9%)
  other arithmetic  11.8 us (8%)
  between operations  2.32 us (2%)
    ppermute x8, waiting for transfers between devices, passed_along(): lax.ppermute(value, axis, [(source, source + steps) for source in range(l...  31.7 us
    ppermute x8, starting transfers between devices, passed_along(): lax.ppermute(value, axis, [(source, source + steps) for source in range(l...  20.2 us
    ppermute x3, waiting for transfers between devices, ctx_sum(): received = lax.ppermute(sent, 'ctx', [(i, i ^ step) for i in range(count)])  14.9 us
    dot_general x10, matrix products, multiply_by_transpose(): lax.dot_general(first_op, second_op, (((1,), (1,)), ((), ())), preferred_...  11.2 us
    unnamed x124, local copies, waits for them, and re-layouts  6.11 us
    dot_general x1, matrix products, on_device(): jnp.einsum('hts,sd->thd', grad_scores, keys_all, preferred_element_type=j...  5.56 us
    dot_general x10, matrix products, matrix_product(): return jnp.dot(first_op, second_op, preferred_element_type=jnp.float32)  5.46 us
    dot_general x1, matrix products, on_device(): jnp.einsum('hts,thd->sd', grad_scores, query_normed, preferred_element_ty...  4.86 us
  transfers between devices with their start and end apart: 18, of which 11 were waited for; matrix products, arithmetic and copies ran while one was open for 9% of the time, Pallas kernels for 0%

profile of v6, /device:TPU:0, one launch (start us, length us, event | category | flops | bytes accessed | tf_op | source)
XLA Modules:
  0.0 138.9 jit_solution(5452594006358962135)
XLA Ops:
  0.7 1.5 %fusion.26 = f32[128]{0:T(128)S(1)} fusion(bf16[128,2688]{1,0:T(8,128)(2,1)} %param.20), kind=kLoop, calls=%fused_computation.41 | loop fusion | flops 1032064 | bytes 688640 | tf_op jit(solution)/shard_map/reduce_sum | solution.py:21
  9.8 5.9 %collective-permute-start.1 = (bf16[272,256]{0,1:T(8,128)(2,1)S(1)}, bf16[272,256]{0,1:T(8,128)(2,1)S(1)}, u32[]{:S(2)}, u32[]{:S(2)}) collective-permute-start(bf16[272,256]{0,1:T(8,128)(2,1)S(1)} %fusion.71), channel_id=1, source_target_pairs={{0,8},{2,10},{4,12},{6,14},{1,9},{3,11},{5,13},{7,15},{16,24},{18,... | collective-permute-start | bytes 417800 | tf_op jit(solution)/shard_map/ppermute | solution.py:17
  15.6 4.4 %collective-permute-start.2 = (bf16[272,256]{0,1:T(8,128)(2,1)S(1)}, bf16[272,256]{0,1:T(8,128)(2,1)S(1)}, u32[]{:S(2)}, u32[]{:S(2)}) collective-permute-start(bf16[272,256]{0,1:T(8,128)(2,1)S(1)} %fusion.71), channel_id=1, source_target_pairs={{0,6},{2,8},{4,10},{6,12},{8,14},{1,7},{3,9},{5,11},{7,13},{9,15},... | collective-permute-start | bytes 417800 | tf_op jit(solution)/shard_map/ppermute | solution.py:17
  21.4 3.1 %collective-permute-start.4 = (bf16[272,256]{0,1:T(8,128)(2,1)S(1)}, bf16[272,256]{0,1:T(8,128)(2,1)S(1)}, u32[]{:S(2)}, u32[]{:S(2)}) collective-permute-start(bf16[272,256]{0,1:T(8,128)(2,1)S(1)} %fusion.71), channel_id=1, source_target_pairs={{0,2},{2,4},{4,6},{6,8},{8,10},{10,12},{12,14},{1,3},{3,5},{5,7},{... | collective-permute-start | bytes 417800 | tf_op jit(solution)/shard_map/ppermute | solution.py:17
  25.6 3.0 %collective-permute-done.3 = bf16[272,256]{0,1:T(8,128)(2,1)S(1)} collective-permute-done((bf16[272,256]{0,1:T(8,128)(2,1)S(1)}, bf16[272,256]{0,1:T(8,128)(2,1)S(1)}, u32[]{:S(2)}, u32[]{:S(2)}) %collective-permute-start.3) | collective-permute-done | bytes 139296 | tf_op jit(solution)/shard_map/ppermute | solution.py:17
  29.7 2.4 %fusion.31 = f32[2,256,1280]{1,2,0:T(8,128)} fusion(pred[256,1280]{0,1:T(8,128)(4,1)S(1)} %fusion.35, bf16[1280,256]{0,1:T(8,128)(2,1)S(1)} %maximum_dynamic-update-slice_fusion, f32[256,256]{0,1:T(8,128)S(1)} %get-tuple-element.49, f32[128]{0:T(128)S(1)} %copy-done.53, f32[256,2]{0,1:T(2,128)S(1)} %add_rsqrt_fusion), kind=kOutput, calls=%fused_computation.54 | convolution fusion | flops 169936640 | bytes 3541504 | tf_op jit(solution)/shard_map/div | solution.py:175
  32.2 2.2 %fusion.46 = bf16[128,2,256]{2,0,1:T(8,128)(2,1)S(1)} fusion(f32[2,256,1280]{1,2,0:T(8,128)} %fusion.31, bf16[1280,256]{0,1:T(8,128)(2,1)S(1)} %maximum_dynamic-update-slice_fusion, f32[256]{0:T(256)S(1)} %fusion.82), kind=kOutput, calls=%fused_computation.69 | convolution fusion | flops 168558592 | bytes 3081216 | tf_op jit(solution)/shard_map/hts,sd->thd/dot_general | solution.py:177
  38.9 1.7 %multiply_reduce_fusion.2 = (f32[128]{0:T(128)S(1)}, f32[128,2688]{1,0:T(8,128)S(1)}) fusion(bf16[128,16]{0,1:T(8,128)(2,1)S(1)} %add_convert_fusion.3, bf16[16,2688]{1,0:T(8,128)(2,1)S(1)} %copy-done.26, bf16[128,2688]{1,0:T(8,128)(2,1)} %collective-permute-done.5, bf16[256,2688]{1,0:T(8,128)(2,1)S(1)} %convolution_convert_fusion, s32[]{:T(128)S(6)} %select_n.62), kind=kOutput, calls=%fused_computation.48 | convolution fusion | flops 13418368 | bytes 2843140 | tf_op jit(solution)/shard_map/dot_general | solution.py:33
  48.1 2.0 %convolution_bitcast_fusion = f32[2,256,1280]{1,2,0:T(8,128)} fusion(bf16[256,2,128]{0,2,1:T(8,128)(2,1)S(1)} %bitcast.100, bf16[1280,256]{0,1:T(8,128)(2,1)S(1)} %copy-done.14), kind=kOutput, calls=%fused_computation.12 | convolution fusion | flops 167772160 | bytes 3080192 | tf_op jit(solution)/shard_map/thd,sd->hts/dot_general | solution.py:212
  51.1 5.6 %multiply_reduce_fusion.3 = (f32[256,2]{0,1:T(2,128)S(1)}, f32[256,2,128]{0,2,1:T(8,128)}) fusion(f32[256,256]{0,1:T(8,128)} %copy-done.27, f32[256,2]{0,1:T(2,128)S(1)} %add_rsqrt_fusion, f32[128]{0:T(128)S(1)} %copy-done.54, f32[2,256,1280]{1,2,0:T(8,128)} %fusion.31, f32[2,256,1280]{1,2,0:T(8,128)} %convolution_bitcast_fusion, ...), kind=kOutput, calls=%fused_computation.119 | convolution fusion | flops 171312384 | bytes 11342336 | tf_op jit(solution)/shard_map/hts,sd->thd/dot_general | solution.py:217
  56.6 4.9 %convolution_bitcast_fusion.2 = f32[1280,128]{0,1:T(8,128)S(1)} fusion(f32[2,256,1280]{1,2,0:T(8,128)} %fusion.31, f32[2,256,1280]{1,2,0:T(8,128)} %convolution_bitcast_fusion, f32[256,256]{0,1:T(8,128)} %copy-done.27, f32[128]{0:T(128)S(1)} %copy-done.54, f32[256,2]{0,1:T(2,128)S(1)} %add_rsqrt_fusion), kind=kOutput, calls=%fused_computation.18 | convolution fusion | flops 171247360 | bytes 6162944 | tf_op jit(solution)/shard_map/hts,thd->sd/dot_general | solution.py:220
  63.7 2.2 %fusion.100 = f32[256,2688]{1,0:T(8,128)} fusion(bf16[256,256]{0,1:T(8,128)(2,1)S(1)} %bitcast.98, bf16[2688,256]{1,0:T(8,128)(2,1)S(1)} %copy-done), kind=kOutput, calls=%fused_computation.196 | convolution fusion | flops 352321536 | bytes 4259840 | tf_op jit(solution)/shard_map/dot_general | solution.py:37
  66.9 1.5 %reshape.265 = bf16[21504]{0:T(1024)(128)(2,1)} reshape(bf16[16,1344]{1,0:T(8,128)(2,1)} %fusion.11) | data formatting | bytes 86016 | tf_op jit(solution)/shard_map/reshape | solution.py:83
  68.6 1.6 %collective-permute-start.10 = (bf16[256,256]{0,1:T(8,128)(2,1)S(1)}, bf16[256,256]{0,1:T(8,128)(2,1)S(1)}, u32[]{:S(2)}, u32[]{:S(2)}) collective-permute-start(bf16[256,256]{0,1:T(8,128)(2,1)S(1)} %get-tuple-element.37), channel_id=1, source_target_pairs={{4,0},{6,2},{8,4},{10,6},{12,8},{14,10},{5,1},{7,3},{9,5},{11,7},{... | collective-permute-start | bytes 393224 | tf_op jit(solution)/shard_map/ppermute | solution.py:17
  74.3 7.8 %collective-permute-done.10 = bf16[256,256]{0,1:T(8,128)(2,1)S(1)} collective-permute-done((bf16[256,256]{0,1:T(8,128)(2,1)S(1)}, bf16[256,256]{0,1:T(8,128)(2,1)S(1)}, u32[]{:S(2)}, u32[]{:S(2)}) %collective-permute-start.10) | collective-permute-done | bytes 131104 | tf_op jit(solution)/shard_map/ppermute | solution.py:17
  82.1 10.2 %collective-permute-done.11 = bf16[256,256]{0,1:T(8,128)(2,1)S(1)} collective-permute-done((bf16[256,256]{0,1:T(8,128)(2,1)S(1)}, bf16[256,256]{0,1:T(8,128)(2,1)S(1)}, u32[]{:S(2)}, u32[]{:S(2)}) %collective-permute-start.11) | collective-permute-done | bytes 131104 | tf_op jit(solution)/shard_map/ppermute | solution.py:17
  92.3 10.7 %collective-permute-done.12 = bf16[256,256]{0,1:T(8,128)(2,1)S(1)} collective-permute-done((bf16[256,256]{0,1:T(8,128)(2,1)S(1)}, bf16[256,256]{0,1:T(8,128)(2,1)S(1)}, u32[]{:S(2)}, u32[]{:S(2)}) %collective-permute-start.12) | collective-permute-done | bytes 131104 | tf_op jit(solution)/shard_map/ppermute | solution.py:17
  105.3 2.1 %convolution_add_fusion.1 = f32[256,2688]{1,0:T(8,128)} fusion(f32[256,2688]{1,0:T(8,128)S(1)} %copy-done.2, bf16[256,128]{0,1:T(8,128)(2,1)S(1)} %multiply_convert_fusion.4, bf16[2688,128]{1,0:T(8,128)(2,1)S(1)} %copy-done.16), kind=kOutput, calls=%fused_computation.2 | convolution fusion | flops 176848896 | bytes 6258688 | tf_op jit(solution)/shard_map/dot_general | solution.py:37
  107.4 2.1 %fusion.72 = f32[256,2688]{1,0:T(8,128)} fusion(bf16[2688,48]{0,1:T(8,128)(2,1)S(1)} %copy-done.29, bf16[256,16]{0,1:T(8,128)(2,1)S(1)} %fusion.52, bf16[256,16]{0,1:T(8,128)(2,1)S(1)} %fusion.51, bf16[256,16]{0,1:T(8,128)(2,1)S(1)} %fusion.50), kind=kOutput, calls=%fused_computation.143 | convolution fusion | flops 66134016 | bytes 3035136 | tf_op jit(solution)/shard_map/dot_general | solution.py:37
  110.7 3.4 %fusion.2 = bf16[256,2688]{1,0:T(8,128)(2,1)S(1)} fusion(f32[256,2688]{1,0:T(8,128)} %fusion.72, f32[256,2688]{1,0:T(8,128)} %convolution_add_fusion.1, bf16[2688,128]{1,0:T(8,128)(2,1)} %param.30, f32[256,256]{0,1:T(8,128)S(1)} %fusion.70), kind=kOutput, calls=%fused_computation.5 | convolution fusion | flops 178225152 | bytes 7634944 | tf_op jit(solution)/shard_map/dot_general | solution.py:37
  114.1 2.9 %collective-permute-done.15 = bf16[98304]{0:T(1024)(128)(2,1)S(1)} collective-permute-done((bf16[98304]{0:T(1024)(128)(2,1)S(1)}, bf16[98304]{0:T(1024)(128)(2,1)S(1)}, u32[]{:S(2)}, u32[]{:S(2)}) %collective-permute-start.15) | collective-permute-done | bytes 196640 | tf_op jit(solution)/shard_map/ppermute | solution.py:87
  117.1 3.0 %collective-permute-start.16 = (bf16[98304]{0:T(1024)(128)(2,1)S(1)}, bf16[98304]{0:T(1024)(128)(2,1)S(1)}, u32[]{:S(2)}, u32[]{:S(2)}) collective-permute-start(bf16[98304]{0:T(1024)(128)(2,1)S(1)} %add_convert_fusion.1), channel_id=1, source_target_pairs={{0,4},{2,6},{4,0},{6,2},{8,12},{10,14},{12,8},{14,10},{1,5},{3,7},... | collective-permute-start | bytes 589832 | tf_op jit(solution)/shard_map/ppermute | solution.py:87
  120.2 4.1 %collective-permute-done.16 = bf16[98304]{0:T(1024)(128)(2,1)S(1)} collective-permute-done((bf16[98304]{0:T(1024)(128)(2,1)S(1)}, bf16[98304]{0:T(1024)(128)(2,1)S(1)}, u32[]{:S(2)}, u32[]{:S(2)}) %collective-permute-start.16) | collective-permute-done | bytes 196640 | tf_op jit(solution)/shard_map/ppermute | solution.py:87
  127.0 7.9 %collective-permute-done.17 = bf16[98304]{0:T(1024)(128)(2,1)S(1)} collective-permute-done((bf16[98304]{0:T(1024)(128)(2,1)S(1)}, bf16[98304]{0:T(1024)(128)(2,1)S(1)}, u32[]{:S(2)}, u32[]{:S(2)}) %collective-permute-start.17) | collective-permute-done | bytes 196640 | tf_op jit(solution)/shard_map/ppermute | solution.py:87
  (229 shorter events, 40.5 us)
Async XLA Ops:
  3.5 2.3 %collective-permute-start = (bf16[128,2688]{1,0:T(8,128)(2,1)S(1)}, bf16[128,2688]{1,0:T(8,128)(2,1)S(1)}, u32[]{:S(2)}, u32[]{:S(2)}) collective-permute-start(bf16[128,2688]{1,0:T(8,128)(2,1)S(1)} %fusion.21), channel_id=1, source_target_pairs={{0,1},{1,0},{2,3},{3,2},{4,5},{5,4},{6,7},{7,6},{8,9},{9,8},{10,11... | collective-permute-start | bytes 2064392 | tf_op jit(solution)/shard_map/ppermute | solution.py:72
  9.8 15.8 %collective-permute-start.1 = (bf16[272,256]{0,1:T(8,128)(2,1)S(1)}, bf16[272,256]{0,1:T(8,128)(2,1)S(1)}, u32[]{:S(2)}, u32[]{:S(2)}) collective-permute-start(bf16[272,256]{0,1:T(8,128)(2,1)S(1)} %fusion.71), channel_id=1, source_target_pairs={{0,8},{2,10},{4,12},{6,14},{1,9},{3,11},{5,13},{7,15},{16,24},{18,... | collective-permute-start | bytes 417800 | tf_op jit(solution)/shard_map/ppermute | solution.py:17
  15.6 9.9 %collective-permute-start.2 = (bf16[272,256]{0,1:T(8,128)(2,1)S(1)}, bf16[272,256]{0,1:T(8,128)(2,1)S(1)}, u32[]{:S(2)}, u32[]{:S(2)}) collective-permute-start(bf16[272,256]{0,1:T(8,128)(2,1)S(1)} %fusion.71), channel_id=1, source_target_pairs={{0,6},{2,8},{4,10},{6,12},{8,14},{1,7},{3,9},{5,11},{7,13},{9,15},... | collective-permute-start | bytes 417800 | tf_op jit(solution)/shard_map/ppermute | solution.py:17
  20.1 8.5 %collective-permute-start.3 = (bf16[272,256]{0,1:T(8,128)(2,1)S(1)}, bf16[272,256]{0,1:T(8,128)(2,1)S(1)}, u32[]{:S(2)}, u32[]{:S(2)}) collective-permute-start(bf16[272,256]{0,1:T(8,128)(2,1)S(1)} %fusion.71), channel_id=1, source_target_pairs={{0,4},{2,6},{4,8},{6,10},{8,12},{10,14},{1,5},{3,7},{5,9},{7,11},{... | collective-permute-start | bytes 417800 | tf_op jit(solution)/shard_map/ppermute | solution.py:17
  21.4 7.2 %collective-permute-start.4 = (bf16[272,256]{0,1:T(8,128)(2,1)S(1)}, bf16[272,256]{0,1:T(8,128)(2,1)S(1)}, u32[]{:S(2)}, u32[]{:S(2)}) collective-permute-start(bf16[272,256]{0,1:T(8,128)(2,1)S(1)} %fusion.71), channel_id=1, source_target_pairs={{0,2},{2,4},{4,6},{6,8},{8,10},{10,12},{12,14},{1,3},{3,5},{5,7},{... | collective-permute-start | bytes 417800 | tf_op jit(solution)/shard_map/ppermute | solution.py:17
  35.9 3.0 %collective-permute-start.5 = (bf16[128,2688]{1,0:T(8,128)(2,1)}, bf16[128,2688]{1,0:T(8,128)(2,1)}, u32[]{:S(2)}, u32[]{:S(2)}) collective-permute-start(bf16[128,2688]{1,0:T(8,128)(2,1)} %constant_dynamic-slice_fusion.3), channel_id=1, source_target_pairs={{0,1},{1,0},{2,3},{3,2},{4,5},{5,4},{6,7},{7,6},{8,9},{9,8},{10,11... | collective-permute-start | bytes 2064392 | tf_op jit(solution)/shard_map/ppermute | solution.py:65
  36.7 1.5 %collective-permute-start.6 = (bf16[128,16]{0,1:T(8,128)(2,1)S(1)}, bf16[128,16]{0,1:T(8,128)(2,1)}, u32[]{:S(2)}, u32[]{:S(2)}) collective-permute-start(bf16[128,16]{0,1:T(8,128)(2,1)S(1)} %constant_dynamic-slice_fusion.2), channel_id=1, source_target_pairs={{0,1},{1,0},{2,3},{3,2},{4,5},{5,4},{6,7},{7,6},{8,9},{9,8},{10,11... | collective-permute-start | bytes 12296 | tf_op jit(solution)/shard_map/ppermute | solution.py:65
  42.5 1.2 collective-permute-start.8
  42.9 2.3 %collective-permute-start.7 = (bf16[128,2688]{1,0:T(8,128)(2,1)S(1)}, bf16[128,2688]{1,0:T(8,128)(2,1)}, u32[]{:S(2)}, u32[]{:S(2)}) collective-permute-start(bf16[128,2688]{1,0:T(8,128)(2,1)S(1)} %get-tuple-element.28), channel_id=1, source_target_pairs={{0,1},{1,0},{2,3},{3,2},{4,5},{5,4},{6,7},{7,6},{8,9},{9,8},{10,11... | collective-permute-start | bytes 2064392 | tf_op jit(solution)/shard_map/ppermute | solution.py:72
  68.5 34.6 %copy-start.6 = (f32[1280,128]{0,1:T(8,128)S(1)}, f32[1280,128]{0,1:T(8,128)}, u32[]{:S(2)}) copy-start(f32[1280,128]{0,1:T(8,128)} %copy-done.5) | copy-start | bytes 1966084
  68.6 34.6 %copy-start.12 = (f32[256,128]{0,1:T(8,128)S(1)}, f32[256,128]{0,1:T(8,128)}, u32[]{:S(2)}) copy-start(f32[256,128]{0,1:T(8,128)} %copy-done.11) | copy-start | bytes 393220
  68.6 34.6 %copy-start.41 = (f32[256]{0:T(256)S(1)}, f32[256]{0:T(256)}, u32[]{:S(2)}) copy-start(f32[256]{0:T(256)} %copy-done.40) | copy-start | bytes 3076
  68.6 34.6 %copy-start.49 = (f32[128]{0:T(128)S(1)}, f32[128]{0:T(128)}, u32[]{:S(2)}) copy-start(f32[128]{0:T(128)} %param.26) | copy-start | bytes 1540
  68.6 34.7 %copy-start.43 = (bf16[16,128]{1,0:T(8,128)(2,1)S(1)}, bf16[16,128]{1,0:T(8,128)(2,1)}, u32[]{:S(2)}) copy-start(bf16[16,128]{1,0:T(8,128)(2,1)} %param.35) | copy-start | bytes 12292
  68.6 13.5 %collective-permute-start.10 = (bf16[256,256]{0,1:T(8,128)(2,1)S(1)}, bf16[256,256]{0,1:T(8,128)(2,1)S(1)}, u32[]{:S(2)}, u32[]{:S(2)}) collective-permute-start(bf16[256,256]{0,1:T(8,128)(2,1)S(1)} %get-tuple-element.37), channel_id=1, source_target_pairs={{4,0},{6,2},{8,4},{10,6},{12,8},{14,10},{5,1},{7,3},{9,5},{11,7},{... | collective-permute-start | bytes 393224 | tf_op jit(solution)/shard_map/ppermute | solution.py:17
  70.2 22.1 %collective-permute-start.11 = (bf16[256,256]{0,1:T(8,128)(2,1)S(1)}, bf16[256,256]{0,1:T(8,128)(2,1)S(1)}, u32[]{:S(2)}, u32[]{:S(2)}) collective-permute-start(bf16[256,256]{0,1:T(8,128)(2,1)S(1)} %get-tuple-element.36), channel_id=1, source_target_pairs={{6,0},{8,2},{10,4},{12,6},{14,8},{7,1},{9,3},{11,5},{13,7},{15,9},... | collective-permute-start | bytes 393224 | tf_op jit(solution)/shard_map/ppermute | solution.py:17
  71.5 31.5 %collective-permute-start.12 = (bf16[256,256]{0,1:T(8,128)(2,1)S(1)}, bf16[256,256]{0,1:T(8,128)(2,1)S(1)}, u32[]{:S(2)}, u32[]{:S(2)}) collective-permute-start(bf16[256,256]{0,1:T(8,128)(2,1)S(1)} %get-tuple-element.35), channel_id=1, source_target_pairs={{8,0},{10,2},{12,4},{14,6},{9,1},{11,3},{13,5},{15,7},{24,16},{26,... | collective-permute-start | bytes 393224 | tf_op jit(solution)/shard_map/ppermute | solution.py:17
  72.8 30.3 %collective-permute-start.9 = (bf16[256,256]{0,1:T(8,128)(2,1)S(1)}, bf16[256,256]{0,1:T(8,128)(2,1)S(1)}, u32[]{:S(2)}, u32[]{:S(2)}) collective-permute-start(bf16[256,256]{0,1:T(8,128)(2,1)S(1)} %get-tuple-element.34), channel_id=1, source_target_pairs={{2,0},{4,2},{6,4},{8,6},{10,8},{12,10},{14,12},{3,1},{5,3},{7,5},{... | collective-permute-start | bytes 393224 | tf_op jit(solution)/shard_map/ppermute | solution.py:17
  74.3 29.4 %copy-start.20 = (bf16[128,2688]{1,0:T(8,128)(2,1)S(1)}, bf16[128,2688]{1,0:T(8,128)(2,1)}, u32[]{:S(2)}) copy-start(bf16[128,2688]{1,0:T(8,128)(2,1)} %copy-done.19) | copy-start | bytes 2064388
  104.2 5.3 %collective-permute-start.14 = (bf16[1344,48]{0,1:T(8,128)(2,1)S(1)}, bf16[1344,48]{0,1:T(8,128)(2,1)S(1)}, u32[]{:S(2)}, u32[]{:S(2)}) collective-permute-start(bf16[1344,48]{0,1:T(8,128)(2,1)S(1)} %constant_dynamic-slice_fusion), channel_id=1, source_target_pairs={{0,1},{1,0},{2,3},{3,2},{4,5},{5,4},{6,7},{7,6},{8,9},{9,8},{10,11... | collective-permute-start | bytes 387080 | tf_op jit(solution)/shard_map/ppermute | solution.py:65
  110.6 6.4 %collective-permute-start.15 = (bf16[98304]{0:T(1024)(128)(2,1)S(1)}, bf16[98304]{0:T(1024)(128)(2,1)S(1)}, u32[]{:S(2)}, u32[]{:S(2)}) collective-permute-start(bf16[98304]{0:T(1024)(128)(2,1)S(1)} %constant_dynamic-update-slice_fusion.6), channel_id=1, source_target_pairs={{0,2},{2,0},{4,6},{6,4},{8,10},{10,8},{12,14},{14,12},{1,3},{3,1},... | collective-permute-start | bytes 589832 | tf_op jit(solution)/shard_map/ppermute | solution.py:87
  117.1 7.2 %collective-permute-start.16 = (bf16[98304]{0:T(1024)(128)(2,1)S(1)}, bf16[98304]{0:T(1024)(128)(2,1)S(1)}, u32[]{:S(2)}, u32[]{:S(2)}) collective-permute-start(bf16[98304]{0:T(1024)(128)(2,1)S(1)} %add_convert_fusion.1), channel_id=1, source_target_pairs={{0,4},{2,6},{4,0},{6,2},{8,12},{10,14},{12,8},{14,10},{1,5},{3,7},... | collective-permute-start | bytes 589832 | tf_op jit(solution)/shard_map/ppermute | solution.py:87
  120.1 5.0 %collective-permute-start.13 = (bf16[128,2688]{1,0:T(8,128)(2,1)S(1)}, bf16[128,2688]{1,0:T(8,128)(2,1)S(1)}, u32[]{:S(2)}, u32[]{:S(2)}) collective-permute-start(bf16[128,2688]{1,0:T(8,128)(2,1)S(1)} %constant_dynamic-slice_fusion.1), channel_id=1, source_target_pairs={{0,1},{1,0},{2,3},{3,2},{4,5},{5,4},{6,7},{7,6},{8,9},{9,8},{10,11... | collective-permute-start | bytes 2064392 | tf_op jit(solution)/shard_map/ppermute | solution.py:65
  124.3 10.5 %collective-permute-start.17 = (bf16[98304]{0:T(1024)(128)(2,1)S(1)}, bf16[98304]{0:T(1024)(128)(2,1)S(1)}, u32[]{:S(2)}, u32[]{:S(2)}) collective-permute-start(bf16[98304]{0:T(1024)(128)(2,1)S(1)} %add_convert_fusion), channel_id=1, source_target_pairs={{0,8},{2,10},{4,12},{6,14},{8,0},{10,2},{12,4},{14,6},{1,9},{3,11}... | collective-permute-start | bytes 589832 | tf_op jit(solution)/shard_map/ppermute | solution.py:87
  (49 other events, 283.3 us)

commit v7 on v6

--- a/solution.py
+++ b/solution.py
@@ -225,14 +225,18 @@
     )
     grad_pairs = jnp.concatenate([grad_keys, grad_values], axis=1)
     own_grads = grad_pairs[reach_shards * shard_len :]
-    for hop_index in range(1, send_count + 1):
-        own_grads = own_grads + passed_along(
-            grad_pairs[
-                (reach_shards - hop_index) * shard_len : (reach_shards - hop_index + 1) * shard_len
-            ].astype(jnp.bfloat16),
-            "ctx",
-            -hop_index,
-        ).astype(jnp.float32)
+
+    def hop_block(hop_index):
+        first_row = (reach_shards - hop_index) * shard_len
+        return grad_pairs[first_row : first_row + shard_len]
+
+    if send_count > 0:
+        running = hop_block(send_count)
+        for hop_index in range(send_count - 1, 0, -1):
+            arrived = passed_along(running.astype(jnp.bfloat16), "ctx", -1)
+            running = arrived.astype(jnp.float32) + hop_block(hop_index)
+        arrived = passed_along(running.astype(jnp.bfloat16), "ctx", -1)
+        own_grads = own_grads + arrived.astype(jnp.float32)
     query_prenorm_gradient = (
         norm_back(query_heads, query_norm_gain, grad_query)
         .reshape(shard_len, heads_here * head_dim)

time: 140 us -> 149 us (1.064)
  starting transfers between devices: 25.8 us -> 30.1 us
  local copies, waits for them, and re-layouts: 12.7 us -> 16.9 us
  waiting for transfers between devices: 49.3 us -> 47.4 us
  other arithmetic: 11.8 us -> 13.3 us
    ppermute x3, starting transfers between devices: 3.86 us -> 8.11 us  [ctx_sum(): received = lax.ppermute(sent, 'ctx', [(i, i ^ step) for i in range(count)])]
    unnamed x124 -> x130, local copies, waits for them, and re-layouts: 6.11 us -> 8.64 us
    ppermute x3, waiting for transfers between devices: 14.9 us -> 12.6 us  [ctx_sum(): received = lax.ppermute(sent, 'ctx', [(i, i ^ step) for i in range(count)])]
    convert_element_type x0 -> x3, other arithmetic: none -> 1.65 us  [on_device(): arrived = passed_along(running.astype(jnp.bfloat16), 'ctx', -1)]
  transfers between devices with their start and end apart: 18 -> 18, of which waited for: 11 -> 12; matrix products, arithmetic and copies ran while one was open for 9% -> 13% of each run, Pallas kernels for 0% -> 0%
where the time goes in v7:
time: 149 us; the launch traced here: 148 us
  waiting for transfers between devices  47.4 us (32%)
  matrix products  38.1 us (26%)
  starting transfers between devices  30.1 us (20%)
  local copies, waits for them, and re-layouts  16.9 us (11%)
  other arithmetic  13.3 us (9%)
  between operations  2.3 us (2%)
    ppermute x8, waiting for transfers between devices, passed_along(): lax.ppermute(value, axis, [(source, source + steps) for source in range(l...  32.7 us
    ppermute x8, starting transfers between devices, passed_along(): lax.ppermute(value, axis, [(source, source + steps) for source in range(l...  20.3 us
    ppermute x3, waiting for transfers between devices, ctx_sum(): received = lax.ppermute(sent, 'ctx', [(i, i ^ step) for i in range(count)])  12.6 us
    dot_general x10, matrix products, multiply_by_transpose(): lax.dot_general(first_op, second_op, (((1,), (1,)), ((), ())), preferred_...  11.6 us
    unnamed x130, local copies, waits for them, and re-layouts  8.64 us
    ppermute x3, starting transfers between devices, ctx_sum(): received = lax.ppermute(sent, 'ctx', [(i, i ^ step) for i in range(count)])  8.11 us
    dot_general x1, matrix products, on_device(): jnp.einsum('hts,sd->thd', grad_scores, keys_all, preferred_element_type=j...  5.56 us
    dot_general x10, matrix products, matrix_product(): return jnp.dot(first_op, second_op, preferred_element_type=jnp.float32)  5.46 us
  transfers between devices with their start and end apart: 18, of which 12 were waited for; matrix products, arithmetic and copies ran while one was open for 13% of the time, Pallas kernels for 0%

profile of v7, /device:TPU:0, one launch (start us, length us, event | category | flops | bytes accessed | tf_op | source)
XLA Modules:
  0.0 148.1 jit_solution(1419604009782279651)
XLA Ops:
  0.7 1.5 fusion.26
  9.8 5.9 %collective-permute-start.1 = (bf16[272,256]{0,1:T(8,128)(2,1)S(1)}, bf16[272,256]{0,1:T(8,128)(2,1)S(1)}, u32[]{:S(2)}, u32[]{:S(2)}) collective-permute-start(bf16[272,256]{0,1:T(8,128)(2,1)S(1)} %fusion.77), channel_id=1, source_target_pairs={{0,8},{2,10},{4,12},{6,14},{1,9},{3,11},{5,13},{7,15},{16,24},{18,... | collective-permute-start | bytes 417800 | tf_op jit(solution)/shard_map/ppermute | solution.py:17
  15.6 4.4 %collective-permute-start.2 = (bf16[272,256]{0,1:T(8,128)(2,1)S(1)}, bf16[272,256]{0,1:T(8,128)(2,1)S(1)}, u32[]{:S(2)}, u32[]{:S(2)}) collective-permute-start(bf16[272,256]{0,1:T(8,128)(2,1)S(1)} %fusion.77), channel_id=1, source_target_pairs={{0,6},{2,8},{4,10},{6,12},{8,14},{1,7},{3,9},{5,11},{7,13},{9,15},... | collective-permute-start | bytes 417800 | tf_op jit(solution)/shard_map/ppermute | solution.py:17
  21.4 3.1 %collective-permute-start.4 = (bf16[272,256]{0,1:T(8,128)(2,1)S(1)}, bf16[272,256]{0,1:T(8,128)(2,1)S(1)}, u32[]{:S(2)}, u32[]{:S(2)}) collective-permute-start(bf16[272,256]{0,1:T(8,128)(2,1)S(1)} %fusion.77), channel_id=1, source_target_pairs={{0,2},{2,4},{4,6},{6,8},{8,10},{10,12},{12,14},{1,3},{3,5},{5,7},{... | collective-permute-start | bytes 417800 | tf_op jit(solution)/shard_map/ppermute | solution.py:17
  25.6 3.0 %collective-permute-done.3 = bf16[272,256]{0,1:T(8,128)(2,1)S(1)} collective-permute-done((bf16[272,256]{0,1:T(8,128)(2,1)S(1)}, bf16[272,256]{0,1:T(8,128)(2,1)S(1)}, u32[]{:S(2)}, u32[]{:S(2)}) %collective-permute-start.3) | collective-permute-done | bytes 139296 | tf_op jit(solution)/shard_map/ppermute | solution.py:17
  29.8 2.4 %fusion.30 = f32[2,256,1280]{1,2,0:T(8,128)} fusion(pred[256,1280]{0,1:T(8,128)(4,1)S(1)} %fusion.34, bf16[1280,256]{0,1:T(8,128)(2,1)S(1)} %maximum_dynamic-update-slice_fusion, f32[256,256]{0,1:T(8,128)S(1)} %get-tuple-element.45, f32[128]{0:T(128)S(1)} %copy-done.56, f32[256,2]{0,1:T(2,128)S(1)} %add_rsqrt_fusion), kind=kOutput, calls=%fused_computation.58 | convolution fusion | flops 169936640 | bytes 3541504 | tf_op jit(solution)/shard_map/div | solution.py:175
  32.2 2.2 %fusion.45 = bf16[128,2,256]{2,0,1:T(8,128)(2,1)S(1)} fusion(f32[2,256,1280]{1,2,0:T(8,128)} %fusion.30, bf16[1280,256]{0,1:T(8,128)(2,1)S(1)} %maximum_dynamic-update-slice_fusion, f32[256]{0:T(256)S(1)} %copy-done.54), kind=kOutput, calls=%fused_computation.73 | convolution fusion | flops 168558592 | bytes 3081216 | tf_op jit(solution)/shard_map/hts,sd->thd/dot_general | solution.py:177
  38.9 1.7 %multiply_reduce_fusion.2 = (f32[128]{0:T(128)S(1)}, f32[128,2688]{1,0:T(8,128)S(1)}) fusion(bf16[128,16]{0,1:T(8,128)(2,1)S(1)} %add_convert_fusion.3, bf16[16,2688]{1,0:T(8,128)(2,1)S(1)} %copy-done.27, bf16[128,2688]{1,0:T(8,128)(2,1)} %collective-permute-done.5, bf16[256,2688]{1,0:T(8,128)(2,1)S(1)} %convolution_convert_fusion, s32[]{:T(128)S(6)} %select_n.62), kind=kOutput, calls=%fused_computation.53 | convolution fusion | flops 13418368 | bytes 2843140 | tf_op jit(solution)/shard_map/dot_general | solution.py:33
  48.1 2.0 %convolution_bitcast_fusion = f32[2,256,1280]{1,2,0:T(8,128)} fusion(bf16[256,2,128]{0,2,1:T(8,128)(2,1)S(1)} %bitcast.100, bf16[1280,256]{0,1:T(8,128)(2,1)S(1)} %copy-done.14), kind=kOutput, calls=%fused_computation.12 | convolution fusion | flops 167772160 | bytes 3080192 | tf_op jit(solution)/shard_map/thd,sd->hts/dot_general | solution.py:212
  51.1 5.6 %multiply_reduce_fusion.3 = (f32[256,2]{0,1:T(2,128)S(1)}, f32[256,2,128]{0,2,1:T(8,128)}) fusion(f32[256,256]{0,1:T(8,128)} %copy-done.28, f32[256,2]{0,1:T(2,128)S(1)} %copy-done.48, f32[128]{0:T(128)S(1)} %copy-done.57, f32[2,256,1280]{1,2,0:T(8,128)} %fusion.30, f32[2,256,1280]{1,2,0:T(8,128)} %convolution_bitcast_fusion, ...), kind=kOutput, calls=%fused_computation.131 | convolution fusion | flops 171312384 | bytes 11342336 | tf_op jit(solution)/shard_map/hts,sd->thd/dot_general | solution.py:217
  56.7 4.9 %convolution_bitcast_fusion.2 = f32[1280,128]{0,1:T(8,128)S(1)} fusion(f32[2,256,1280]{1,2,0:T(8,128)} %fusion.30, f32[2,256,1280]{1,2,0:T(8,128)} %convolution_bitcast_fusion, f32[256,256]{0,1:T(8,128)} %copy-done.28, f32[128]{0:T(128)S(1)} %copy-done.57, f32[256,2]{0,1:T(2,128)S(1)} %copy-done.48), kind=kOutput, calls=%fused_computation.18 | convolution fusion | flops 171247360 | bytes 6162944 | tf_op jit(solution)/shard_map/hts,thd->sd/dot_general | solution.py:220
  63.1 10.1 %collective-permute-done.9 = bf16[256,256]{0,1:T(8,128)(2,1)S(1)} collective-permute-done((bf16[256,256]{0,1:T(8,128)(2,1)S(1)}, bf16[256,256]{0,1:T(8,128)(2,1)S(1)}, u32[]{:S(2)}, u32[]{:S(2)}) %collective-permute-start.9) | collective-permute-done | bytes 131104 | tf_op jit(solution)/shard_map/ppermute | solution.py:17
  74.6 2.1 %fusion.105 = f32[256,2688]{1,0:T(8,128)} fusion(bf16[256,256]{0,1:T(8,128)(2,1)S(1)} %bitcast.97, bf16[2688,256]{1,0:T(8,128)(2,1)S(1)} %copy-done), kind=kOutput, calls=%fused_computation.207 | convolution fusion | flops 352321536 | bytes 4259840 | tf_op jit(solution)/shard_map/dot_general | solution.py:37
  76.7 5.2 %collective-permute-done.10 = bf16[256,256]{0,1:T(8,128)(2,1)S(1)} collective-permute-done((bf16[256,256]{0,1:T(8,128)(2,1)S(1)}, bf16[256,256]{0,1:T(8,128)(2,1)S(1)}, u32[]{:S(2)}, u32[]{:S(2)}) %collective-permute-start.10) | collective-permute-done | bytes 131104 | tf_op jit(solution)/shard_map/ppermute | solution.py:17
  85.2 1.5 %reshape.265 = bf16[21504]{0:T(1024)(128)(2,1)} reshape(bf16[16,1344]{1,0:T(8,128)(2,1)} %fusion.11) | data formatting | bytes 86016 | tf_op jit(solution)/shard_map/reshape | solution.py:83
  87.5 8.3 %collective-permute-done.11 = bf16[256,256]{0,1:T(8,128)(2,1)} collective-permute-done((bf16[256,256]{0,1:T(8,128)(2,1)}, bf16[256,256]{0,1:T(8,128)(2,1)}, u32[]{:S(2)}, u32[]{:S(2)}) %collective-permute-start.11) | collective-permute-done | bytes 131104 | tf_op jit(solution)/shard_map/ppermute | solution.py:17
  99.0 6.1 %collective-permute-done.12 = bf16[256,256]{0,1:T(8,128)(2,1)S(1)} collective-permute-done((bf16[256,256]{0,1:T(8,128)(2,1)S(1)}, bf16[256,256]{0,1:T(8,128)(2,1)S(1)}, u32[]{:S(2)}, u32[]{:S(2)}) %collective-permute-start.12) | collective-permute-done | bytes 131104 | tf_op jit(solution)/shard_map/ppermute | solution.py:17
  107.7 2.1 %convolution_add_fusion.1 = f32[256,2688]{1,0:T(8,128)} fusion(f32[256,2688]{1,0:T(8,128)S(1)} %copy-done.2, bf16[256,128]{0,1:T(8,128)(2,1)S(1)} %multiply_convert_fusion.4, bf16[2688,128]{1,0:T(8,128)(2,1)S(1)} %copy-done.16), kind=kOutput, calls=%fused_computation.2 | convolution fusion | flops 176848896 | bytes 6258688 | tf_op jit(solution)/shard_map/dot_general | solution.py:37
  109.8 2.1 %fusion.78 = f32[256,2688]{1,0:T(8,128)} fusion(bf16[2688,48]{0,1:T(8,128)(2,1)S(1)} %copy-done.32, bf16[256,16]{0,1:T(8,128)(2,1)S(1)} %fusion.51, bf16[256,16]{0,1:T(8,128)(2,1)S(1)} %fusion.50, bf16[256,16]{0,1:T(8,128)(2,1)S(1)} %fusion.49), kind=kOutput, calls=%fused_computation.155 | convolution fusion | flops 66134016 | bytes 3035136 | tf_op jit(solution)/shard_map/dot_general | solution.py:37
  118.1 2.9 %collective-permute-start.15 = (bf16[98304]{0:T(1024)(128)(2,1)S(1)}, bf16[98304]{0:T(1024)(128)(2,1)S(1)}, u32[]{:S(2)}, u32[]{:S(2)}) collective-permute-start(bf16[98304]{0:T(1024)(128)(2,1)S(1)} %constant_dynamic-update-slice_fusion.6), channel_id=1, source_target_pairs={{0,2},{2,0},{4,6},{6,4},{8,10},{10,8},{12,14},{14,12},{1,3},{3,1},... | collective-permute-start | bytes 589832 | tf_op jit(solution)/shard_map/ppermute | solution.py:87
  121.1 3.2 %fusion.2 = bf16[256,2688]{1,0:T(8,128)(2,1)S(1)} fusion(f32[256,2688]{1,0:T(8,128)} %fusion.78, f32[256,2688]{1,0:T(8,128)} %convolution_add_fusion.1, bf16[2688,128]{1,0:T(8,128)(2,1)S(1)} %copy-done.26, f32[256,256]{0,1:T(8,128)S(1)} %copy-done.5), kind=kOutput, calls=%fused_computation.5 | convolution fusion | flops 178225152 | bytes 7634944 | tf_op jit(solution)/shard_map/dot_general | solution.py:37
  125.7 4.2 %collective-permute-start.16 = (bf16[98304]{0:T(1024)(128)(2,1)S(1)}, bf16[98304]{0:T(1024)(128)(2,1)S(1)}, u32[]{:S(2)}, u32[]{:S(2)}) collective-permute-start(bf16[98304]{0:T(1024)(128)(2,1)S(1)} %add_convert_fusion.1), channel_id=1, source_target_pairs={{0,4},{2,6},{4,0},{6,2},{8,12},{10,14},{12,8},{14,10},{1,5},{3,7},... | collective-permute-start | bytes 589832 | tf_op jit(solution)/shard_map/ppermute | solution.py:87
  129.9 3.8 %collective-permute-done.16 = bf16[98304]{0:T(1024)(128)(2,1)S(1)} collective-permute-done((bf16[98304]{0:T(1024)(128)(2,1)S(1)}, bf16[98304]{0:T(1024)(128)(2,1)S(1)}, u32[]{:S(2)}, u32[]{:S(2)}) %collective-permute-start.16) | collective-permute-done | bytes 196640 | tf_op jit(solution)/shard_map/ppermute | solution.py:87
  136.7 7.4 %collective-permute-done.17 = bf16[98304]{0:T(1024)(128)(2,1)S(1)} collective-permute-done((bf16[98304]{0:T(1024)(128)(2,1)S(1)}, bf16[98304]{0:T(1024)(128)(2,1)S(1)}, u32[]{:S(2)}, u32[]{:S(2)}) %collective-permute-start.17) | collective-permute-done | bytes 196640 | tf_op jit(solution)/shard_map/ppermute | solution.py:87
  (237 shorter events, 50.3 us)
Async XLA Ops:
  0.6 24.1 %copy-start = (bf16[2688,256]{1,0:T(8,128)(2,1)S(1)}, bf16[2688,256]{1,0:T(8,128)(2,1)}, u32[]{:S(2)}) copy-start(bf16[2688,256]{1,0:T(8,128)(2,1)} %param.28) | copy-start | bytes 4128772
  3.5 2.3 %collective-permute-start = (bf16[128,2688]{1,0:T(8,128)(2,1)S(1)}, bf16[128,2688]{1,0:T(8,128)(2,1)S(1)}, u32[]{:S(2)}, u32[]{:S(2)}) collective-permute-start(bf16[128,2688]{1,0:T(8,128)(2,1)S(1)} %fusion.21), channel_id=1, source_target_pairs={{0,1},{1,0},{2,3},{3,2},{4,5},{5,4},{6,7},{7,6},{8,9},{9,8},{10,11... | collective-permute-start | bytes 2064392 | tf_op jit(solution)/shard_map/ppermute | solution.py:72
  6.2 18.5 %copy-start.17 = (bf16[128,2688]{1,0:T(8,128)(2,1)}, bf16[128,2688]{1,0:T(8,128)(2,1)S(1)}, u32[]{:S(2)}) copy-start(bf16[128,2688]{1,0:T(8,128)(2,1)S(1)} %get-tuple-element.32) | copy-start | bytes 2064388
  6.2 18.5 %copy-start.19 = (bf16[128,2688]{1,0:T(8,128)(2,1)}, bf16[128,2688]{1,0:T(8,128)(2,1)S(1)}, u32[]{:S(2)}) copy-start(bf16[128,2688]{1,0:T(8,128)(2,1)S(1)} %get-tuple-element.33) | copy-start | bytes 2064388
  7.0 79.7 %copy-start.35 = (bf16[256,48]{0,1:T(8,128)(2,1)}, bf16[256,48]{0,1:T(8,128)(2,1)S(1)}, u32[]{:S(2)}) copy-start(bf16[256,48]{0,1:T(8,128)(2,1)S(1)} %convolution_convert_fusion.2) | copy-start | bytes 73732
  9.8 15.8 %collective-permute-start.1 = (bf16[272,256]{0,1:T(8,128)(2,1)S(1)}, bf16[272,256]{0,1:T(8,128)(2,1)S(1)}, u32[]{:S(2)}, u32[]{:S(2)}) collective-permute-start(bf16[272,256]{0,1:T(8,128)(2,1)S(1)} %fusion.77), channel_id=1, source_target_pairs={{0,8},{2,10},{4,12},{6,14},{1,9},{3,11},{5,13},{7,15},{16,24},{18,... | collective-permute-start | bytes 417800 | tf_op jit(solution)/shard_map/ppermute | solution.py:17
  15.6 9.9 %collective-permute-start.2 = (bf16[272,256]{0,1:T(8,128)(2,1)S(1)}, bf16[272,256]{0,1:T(8,128)(2,1)S(1)}, u32[]{:S(2)}, u32[]{:S(2)}) collective-permute-start(bf16[272,256]{0,1:T(8,128)(2,1)S(1)} %fusion.77), channel_id=1, source_target_pairs={{0,6},{2,8},{4,10},{6,12},{8,14},{1,7},{3,9},{5,11},{7,13},{9,15},... | collective-permute-start | bytes 417800 | tf_op jit(solution)/shard_map/ppermute | solution.py:17
  20.1 8.5 %collective-permute-start.3 = (bf16[272,256]{0,1:T(8,128)(2,1)S(1)}, bf16[272,256]{0,1:T(8,128)(2,1)S(1)}, u32[]{:S(2)}, u32[]{:S(2)}) collective-permute-start(bf16[272,256]{0,1:T(8,128)(2,1)S(1)} %fusion.77), channel_id=1, source_target_pairs={{0,4},{2,6},{4,8},{6,10},{8,12},{10,14},{1,5},{3,7},{5,9},{7,11},{... | collective-permute-start | bytes 417800 | tf_op jit(solution)/shard_map/ppermute | solution.py:17
  21.4 7.2 %collective-permute-start.4 = (bf16[272,256]{0,1:T(8,128)(2,1)S(1)}, bf16[272,256]{0,1:T(8,128)(2,1)S(1)}, u32[]{:S(2)}, u32[]{:S(2)}) collective-permute-start(bf16[272,256]{0,1:T(8,128)(2,1)S(1)} %fusion.77), channel_id=1, source_target_pairs={{0,2},{2,4},{4,6},{6,8},{8,10},{10,12},{12,14},{1,3},{3,5},{5,7},{... | collective-permute-start | bytes 417800 | tf_op jit(solution)/shard_map/ppermute | solution.py:17
  35.9 3.0 %collective-permute-start.5 = (bf16[128,2688]{1,0:T(8,128)(2,1)}, bf16[128,2688]{1,0:T(8,128)(2,1)}, u32[]{:S(2)}, u32[]{:S(2)}) collective-permute-start(bf16[128,2688]{1,0:T(8,128)(2,1)} %constant_dynamic-slice_fusion.3), channel_id=1, source_target_pairs={{0,1},{1,0},{2,3},{3,2},{4,5},{5,4},{6,7},{7,6},{8,9},{9,8},{10,11... | collective-permute-start | bytes 2064392 | tf_op jit(solution)/shard_map/ppermute | solution.py:65
  36.7 1.5 %collective-permute-start.6 = (bf16[128,16]{0,1:T(8,128)(2,1)S(1)}, bf16[128,16]{0,1:T(8,128)(2,1)}, u32[]{:S(2)}, u32[]{:S(2)}) collective-permute-start(bf16[128,16]{0,1:T(8,128)(2,1)S(1)} %constant_dynamic-slice_fusion.2), channel_id=1, source_target_pairs={{0,1},{1,0},{2,3},{3,2},{4,5},{5,4},{6,7},{7,6},{8,9},{9,8},{10,11... | collective-permute-start | bytes 12296 | tf_op jit(solution)/shard_map/ppermute | solution.py:65
  42.6 1.2 collective-permute-start.8
  42.9 2.3 %collective-permute-start.7 = (bf16[128,2688]{1,0:T(8,128)(2,1)S(1)}, bf16[128,2688]{1,0:T(8,128)(2,1)}, u32[]{:S(2)}, u32[]{:S(2)}) collective-permute-start(bf16[128,2688]{1,0:T(8,128)(2,1)S(1)} %get-tuple-element.28), channel_id=1, source_target_pairs={{0,1},{1,0},{2,3},{3,2},{4,5},{5,4},{6,7},{7,6},{8,9},{9,8},{10,11... | collective-permute-start | bytes 2064392 | tf_op jit(solution)/shard_map/ppermute | solution.py:72
  61.6 11.6 %collective-permute-start.9 = (bf16[256,256]{0,1:T(8,128)(2,1)S(1)}, bf16[256,256]{0,1:T(8,128)(2,1)S(1)}, u32[]{:S(2)}, u32[]{:S(2)}) collective-permute-start(bf16[256,256]{0,1:T(8,128)(2,1)S(1)} %fusion.71), channel_id=1, source_target_pairs={{2,0},{4,2},{6,4},{8,6},{10,8},{12,10},{14,12},{3,1},{5,3},{7,5},{... | collective-permute-start | bytes 393224 | tf_op jit(solution)/shard_map/ppermute | solution.py:17
  73.3 8.7 %collective-permute-start.10 = (bf16[256,256]{0,1:T(8,128)(2,1)S(1)}, bf16[256,256]{0,1:T(8,128)(2,1)S(1)}, u32[]{:S(2)}, u32[]{:S(2)}) collective-permute-start(bf16[256,256]{0,1:T(8,128)(2,1)S(1)} %fusion.74), channel_id=1, source_target_pairs={{2,0},{4,2},{6,4},{8,6},{10,8},{12,10},{14,12},{3,1},{5,3},{7,5},{... | collective-permute-start | bytes 393224 | tf_op jit(solution)/shard_map/ppermute | solution.py:17
  82.6 13.2 %collective-permute-start.11 = (bf16[256,256]{0,1:T(8,128)(2,1)}, bf16[256,256]{0,1:T(8,128)(2,1)}, u32[]{:S(2)}, u32[]{:S(2)}) collective-permute-start(bf16[256,256]{0,1:T(8,128)(2,1)} %fusion.67), channel_id=1, source_target_pairs={{2,0},{4,2},{6,4},{8,6},{10,8},{12,10},{14,12},{3,1},{5,3},{7,5},{... | collective-permute-start | bytes 393224 | tf_op jit(solution)/shard_map/ppermute | solution.py:17
  87.5 17.7 %copy-start.42 = (f32[256]{0:T(256)S(1)}, f32[256]{0:T(256)}, u32[]{:S(2)}) copy-start(f32[256]{0:T(256)} %copy-done.41) | copy-start | bytes 3076
  87.5 17.7 %copy-start.52 = (f32[128]{0:T(128)S(1)}, f32[128]{0:T(128)}, u32[]{:S(2)}) copy-start(f32[128]{0:T(128)} %param.26) | copy-start | bytes 1540
  96.8 8.3 %collective-permute-start.12 = (bf16[256,256]{0,1:T(8,128)(2,1)S(1)}, bf16[256,256]{0,1:T(8,128)(2,1)S(1)}, u32[]{:S(2)}, u32[]{:S(2)}) collective-permute-start(bf16[256,256]{0,1:T(8,128)(2,1)S(1)} %fusion.76), channel_id=1, source_target_pairs={{2,0},{4,2},{6,4},{8,6},{10,8},{12,10},{14,12},{3,1},{5,3},{7,5},{... | collective-permute-start | bytes 393224 | tf_op jit(solution)/shard_map/ppermute | solution.py:17
  106.6 5.3 %collective-permute-start.14 = (bf16[1344,48]{0,1:T(8,128)(2,1)S(1)}, bf16[1344,48]{0,1:T(8,128)(2,1)S(1)}, u32[]{:S(2)}, u32[]{:S(2)}) collective-permute-start(bf16[1344,48]{0,1:T(8,128)(2,1)S(1)} %constant_dynamic-slice_fusion), channel_id=1, source_target_pairs={{0,1},{1,0},{2,3},{3,2},{4,5},{5,4},{6,7},{7,6},{8,9},{9,8},{10,11... | collective-permute-start | bytes 387080 | tf_op jit(solution)/shard_map/ppermute | solution.py:65
  118.1 7.5 %collective-permute-start.15 = (bf16[98304]{0:T(1024)(128)(2,1)S(1)}, bf16[98304]{0:T(1024)(128)(2,1)S(1)}, u32[]{:S(2)}, u32[]{:S(2)}) collective-permute-start(bf16[98304]{0:T(1024)(128)(2,1)S(1)} %constant_dynamic-update-slice_fusion.6), channel_id=1, source_target_pairs={{0,2},{2,0},{4,6},{6,4},{8,10},{10,8},{12,14},{14,12},{1,3},{3,1},... | collective-permute-start | bytes 589832 | tf_op jit(solution)/shard_map/ppermute | solution.py:87
  125.7 8.1 %collective-permute-start.16 = (bf16[98304]{0:T(1024)(128)(2,1)S(1)}, bf16[98304]{0:T(1024)(128)(2,1)S(1)}, u32[]{:S(2)}, u32[]{:S(2)}) collective-permute-start(bf16[98304]{0:T(1024)(128)(2,1)S(1)} %add_convert_fusion.1), channel_id=1, source_target_pairs={{0,4},{2,6},{4,0},{6,2},{8,12},{10,14},{12,8},{14,10},{1,5},{3,7},... | collective-permute-start | bytes 589832 | tf_op jit(solution)/shard_map/ppermute | solution.py:87
  129.9 5.0 %collective-permute-start.13 = (bf16[128,2688]{1,0:T(8,128)(2,1)S(1)}, bf16[128,2688]{1,0:T(8,128)(2,1)S(1)}, u32[]{:S(2)}, u32[]{:S(2)}) collective-permute-start(bf16[128,2688]{1,0:T(8,128)(2,1)S(1)} %constant_dynamic-slice_fusion.1), channel_id=1, source_target_pairs={{0,1},{1,0},{2,3},{3,2},{4,5},{5,4},{6,7},{7,6},{8,9},{9,8},{10,11... | collective-permute-start | bytes 2064392 | tf_op jit(solution)/shard_map/ppermute | solution.py:65
  133.8 10.3 %collective-permute-start.17 = (bf16[98304]{0:T(1024)(128)(2,1)S(1)}, bf16[98304]{0:T(1024)(128)(2,1)S(1)}, u32[]{:S(2)}, u32[]{:S(2)}) collective-permute-start(bf16[98304]{0:T(1024)(128)(2,1)S(1)} %add_convert_fusion), channel_id=1, source_target_pairs={{0,8},{2,10},{4,12},{6,14},{8,0},{10,2},{12,4},{14,6},{1,9},{3,11}... | collective-permute-start | bytes 589832 | tf_op jit(solution)/shard_map/ppermute | solution.py:87
  (52 other events, 208.6 us)

commit v8 on v6

--- a/solution.py
+++ b/solution.py
@@ -213,7 +213,9 @@
         "thd,sd->hts", grad_heads, values_all, preferred_element_type=jnp.float32
     )
     inner_sum = jnp.sum(attn_probs * grad_probs, axis=-1, keepdims=True)
-    grad_scores = (attn_probs * (grad_probs - inner_sum) * score_scale).astype(jnp.bfloat16)
+    grad_scores = lax.optimization_barrier(
+        (attn_probs * (grad_probs - inner_sum) * score_scale).astype(jnp.bfloat16)
+    )
     grad_query = jnp.einsum(
         "hts,sd->thd", grad_scores, keys_all, preferred_element_type=jnp.float32
     )

time: 140 us -> 135 us (0.964)
  matrix products: 37 us -> 27 us
  local copies, waits for them, and re-layouts: 12.7 us -> 17.3 us
    dot_general x1, matrix products: 5.56 us -> 0.36 us  [on_device(): jnp.einsum('hts,sd->thd', grad_scores, keys_all, preferred_element_type=j...]
    dot_general x1, matrix products: 4.86 us -> 0.55 us  [on_device(): jnp.einsum('hts,thd->sd', grad_scores, query_normed, preferred_element_ty...]
    unnamed x124, local copies, waits for them, and re-layouts: 6.11 us -> 9.04 us
    dot_general x1, matrix products: 2.05 us -> 0.52 us  [on_device(): jnp.einsum('thd,sd->hts', grad_heads, values_all, preferred_element_type=...]
  transfers between devices with their start and end apart: 18 -> 18, of which waited for: 11 -> 11; matrix products, arithmetic and copies ran while one was open for 9% -> 10% of each run, Pallas kernels for 0% -> 0%
where the time goes in v8:
time: 135 us; the launch traced here: 134 us
  waiting for transfers between devices  48.5 us (36%)
  matrix products  27 us (20%)
  starting transfers between devices  25.8 us (19%)
  local copies, waits for them, and re-layouts  17.3 us (13%)
  other arithmetic  12.7 us (9%)
  between operations  2.3 us (2%)
    ppermute x8, waiting for transfers between devices, passed_along(): lax.ppermute(value, axis, [(source, source + steps) for source in range(l...  31.1 us
    ppermute x8, starting transfers between devices, passed_along(): lax.ppermute(value, axis, [(source, source + steps) for source in range(l...  20.2 us
    ppermute x3, waiting for transfers between devices, ctx_sum(): received = lax.ppermute(sent, 'ctx', [(i, i ^ step) for i in range(count)])  15.1 us
    dot_general x10, matrix products, multiply_by_transpose(): lax.dot_general(first_op, second_op, (((1,), (1,)), ((), ())), preferred_...  10.9 us
    unnamed x124, local copies, waits for them, and re-layouts  9.04 us
    dot_general x10, matrix products, matrix_product(): return jnp.dot(first_op, second_op, preferred_element_type=jnp.float32)  5.47 us
    dot_general x6, matrix products, transpose_multiply(): lax.dot_general(first_op, second_op, (((0,), (0,)), ((), ())), preferred_...  4.02 us
    ppermute x3, starting transfers between devices, ctx_sum(): received = lax.ppermute(sent, 'ctx', [(i, i ^ step) for i in range(count)])  3.89 us
  transfers between devices with their start and end apart: 18, of which 11 were waited for; matrix products, arithmetic and copies ran while one was open for 10% of the time, Pallas kernels for 0%

profile of v8, /device:TPU:0, one launch (start us, length us, event | category | flops | bytes accessed | tf_op | source)
XLA Modules:
  0.0 133.5 jit_solution(2519028006275184570)
XLA Ops:
  0.7 1.5 %fusion.21 = f32[128]{0:T(128)S(1)} fusion(bf16[128,2688]{1,0:T(8,128)(2,1)} %param.20), kind=kLoop, calls=%fused_computation.40 | loop fusion | flops 1032064 | bytes 688640 | tf_op jit(solution)/shard_map/reduce_sum | solution.py:21
  2.2 1.3 fusion.16
  9.8 5.9 %collective-permute-start.1 = (bf16[272,256]{0,1:T(8,128)(2,1)S(1)}, bf16[272,256]{0,1:T(8,128)(2,1)S(1)}, u32[]{:S(2)}, u32[]{:S(2)}) collective-permute-start(bf16[272,256]{0,1:T(8,128)(2,1)S(1)} %fusion.59), channel_id=1, source_target_pairs={{0,8},{2,10},{4,12},{6,14},{1,9},{3,11},{5,13},{7,15},{16,24},{18,... | collective-permute-start | bytes 417800 | tf_op jit(solution)/shard_map/ppermute | solution.py:17
  15.6 4.4 %collective-permute-start.2 = (bf16[272,256]{0,1:T(8,128)(2,1)S(1)}, bf16[272,256]{0,1:T(8,128)(2,1)S(1)}, u32[]{:S(2)}, u32[]{:S(2)}) collective-permute-start(bf16[272,256]{0,1:T(8,128)(2,1)S(1)} %fusion.59), channel_id=1, source_target_pairs={{0,6},{2,8},{4,10},{6,12},{8,14},{1,7},{3,9},{5,11},{7,13},{9,15},... | collective-permute-start | bytes 417800 | tf_op jit(solution)/shard_map/ppermute | solution.py:17
  21.4 3.1 %collective-permute-start.4 = (bf16[272,256]{0,1:T(8,128)(2,1)S(1)}, bf16[272,256]{0,1:T(8,128)(2,1)S(1)}, u32[]{:S(2)}, u32[]{:S(2)}) collective-permute-start(bf16[272,256]{0,1:T(8,128)(2,1)S(1)} %fusion.59), channel_id=1, source_target_pairs={{0,2},{2,4},{4,6},{6,8},{8,10},{10,12},{12,14},{1,3},{3,5},{5,7},{... | collective-permute-start | bytes 417800 | tf_op jit(solution)/shard_map/ppermute | solution.py:17
  25.6 3.0 %collective-permute-done.3 = bf16[272,256]{0,1:T(8,128)(2,1)S(1)} collective-permute-done((bf16[272,256]{0,1:T(8,128)(2,1)S(1)}, bf16[272,256]{0,1:T(8,128)(2,1)S(1)}, u32[]{:S(2)}, u32[]{:S(2)}) %collective-permute-start.3) | collective-permute-done | bytes 139296 | tf_op jit(solution)/shard_map/ppermute | solution.py:17
  29.8 2.4 %fusion.24 = f32[2,256,1280]{1,2,0:T(8,128)} fusion(pred[256,1280]{0,1:T(8,128)(4,1)S(1)} %fusion.28, bf16[1280,256]{0,1:T(8,128)(2,1)S(1)} %maximum_dynamic-update-slice_fusion, f32[256,256]{0,1:T(8,128)S(1)} %get-tuple-element.49, f32[128]{0:T(128)S(1)} %copy-done.51, f32[256,2]{0,1:T(2,128)S(1)} %add_rsqrt_fusion), kind=kOutput, calls=%fused_computation.51 | convolution fusion | flops 169936640 | bytes 3541504 | tf_op jit(solution)/shard_map/div | solution.py:175
  32.2 2.2 %fusion.34 = bf16[128,2,256]{2,0,1:T(8,128)(2,1)S(1)} fusion(f32[2,256,1280]{1,2,0:T(8,128)} %fusion.24, bf16[1280,256]{0,1:T(8,128)(2,1)S(1)} %maximum_dynamic-update-slice_fusion, f32[256]{0:T(256)S(1)} %copy-done.53), kind=kOutput, calls=%fused_computation.66 | convolution fusion | flops 168558592 | bytes 3081216 | tf_op jit(solution)/shard_map/hts,sd->thd/dot_general | solution.py:177
  38.9 1.7 %multiply_reduce_fusion.2 = (f32[128]{0:T(128)S(1)}, f32[128,2688]{1,0:T(8,128)S(1)}) fusion(bf16[128,16]{0,1:T(8,128)(2,1)S(1)} %add_convert_fusion.3, bf16[16,2688]{1,0:T(8,128)(2,1)S(1)} %copy-done.25, bf16[128,2688]{1,0:T(8,128)(2,1)} %collective-permute-done.5, bf16[256,2688]{1,0:T(8,128)(2,1)S(1)} %convolution_convert_fusion, s32[]{:T(128)S(6)} %select_n.62), kind=kOutput, calls=%fused_computation.47 | convolution fusion | flops 13418368 | bytes 2843140 | tf_op jit(solution)/shard_map/dot_general | solution.py:33
  52.8 2.1 %fusion.82 = f32[256,2688]{1,0:T(8,128)} fusion(bf16[256,256]{0,1:T(8,128)(2,1)S(1)} %bitcast.100, bf16[2688,256]{1,0:T(8,128)(2,1)S(1)} %copy-done), kind=kOutput, calls=%fused_computation.189 | convolution fusion | flops 352321536 | bytes 4259840 | tf_op jit(solution)/shard_map/dot_general | solution.py:37
  56.0 1.5 %reshape.265 = bf16[21504]{0:T(1024)(128)(2,1)} reshape(bf16[16,1344]{1,0:T(8,128)(2,1)} %fusion.11) | data formatting | bytes 86016 | tf_op jit(solution)/shard_map/reshape | solution.py:83
  57.6 1.4 %collective-permute-start.10 = (bf16[256,256]{0,1:T(8,128)(2,1)S(1)}, bf16[256,256]{0,1:T(8,128)(2,1)S(1)}, u32[]{:S(2)}, u32[]{:S(2)}) collective-permute-start(bf16[256,256]{0,1:T(8,128)(2,1)S(1)} %get-tuple-element.37), channel_id=1, source_target_pairs={{4,0},{6,2},{8,4},{10,6},{12,8},{14,10},{5,1},{7,3},{9,5},{11,7},{... | collective-permute-start | bytes 393224 | tf_op jit(solution)/shard_map/ppermute | solution.py:17
  60.4 1.5 %collective-permute-start.12 = (bf16[256,256]{0,1:T(8,128)(2,1)S(1)}, bf16[256,256]{0,1:T(8,128)(2,1)S(1)}, u32[]{:S(2)}, u32[]{:S(2)}) collective-permute-start(bf16[256,256]{0,1:T(8,128)(2,1)S(1)} %get-tuple-element.35), channel_id=1, source_target_pairs={{8,0},{10,2},{12,4},{14,6},{9,1},{11,3},{13,5},{15,7},{24,16},{26,... | collective-permute-start | bytes 393224 | tf_op jit(solution)/shard_map/ppermute | solution.py:17
  63.9 7.3 %collective-permute-done.10 = bf16[256,256]{0,1:T(8,128)(2,1)S(1)} collective-permute-done((bf16[256,256]{0,1:T(8,128)(2,1)S(1)}, bf16[256,256]{0,1:T(8,128)(2,1)S(1)}, u32[]{:S(2)}, u32[]{:S(2)}) %collective-permute-start.10) | collective-permute-done | bytes 131104 | tf_op jit(solution)/shard_map/ppermute | solution.py:17
  71.2 10.2 %collective-permute-done.11 = bf16[256,256]{0,1:T(8,128)(2,1)S(1)} collective-permute-done((bf16[256,256]{0,1:T(8,128)(2,1)S(1)}, bf16[256,256]{0,1:T(8,128)(2,1)S(1)}, u32[]{:S(2)}, u32[]{:S(2)}) %collective-permute-start.11) | collective-permute-done | bytes 131104 | tf_op jit(solution)/shard_map/ppermute | solution.py:17
  81.4 10.7 %collective-permute-done.12 = bf16[256,256]{0,1:T(8,128)(2,1)S(1)} collective-permute-done((bf16[256,256]{0,1:T(8,128)(2,1)S(1)}, bf16[256,256]{0,1:T(8,128)(2,1)S(1)}, u32[]{:S(2)}, u32[]{:S(2)}) %collective-permute-start.12) | collective-permute-done | bytes 131104 | tf_op jit(solution)/shard_map/ppermute | solution.py:17
  94.8 2.1 %convolution_add_fusion.1 = f32[256,2688]{1,0:T(8,128)} fusion(f32[256,2688]{1,0:T(8,128)S(1)} %copy-done.3, bf16[256,128]{0,1:T(8,128)(2,1)S(1)} %multiply_convert_fusion.4, bf16[2688,128]{1,0:T(8,128)(2,1)S(1)} %copy-done.18), kind=kOutput, calls=%fused_computation.2 | convolution fusion | flops 176848896 | bytes 6258688 | tf_op jit(solution)/shard_map/dot_general | solution.py:37
  96.9 2.1 %fusion.60 = f32[256,2688]{1,0:T(8,128)} fusion(bf16[2688,48]{0,1:T(8,128)(2,1)S(1)} %copy-done.27, bf16[256,16]{0,1:T(8,128)(2,1)S(1)} %fusion.40, bf16[256,16]{0,1:T(8,128)(2,1)S(1)} %fusion.39, bf16[256,16]{0,1:T(8,128)(2,1)S(1)} %fusion.38), kind=kOutput, calls=%fused_computation.140 | convolution fusion | flops 66134016 | bytes 3035136 | tf_op jit(solution)/shard_map/dot_general | solution.py:37
  105.2 3.2 %fusion.2 = bf16[256,2688]{1,0:T(8,128)(2,1)S(1)} fusion(f32[256,2688]{1,0:T(8,128)} %fusion.60, f32[256,2688]{1,0:T(8,128)} %convolution_add_fusion.1, bf16[2688,128]{1,0:T(8,128)(2,1)S(1)} %copy-done.24, f32[256,256]{0,1:T(8,128)S(1)} %copy-done.5), kind=kOutput, calls=%fused_computation.5 | convolution fusion | flops 178225152 | bytes 7634944 | tf_op jit(solution)/shard_map/dot_general | solution.py:37
  108.4 3.1 %collective-permute-done.15 = bf16[98304]{0:T(1024)(128)(2,1)S(1)} collective-permute-done((bf16[98304]{0:T(1024)(128)(2,1)S(1)}, bf16[98304]{0:T(1024)(128)(2,1)S(1)}, u32[]{:S(2)}, u32[]{:S(2)}) %collective-permute-start.15) | collective-permute-done | bytes 196640 | tf_op jit(solution)/shard_map/ppermute | solution.py:87
  111.5 3.1 %collective-permute-start.16 = (bf16[98304]{0:T(1024)(128)(2,1)S(1)}, bf16[98304]{0:T(1024)(128)(2,1)S(1)}, u32[]{:S(2)}, u32[]{:S(2)}) collective-permute-start(bf16[98304]{0:T(1024)(128)(2,1)S(1)} %add_convert_fusion.1), channel_id=1, source_target_pairs={{0,4},{2,6},{4,0},{6,2},{8,12},{10,14},{12,8},{14,10},{1,5},{3,7},... | collective-permute-start | bytes 589832 | tf_op jit(solution)/shard_map/ppermute | solution.py:87
  114.8 4.1 %collective-permute-done.16 = bf16[98304]{0:T(1024)(128)(2,1)S(1)} collective-permute-done((bf16[98304]{0:T(1024)(128)(2,1)S(1)}, bf16[98304]{0:T(1024)(128)(2,1)S(1)}, u32[]{:S(2)}, u32[]{:S(2)}) %collective-permute-start.16) | collective-permute-done | bytes 196640 | tf_op jit(solution)/shard_map/ppermute | solution.py:87
  120.3 1.3 %fusion.20 = bf16[128,2688]{1,0:T(8,128)(2,1)} fusion(bf16[128,2688]{1,0:T(8,128)(2,1)S(1)} %copy-done.2, bf16[128,2688]{1,0:T(8,128)(2,1)S(1)} %collective-permute-done.13, f32[128]{0:T(128)S(1)} %broadcast_multiply_fusion.2, f32[2688]{0:T(1024)S(1)} %copy-done.29, f32[128]{0:T(128)S(1)} %copy-done.47, bf16[256,2688]{1,0:T(8,128)(2,1)S(1)} %fusion.2, ...), kind=kLoop, calls=%fused_computation.39 | loop fusion | flops 3440640 | bytes 2764292 | tf_op jit(solution)/shard_map/convert_element_type | solution.py:265
  121.6 7.9 %collective-permute-done.17 = bf16[98304]{0:T(1024)(128)(2,1)S(1)} collective-permute-done((bf16[98304]{0:T(1024)(128)(2,1)S(1)}, bf16[98304]{0:T(1024)(128)(2,1)S(1)}, u32[]{:S(2)}, u32[]{:S(2)}) %collective-permute-start.17) | collective-permute-done | bytes 196640 | tf_op jit(solution)/shard_map/ppermute | solution.py:87
  (230 shorter events, 44.2 us)
Async XLA Ops:
  3.5 2.3 %collective-permute-start = (bf16[128,2688]{1,0:T(8,128)(2,1)S(1)}, bf16[128,2688]{1,0:T(8,128)(2,1)S(1)}, u32[]{:S(2)}, u32[]{:S(2)}) collective-permute-start(bf16[128,2688]{1,0:T(8,128)(2,1)S(1)} %fusion.16), channel_id=1, source_target_pairs={{0,1},{1,0},{2,3},{3,2},{4,5},{5,4},{6,7},{7,6},{8,9},{9,8},{10,11... | collective-permute-start | bytes 2064392 | tf_op jit(solution)/shard_map/ppermute | solution.py:72
  7.0 45.0 %copy-start.30 = (bf16[256,48]{0,1:T(8,128)(2,1)}, bf16[256,48]{0,1:T(8,128)(2,1)S(1)}, u32[]{:S(2)}) copy-start(bf16[256,48]{0,1:T(8,128)(2,1)S(1)} %convolution_convert_fusion.2) | copy-start | bytes 73732
  9.8 15.8 %collective-permute-start.1 = (bf16[272,256]{0,1:T(8,128)(2,1)S(1)}, bf16[272,256]{0,1:T(8,128)(2,1)S(1)}, u32[]{:S(2)}, u32[]{:S(2)}) collective-permute-start(bf16[272,256]{0,1:T(8,128)(2,1)S(1)} %fusion.59), channel_id=1, source_target_pairs={{0,8},{2,10},{4,12},{6,14},{1,9},{3,11},{5,13},{7,15},{16,24},{18,... | collective-permute-start | bytes 417800 | tf_op jit(solution)/shard_map/ppermute | solution.py:17
  15.6 9.9 %collective-permute-start.2 = (bf16[272,256]{0,1:T(8,128)(2,1)S(1)}, bf16[272,256]{0,1:T(8,128)(2,1)S(1)}, u32[]{:S(2)}, u32[]{:S(2)}) collective-permute-start(bf16[272,256]{0,1:T(8,128)(2,1)S(1)} %fusion.59), channel_id=1, source_target_pairs={{0,6},{2,8},{4,10},{6,12},{8,14},{1,7},{3,9},{5,11},{7,13},{9,15},... | collective-permute-start | bytes 417800 | tf_op jit(solution)/shard_map/ppermute | solution.py:17
  20.1 8.5 %collective-permute-start.3 = (bf16[272,256]{0,1:T(8,128)(2,1)S(1)}, bf16[272,256]{0,1:T(8,128)(2,1)S(1)}, u32[]{:S(2)}, u32[]{:S(2)}) collective-permute-start(bf16[272,256]{0,1:T(8,128)(2,1)S(1)} %fusion.59), channel_id=1, source_target_pairs={{0,4},{2,6},{4,8},{6,10},{8,12},{10,14},{1,5},{3,7},{5,9},{7,11},{... | collective-permute-start | bytes 417800 | tf_op jit(solution)/shard_map/ppermute | solution.py:17
  21.4 7.2 %collective-permute-start.4 = (bf16[272,256]{0,1:T(8,128)(2,1)S(1)}, bf16[272,256]{0,1:T(8,128)(2,1)S(1)}, u32[]{:S(2)}, u32[]{:S(2)}) collective-permute-start(bf16[272,256]{0,1:T(8,128)(2,1)S(1)} %fusion.59), channel_id=1, source_target_pairs={{0,2},{2,4},{4,6},{6,8},{8,10},{10,12},{12,14},{1,3},{3,5},{5,7},{... | collective-permute-start | bytes 417800 | tf_op jit(solution)/shard_map/ppermute | solution.py:17
  35.9 3.0 %collective-permute-start.5 = (bf16[128,2688]{1,0:T(8,128)(2,1)}, bf16[128,2688]{1,0:T(8,128)(2,1)}, u32[]{:S(2)}, u32[]{:S(2)}) collective-permute-start(bf16[128,2688]{1,0:T(8,128)(2,1)} %constant_dynamic-slice_fusion.3), channel_id=1, source_target_pairs={{0,1},{1,0},{2,3},{3,2},{4,5},{5,4},{6,7},{7,6},{8,9},{9,8},{10,11... | collective-permute-start | bytes 2064392 | tf_op jit(solution)/shard_map/ppermute | solution.py:65
  36.7 1.5 %collective-permute-start.6 = (bf16[128,16]{0,1:T(8,128)(2,1)S(1)}, bf16[128,16]{0,1:T(8,128)(2,1)}, u32[]{:S(2)}, u32[]{:S(2)}) collective-permute-start(bf16[128,16]{0,1:T(8,128)(2,1)S(1)} %constant_dynamic-slice_fusion.2), channel_id=1, source_target_pairs={{0,1},{1,0},{2,3},{3,2},{4,5},{5,4},{6,7},{7,6},{8,9},{9,8},{10,11... | collective-permute-start | bytes 12296 | tf_op jit(solution)/shard_map/ppermute | solution.py:65
  42.6 1.2 collective-permute-start.8
  42.9 2.3 %collective-permute-start.7 = (bf16[128,2688]{1,0:T(8,128)(2,1)S(1)}, bf16[128,2688]{1,0:T(8,128)(2,1)}, u32[]{:S(2)}, u32[]{:S(2)}) collective-permute-start(bf16[128,2688]{1,0:T(8,128)(2,1)S(1)} %get-tuple-element.28), channel_id=1, source_target_pairs={{0,1},{1,0},{2,3},{3,2},{4,5},{5,4},{6,7},{7,6},{8,9},{9,8},{10,11... | collective-permute-start | bytes 2064392 | tf_op jit(solution)/shard_map/ppermute | solution.py:72
  57.6 34.6 %copy-start.16 = (f32[256,128]{0,1:T(8,128)S(1)}, f32[256,128]{0,1:T(8,128)}, u32[]{:S(2)}) copy-start(f32[256,128]{0,1:T(8,128)} %copy-done.15) | copy-start | bytes 393220
  57.6 34.6 %copy-start.41 = (f32[256]{0:T(256)S(1)}, f32[256]{0:T(256)}, u32[]{:S(2)}) copy-start(f32[256]{0:T(256)} %copy-done.40) | copy-start | bytes 3076
  57.6 34.6 %copy-start.49 = (f32[128]{0:T(128)S(1)}, f32[128]{0:T(128)}, u32[]{:S(2)}) copy-start(f32[128]{0:T(128)} %param.26) | copy-start | bytes 1540
  57.6 34.7 %copy-start.43 = (bf16[16,128]{1,0:T(8,128)(2,1)S(1)}, bf16[16,128]{1,0:T(8,128)(2,1)}, u32[]{:S(2)}) copy-start(bf16[16,128]{1,0:T(8,128)(2,1)} %param.35) | copy-start | bytes 12292
  57.6 13.6 %collective-permute-start.10 = (bf16[256,256]{0,1:T(8,128)(2,1)S(1)}, bf16[256,256]{0,1:T(8,128)(2,1)S(1)}, u32[]{:S(2)}, u32[]{:S(2)}) collective-permute-start(bf16[256,256]{0,1:T(8,128)(2,1)S(1)} %get-tuple-element.37), channel_id=1, source_target_pairs={{4,0},{6,2},{8,4},{10,6},{12,8},{14,10},{5,1},{7,3},{9,5},{11,7},{... | collective-permute-start | bytes 393224 | tf_op jit(solution)/shard_map/ppermute | solution.py:17
  59.1 22.3 %collective-permute-start.11 = (bf16[256,256]{0,1:T(8,128)(2,1)S(1)}, bf16[256,256]{0,1:T(8,128)(2,1)S(1)}, u32[]{:S(2)}, u32[]{:S(2)}) collective-permute-start(bf16[256,256]{0,1:T(8,128)(2,1)S(1)} %get-tuple-element.36), channel_id=1, source_target_pairs={{6,0},{8,2},{10,4},{12,6},{14,8},{7,1},{9,3},{11,5},{13,7},{15,9},... | collective-permute-start | bytes 393224 | tf_op jit(solution)/shard_map/ppermute | solution.py:17
  60.4 31.7 %collective-permute-start.12 = (bf16[256,256]{0,1:T(8,128)(2,1)S(1)}, bf16[256,256]{0,1:T(8,128)(2,1)S(1)}, u32[]{:S(2)}, u32[]{:S(2)}) collective-permute-start(bf16[256,256]{0,1:T(8,128)(2,1)S(1)} %get-tuple-element.35), channel_id=1, source_target_pairs={{8,0},{10,2},{12,4},{14,6},{9,1},{11,3},{13,5},{15,7},{24,16},{26,... | collective-permute-start | bytes 393224 | tf_op jit(solution)/shard_map/ppermute | solution.py:17
  61.9 30.2 %collective-permute-start.9 = (bf16[256,256]{0,1:T(8,128)(2,1)S(1)}, bf16[256,256]{0,1:T(8,128)(2,1)S(1)}, u32[]{:S(2)}, u32[]{:S(2)}) collective-permute-start(bf16[256,256]{0,1:T(8,128)(2,1)S(1)} %get-tuple-element.34), channel_id=1, source_target_pairs={{2,0},{4,2},{6,4},{8,6},{10,8},{12,10},{14,12},{3,1},{5,3},{7,5},{... | collective-permute-start | bytes 393224 | tf_op jit(solution)/shard_map/ppermute | solution.py:17
  63.9 29.2 %copy-start.22 = (bf16[128,2688]{1,0:T(8,128)(2,1)S(1)}, bf16[128,2688]{1,0:T(8,128)(2,1)}, u32[]{:S(2)}) copy-start(bf16[128,2688]{1,0:T(8,128)(2,1)} %copy-done.21) | copy-start | bytes 2064388
  93.7 5.3 %collective-permute-start.14 = (bf16[1344,48]{0,1:T(8,128)(2,1)S(1)}, bf16[1344,48]{0,1:T(8,128)(2,1)S(1)}, u32[]{:S(2)}, u32[]{:S(2)}) collective-permute-start(bf16[1344,48]{0,1:T(8,128)(2,1)S(1)} %constant_dynamic-slice_fusion), channel_id=1, source_target_pairs={{0,1},{1,0},{2,3},{3,2},{4,5},{5,4},{6,7},{7,6},{8,9},{9,8},{10,11... | collective-permute-start | bytes 387080 | tf_op jit(solution)/shard_map/ppermute | solution.py:65
  105.2 6.3 %collective-permute-start.15 = (bf16[98304]{0:T(1024)(128)(2,1)S(1)}, bf16[98304]{0:T(1024)(128)(2,1)S(1)}, u32[]{:S(2)}, u32[]{:S(2)}) collective-permute-start(bf16[98304]{0:T(1024)(128)(2,1)S(1)} %constant_dynamic-update-slice_fusion.6), channel_id=1, source_target_pairs={{0,2},{2,0},{4,6},{6,4},{8,10},{10,8},{12,14},{14,12},{1,3},{3,1},... | collective-permute-start | bytes 589832 | tf_op jit(solution)/shard_map/ppermute | solution.py:87
  111.5 7.4 %collective-permute-start.16 = (bf16[98304]{0:T(1024)(128)(2,1)S(1)}, bf16[98304]{0:T(1024)(128)(2,1)S(1)}, u32[]{:S(2)}, u32[]{:S(2)}) collective-permute-start(bf16[98304]{0:T(1024)(128)(2,1)S(1)} %add_convert_fusion.1), channel_id=1, source_target_pairs={{0,4},{2,6},{4,0},{6,2},{8,12},{10,14},{12,8},{14,10},{1,5},{3,7},... | collective-permute-start | bytes 589832 | tf_op jit(solution)/shard_map/ppermute | solution.py:87
  114.7 5.1 %collective-permute-start.13 = (bf16[128,2688]{1,0:T(8,128)(2,1)S(1)}, bf16[128,2688]{1,0:T(8,128)(2,1)S(1)}, u32[]{:S(2)}, u32[]{:S(2)}) collective-permute-start(bf16[128,2688]{1,0:T(8,128)(2,1)S(1)} %constant_dynamic-slice_fusion.1), channel_id=1, source_target_pairs={{0,1},{1,0},{2,3},{3,2},{4,5},{5,4},{6,7},{7,6},{8,9},{9,8},{10,11... | collective-permute-start | bytes 2064392 | tf_op jit(solution)/shard_map/ppermute | solution.py:65
  119.0 10.5 %collective-permute-start.17 = (bf16[98304]{0:T(1024)(128)(2,1)S(1)}, bf16[98304]{0:T(1024)(128)(2,1)S(1)}, u32[]{:S(2)}, u32[]{:S(2)}) collective-permute-start(bf16[98304]{0:T(1024)(128)(2,1)S(1)} %add_convert_fusion), channel_id=1, source_target_pairs={{0,8},{2,10},{4,12},{6,14},{8,0},{10,2},{12,4},{14,6},{1,9},{3,11}... | collective-permute-start | bytes 589832 | tf_op jit(solution)/shard_map/ppermute | solution.py:87
  (49 other events, 265.3 us)

commit v9 on v8

--- a/solution.py
+++ b/solution.py
@@ -127,19 +127,26 @@
     tok_float = tokens.astype(jnp.float32)
     normed_rows = norm_rows(tok_float, input_norm_gain).astype(jnp.bfloat16)
     normalized_input = tp_gather(normed_rows)
-    middle_list = matrix_product(normalized_input, adapter_down_maps).astype(jnp.bfloat16)
+    query_width = query_projection.shape[1]
+    key_end = query_width + head_dim
+    value_end = key_end + head_dim
+    all_weights = jnp.concatenate(
+        [query_projection, key_projection, value_projection, adapter_down_maps], axis=1
+    )
+    projected = matrix_product(normalized_input, all_weights)
+    middle_list = projected[:, value_end:].astype(jnp.bfloat16)
     middle_query = middle_list[:, :adapter_product]
     middle_key = middle_list[:, adapter_product : 2 * adapter_product]
     middle_value = middle_list[:, 2 * adapter_product :]
-    query_before_norm = matrix_product(
-        normalized_input, query_projection
-    ) + adapter_scale * matrix_product(middle_query, adapter_query_up)
-    key_before_norm = matrix_product(
-        normalized_input, key_projection
-    ) + adapter_scale * matrix_product(middle_key, adapter_key_up)
-    value_before_norm = matrix_product(
-        normalized_input, value_projection
-    ) + adapter_scale * matrix_product(middle_value, adapter_value_up)
+    query_before_norm = projected[:, :query_width] + adapter_scale * matrix_product(
+        middle_query, adapter_query_up
+    )
+    key_before_norm = projected[:, query_width:key_end] + adapter_scale * matrix_product(
+        middle_key, adapter_key_up
+    )
+    value_before_norm = projected[:, key_end:value_end] + adapter_scale * matrix_product(
+        middle_value, adapter_value_up
+    )
     query_heads = query_before_norm.reshape(shard_len, heads_here, head_dim)
     query_normed = norm_rows(query_heads, query_norm_gain).astype(jnp.bfloat16)
     key_normed = norm_rows(key_before_norm, key_norm_gain).astype(jnp.bfloat16)
@@ -255,11 +262,12 @@
         ],
         axis=1,
     ).astype(jnp.bfloat16)
-    grad_normed = (
-        multiply_by_transpose(query_prenorm_gradient, query_projection)
-        + multiply_by_transpose(key_prenorm_gradient, key_projection)
-        + multiply_by_transpose(value_prenorm_gradient, value_projection)
-        + multiply_by_transpose(middle_gradients, adapter_down_maps)
+    grad_normed = multiply_by_transpose(
+        jnp.concatenate(
+            [query_prenorm_gradient, key_prenorm_gradient, value_prenorm_gradient, middle_gradients],
+            axis=1,
+        ),
+        all_weights,
     )
     grad_normed_rows = tp_sum_scatter(grad_normed.astype(jnp.bfloat16))
     grad_in = norm_back(tok_float, input_norm_gain, grad_normed_rows).astype(jnp.bfloat16)

time: 135 us -> 130 us (0.963)
  matrix products: 27 us -> 20.3 us
  starting transfers between devices: 25.8 us -> 29.7 us
  waiting for transfers between devices: 48.5 us -> 46.4 us
    dot_general x10 -> x7, matrix products: 10.9 us -> 4.64 us  [multiply_by_transpose(): lax.dot_general(first_op, second_op, (((1,), (1,)), ((), ())), preferred_...]
    ppermute x3, starting transfers between devices: 3.89 us -> 8.32 us  [ctx_sum(): received = lax.ppermute(sent, 'ctx', [(i, i ^ step) for i in range(count)])]
    ppermute x8, waiting for transfers between devices: 31.1 us -> 28.6 us  [passed_along(): lax.ppermute(value, axis, [(source, source + steps) for source in range(l...]
    unnamed x124 -> x107, local copies, waits for them, and re-layouts: 9.04 us -> 9.45 us
    dot_general x10 -> x7, matrix products: 5.47 us -> 5.68 us  [matrix_product(): return jnp.dot(first_op, second_op, preferred_element_type=jnp.float32)]
  transfers between devices with their start and end apart: 18 -> 18, of which waited for: 11 -> 8; matrix products, arithmetic and copies ran while one was open for 10% -> 10% of each run, Pallas kernels for 0% -> 0%
where the time goes in v9:
time: 130 us; the launch traced here: 129 us
  waiting for transfers between devices  46.4 us (36%)
  starting transfers between devices  29.7 us (23%)
  matrix products  20.3 us (16%)
  local copies, waits for them, and re-layouts  17.6 us (14%)
  other arithmetic  13 us (10%)
  between operations  2.31 us (2%)
    ppermute x8, waiting for transfers between devices, passed_along(): lax.ppermute(value, axis, [(source, source + steps) for source in range(l...  28.6 us
    ppermute x8, starting transfers between devices, passed_along(): lax.ppermute(value, axis, [(source, source + steps) for source in range(l...  19.7 us
    ppermute x3, waiting for transfers between devices, ctx_sum(): received = lax.ppermute(sent, 'ctx', [(i, i ^ step) for i in range(count)])  15.5 us
    unnamed x107, local copies, waits for them, and re-layouts  9.45 us
    ppermute x3, starting transfers between devices, ctx_sum(): received = lax.ppermute(sent, 'ctx', [(i, i ^ step) for i in range(count)])  8.32 us
    dot_general x7, matrix products, matrix_product(): return jnp.dot(first_op, second_op, preferred_element_type=jnp.float32)  5.68 us
    dot_general x7, matrix products, multiply_by_transpose(): lax.dot_general(first_op, second_op, (((1,), (1,)), ((), ())), preferred_...  4.64 us
    dot_general x6, matrix products, transpose_multiply(): lax.dot_general(first_op, second_op, (((0,), (0,)), ((), ())), preferred_...  3.45 us
  transfers between devices with their start and end apart: 18, of which 8 were waited for; matrix products, arithmetic and copies ran while one was open for 10% of the time, Pallas kernels for 0%

profile of v9, /device:TPU:0, one launch (start us, length us, event | category | flops | bytes accessed | tf_op | source)
XLA Modules:
  0.0 129.3 jit_solution(16066198293383734699)
XLA Ops:
  0.7 1.4 %fusion.19 = f32[128]{0:T(128)S(1)} fusion(bf16[128,2688]{1,0:T(8,128)(2,1)} %param.20), kind=kLoop, calls=%fused_computation.38 | loop fusion | flops 1032064 | bytes 688640 | tf_op jit(solution)/shard_map/reduce_sum | solution.py:21
  2.1 1.4 %fusion.14 = bf16[128,2688]{1,0:T(8,128)(2,1)S(1)} fusion(bf16[128,2688]{1,0:T(8,128)(2,1)} %param.20, f32[2688]{0:T(1024)} %param.24, f32[128]{0:T(128)S(1)} %add_rsqrt_fusion.3), kind=kLoop, calls=%fused_computation.33 | loop fusion | flops 1376256 | bytes 1387520 | tf_op jit(solution)/shard_map/convert_element_type | solution.py:128
  4.8 2.1 %copy.35 = bf16[2688,48]{1,0:T(8,128)(2,1)} copy(bf16[2688,48]{0,1:T(8,128)(2,1)} %param.32) | data formatting | bytes 516096 | tf_op args[12]
  9.1 2.6 %fusion.86 = (bf16[256,560]{0,1:T(8,128)(2,1)S(1)}, f32[256,560]{0,1:T(8,128)S(1)}) fusion(bf16[2688,48]{1,0:T(8,128)(2,1)S(1)} %copy-done.16, bf16[2688,128]{1,0:T(8,128)(2,1)S(1)} %copy-done.44, bf16[2688,128]{1,0:T(8,128)(2,1)} %param.29, bf16[2688,256]{1,0:T(8,128)(2,1)S(1)} %copy-done.43, bf16[128,2688]{1,0:T(8,128)(2,1)S(1)} %get-tuple-element.35, ...), kind=kOutput, calls=%fused_computation.197 | convolution fusion | flops 785641472 | bytes 5246976 | tf_op jit(solution)/shard_map/dot_general | solution.py:33
  12.4 4.4 %collective-permute-start.4 = (bf16[272,256]{0,1:T(8,128)(2,1)S(1)}, bf16[272,256]{0,1:T(8,128)(2,1)S(1)}, u32[]{:S(2)}, u32[]{:S(2)}) collective-permute-start(bf16[272,256]{0,1:T(8,128)(2,1)S(1)} %fusion.57), channel_id=1, source_target_pairs={{0,2},{2,4},{4,6},{6,8},{8,10},{10,12},{12,14},{1,3},{3,5},{5,7},{... | collective-permute-start | bytes 417800 | tf_op jit(solution)/shard_map/ppermute | solution.py:17
  16.9 3.5 %collective-permute-start.3 = (bf16[272,256]{0,1:T(8,128)(2,1)S(1)}, bf16[272,256]{0,1:T(8,128)(2,1)S(1)}, u32[]{:S(2)}, u32[]{:S(2)}) collective-permute-start(bf16[272,256]{0,1:T(8,128)(2,1)S(1)} %fusion.57), channel_id=1, source_target_pairs={{0,4},{2,6},{4,8},{6,10},{8,12},{10,14},{1,5},{3,7},{5,9},{7,11},{... | collective-permute-start | bytes 417800 | tf_op jit(solution)/shard_map/ppermute | solution.py:17
  20.4 4.5 %collective-permute-start.2 = (bf16[272,256]{0,1:T(8,128)(2,1)S(1)}, bf16[272,256]{0,1:T(8,128)(2,1)S(1)}, u32[]{:S(2)}, u32[]{:S(2)}) collective-permute-start(bf16[272,256]{0,1:T(8,128)(2,1)S(1)} %fusion.57), channel_id=1, source_target_pairs={{0,6},{2,8},{4,10},{6,12},{8,14},{1,7},{3,9},{5,11},{7,13},{9,15},... | collective-permute-start | bytes 417800 | tf_op jit(solution)/shard_map/ppermute | solution.py:17
  24.8 1.9 %collective-permute-start.1 = (bf16[272,256]{0,1:T(8,128)(2,1)S(1)}, bf16[272,256]{0,1:T(8,128)(2,1)S(1)}, u32[]{:S(2)}, u32[]{:S(2)}) collective-permute-start(bf16[272,256]{0,1:T(8,128)(2,1)S(1)} %fusion.57), channel_id=1, source_target_pairs={{0,8},{2,10},{4,12},{6,14},{1,9},{3,11},{5,13},{7,15},{16,24},{18,... | collective-permute-start | bytes 417800 | tf_op jit(solution)/shard_map/ppermute | solution.py:17
  27.1 6.2 %collective-permute-done.1 = bf16[272,256]{0,1:T(8,128)(2,1)S(1)} collective-permute-done((bf16[272,256]{0,1:T(8,128)(2,1)S(1)}, bf16[272,256]{0,1:T(8,128)(2,1)S(1)}, u32[]{:S(2)}, u32[]{:S(2)}) %collective-permute-start.1) | collective-permute-done | bytes 139296 | tf_op jit(solution)/shard_map/ppermute | solution.py:17
  34.6 2.4 %fusion.22 = f32[2,256,1280]{1,2,0:T(8,128)} fusion(pred[256,1280]{0,1:T(8,128)(4,1)S(1)} %fusion.26, bf16[1280,256]{0,1:T(8,128)(2,1)S(1)} %maximum_dynamic-update-slice_fusion, f32[256,256]{0,1:T(8,128)S(1)} %get-tuple-element.53, f32[128]{0:T(128)S(1)} %copy-done.39, f32[256,2]{0,1:T(2,128)S(1)} %add_rsqrt_fusion), kind=kOutput, calls=%fused_computation.49 | convolution fusion | flops 169936640 | bytes 3541504 | tf_op jit(solution)/shard_map/div | solution.py:182
  37.1 2.1 %fusion.32 = bf16[128,2,256]{2,0,1:T(8,128)(2,1)S(1)} fusion(f32[2,256,1280]{1,2,0:T(8,128)} %fusion.22, bf16[1280,256]{0,1:T(8,128)(2,1)S(1)} %maximum_dynamic-update-slice_fusion, f32[256]{0:T(256)S(1)} %fusion.73), kind=kOutput, calls=%fused_computation.63 | convolution fusion | flops 168558592 | bytes 3081216 | tf_op jit(solution)/shard_map/hts,sd->thd/dot_general | solution.py:184
  41.3 1.6 %collective-permute-done.6 = bf16[128,16]{0,1:T(8,128)(2,1)} collective-permute-done((bf16[128,16]{0,1:T(8,128)(2,1)S(1)}, bf16[128,16]{0,1:T(8,128)(2,1)}, u32[]{:S(2)}, u32[]{:S(2)}) %collective-permute-start.6) | collective-permute-done | bytes 4128 | tf_op jit(solution)/shard_map/ppermute | solution.py:65
  43.7 1.7 %multiply_reduce_fusion.2 = (f32[128]{0:T(128)S(1)}, f32[128,2688]{1,0:T(8,128)S(1)}) fusion(bf16[128,16]{0,1:T(8,128)(2,1)S(1)} %add_convert_fusion.3, bf16[16,2688]{1,0:T(8,128)(2,1)S(1)} %copy-done.18, bf16[128,2688]{1,0:T(8,128)(2,1)} %collective-permute-done.5, bf16[256,2688]{1,0:T(8,128)(2,1)S(1)} %convolution_convert_fusion.1, s32[]{:T(128)S(6)} %select_n.62), kind=kOutput, calls=%fused_computation.45 | convolution fusion | flops 13418368 | bytes 2843140 | tf_op jit(solution)/shard_map/dot_general | solution.py:33
  60.4 1.5 %collective-permute-start.10 = (bf16[256,256]{0,1:T(8,128)(2,1)S(1)}, bf16[256,256]{0,1:T(8,128)(2,1)S(1)}, u32[]{:S(2)}, u32[]{:S(2)}) collective-permute-start(bf16[256,256]{0,1:T(8,128)(2,1)S(1)} %get-tuple-element.39), channel_id=1, source_target_pairs={{4,0},{6,2},{8,4},{10,6},{12,8},{14,10},{5,1},{7,3},{9,5},{11,7},{... | collective-permute-start | bytes 393224 | tf_op jit(solution)/shard_map/ppermute | solution.py:17
  62.0 2.9 %collective-permute-done.9 = bf16[256,256]{0,1:T(8,128)(2,1)S(1)} collective-permute-done((bf16[256,256]{0,1:T(8,128)(2,1)S(1)}, bf16[256,256]{0,1:T(8,128)(2,1)S(1)}, u32[]{:S(2)}, u32[]{:S(2)}) %collective-permute-start.9) | collective-permute-done | bytes 131104 | tf_op jit(solution)/shard_map/ppermute | solution.py:17
  64.9 19.4 %collective-permute-done.12 = bf16[256,256]{0,1:T(8,128)(2,1)S(1)} collective-permute-done((bf16[256,256]{0,1:T(8,128)(2,1)S(1)}, bf16[256,256]{0,1:T(8,128)(2,1)S(1)}, u32[]{:S(2)}, u32[]{:S(2)}) %collective-permute-start.12) | collective-permute-done | bytes 131104 | tf_op jit(solution)/shard_map/ppermute | solution.py:17
  88.9 1.7 %add_convert_fusion.2 = bf16[1344,48]{0,1:T(8,128)(2,1)} fusion(bf16[1344,48]{0,1:T(8,128)(2,1)} %collective-permute-done.14, bf16[2688,48]{0,1:T(8,128)(2,1)S(1)} %convolution_convert_fusion.2, s32[]{:T(128)S(6)} %select_n.69), kind=kLoop, calls=%fused_computation.103 | loop fusion | flops 258048 | bytes 387076 | tf_op jit(solution)/shard_map/convert.15
  96.1 4.3 %collective-permute-start.15 = (bf16[98304]{0:T(1024)(128)(2,1)S(1)}, bf16[98304]{0:T(1024)(128)(2,1)S(1)}, u32[]{:S(2)}, u32[]{:S(2)}) collective-permute-start(bf16[98304]{0:T(1024)(128)(2,1)S(1)} %constant_dynamic-update-slice_fusion.12), channel_id=1, source_target_pairs={{0,2},{2,0},{4,6},{6,4},{8,10},{10,8},{12,14},{14,12},{1,3},{3,1},... | collective-permute-start | bytes 589832 | tf_op jit(solution)/shard_map/ppermute | solution.py:87
  100.4 3.2 %convolution_convert_fusion = bf16[256,2688]{1,0:T(8,128)(2,1)S(1)} fusion(bf16[256,560]{0,1:T(8,128)(2,1)} %copy-done.21, bf16[2688,48]{1,0:T(8,128)(2,1)S(1)} %copy-done.17, bf16[2688,128]{1,0:T(8,128)(2,1)} %param.30, bf16[2688,128]{1,0:T(8,128)(2,1)} %param.29, bf16[2688,256]{1,0:T(8,128)(2,1)} %param.28), kind=kOutput, calls=%fused_computation.1 | convolution fusion | flops 783433728 | bytes 4673536 | tf_op jit(solution)/shard_map/dot_general | solution.py:37
  103.6 2.4 %collective-permute-done.15 = bf16[98304]{0:T(1024)(128)(2,1)S(1)} collective-permute-done((bf16[98304]{0:T(1024)(128)(2,1)S(1)}, bf16[98304]{0:T(1024)(128)(2,1)S(1)}, u32[]{:S(2)}, u32[]{:S(2)}) %collective-permute-start.15) | collective-permute-done | bytes 196640 | tf_op jit(solution)/shard_map/ppermute | solution.py:87
  106.0 3.3 %collective-permute-start.16 = (bf16[98304]{0:T(1024)(128)(2,1)S(1)}, bf16[98304]{0:T(1024)(128)(2,1)S(1)}, u32[]{:S(2)}, u32[]{:S(2)}) collective-permute-start(bf16[98304]{0:T(1024)(128)(2,1)S(1)} %add_convert_fusion.1), channel_id=1, source_target_pairs={{0,4},{2,6},{4,0},{6,2},{8,12},{10,14},{12,8},{14,10},{1,5},{3,7},... | collective-permute-start | bytes 589832 | tf_op jit(solution)/shard_map/ppermute | solution.py:87
  109.4 4.7 %collective-permute-done.16 = bf16[98304]{0:T(1024)(128)(2,1)S(1)} collective-permute-done((bf16[98304]{0:T(1024)(128)(2,1)S(1)}, bf16[98304]{0:T(1024)(128)(2,1)S(1)}, u32[]{:S(2)}, u32[]{:S(2)}) %collective-permute-start.16) | collective-permute-done | bytes 196640 | tf_op jit(solution)/shard_map/ppermute | solution.py:87
  115.4 1.3 %fusion.18 = bf16[128,2688]{1,0:T(8,128)(2,1)} fusion(bf16[128,2688]{1,0:T(8,128)(2,1)S(1)} %copy-done.2, bf16[128,2688]{1,0:T(8,128)(2,1)S(1)} %collective-permute-done.13, f32[128]{0:T(128)S(1)} %broadcast_multiply_fusion.2, f32[2688]{0:T(1024)S(1)} %copy-done.20, f32[128]{0:T(128)S(1)} %copy-done.35, bf16[256,2688]{1,0:T(8,128)(2,1)S(1)} %convolution_convert_fusion, ...), kind=kLoop, calls=%fused_computation.37 | loop fusion | flops 3440640 | bytes 2764292 | tf_op jit(solution)/shard_map/convert_element_type | solution.py:273
  116.7 8.5 %collective-permute-done.17 = bf16[98304]{0:T(1024)(128)(2,1)S(1)} collective-permute-done((bf16[98304]{0:T(1024)(128)(2,1)S(1)}, bf16[98304]{0:T(1024)(128)(2,1)S(1)}, u32[]{:S(2)}, u32[]{:S(2)}) %collective-permute-start.17) | collective-permute-done | bytes 196640 | tf_op jit(solution)/shard_map/ppermute | solution.py:87
  (207 shorter events, 38.0 us)
Async XLA Ops:
  0.6 38.5 %copy-start = (bf16[256,2688]{1,0:T(8,128)(2,1)S(1)}, bf16[256,2688]{1,0:T(8,128)(2,1)}, u32[]{:S(2)}) copy-start(bf16[256,2688]{1,0:T(8,128)(2,1)} %param.31) | copy-start | bytes 4128772
  3.5 3.4 %collective-permute-start = (bf16[128,2688]{1,0:T(8,128)(2,1)S(1)}, bf16[128,2688]{1,0:T(8,128)(2,1)S(1)}, u32[]{:S(2)}, u32[]{:S(2)}) collective-permute-start(bf16[128,2688]{1,0:T(8,128)(2,1)S(1)} %fusion.14), channel_id=1, source_target_pairs={{0,1},{1,0},{2,3},{3,2},{4,5},{5,4},{6,7},{7,6},{8,9},{9,8},{10,11... | collective-permute-start | bytes 2064392 | tf_op jit(solution)/shard_map/ppermute | solution.py:72
  6.9 30.1 %copy-start.41 = (f32[256]{0:T(256)}, f32[256]{0:T(256)S(1)}, u32[]{:S(2)}) copy-start(f32[256]{0:T(256)S(1)} %fusion.73) | copy-start | bytes 3076
  12.4 21.0 %collective-permute-start.4 = (bf16[272,256]{0,1:T(8,128)(2,1)S(1)}, bf16[272,256]{0,1:T(8,128)(2,1)S(1)}, u32[]{:S(2)}, u32[]{:S(2)}) collective-permute-start(bf16[272,256]{0,1:T(8,128)(2,1)S(1)} %fusion.57), channel_id=1, source_target_pairs={{0,2},{2,4},{4,6},{6,8},{8,10},{10,12},{12,14},{1,3},{3,5},{5,7},{... | collective-permute-start | bytes 417800 | tf_op jit(solution)/shard_map/ppermute | solution.py:17
  16.9 16.5 %collective-permute-start.3 = (bf16[272,256]{0,1:T(8,128)(2,1)S(1)}, bf16[272,256]{0,1:T(8,128)(2,1)S(1)}, u32[]{:S(2)}, u32[]{:S(2)}) collective-permute-start(bf16[272,256]{0,1:T(8,128)(2,1)S(1)} %fusion.57), channel_id=1, source_target_pairs={{0,4},{2,6},{4,8},{6,10},{8,12},{10,14},{1,5},{3,7},{5,9},{7,11},{... | collective-permute-start | bytes 417800 | tf_op jit(solution)/shard_map/ppermute | solution.py:17
  20.4 13.0 %collective-permute-start.2 = (bf16[272,256]{0,1:T(8,128)(2,1)S(1)}, bf16[272,256]{0,1:T(8,128)(2,1)S(1)}, u32[]{:S(2)}, u32[]{:S(2)}) collective-permute-start(bf16[272,256]{0,1:T(8,128)(2,1)S(1)} %fusion.57), channel_id=1, source_target_pairs={{0,6},{2,8},{4,10},{6,12},{8,14},{1,7},{3,9},{5,11},{7,13},{9,15},... | collective-permute-start | bytes 417800 | tf_op jit(solution)/shard_map/ppermute | solution.py:17
  24.8 8.5 %collective-permute-start.1 = (bf16[272,256]{0,1:T(8,128)(2,1)S(1)}, bf16[272,256]{0,1:T(8,128)(2,1)S(1)}, u32[]{:S(2)}, u32[]{:S(2)}) collective-permute-start(bf16[272,256]{0,1:T(8,128)(2,1)S(1)} %fusion.57), channel_id=1, source_target_pairs={{0,8},{2,10},{4,12},{6,14},{1,9},{3,11},{5,13},{7,15},{16,24},{18,... | collective-permute-start | bytes 417800 | tf_op jit(solution)/shard_map/ppermute | solution.py:17
  40.7 3.0 %collective-permute-start.5 = (bf16[128,2688]{1,0:T(8,128)(2,1)}, bf16[128,2688]{1,0:T(8,128)(2,1)}, u32[]{:S(2)}, u32[]{:S(2)}) collective-permute-start(bf16[128,2688]{1,0:T(8,128)(2,1)} %constant_dynamic-slice_fusion.3), channel_id=1, source_target_pairs={{0,1},{1,0},{2,3},{3,2},{4,5},{5,4},{6,7},{7,6},{8,9},{9,8},{10,11... | collective-permute-start | bytes 2064392 | tf_op jit(solution)/shard_map/ppermute | solution.py:65
  40.8 2.1 %collective-permute-start.6 = (bf16[128,16]{0,1:T(8,128)(2,1)S(1)}, bf16[128,16]{0,1:T(8,128)(2,1)}, u32[]{:S(2)}, u32[]{:S(2)}) collective-permute-start(bf16[128,16]{0,1:T(8,128)(2,1)S(1)} %constant_dynamic-slice_fusion.2), channel_id=1, source_target_pairs={{0,1},{1,0},{2,3},{3,2},{4,5},{5,4},{6,7},{7,6},{8,9},{9,8},{10,11... | collective-permute-start | bytes 12296 | tf_op jit(solution)/shard_map/ppermute | solution.py:65
  47.3 1.2 collective-permute-start.8
  47.5 2.3 %collective-permute-start.7 = (bf16[128,2688]{1,0:T(8,128)(2,1)S(1)}, bf16[128,2688]{1,0:T(8,128)(2,1)}, u32[]{:S(2)}, u32[]{:S(2)}) collective-permute-start(bf16[128,2688]{1,0:T(8,128)(2,1)S(1)} %get-tuple-element.30), channel_id=1, source_target_pairs={{0,1},{1,0},{2,3},{3,2},{4,5},{5,4},{6,7},{7,6},{8,9},{9,8},{10,11... | collective-permute-start | bytes 2064392 | tf_op jit(solution)/shard_map/ppermute | solution.py:72
  56.5 8.4 %collective-permute-start.9 = (bf16[256,256]{0,1:T(8,128)(2,1)S(1)}, bf16[256,256]{0,1:T(8,128)(2,1)S(1)}, u32[]{:S(2)}, u32[]{:S(2)}) collective-permute-start(bf16[256,256]{0,1:T(8,128)(2,1)S(1)} %get-tuple-element.36), channel_id=1, source_target_pairs={{2,0},{4,2},{6,4},{8,6},{10,8},{12,10},{14,12},{3,1},{5,3},{7,5},{... | collective-permute-start | bytes 393224 | tf_op jit(solution)/shard_map/ppermute | solution.py:17
  57.8 26.6 %collective-permute-start.12 = (bf16[256,256]{0,1:T(8,128)(2,1)S(1)}, bf16[256,256]{0,1:T(8,128)(2,1)S(1)}, u32[]{:S(2)}, u32[]{:S(2)}) collective-permute-start(bf16[256,256]{0,1:T(8,128)(2,1)S(1)} %get-tuple-element.37), channel_id=1, source_target_pairs={{8,0},{10,2},{12,4},{14,6},{9,1},{11,3},{13,5},{15,7},{24,16},{26,... | collective-permute-start | bytes 393224 | tf_op jit(solution)/shard_map/ppermute | solution.py:17
  59.1 25.3 %collective-permute-start.11 = (bf16[256,256]{0,1:T(8,128)(2,1)S(1)}, bf16[256,256]{0,1:T(8,128)(2,1)S(1)}, u32[]{:S(2)}, u32[]{:S(2)}) collective-permute-start(bf16[256,256]{0,1:T(8,128)(2,1)S(1)} %get-tuple-element.38), channel_id=1, source_target_pairs={{6,0},{8,2},{10,4},{12,6},{14,8},{7,1},{9,3},{11,5},{13,7},{15,9},... | collective-permute-start | bytes 393224 | tf_op jit(solution)/shard_map/ppermute | solution.py:17
  60.4 24.0 %collective-permute-start.10 = (bf16[256,256]{0,1:T(8,128)(2,1)S(1)}, bf16[256,256]{0,1:T(8,128)(2,1)S(1)}, u32[]{:S(2)}, u32[]{:S(2)}) collective-permute-start(bf16[256,256]{0,1:T(8,128)(2,1)S(1)} %get-tuple-element.39), channel_id=1, source_target_pairs={{4,0},{6,2},{8,4},{10,6},{12,8},{14,10},{5,1},{7,3},{9,5},{11,7},{... | collective-permute-start | bytes 393224 | tf_op jit(solution)/shard_map/ppermute | solution.py:17
  62.0 22.9 %copy-start.30 = (bf16[16,128]{1,0:T(8,128)(2,1)S(1)}, bf16[16,128]{1,0:T(8,128)(2,1)}, u32[]{:S(2)}) copy-start(bf16[16,128]{1,0:T(8,128)(2,1)} %param.34) | copy-start | bytes 12292
  62.0 23.0 %copy-start.32 = (bf16[16,128]{1,0:T(8,128)(2,1)S(1)}, bf16[16,128]{1,0:T(8,128)(2,1)}, u32[]{:S(2)}) copy-start(bf16[16,128]{1,0:T(8,128)(2,1)} %param.35) | copy-start | bytes 12292
  62.0 23.2 %copy-start.13 = (bf16[128,2688]{1,0:T(8,128)(2,1)S(1)}, bf16[128,2688]{1,0:T(8,128)(2,1)}, u32[]{:S(2)}) copy-start(bf16[128,2688]{1,0:T(8,128)(2,1)} %copy-done.12) | copy-start | bytes 2064388
  62.0 23.2 %copy-start.15 = (bf16[128,2688]{1,0:T(8,128)(2,1)S(1)}, bf16[128,2688]{1,0:T(8,128)(2,1)}, u32[]{:S(2)}) copy-start(bf16[128,2688]{1,0:T(8,128)(2,1)} %copy-done.14) | copy-start | bytes 2064388
  86.3 2.7 %collective-permute-start.14 = (bf16[1344,48]{0,1:T(8,128)(2,1)}, bf16[1344,48]{0,1:T(8,128)(2,1)}, u32[]{:S(2)}, u32[]{:S(2)}) collective-permute-start(bf16[1344,48]{0,1:T(8,128)(2,1)} %constant_dynamic-slice_fusion), channel_id=1, source_target_pairs={{0,1},{1,0},{2,3},{3,2},{4,5},{5,4},{6,7},{7,6},{8,9},{9,8},{10,11... | collective-permute-start | bytes 387080 | tf_op jit(solution)/shard_map/ppermute | solution.py:65
  96.1 9.8 %collective-permute-start.15 = (bf16[98304]{0:T(1024)(128)(2,1)S(1)}, bf16[98304]{0:T(1024)(128)(2,1)S(1)}, u32[]{:S(2)}, u32[]{:S(2)}) collective-permute-start(bf16[98304]{0:T(1024)(128)(2,1)S(1)} %constant_dynamic-update-slice_fusion.12), channel_id=1, source_target_pairs={{0,2},{2,0},{4,6},{6,4},{8,10},{10,8},{12,14},{14,12},{1,3},{3,1},... | collective-permute-start | bytes 589832 | tf_op jit(solution)/shard_map/ppermute | solution.py:87
  106.0 8.1 %collective-permute-start.16 = (bf16[98304]{0:T(1024)(128)(2,1)S(1)}, bf16[98304]{0:T(1024)(128)(2,1)S(1)}, u32[]{:S(2)}, u32[]{:S(2)}) collective-permute-start(bf16[98304]{0:T(1024)(128)(2,1)S(1)} %add_convert_fusion.1), channel_id=1, source_target_pairs={{0,4},{2,6},{4,0},{6,2},{8,12},{10,14},{12,8},{14,10},{1,5},{3,7},... | collective-permute-start | bytes 589832 | tf_op jit(solution)/shard_map/ppermute | solution.py:87
  109.3 5.6 %collective-permute-start.13 = (bf16[128,2688]{1,0:T(8,128)(2,1)S(1)}, bf16[128,2688]{1,0:T(8,128)(2,1)S(1)}, u32[]{:S(2)}, u32[]{:S(2)}) collective-permute-start(bf16[128,2688]{1,0:T(8,128)(2,1)S(1)} %constant_dynamic-slice_fusion.1), channel_id=1, source_target_pairs={{0,1},{1,0},{2,3},{3,2},{4,5},{5,4},{6,7},{7,6},{8,9},{9,8},{10,11... | collective-permute-start | bytes 2064392 | tf_op jit(solution)/shard_map/ppermute | solution.py:65
  114.1 11.1 %collective-permute-start.17 = (bf16[98304]{0:T(1024)(128)(2,1)S(1)}, bf16[98304]{0:T(1024)(128)(2,1)S(1)}, u32[]{:S(2)}, u32[]{:S(2)}) collective-permute-start(bf16[98304]{0:T(1024)(128)(2,1)S(1)} %add_convert_fusion), channel_id=1, source_target_pairs={{0,8},{2,10},{4,12},{6,14},{8,0},{10,2},{12,4},{14,6},{1,9},{3,11}... | collective-permute-start | bytes 589832 | tf_op jit(solution)/shard_map/ppermute | solution.py:87
  (39 other events, 280.1 us)

commit v10 on v9

--- a/solution.py
+++ b/solution.py
@@ -234,14 +234,27 @@
     )
     grad_pairs = jnp.concatenate([grad_keys, grad_values], axis=1)
     own_grads = grad_pairs[reach_shards * shard_len :]
-    for hop_index in range(1, send_count + 1):
-        own_grads = own_grads + passed_along(
-            grad_pairs[
-                (reach_shards - hop_index) * shard_len : (reach_shards - hop_index + 1) * shard_len
-            ].astype(jnp.bfloat16),
-            "ctx",
-            -hop_index,
+
+    def hop_block(hop_index):
+        first_row = (reach_shards - hop_index) * shard_len
+        return grad_pairs[first_row : first_row + shard_len]
+
+    if send_count == 4:
+        far = passed_along(
+            jnp.concatenate([hop_block(3), hop_block(4)], axis=0).astype(jnp.bfloat16), "ctx", -2
         ).astype(jnp.float32)
+        near_sum = hop_block(1) + far[:shard_len]
+        next_sum = hop_block(2) + far[shard_len:]
+        own_grads = (
+            own_grads
+            + passed_along(near_sum.astype(jnp.bfloat16), "ctx", -1).astype(jnp.float32)
+            + passed_along(next_sum.astype(jnp.bfloat16), "ctx", -2).astype(jnp.float32)
+        )
+    else:
+        for hop_index in range(1, send_count + 1):
+            own_grads = own_grads + passed_along(
+                hop_block(hop_index).astype(jnp.bfloat16), "ctx", -hop_index
+            ).astype(jnp.float32)
     query_prenorm_gradient = (
         norm_back(query_heads, query_norm_gain, grad_query)
         .reshape(shard_len, heads_here * head_dim)

time: 130 us -> 128 us (0.985)
  starting transfers between devices: 29.7 us -> 24.4 us
  waiting for transfers between devices: 46.4 us -> 49.8 us
    ppermute x3, starting transfers between devices: 8.32 us -> 4.35 us  [ctx_sum(): received = lax.ppermute(sent, 'ctx', [(i, i ^ step) for i in range(count)])]
    ppermute x8 -> x7, waiting for transfers between devices: 28.6 us -> 32.2 us  [passed_along(): lax.ppermute(value, axis, [(source, source + steps) for source in range(l...]
    ppermute x8 -> x7, starting transfers between devices: 19.7 us -> 18.4 us  [passed_along(): lax.ppermute(value, axis, [(source, source + steps) for source in range(l...]
  transfers between devices with their start and end apart: 18 -> 17, of which waited for: 8 -> 9; matrix products, arithmetic and copies ran while one was open for 10% -> 10% of each run, Pallas kernels for 0% -> 0%
where the time goes in v10:
time: 128 us; the launch traced here: 127 us
  waiting for transfers between devices  49.8 us (39%)
  starting transfers between devices  24.4 us (19%)
  matrix products  20.3 us (16%)
  local copies, waits for them, and re-layouts  17.6 us (14%)
  other arithmetic  13.1 us (10%)
  between operations  2.31 us (2%)
    ppermute x7, waiting for transfers between devices, passed_along(): lax.ppermute(value, axis, [(source, source + steps) for source in range(l...  32.2 us
    ppermute x7, starting transfers between devices, passed_along(): lax.ppermute(value, axis, [(source, source + steps) for source in range(l...  18.4 us
    ppermute x3, waiting for transfers between devices, ctx_sum(): received = lax.ppermute(sent, 'ctx', [(i, i ^ step) for i in range(count)])  15.3 us
    unnamed x107, local copies, waits for them, and re-layouts  9.45 us
    dot_general x7, matrix products, matrix_product(): return jnp.dot(first_op, second_op, preferred_element_type=jnp.float32)  5.68 us
    dot_general x7, matrix products, multiply_by_transpose(): lax.dot_general(first_op, second_op, (((1,), (1,)), ((), ())), preferred_...  4.64 us
    ppermute x3, starting transfers between devices, ctx_sum(): received = lax.ppermute(sent, 'ctx', [(i, i ^ step) for i in range(count)])  4.35 us
    dot_general x6, matrix products, transpose_multiply(): lax.dot_general(first_op, second_op, (((0,), (0,)), ((), ())), preferred_...  3.45 us
  transfers between devices with their start and end apart: 17, of which 9 were waited for; matrix products, arithmetic and copies ran while one was open for 10% of the time, Pallas kernels for 0%

profile of v10, /device:TPU:0, one launch (start us, length us, event | category | flops | bytes accessed | tf_op | source)
XLA Modules:
  0.0 127.5 jit_solution(7485435285551767286)
XLA Ops:
  0.7 1.4 %fusion.19 = f32[128]{0:T(128)S(1)} fusion(bf16[128,2688]{1,0:T(8,128)(2,1)} %param.20), kind=kLoop, calls=%fused_computation.42 | loop fusion | flops 1032064 | bytes 688640 | tf_op jit(solution)/shard_map/reduce_sum | solution.py:21
  2.1 1.4 %fusion.14 = bf16[128,2688]{1,0:T(8,128)(2,1)S(1)} fusion(bf16[128,2688]{1,0:T(8,128)(2,1)} %param.20, f32[2688]{0:T(1024)} %param.24, f32[128]{0:T(128)S(1)} %add_rsqrt_fusion.3), kind=kLoop, calls=%fused_computation.37 | loop fusion | flops 1376256 | bytes 1387520 | tf_op jit(solution)/shard_map/convert_element_type | solution.py:128
  4.8 2.1 %copy.35 = bf16[2688,48]{1,0:T(8,128)(2,1)} copy(bf16[2688,48]{0,1:T(8,128)(2,1)} %param.32) | data formatting | bytes 516096 | tf_op args[12]
  9.1 2.6 %fusion.90 = (bf16[256,560]{0,1:T(8,128)(2,1)S(1)}, f32[256,560]{0,1:T(8,128)S(1)}) fusion(bf16[2688,48]{1,0:T(8,128)(2,1)S(1)} %copy-done.16, bf16[2688,128]{1,0:T(8,128)(2,1)S(1)} %copy-done.44, bf16[2688,128]{1,0:T(8,128)(2,1)} %param.29, bf16[2688,256]{1,0:T(8,128)(2,1)S(1)} %copy-done.43, bf16[128,2688]{1,0:T(8,128)(2,1)S(1)} %get-tuple-element.37, ...), kind=kOutput, calls=%fused_computation.206 | convolution fusion | flops 785641472 | bytes 5246976 | tf_op jit(solution)/shard_map/dot_general | solution.py:33
  12.4 4.4 %collective-permute-start.4 = (bf16[272,256]{0,1:T(8,128)(2,1)S(1)}, bf16[272,256]{0,1:T(8,128)(2,1)S(1)}, u32[]{:S(2)}, u32[]{:S(2)}) collective-permute-start(bf16[272,256]{0,1:T(8,128)(2,1)S(1)} %fusion.61), channel_id=1, source_target_pairs={{0,2},{2,4},{4,6},{6,8},{8,10},{10,12},{12,14},{1,3},{3,5},{5,7},{... | collective-permute-start | bytes 417800 | tf_op jit(solution)/shard_map/ppermute | solution.py:17
  16.9 3.5 %collective-permute-start.3 = (bf16[272,256]{0,1:T(8,128)(2,1)S(1)}, bf16[272,256]{0,1:T(8,128)(2,1)S(1)}, u32[]{:S(2)}, u32[]{:S(2)}) collective-permute-start(bf16[272,256]{0,1:T(8,128)(2,1)S(1)} %fusion.61), channel_id=1, source_target_pairs={{0,4},{2,6},{4,8},{6,10},{8,12},{10,14},{1,5},{3,7},{5,9},{7,11},{... | collective-permute-start | bytes 417800 | tf_op jit(solution)/shard_map/ppermute | solution.py:17
  20.4 4.5 %collective-permute-start.2 = (bf16[272,256]{0,1:T(8,128)(2,1)S(1)}, bf16[272,256]{0,1:T(8,128)(2,1)S(1)}, u32[]{:S(2)}, u32[]{:S(2)}) collective-permute-start(bf16[272,256]{0,1:T(8,128)(2,1)S(1)} %fusion.61), channel_id=1, source_target_pairs={{0,6},{2,8},{4,10},{6,12},{8,14},{1,7},{3,9},{5,11},{7,13},{9,15},... | collective-permute-start | bytes 417800 | tf_op jit(solution)/shard_map/ppermute | solution.py:17
  24.8 1.9 %collective-permute-start.1 = (bf16[272,256]{0,1:T(8,128)(2,1)S(1)}, bf16[272,256]{0,1:T(8,128)(2,1)S(1)}, u32[]{:S(2)}, u32[]{:S(2)}) collective-permute-start(bf16[272,256]{0,1:T(8,128)(2,1)S(1)} %fusion.61), channel_id=1, source_target_pairs={{0,8},{2,10},{4,12},{6,14},{1,9},{3,11},{5,13},{7,15},{16,24},{18,... | collective-permute-start | bytes 417800 | tf_op jit(solution)/shard_map/ppermute | solution.py:17
  27.1 6.2 %collective-permute-done.1 = bf16[272,256]{0,1:T(8,128)(2,1)S(1)} collective-permute-done((bf16[272,256]{0,1:T(8,128)(2,1)S(1)}, bf16[272,256]{0,1:T(8,128)(2,1)S(1)}, u32[]{:S(2)}, u32[]{:S(2)}) %collective-permute-start.1) | collective-permute-done | bytes 139296 | tf_op jit(solution)/shard_map/ppermute | solution.py:17
  34.6 2.4 %fusion.22 = f32[2,256,1280]{1,2,0:T(8,128)} fusion(pred[256,1280]{0,1:T(8,128)(4,1)S(1)} %fusion.26, bf16[1280,256]{0,1:T(8,128)(2,1)S(1)} %maximum_dynamic-update-slice_fusion, f32[256,256]{0,1:T(8,128)S(1)} %get-tuple-element.53, f32[128]{0:T(128)S(1)} %copy-done.39, f32[256,2]{0,1:T(2,128)S(1)} %add_rsqrt_fusion), kind=kOutput, calls=%fused_computation.53 | convolution fusion | flops 169936640 | bytes 3541504 | tf_op jit(solution)/shard_map/div | solution.py:182
  37.1 2.1 %fusion.32 = bf16[128,2,256]{2,0,1:T(8,128)(2,1)S(1)} fusion(f32[2,256,1280]{1,2,0:T(8,128)} %fusion.22, bf16[1280,256]{0,1:T(8,128)(2,1)S(1)} %maximum_dynamic-update-slice_fusion, f32[256]{0:T(256)S(1)} %fusion.77), kind=kOutput, calls=%fused_computation.67 | convolution fusion | flops 168558592 | bytes 3081216 | tf_op jit(solution)/shard_map/hts,sd->thd/dot_general | solution.py:184
  41.3 1.6 %collective-permute-done.6 = bf16[128,16]{0,1:T(8,128)(2,1)} collective-permute-done((bf16[128,16]{0,1:T(8,128)(2,1)S(1)}, bf16[128,16]{0,1:T(8,128)(2,1)}, u32[]{:S(2)}, u32[]{:S(2)}) %collective-permute-start.6) | collective-permute-done | bytes 4128 | tf_op jit(solution)/shard_map/ppermute | solution.py:65
  43.7 1.7 %multiply_reduce_fusion.2 = (f32[128]{0:T(128)S(1)}, f32[128,2688]{1,0:T(8,128)S(1)}) fusion(bf16[128,16]{0,1:T(8,128)(2,1)S(1)} %add_convert_fusion.3, bf16[16,2688]{1,0:T(8,128)(2,1)S(1)} %copy-done.18, bf16[128,2688]{1,0:T(8,128)(2,1)} %collective-permute-done.5, bf16[256,2688]{1,0:T(8,128)(2,1)S(1)} %convolution_convert_fusion.1, s32[]{:T(128)S(6)} %select_n.62), kind=kOutput, calls=%fused_computation.49 | convolution fusion | flops 13418368 | bytes 2843140 | tf_op jit(solution)/shard_map/dot_general | solution.py:33
  57.8 12.8 %collective-permute-done.9 = bf16[512,256]{0,1:T(8,128)(2,1)S(1)} collective-permute-done((bf16[512,256]{0,1:T(8,128)(2,1)S(1)}, bf16[512,256]{0,1:T(8,128)(2,1)S(1)}, u32[]{:S(2)}, u32[]{:S(2)}) %collective-permute-start.9) | collective-permute-done | bytes 262176 | tf_op jit(solution)/shard_map/ppermute | solution.py:17
  72.0 1.5 %collective-permute-start.11 = (bf16[256,256]{0,1:T(8,128)(2,1)S(1)}, bf16[256,256]{0,1:T(8,128)(2,1)S(1)}, u32[]{:S(2)}, u32[]{:S(2)}) collective-permute-start(bf16[256,256]{0,1:T(8,128)(2,1)S(1)} %get-tuple-element.31), channel_id=1, source_target_pairs={{4,0},{6,2},{8,4},{10,6},{12,8},{14,10},{5,1},{7,3},{9,5},{11,7},{... | collective-permute-start | bytes 393224 | tf_op jit(solution)/shard_map/ppermute | solution.py:17
  73.6 9.2 %collective-permute-done.10 = bf16[256,256]{0,1:T(8,128)(2,1)S(1)} collective-permute-done((bf16[256,256]{0,1:T(8,128)(2,1)S(1)}, bf16[256,256]{0,1:T(8,128)(2,1)S(1)}, u32[]{:S(2)}, u32[]{:S(2)}) %collective-permute-start.10) | collective-permute-done | bytes 131104 | tf_op jit(solution)/shard_map/ppermute | solution.py:17
  82.9 4.0 %collective-permute-done.11 = bf16[256,256]{0,1:T(8,128)(2,1)S(1)} collective-permute-done((bf16[256,256]{0,1:T(8,128)(2,1)S(1)}, bf16[256,256]{0,1:T(8,128)(2,1)S(1)}, u32[]{:S(2)}, u32[]{:S(2)}) %collective-permute-start.11) | collective-permute-done | bytes 131104 | tf_op jit(solution)/shard_map/ppermute | solution.py:17
  91.4 1.7 %add_convert_fusion.2 = bf16[1344,48]{0,1:T(8,128)(2,1)} fusion(bf16[1344,48]{0,1:T(8,128)(2,1)} %collective-permute-done.13, bf16[2688,48]{0,1:T(8,128)(2,1)S(1)} %convolution_convert_fusion.2, s32[]{:T(128)S(6)} %select_n.69), kind=kLoop, calls=%fused_computation.107 | loop fusion | flops 258048 | bytes 387076 | tf_op jit(solution)/shard_map/convert.15
  98.5 3.2 %convolution_convert_fusion = bf16[256,2688]{1,0:T(8,128)(2,1)S(1)} fusion(bf16[256,560]{0,1:T(8,128)(2,1)} %copy-done.21, bf16[2688,48]{1,0:T(8,128)(2,1)S(1)} %copy-done.17, bf16[2688,128]{1,0:T(8,128)(2,1)} %param.30, bf16[2688,128]{1,0:T(8,128)(2,1)} %param.29, bf16[2688,256]{1,0:T(8,128)(2,1)} %param.28), kind=kOutput, calls=%fused_computation.1 | convolution fusion | flops 783433728 | bytes 4673536 | tf_op jit(solution)/shard_map/dot_general | solution.py:37
  101.7 4.1 %collective-permute-done.14 = bf16[98304]{0:T(1024)(128)(2,1)S(1)} collective-permute-done((bf16[98304]{0:T(1024)(128)(2,1)S(1)}, bf16[98304]{0:T(1024)(128)(2,1)S(1)}, u32[]{:S(2)}, u32[]{:S(2)}) %collective-permute-start.14) | collective-permute-done | bytes 196640 | tf_op jit(solution)/shard_map/ppermute | solution.py:87
  105.9 1.5 %collective-permute-start.15 = (bf16[98304]{0:T(1024)(128)(2,1)S(1)}, bf16[98304]{0:T(1024)(128)(2,1)S(1)}, u32[]{:S(2)}, u32[]{:S(2)}) collective-permute-start(bf16[98304]{0:T(1024)(128)(2,1)S(1)} %add_convert_fusion.1), channel_id=1, source_target_pairs={{0,4},{2,6},{4,0},{6,2},{8,12},{10,14},{12,8},{14,10},{1,5},{3,7},... | collective-permute-start | bytes 589832 | tf_op jit(solution)/shard_map/ppermute | solution.py:87
  107.5 4.9 %collective-permute-done.15 = bf16[98304]{0:T(1024)(128)(2,1)S(1)} collective-permute-done((bf16[98304]{0:T(1024)(128)(2,1)S(1)}, bf16[98304]{0:T(1024)(128)(2,1)S(1)}, u32[]{:S(2)}, u32[]{:S(2)}) %collective-permute-start.15) | collective-permute-done | bytes 196640 | tf_op jit(solution)/shard_map/ppermute | solution.py:87
  112.5 2.8 %collective-permute-start.16 = (bf16[98304]{0:T(1024)(128)(2,1)S(1)}, bf16[98304]{0:T(1024)(128)(2,1)S(1)}, u32[]{:S(2)}, u32[]{:S(2)}) collective-permute-start(bf16[98304]{0:T(1024)(128)(2,1)S(1)} %add_convert_fusion), channel_id=1, source_target_pairs={{0,8},{2,10},{4,12},{6,14},{8,0},{10,2},{12,4},{14,6},{1,9},{3,11}... | collective-permute-start | bytes 589832 | tf_op jit(solution)/shard_map/ppermute | solution.py:87
  117.2 6.3 %collective-permute-done.16 = bf16[98304]{0:T(1024)(128)(2,1)S(1)} collective-permute-done((bf16[98304]{0:T(1024)(128)(2,1)S(1)}, bf16[98304]{0:T(1024)(128)(2,1)S(1)}, u32[]{:S(2)}, u32[]{:S(2)}) %collective-permute-start.16) | collective-permute-done | bytes 196640 | tf_op jit(solution)/shard_map/ppermute | solution.py:87
  (208 shorter events, 37.4 us)
Async XLA Ops:
  0.6 38.5 %copy-start = (bf16[256,2688]{1,0:T(8,128)(2,1)S(1)}, bf16[256,2688]{1,0:T(8,128)(2,1)}, u32[]{:S(2)}) copy-start(bf16[256,2688]{1,0:T(8,128)(2,1)} %param.31) | copy-start | bytes 4128772
  3.5 3.4 %collective-permute-start = (bf16[128,2688]{1,0:T(8,128)(2,1)S(1)}, bf16[128,2688]{1,0:T(8,128)(2,1)S(1)}, u32[]{:S(2)}, u32[]{:S(2)}) collective-permute-start(bf16[128,2688]{1,0:T(8,128)(2,1)S(1)} %fusion.14), channel_id=1, source_target_pairs={{0,1},{1,0},{2,3},{3,2},{4,5},{5,4},{6,7},{7,6},{8,9},{9,8},{10,11... | collective-permute-start | bytes 2064392 | tf_op jit(solution)/shard_map/ppermute | solution.py:72
  6.9 30.1 %copy-start.41 = (f32[256]{0:T(256)}, f32[256]{0:T(256)S(1)}, u32[]{:S(2)}) copy-start(f32[256]{0:T(256)S(1)} %fusion.77) | copy-start | bytes 3076
  9.1 17.7 %copy-start.23 = (bf16[16,256]{1,0:T(8,128)(2,1)S(1)}, bf16[16,256]{1,0:T(8,128)(2,1)}, u32[]{:S(2)}) copy-start(bf16[16,256]{1,0:T(8,128)(2,1)} %param.33) | copy-start | bytes 24580
  11.8 15.3 %copy-start.33 = (bf16[256,560]{0,1:T(8,128)(2,1)}, bf16[256,560]{0,1:T(8,128)(2,1)S(1)}, u32[]{:S(2)}) copy-start(bf16[256,560]{0,1:T(8,128)(2,1)S(1)} %get-tuple-element.48) | copy-start | bytes 860164
  12.3 22.3 %copy-start.27 = (f32[256]{0:T(256)}, f32[256]{0:T(256)S(1)}, u32[]{:S(2)}) copy-start(f32[256]{0:T(256)S(1)} %add_rsqrt_fusion.1) | copy-start | bytes 3076
  12.4 22.2 %copy-start.39 = (f32[128]{0:T(128)S(1)}, f32[128]{0:T(128)}, u32[]{:S(2)}) copy-start(f32[128]{0:T(128)} %param.25) | copy-start | bytes 1540
  12.4 21.0 %collective-permute-start.4 = (bf16[272,256]{0,1:T(8,128)(2,1)S(1)}, bf16[272,256]{0,1:T(8,128)(2,1)S(1)}, u32[]{:S(2)}, u32[]{:S(2)}) collective-permute-start(bf16[272,256]{0,1:T(8,128)(2,1)S(1)} %fusion.61), channel_id=1, source_target_pairs={{0,2},{2,4},{4,6},{6,8},{8,10},{10,12},{12,14},{1,3},{3,5},{5,7},{... | collective-permute-start | bytes 417800 | tf_op jit(solution)/shard_map/ppermute | solution.py:17
  16.9 16.5 %collective-permute-start.3 = (bf16[272,256]{0,1:T(8,128)(2,1)S(1)}, bf16[272,256]{0,1:T(8,128)(2,1)S(1)}, u32[]{:S(2)}, u32[]{:S(2)}) collective-permute-start(bf16[272,256]{0,1:T(8,128)(2,1)S(1)} %fusion.61), channel_id=1, source_target_pairs={{0,4},{2,6},{4,8},{6,10},{8,12},{10,14},{1,5},{3,7},{5,9},{7,11},{... | collective-permute-start | bytes 417800 | tf_op jit(solution)/shard_map/ppermute | solution.py:17
  20.4 13.0 %collective-permute-start.2 = (bf16[272,256]{0,1:T(8,128)(2,1)S(1)}, bf16[272,256]{0,1:T(8,128)(2,1)S(1)}, u32[]{:S(2)}, u32[]{:S(2)}) collective-permute-start(bf16[272,256]{0,1:T(8,128)(2,1)S(1)} %fusion.61), channel_id=1, source_target_pairs={{0,6},{2,8},{4,10},{6,12},{8,14},{1,7},{3,9},{5,11},{7,13},{9,15},... | collective-permute-start | bytes 417800 | tf_op jit(solution)/shard_map/ppermute | solution.py:17
  24.8 8.5 %collective-permute-start.1 = (bf16[272,256]{0,1:T(8,128)(2,1)S(1)}, bf16[272,256]{0,1:T(8,128)(2,1)S(1)}, u32[]{:S(2)}, u32[]{:S(2)}) collective-permute-start(bf16[272,256]{0,1:T(8,128)(2,1)S(1)} %fusion.61), channel_id=1, source_target_pairs={{0,8},{2,10},{4,12},{6,14},{1,9},{3,11},{5,13},{7,15},{16,24},{18,... | collective-permute-start | bytes 417800 | tf_op jit(solution)/shard_map/ppermute | solution.py:17
  40.7 3.0 %collective-permute-start.5 = (bf16[128,2688]{1,0:T(8,128)(2,1)}, bf16[128,2688]{1,0:T(8,128)(2,1)}, u32[]{:S(2)}, u32[]{:S(2)}) collective-permute-start(bf16[128,2688]{1,0:T(8,128)(2,1)} %constant_dynamic-slice_fusion.3), channel_id=1, source_target_pairs={{0,1},{1,0},{2,3},{3,2},{4,5},{5,4},{6,7},{7,6},{8,9},{9,8},{10,11... | collective-permute-start | bytes 2064392 | tf_op jit(solution)/shard_map/ppermute | solution.py:65
  40.8 2.1 %collective-permute-start.6 = (bf16[128,16]{0,1:T(8,128)(2,1)S(1)}, bf16[128,16]{0,1:T(8,128)(2,1)}, u32[]{:S(2)}, u32[]{:S(2)}) collective-permute-start(bf16[128,16]{0,1:T(8,128)(2,1)S(1)} %constant_dynamic-slice_fusion.2), channel_id=1, source_target_pairs={{0,1},{1,0},{2,3},{3,2},{4,5},{5,4},{6,7},{7,6},{8,9},{9,8},{10,11... | collective-permute-start | bytes 12296 | tf_op jit(solution)/shard_map/ppermute | solution.py:65
  47.3 1.2 collective-permute-start.8
  47.5 2.3 %collective-permute-start.7 = (bf16[128,2688]{1,0:T(8,128)(2,1)S(1)}, bf16[128,2688]{1,0:T(8,128)(2,1)}, u32[]{:S(2)}, u32[]{:S(2)}) collective-permute-start(bf16[128,2688]{1,0:T(8,128)(2,1)S(1)} %get-tuple-element.32), channel_id=1, source_target_pairs={{0,1},{1,0},{2,3},{3,2},{4,5},{5,4},{6,7},{7,6},{8,9},{9,8},{10,11... | collective-permute-start | bytes 2064392 | tf_op jit(solution)/shard_map/ppermute | solution.py:72
  56.1 14.4 %collective-permute-start.9 = (bf16[512,256]{0,1:T(8,128)(2,1)S(1)}, bf16[512,256]{0,1:T(8,128)(2,1)S(1)}, u32[]{:S(2)}, u32[]{:S(2)}) collective-permute-start(bf16[512,256]{0,1:T(8,128)(2,1)S(1)} %pad_maximum_fusion.15), channel_id=1, source_target_pairs={{4,0},{6,2},{8,4},{10,6},{12,8},{14,10},{5,1},{7,3},{9,5},{11,7},{... | collective-permute-start | bytes 786440 | tf_op jit(solution)/shard_map/ppermute | solution.py:17
  70.7 12.2 %collective-permute-start.10 = (bf16[256,256]{0,1:T(8,128)(2,1)S(1)}, bf16[256,256]{0,1:T(8,128)(2,1)S(1)}, u32[]{:S(2)}, u32[]{:S(2)}) collective-permute-start(bf16[256,256]{0,1:T(8,128)(2,1)S(1)} %get-tuple-element.30), channel_id=1, source_target_pairs={{2,0},{4,2},{6,4},{8,6},{10,8},{12,10},{14,12},{3,1},{5,3},{7,5},{... | collective-permute-start | bytes 393224 | tf_op jit(solution)/shard_map/ppermute | solution.py:17
  72.0 14.9 %collective-permute-start.11 = (bf16[256,256]{0,1:T(8,128)(2,1)S(1)}, bf16[256,256]{0,1:T(8,128)(2,1)S(1)}, u32[]{:S(2)}, u32[]{:S(2)}) collective-permute-start(bf16[256,256]{0,1:T(8,128)(2,1)S(1)} %get-tuple-element.31), channel_id=1, source_target_pairs={{4,0},{6,2},{8,4},{10,6},{12,8},{14,10},{5,1},{7,3},{9,5},{11,7},{... | collective-permute-start | bytes 393224 | tf_op jit(solution)/shard_map/ppermute | solution.py:17
  73.6 14.0 %copy-start.13 = (bf16[128,2688]{1,0:T(8,128)(2,1)S(1)}, bf16[128,2688]{1,0:T(8,128)(2,1)}, u32[]{:S(2)}) copy-start(bf16[128,2688]{1,0:T(8,128)(2,1)} %copy-done.12) | copy-start | bytes 2064388
  88.7 2.7 %collective-permute-start.13 = (bf16[1344,48]{0,1:T(8,128)(2,1)}, bf16[1344,48]{0,1:T(8,128)(2,1)}, u32[]{:S(2)}, u32[]{:S(2)}) collective-permute-start(bf16[1344,48]{0,1:T(8,128)(2,1)} %constant_dynamic-slice_fusion), channel_id=1, source_target_pairs={{0,1},{1,0},{2,3},{3,2},{4,5},{5,4},{6,7},{7,6},{8,9},{9,8},{10,11... | collective-permute-start | bytes 387080 | tf_op jit(solution)/shard_map/ppermute | solution.py:65
  98.5 7.3 %collective-permute-start.14 = (bf16[98304]{0:T(1024)(128)(2,1)S(1)}, bf16[98304]{0:T(1024)(128)(2,1)S(1)}, u32[]{:S(2)}, u32[]{:S(2)}) collective-permute-start(bf16[98304]{0:T(1024)(128)(2,1)S(1)} %constant_dynamic-update-slice_fusion.12), channel_id=1, source_target_pairs={{0,2},{2,0},{4,6},{6,4},{8,10},{10,8},{12,14},{14,12},{1,3},{3,1},... | collective-permute-start | bytes 589832 | tf_op jit(solution)/shard_map/ppermute | solution.py:87
  105.9 6.6 %collective-permute-start.15 = (bf16[98304]{0:T(1024)(128)(2,1)S(1)}, bf16[98304]{0:T(1024)(128)(2,1)S(1)}, u32[]{:S(2)}, u32[]{:S(2)}) collective-permute-start(bf16[98304]{0:T(1024)(128)(2,1)S(1)} %add_convert_fusion.1), channel_id=1, source_target_pairs={{0,4},{2,6},{4,0},{6,2},{8,12},{10,14},{12,8},{14,10},{1,5},{3,7},... | collective-permute-start | bytes 589832 | tf_op jit(solution)/shard_map/ppermute | solution.py:87
  107.5 7.9 %collective-permute-start.12 = (bf16[128,2688]{1,0:T(8,128)(2,1)S(1)}, bf16[128,2688]{1,0:T(8,128)(2,1)S(1)}, u32[]{:S(2)}, u32[]{:S(2)}) collective-permute-start(bf16[128,2688]{1,0:T(8,128)(2,1)S(1)} %constant_dynamic-slice_fusion.1), channel_id=1, source_target_pairs={{0,1},{1,0},{2,3},{3,2},{4,5},{5,4},{6,7},{7,6},{8,9},{9,8},{10,11... | collective-permute-start | bytes 2064392 | tf_op jit(solution)/shard_map/ppermute | solution.py:65
  112.5 10.9 %collective-permute-start.16 = (bf16[98304]{0:T(1024)(128)(2,1)S(1)}, bf16[98304]{0:T(1024)(128)(2,1)S(1)}, u32[]{:S(2)}, u32[]{:S(2)}) collective-permute-start(bf16[98304]{0:T(1024)(128)(2,1)S(1)} %add_convert_fusion), channel_id=1, source_target_pairs={{0,8},{2,10},{4,12},{6,14},{8,0},{10,2},{12,4},{14,6},{1,9},{3,11}... | collective-permute-start | bytes 589832 | tf_op jit(solution)/shard_map/ppermute | solution.py:87
  (38 other events, 216.9 us)

commit v11 on v10

--- a/solution.py
+++ b/solution.py
@@ -159,12 +159,24 @@
     code_rows = jnp.zeros((16, local_pair.shape[1]), jnp.bfloat16)
     code_rows = code_rows.at[0, :shard_len].set(local_codes.astype(jnp.bfloat16))
     payload = jnp.concatenate([local_pair, code_rows], axis=0)
-    received = []
-    for hop_index in range(1, send_count + 1):
-        arrived = passed_along(payload, "ctx", hop_index)
-        received.append(
-            (arrived[:shard_len], arrived[shard_len, :shard_len].astype(jnp.int32))
-        )
+    payload_rows = payload.shape[0]
+    if send_count == 4:
+        two_back = passed_along(payload, "ctx", 2)
+        odd_back = passed_along(jnp.concatenate([payload, two_back], axis=0), "ctx", 1)
+        arrivals = [
+            odd_back[:payload_rows],
+            two_back,
+            odd_back[payload_rows:],
+            passed_along(two_back, "ctx", 2),
+        ]
+    else:
+        arrivals = [
+            passed_along(payload, "ctx", hop_index) for hop_index in range(1, send_count + 1)
+        ]
+    received = [
+        (arrived[:shard_len], arrived[shard_len, :shard_len].astype(jnp.int32))
+        for arrived in arrivals
+    ]
     missing = reach_shards - send_count
     blank_pair = jnp.zeros_like(local_pair)
     blank_codes = jnp.zeros_like(local_codes)

time: 128 us -> 124 us (0.969)
  waiting for transfers between devices: 49.8 us -> 45.6 us
    ppermute x7 -> x6, waiting for transfers between devices: 32.2 us -> 29 us  [passed_along(): lax.ppermute(value, axis, [(source, source + steps) for source in range(l...]
    ppermute x7 -> x6, starting transfers between devices: 18.4 us -> 16.4 us  [passed_along(): lax.ppermute(value, axis, [(source, source + steps) for source in range(l...]
  transfers between devices with their start and end apart: 17 -> 16, of which waited for: 9 -> 11; matrix products, arithmetic and copies ran while one was open for 10% -> 10% of each run, Pallas kernels for 0% -> 0%
where the time goes in v11:
time: 124 us; the launch traced here: 123 us
  waiting for transfers between devices  45.6 us (37%)
  starting transfers between devices  23.3 us (19%)
  matrix products  20.3 us (16%)
  local copies, waits for them, and re-layouts  18 us (15%)
  other arithmetic  13.2 us (11%)
  between operations  2.29 us (2%)
    ppermute x6, waiting for transfers between devices, passed_along(): lax.ppermute(value, axis, [(source, source + steps) for source in range(l...  29 us
    ppermute x6, starting transfers between devices, passed_along(): lax.ppermute(value, axis, [(source, source + steps) for source in range(l...  16.4 us
    ppermute x3, waiting for transfers between devices, ctx_sum(): received = lax.ppermute(sent, 'ctx', [(i, i ^ step) for i in range(count)])  14.3 us
    unnamed x107, local copies, waits for them, and re-layouts  9.9 us
    dot_general x7, matrix products, matrix_product(): return jnp.dot(first_op, second_op, preferred_element_type=jnp.float32)  5.7 us
    ppermute x3, starting transfers between devices, ctx_sum(): received = lax.ppermute(sent, 'ctx', [(i, i ^ step) for i in range(count)])  5.28 us
    dot_general x7, matrix products, multiply_by_transpose(): lax.dot_general(first_op, second_op, (((1,), (1,)), ((), ())), preferred_...  4.63 us
    dot_general x6, matrix products, transpose_multiply(): lax.dot_general(first_op, second_op, (((0,), (0,)), ((), ())), preferred_...  3.45 us
  transfers between devices with their start and end apart: 16, of which 11 were waited for; matrix products, arithmetic and copies ran while one was open for 10% of the time, Pallas kernels for 0%

profile of v11, /device:TPU:0, one launch (start us, length us, event | category | flops | bytes accessed | tf_op | source)
XLA Modules:
  0.0 122.7 jit_solution(690391263005086562)
XLA Ops:
  0.7 1.4 %fusion.19 = f32[128]{0:T(128)S(1)} fusion(bf16[128,2688]{1,0:T(8,128)(2,1)} %param.20), kind=kLoop, calls=%fused_computation.42 | loop fusion | flops 1032064 | bytes 688640 | tf_op jit(solution)/shard_map/reduce_sum | solution.py:21
  2.1 1.4 %fusion.14 = bf16[128,2688]{1,0:T(8,128)(2,1)S(1)} fusion(bf16[128,2688]{1,0:T(8,128)(2,1)} %param.20, f32[2688]{0:T(1024)} %param.24, f32[128]{0:T(128)S(1)} %add_rsqrt_fusion.3), kind=kLoop, calls=%fused_computation.37 | loop fusion | flops 1376256 | bytes 1387520 | tf_op jit(solution)/shard_map/convert_element_type | solution.py:128
  4.8 2.1 %copy.35 = bf16[2688,48]{1,0:T(8,128)(2,1)} copy(bf16[2688,48]{0,1:T(8,128)(2,1)} %param.32) | data formatting | bytes 516096 | tf_op args[12]
  9.2 2.6 %fusion.88 = (bf16[256,560]{0,1:T(8,128)(2,1)S(1)}, f32[256,560]{0,1:T(8,128)S(1)}) fusion(bf16[2688,48]{1,0:T(8,128)(2,1)S(1)} %copy-done.16, bf16[2688,128]{1,0:T(8,128)(2,1)S(1)} %copy-done.44, bf16[2688,128]{1,0:T(8,128)(2,1)} %param.29, bf16[2688,256]{1,0:T(8,128)(2,1)S(1)} %copy-done.43, bf16[128,2688]{1,0:T(8,128)(2,1)S(1)} %get-tuple-element.39, ...), kind=kOutput, calls=%fused_computation.205 | convolution fusion | flops 785641472 | bytes 5246976 | tf_op jit(solution)/shard_map/dot_general | solution.py:33
  13.1 4.5 %collective-permute-start.1 = (bf16[272,256]{0,1:T(8,128)(2,1)S(1)}, bf16[272,256]{0,1:T(8,128)(2,1)S(1)}, u32[]{:S(2)}, u32[]{:S(2)}) collective-permute-start(bf16[272,256]{0,1:T(8,128)(2,1)S(1)} %pad_maximum_fusion.17), channel_id=1, source_target_pairs={{0,4},{2,6},{4,8},{6,10},{8,12},{10,14},{1,5},{3,7},{5,9},{7,11},{... | collective-permute-start | bytes 417800 | tf_op jit(solution)/shard_map/ppermute | solution.py:17
  17.6 4.8 %collective-permute-done.1 = bf16[272,256]{0,1:T(8,128)(2,1)S(1)} collective-permute-done((bf16[272,256]{0,1:T(8,128)(2,1)S(1)}, bf16[272,256]{0,1:T(8,128)(2,1)S(1)}, u32[]{:S(2)}, u32[]{:S(2)}) %collective-permute-start.1) | collective-permute-done | bytes 139296 | tf_op jit(solution)/shard_map/ppermute | solution.py:17
  22.4 4.4 %collective-permute-start.2 = (bf16[272,256]{0,1:T(8,128)(2,1)S(1)}, bf16[272,256]{0,1:T(8,128)(2,1)S(1)}, u32[]{:S(2)}, u32[]{:S(2)}) collective-permute-start(bf16[272,256]{0,1:T(8,128)(2,1)S(1)} %collective-permute-done.1), channel_id=1, source_target_pairs={{0,4},{2,6},{4,8},{6,10},{8,12},{10,14},{1,5},{3,7},{5,9},{7,11},{... | collective-permute-start | bytes 417800 | tf_op jit(solution)/shard_map/ppermute | solution.py:17
  26.9 3.4 %collective-permute-start.3 = (bf16[544,256]{0,1:T(8,128)(2,1)S(1)}, bf16[544,256]{0,1:T(8,128)(2,1)S(1)}, u32[]{:S(2)}, u32[]{:S(2)}) collective-permute-start(bf16[544,256]{0,1:T(8,128)(2,1)S(1)} %pad_maximum_fusion.15), channel_id=1, source_target_pairs={{0,2},{2,4},{4,6},{6,8},{8,10},{10,12},{12,14},{1,3},{3,5},{5,7},{... | collective-permute-start | bytes 835592 | tf_op jit(solution)/shard_map/ppermute | solution.py:17
  30.9 5.9 %collective-permute-done.3 = bf16[544,256]{0,1:T(8,128)(2,1)S(1)} collective-permute-done((bf16[544,256]{0,1:T(8,128)(2,1)S(1)}, bf16[544,256]{0,1:T(8,128)(2,1)S(1)}, u32[]{:S(2)}, u32[]{:S(2)}) %collective-permute-start.3) | collective-permute-done | bytes 278560 | tf_op jit(solution)/shard_map/ppermute | solution.py:17
  37.9 2.4 %fusion.22 = f32[2,256,1280]{1,2,0:T(8,128)} fusion(pred[256,1280]{0,1:T(8,128)(4,1)S(1)} %fusion.26, bf16[1280,256]{0,1:T(8,128)(2,1)S(1)} %maximum_dynamic-update-slice_fusion, f32[256,256]{0,1:T(8,128)S(1)} %get-tuple-element.55, f32[128]{0:T(128)S(1)} %copy-done.39, f32[256,2]{0,1:T(2,128)S(1)} %add_rsqrt_fusion), kind=kOutput, calls=%fused_computation.53 | convolution fusion | flops 169936640 | bytes 3541504 | tf_op jit(solution)/shard_map/div | solution.py:194
  40.3 2.1 %fusion.32 = bf16[128,2,256]{2,0,1:T(8,128)(2,1)S(1)} fusion(f32[2,256,1280]{1,2,0:T(8,128)} %fusion.22, bf16[1280,256]{0,1:T(8,128)(2,1)S(1)} %maximum_dynamic-update-slice_fusion, f32[256]{0:T(256)S(1)} %fusion.75), kind=kOutput, calls=%fused_computation.67 | convolution fusion | flops 168558592 | bytes 3081216 | tf_op jit(solution)/shard_map/hts,sd->thd/dot_general | solution.py:196
  44.6 1.6 %collective-permute-done.5 = bf16[128,16]{0,1:T(8,128)(2,1)} collective-permute-done((bf16[128,16]{0,1:T(8,128)(2,1)S(1)}, bf16[128,16]{0,1:T(8,128)(2,1)}, u32[]{:S(2)}, u32[]{:S(2)}) %collective-permute-start.5) | collective-permute-done | bytes 4128 | tf_op jit(solution)/shard_map/ppermute | solution.py:65
  46.9 1.7 %multiply_reduce_fusion.2 = (f32[128]{0:T(128)S(1)}, f32[128,2688]{1,0:T(8,128)S(1)}) fusion(bf16[128,16]{0,1:T(8,128)(2,1)S(1)} %add_convert_fusion.3, bf16[16,2688]{1,0:T(8,128)(2,1)S(1)} %copy-done.18, bf16[128,2688]{1,0:T(8,128)(2,1)} %collective-permute-done.4, bf16[256,2688]{1,0:T(8,128)(2,1)S(1)} %convolution_convert_fusion.1, s32[]{:T(128)S(6)} %select_n.62), kind=kOutput, calls=%fused_computation.49 | convolution fusion | flops 13418368 | bytes 2843140 | tf_op jit(solution)/shard_map/dot_general | solution.py:33
  61.0 11.4 %collective-permute-done.8 = bf16[512,256]{0,1:T(8,128)(2,1)S(1)} collective-permute-done((bf16[512,256]{0,1:T(8,128)(2,1)S(1)}, bf16[512,256]{0,1:T(8,128)(2,1)S(1)}, u32[]{:S(2)}, u32[]{:S(2)}) %collective-permute-start.8) | collective-permute-done | bytes 262176 | tf_op jit(solution)/shard_map/ppermute | solution.py:17
  73.9 1.5 %collective-permute-start.10 = (bf16[256,256]{0,1:T(8,128)(2,1)S(1)}, bf16[256,256]{0,1:T(8,128)(2,1)S(1)}, u32[]{:S(2)}, u32[]{:S(2)}) collective-permute-start(bf16[256,256]{0,1:T(8,128)(2,1)S(1)} %get-tuple-element.33), channel_id=1, source_target_pairs={{4,0},{6,2},{8,4},{10,6},{12,8},{14,10},{5,1},{7,3},{9,5},{11,7},{... | collective-permute-start | bytes 393224 | tf_op jit(solution)/shard_map/ppermute | solution.py:17
  75.5 4.2 %collective-permute-done.9 = bf16[256,256]{0,1:T(8,128)(2,1)S(1)} collective-permute-done((bf16[256,256]{0,1:T(8,128)(2,1)S(1)}, bf16[256,256]{0,1:T(8,128)(2,1)S(1)}, u32[]{:S(2)}, u32[]{:S(2)}) %collective-permute-start.9) | collective-permute-done | bytes 131104 | tf_op jit(solution)/shard_map/ppermute | solution.py:17
  79.7 2.5 %collective-permute-done.10 = bf16[256,256]{0,1:T(8,128)(2,1)S(1)} collective-permute-done((bf16[256,256]{0,1:T(8,128)(2,1)S(1)}, bf16[256,256]{0,1:T(8,128)(2,1)S(1)}, u32[]{:S(2)}, u32[]{:S(2)}) %collective-permute-start.10) | collective-permute-done | bytes 131104 | tf_op jit(solution)/shard_map/ppermute | solution.py:17
  86.7 1.7 %add_convert_fusion.2 = bf16[1344,48]{0,1:T(8,128)(2,1)} fusion(bf16[1344,48]{0,1:T(8,128)(2,1)} %collective-permute-done.12, bf16[2688,48]{0,1:T(8,128)(2,1)S(1)} %convolution_convert_fusion.2, s32[]{:T(128)S(6)} %select_n.69), kind=kLoop, calls=%fused_computation.106 | loop fusion | flops 258048 | bytes 387076 | tf_op jit(solution)/shard_map/convert.15
  95.1 3.2 %convolution_convert_fusion = bf16[256,2688]{1,0:T(8,128)(2,1)S(1)} fusion(bf16[256,560]{0,1:T(8,128)(2,1)} %copy-done.21, bf16[2688,48]{1,0:T(8,128)(2,1)S(1)} %copy-done.17, bf16[2688,128]{1,0:T(8,128)(2,1)} %param.30, bf16[2688,128]{1,0:T(8,128)(2,1)} %param.29, bf16[2688,256]{1,0:T(8,128)(2,1)} %param.28), kind=kOutput, calls=%fused_computation.1 | convolution fusion | flops 783433728 | bytes 4673536 | tf_op jit(solution)/shard_map/dot_general | solution.py:37
  98.3 2.9 %collective-permute-done.13 = bf16[98304]{0:T(1024)(128)(2,1)S(1)} collective-permute-done((bf16[98304]{0:T(1024)(128)(2,1)S(1)}, bf16[98304]{0:T(1024)(128)(2,1)S(1)}, u32[]{:S(2)}, u32[]{:S(2)}) %collective-permute-start.13) | collective-permute-done | bytes 196640 | tf_op jit(solution)/shard_map/ppermute | solution.py:87
  101.2 1.7 %collective-permute-start.14 = (bf16[98304]{0:T(1024)(128)(2,1)S(1)}, bf16[98304]{0:T(1024)(128)(2,1)S(1)}, u32[]{:S(2)}, u32[]{:S(2)}) collective-permute-start(bf16[98304]{0:T(1024)(128)(2,1)S(1)} %add_convert_fusion.1), channel_id=1, source_target_pairs={{0,4},{2,6},{4,0},{6,2},{8,12},{10,14},{12,8},{14,10},{1,5},{3,7},... | collective-permute-start | bytes 589832 | tf_op jit(solution)/shard_map/ppermute | solution.py:87
  103.0 4.8 %collective-permute-done.14 = bf16[98304]{0:T(1024)(128)(2,1)S(1)} collective-permute-done((bf16[98304]{0:T(1024)(128)(2,1)S(1)}, bf16[98304]{0:T(1024)(128)(2,1)S(1)}, u32[]{:S(2)}, u32[]{:S(2)}) %collective-permute-start.14) | collective-permute-done | bytes 196640 | tf_op jit(solution)/shard_map/ppermute | solution.py:87
  107.9 2.5 %collective-permute-start.15 = (bf16[98304]{0:T(1024)(128)(2,1)S(1)}, bf16[98304]{0:T(1024)(128)(2,1)S(1)}, u32[]{:S(2)}, u32[]{:S(2)}) collective-permute-start(bf16[98304]{0:T(1024)(128)(2,1)S(1)} %add_convert_fusion), channel_id=1, source_target_pairs={{0,8},{2,10},{4,12},{6,14},{8,0},{10,2},{12,4},{14,6},{1,9},{3,11}... | collective-permute-start | bytes 589832 | tf_op jit(solution)/shard_map/ppermute | solution.py:87
  112.2 6.5 %collective-permute-done.15 = bf16[98304]{0:T(1024)(128)(2,1)S(1)} collective-permute-done((bf16[98304]{0:T(1024)(128)(2,1)S(1)}, bf16[98304]{0:T(1024)(128)(2,1)S(1)}, u32[]{:S(2)}, u32[]{:S(2)}) %collective-permute-start.15) | collective-permute-done | bytes 196640 | tf_op jit(solution)/shard_map/ppermute | solution.py:87
  (207 shorter events, 39.4 us)
Async XLA Ops:
  0.6 41.8 %copy-start = (bf16[256,2688]{1,0:T(8,128)(2,1)S(1)}, bf16[256,2688]{1,0:T(8,128)(2,1)}, u32[]{:S(2)}) copy-start(bf16[256,2688]{1,0:T(8,128)(2,1)} %param.31) | copy-start | bytes 4128772
  3.5 3.5 %collective-permute-start = (bf16[128,2688]{1,0:T(8,128)(2,1)S(1)}, bf16[128,2688]{1,0:T(8,128)(2,1)S(1)}, u32[]{:S(2)}, u32[]{:S(2)}) collective-permute-start(bf16[128,2688]{1,0:T(8,128)(2,1)S(1)} %fusion.14), channel_id=1, source_target_pairs={{0,1},{1,0},{2,3},{3,2},{4,5},{5,4},{6,7},{7,6},{8,9},{9,8},{10,11... | collective-permute-start | bytes 2064392 | tf_op jit(solution)/shard_map/ppermute | solution.py:72
  6.9 33.4 %copy-start.41 = (f32[256]{0:T(256)}, f32[256]{0:T(256)S(1)}, u32[]{:S(2)}) copy-start(f32[256]{0:T(256)S(1)} %fusion.75) | copy-start | bytes 3076
  12.6 25.3 %copy-start.3 = (f32[256,256]{0,1:T(8,128)}, f32[256,256]{0,1:T(8,128)S(1)}, u32[]{:S(2)}) copy-start(f32[256,256]{0,1:T(8,128)S(1)} %get-tuple-element.55) | copy-start | bytes 786436
  12.6 18.3 %copy-start.27 = (f32[256]{0:T(256)}, f32[256]{0:T(256)S(1)}, u32[]{:S(2)}) copy-start(f32[256]{0:T(256)S(1)} %add_rsqrt_fusion.1) | copy-start | bytes 3076
  13.1 24.8 %copy-start.39 = (f32[128]{0:T(128)S(1)}, f32[128]{0:T(128)}, u32[]{:S(2)}) copy-start(f32[128]{0:T(128)} %param.25) | copy-start | bytes 1540
  13.1 9.3 %collective-permute-start.1 = (bf16[272,256]{0,1:T(8,128)(2,1)S(1)}, bf16[272,256]{0,1:T(8,128)(2,1)S(1)}, u32[]{:S(2)}, u32[]{:S(2)}) collective-permute-start(bf16[272,256]{0,1:T(8,128)(2,1)S(1)} %pad_maximum_fusion.17), channel_id=1, source_target_pairs={{0,4},{2,6},{4,8},{6,10},{8,12},{10,14},{1,5},{3,7},{5,9},{7,11},{... | collective-permute-start | bytes 417800 | tf_op jit(solution)/shard_map/ppermute | solution.py:17
  17.6 22.7 %copy-start.25 = (f32[256,2]{0,1:T(2,128)}, f32[256,2]{0,1:T(2,128)S(1)}, u32[]{:S(2)}) copy-start(f32[256,2]{0,1:T(2,128)S(1)} %add_rsqrt_fusion) | copy-start | bytes 6148
  22.4 8.4 %collective-permute-start.2 = (bf16[272,256]{0,1:T(8,128)(2,1)S(1)}, bf16[272,256]{0,1:T(8,128)(2,1)S(1)}, u32[]{:S(2)}, u32[]{:S(2)}) collective-permute-start(bf16[272,256]{0,1:T(8,128)(2,1)S(1)} %collective-permute-done.1), channel_id=1, source_target_pairs={{0,4},{2,6},{4,8},{6,10},{8,12},{10,14},{1,5},{3,7},{5,9},{7,11},{... | collective-permute-start | bytes 417800 | tf_op jit(solution)/shard_map/ppermute | solution.py:17
  26.9 9.9 %collective-permute-start.3 = (bf16[544,256]{0,1:T(8,128)(2,1)S(1)}, bf16[544,256]{0,1:T(8,128)(2,1)S(1)}, u32[]{:S(2)}, u32[]{:S(2)}) collective-permute-start(bf16[544,256]{0,1:T(8,128)(2,1)S(1)} %pad_maximum_fusion.15), channel_id=1, source_target_pairs={{0,2},{2,4},{4,6},{6,8},{8,10},{10,12},{12,14},{1,3},{3,5},{5,7},{... | collective-permute-start | bytes 835592 | tf_op jit(solution)/shard_map/ppermute | solution.py:17
  43.9 3.0 %collective-permute-start.4 = (bf16[128,2688]{1,0:T(8,128)(2,1)}, bf16[128,2688]{1,0:T(8,128)(2,1)}, u32[]{:S(2)}, u32[]{:S(2)}) collective-permute-start(bf16[128,2688]{1,0:T(8,128)(2,1)} %constant_dynamic-slice_fusion.3), channel_id=1, source_target_pairs={{0,1},{1,0},{2,3},{3,2},{4,5},{5,4},{6,7},{7,6},{8,9},{9,8},{10,11... | collective-permute-start | bytes 2064392 | tf_op jit(solution)/shard_map/ppermute | solution.py:65
  44.1 2.1 %collective-permute-start.5 = (bf16[128,16]{0,1:T(8,128)(2,1)S(1)}, bf16[128,16]{0,1:T(8,128)(2,1)}, u32[]{:S(2)}, u32[]{:S(2)}) collective-permute-start(bf16[128,16]{0,1:T(8,128)(2,1)S(1)} %constant_dynamic-slice_fusion.2), channel_id=1, source_target_pairs={{0,1},{1,0},{2,3},{3,2},{4,5},{5,4},{6,7},{7,6},{8,9},{9,8},{10,11... | collective-permute-start | bytes 12296 | tf_op jit(solution)/shard_map/ppermute | solution.py:65
  50.5 1.2 %collective-permute-start.7 = (bf16[128,32]{0,1:T(8,128)(2,1)S(1)}, bf16[128,32]{0,1:T(8,128)(2,1)S(1)}, u32[]{:S(2)}, u32[]{:S(2)}) collective-permute-start(bf16[128,32]{0,1:T(8,128)(2,1)S(1)} %pad_maximum_fusion.20), channel_id=1, source_target_pairs={{0,1},{1,0},{2,3},{3,2},{4,5},{5,4},{6,7},{7,6},{8,9},{9,8},{10,11... | collective-permute-start | bytes 24584 | tf_op jit(solution)/shard_map/ppermute | solution.py:72
  50.7 2.3 %collective-permute-start.6 = (bf16[128,2688]{1,0:T(8,128)(2,1)S(1)}, bf16[128,2688]{1,0:T(8,128)(2,1)}, u32[]{:S(2)}, u32[]{:S(2)}) collective-permute-start(bf16[128,2688]{1,0:T(8,128)(2,1)S(1)} %get-tuple-element.34), channel_id=1, source_target_pairs={{0,1},{1,0},{2,3},{3,2},{4,5},{5,4},{6,7},{7,6},{8,9},{9,8},{10,11... | collective-permute-start | bytes 2064392 | tf_op jit(solution)/shard_map/ppermute | solution.py:72
  59.4 13.0 %collective-permute-start.8 = (bf16[512,256]{0,1:T(8,128)(2,1)S(1)}, bf16[512,256]{0,1:T(8,128)(2,1)S(1)}, u32[]{:S(2)}, u32[]{:S(2)}) collective-permute-start(bf16[512,256]{0,1:T(8,128)(2,1)S(1)} %pad_maximum_fusion.16), channel_id=1, source_target_pairs={{4,0},{6,2},{8,4},{10,6},{12,8},{14,10},{5,1},{7,3},{9,5},{11,7},{... | collective-permute-start | bytes 786440 | tf_op jit(solution)/shard_map/ppermute | solution.py:17
  72.6 7.1 %collective-permute-start.9 = (bf16[256,256]{0,1:T(8,128)(2,1)S(1)}, bf16[256,256]{0,1:T(8,128)(2,1)S(1)}, u32[]{:S(2)}, u32[]{:S(2)}) collective-permute-start(bf16[256,256]{0,1:T(8,128)(2,1)S(1)} %get-tuple-element.32), channel_id=1, source_target_pairs={{2,0},{4,2},{6,4},{8,6},{10,8},{12,10},{14,12},{3,1},{5,3},{7,5},{... | collective-permute-start | bytes 393224 | tf_op jit(solution)/shard_map/ppermute | solution.py:17
  73.9 8.3 %collective-permute-start.10 = (bf16[256,256]{0,1:T(8,128)(2,1)S(1)}, bf16[256,256]{0,1:T(8,128)(2,1)S(1)}, u32[]{:S(2)}, u32[]{:S(2)}) collective-permute-start(bf16[256,256]{0,1:T(8,128)(2,1)S(1)} %get-tuple-element.33), channel_id=1, source_target_pairs={{4,0},{6,2},{8,4},{10,6},{12,8},{14,10},{5,1},{7,3},{9,5},{11,7},{... | collective-permute-start | bytes 393224 | tf_op jit(solution)/shard_map/ppermute | solution.py:17
  84.1 2.7 %collective-permute-start.12 = (bf16[1344,48]{0,1:T(8,128)(2,1)}, bf16[1344,48]{0,1:T(8,128)(2,1)}, u32[]{:S(2)}, u32[]{:S(2)}) collective-permute-start(bf16[1344,48]{0,1:T(8,128)(2,1)} %constant_dynamic-slice_fusion), channel_id=1, source_target_pairs={{0,1},{1,0},{2,3},{3,2},{4,5},{5,4},{6,7},{7,6},{8,9},{9,8},{10,11... | collective-permute-start | bytes 387080 | tf_op jit(solution)/shard_map/ppermute | solution.py:65
  93.9 7.3 %collective-permute-start.13 = (bf16[98304]{0:T(1024)(128)(2,1)S(1)}, bf16[98304]{0:T(1024)(128)(2,1)S(1)}, u32[]{:S(2)}, u32[]{:S(2)}) collective-permute-start(bf16[98304]{0:T(1024)(128)(2,1)S(1)} %constant_dynamic-update-slice_fusion.12), channel_id=1, source_target_pairs={{0,2},{2,0},{4,6},{6,4},{8,10},{10,8},{12,14},{14,12},{1,3},{3,1},... | collective-permute-start | bytes 589832 | tf_op jit(solution)/shard_map/ppermute | solution.py:87
  98.2 12.1 %copy-start.20 = (f32[2688]{0:T(1024)S(1)}, f32[2688]{0:T(1024)}, u32[]{:S(2)}) copy-start(f32[2688]{0:T(1024)} %param.24) | copy-start | bytes 32260
  98.2 12.1 %copy-start.35 = (f32[128]{0:T(128)S(1)}, f32[128]{0:T(128)}, u32[]{:S(2)}) copy-start(f32[128]{0:T(128)} %copy-done.34) | copy-start | bytes 1540
  101.2 6.6 %collective-permute-start.14 = (bf16[98304]{0:T(1024)(128)(2,1)S(1)}, bf16[98304]{0:T(1024)(128)(2,1)S(1)}, u32[]{:S(2)}, u32[]{:S(2)}) collective-permute-start(bf16[98304]{0:T(1024)(128)(2,1)S(1)} %add_convert_fusion.1), channel_id=1, source_target_pairs={{0,4},{2,6},{4,0},{6,2},{8,12},{10,14},{12,8},{14,10},{1,5},{3,7},... | collective-permute-start | bytes 589832 | tf_op jit(solution)/shard_map/ppermute | solution.py:87
  102.9 7.4 %collective-permute-start.11 = (bf16[128,2688]{1,0:T(8,128)(2,1)S(1)}, bf16[128,2688]{1,0:T(8,128)(2,1)S(1)}, u32[]{:S(2)}, u32[]{:S(2)}) collective-permute-start(bf16[128,2688]{1,0:T(8,128)(2,1)S(1)} %constant_dynamic-slice_fusion.1), channel_id=1, source_target_pairs={{0,1},{1,0},{2,3},{3,2},{4,5},{5,4},{6,7},{7,6},{8,9},{9,8},{10,11... | collective-permute-start | bytes 2064392 | tf_op jit(solution)/shard_map/ppermute | solution.py:65
  107.9 10.8 %collective-permute-start.15 = (bf16[98304]{0:T(1024)(128)(2,1)S(1)}, bf16[98304]{0:T(1024)(128)(2,1)S(1)}, u32[]{:S(2)}, u32[]{:S(2)}) collective-permute-start(bf16[98304]{0:T(1024)(128)(2,1)S(1)} %add_convert_fusion), channel_id=1, source_target_pairs={{0,8},{2,10},{4,12},{6,14},{8,0},{10,2},{12,4},{14,6},{1,9},{3,11}... | collective-permute-start | bytes 589832 | tf_op jit(solution)/shard_map/ppermute | solution.py:87
  (37 other events, 131.5 us)

commit v12 on v11

--- a/solution.py
+++ b/solution.py
@@ -192,7 +192,7 @@
     )
     weights = jnp.where(allowed[None], jnp.exp(scores), 0.0)
     attn_probs = weights / jnp.sum(weights, axis=-1, keepdims=True)
-    probs_cast = attn_probs.astype(jnp.bfloat16)
+    probs_cast = lax.optimization_barrier(attn_probs.astype(jnp.bfloat16))
     attention_result = jnp.einsum(
         "hts,sd->thd", probs_cast, values_all, preferred_element_type=jnp.float32
     )

time: 124 us -> 129 us (1.040)
  matrix products: 20.3 us -> 23.8 us
  local copies, waits for them, and re-layouts: 18 us -> 20.2 us
  waiting for transfers between devices: 45.6 us -> 44 us
  other arithmetic: 13.2 us -> 14.6 us
    unnamed x107 -> x105, local copies, waits for them, and re-layouts: 9.9 us -> 12 us
    ppermute x6, waiting for transfers between devices: 29 us -> 27.4 us  [passed_along(): lax.ppermute(value, axis, [(source, source + steps) for source in range(l...]
    div x1, matrix products: 2.44 us -> 3.73 us  [on_device(): attn_probs = weights / jnp.sum(weights, axis=-1, keepdims=True)]
  transfers between devices with their start and end apart: 16 -> 16, of which waited for: 11 -> 11; matrix products, arithmetic and copies ran while one was open for 10% -> 11% of each run, Pallas kernels for 0% -> 0%
where the time goes in v12:
time: 129 us; the launch traced here: 128 us
  waiting for transfers between devices  44 us (34%)
  matrix products  23.8 us (18%)
  starting transfers between devices  23.3 us (18%)
  local copies, waits for them, and re-layouts  20.2 us (16%)
  other arithmetic  14.6 us (11%)
  between operations  2.19 us (2%)
    ppermute x6, waiting for transfers between devices, passed_along(): lax.ppermute(value, axis, [(source, source + steps) for source in range(l...  27.4 us
    ppermute x6, starting transfers between devices, passed_along(): lax.ppermute(value, axis, [(source, source + steps) for source in range(l...  16.4 us
    ppermute x3, waiting for transfers between devices, ctx_sum(): received = lax.ppermute(sent, 'ctx', [(i, i ^ step) for i in range(count)])  14.3 us
    unnamed x105, local copies, waits for them, and re-layouts  12 us
    dot_general x7, matrix products, matrix_product(): return jnp.dot(first_op, second_op, preferred_element_type=jnp.float32)  6.34 us
    ppermute x3, starting transfers between devices, ctx_sum(): received = lax.ppermute(sent, 'ctx', [(i, i ^ step) for i in range(count)])  5.23 us
    dot_general x7, matrix products, multiply_by_transpose(): lax.dot_general(first_op, second_op, (((1,), (1,)), ((), ())), preferred_...  4.64 us
    div x1, matrix products, on_device(): attn_probs = weights / jnp.sum(weights, axis=-1, keepdims=True)  3.73 us
  transfers between devices with their start and end apart: 16, of which 11 were waited for; matrix products, arithmetic and copies ran while one was open for 11% of the time, Pallas kernels for 0%

profile of v12, /device:TPU:0, one launch (start us, length us, event | category | flops | bytes accessed | tf_op | source)
XLA Modules:
  0.0 128.0 jit_solution(14475597463501181358)
XLA Ops:
  0.7 1.4 %fusion.19 = f32[128]{0:T(128)S(1)} fusion(bf16[128,2688]{1,0:T(8,128)(2,1)} %param.20), kind=kLoop, calls=%fused_computation.42 | loop fusion | flops 1032064 | bytes 688640 | tf_op jit(solution)/shard_map/reduce_sum | solution.py:21
  4.8 2.1 %copy.35 = bf16[2688,48]{1,0:T(8,128)(2,1)} copy(bf16[2688,48]{0,1:T(8,128)(2,1)} %param.32) | data formatting | bytes 516096 | tf_op args[12]
  9.2 2.6 %fusion.86 = (bf16[256,560]{0,1:T(8,128)(2,1)S(1)}, f32[256,560]{0,1:T(8,128)S(1)}) fusion(bf16[2688,48]{1,0:T(8,128)(2,1)S(1)} %copy-done.15, bf16[2688,128]{1,0:T(8,128)(2,1)S(1)} %copy-done.43, bf16[2688,128]{1,0:T(8,128)(2,1)} %param.29, bf16[2688,256]{1,0:T(8,128)(2,1)S(1)} %copy-done.42, bf16[128,2688]{1,0:T(8,128)(2,1)S(1)} %get-tuple-element.39, ...), kind=kOutput, calls=%fused_computation.203 | convolution fusion | flops 785641472 | bytes 5246976 | tf_op jit(solution)/shard_map/dot_general | solution.py:33
  13.9 4.5 %collective-permute-start.1 = (bf16[272,256]{0,1:T(8,128)(2,1)S(1)}, bf16[272,256]{0,1:T(8,128)(2,1)S(1)}, u32[]{:S(2)}, u32[]{:S(2)}) collective-permute-start(bf16[272,256]{0,1:T(8,128)(2,1)S(1)} %pad_maximum_fusion.17), channel_id=1, source_target_pairs={{0,4},{2,6},{4,8},{6,10},{8,12},{10,14},{1,5},{3,7},{5,9},{7,11},{... | collective-permute-start | bytes 417800 | tf_op jit(solution)/shard_map/ppermute | solution.py:17
  18.5 4.8 %collective-permute-done.1 = bf16[272,256]{0,1:T(8,128)(2,1)S(1)} collective-permute-done((bf16[272,256]{0,1:T(8,128)(2,1)S(1)}, bf16[272,256]{0,1:T(8,128)(2,1)S(1)}, u32[]{:S(2)}, u32[]{:S(2)}) %collective-permute-start.1) | collective-permute-done | bytes 139296 | tf_op jit(solution)/shard_map/ppermute | solution.py:17
  23.2 4.4 %collective-permute-start.2 = (bf16[272,256]{0,1:T(8,128)(2,1)S(1)}, bf16[272,256]{0,1:T(8,128)(2,1)S(1)}, u32[]{:S(2)}, u32[]{:S(2)}) collective-permute-start(bf16[272,256]{0,1:T(8,128)(2,1)S(1)} %collective-permute-done.1), channel_id=1, source_target_pairs={{0,4},{2,6},{4,8},{6,10},{8,12},{10,14},{1,5},{3,7},{5,9},{7,11},{... | collective-permute-start | bytes 417800 | tf_op jit(solution)/shard_map/ppermute | solution.py:17
  27.7 3.4 %collective-permute-start.3 = (bf16[544,256]{0,1:T(8,128)(2,1)S(1)}, bf16[544,256]{0,1:T(8,128)(2,1)S(1)}, u32[]{:S(2)}, u32[]{:S(2)}) collective-permute-start(bf16[544,256]{0,1:T(8,128)(2,1)S(1)} %pad_maximum_fusion.15), channel_id=1, source_target_pairs={{0,2},{2,4},{4,6},{6,8},{8,10},{10,12},{12,14},{1,3},{3,5},{5,7},{... | collective-permute-start | bytes 835592 | tf_op jit(solution)/shard_map/ppermute | solution.py:17
  32.4 5.2 %collective-permute-done.3 = bf16[544,256]{0,1:T(8,128)(2,1)S(1)} collective-permute-done((bf16[544,256]{0,1:T(8,128)(2,1)S(1)}, bf16[544,256]{0,1:T(8,128)(2,1)S(1)}, u32[]{:S(2)}, u32[]{:S(2)}) %collective-permute-start.3) | collective-permute-done | bytes 278560 | tf_op jit(solution)/shard_map/ppermute | solution.py:17
  42.1 3.7 %fusion.87 = (bf16[2,256,1280]{1,2,0:T(8,128)(2,1)S(1)}, f32[2,256,1280]{1,2,0:T(8,128)}) fusion(pred[256,1280]{0,1:T(8,128)(4,1)} %fusion.26, bf16[1280,256]{0,1:T(8,128)(2,1)} %maximum_dynamic-update-slice_fusion, f32[256,256]{0,1:T(8,128)} %get-tuple-element.55, f32[128]{0:T(128)S(1)} %copy-done.38, f32[256,2]{0,1:T(2,128)S(1)} %add_rsqrt_fusion), kind=kOutput, calls=%fused_computation.204 | convolution fusion | flops 170592000 | bytes 4852224 | tf_op jit(solution)/shard_map/div | solution.py:194
  45.8 1.6 %fusion.32 = bf16[128,2,256]{2,0,1:T(8,128)(2,1)S(1)} fusion(bf16[2,256,1280]{1,2,0:T(8,128)(2,1)S(1)} %get-tuple-element.56, bf16[1280,256]{0,1:T(8,128)(2,1)} %maximum_dynamic-update-slice_fusion, f32[256]{0:T(256)S(1)} %fusion.73), kind=kOutput, calls=%fused_computation.67 | convolution fusion | flops 167903232 | bytes 1770496 | tf_op jit(solution)/shard_map/hts,sd->thd/dot_general | solution.py:196
  49.6 1.6 %collective-permute-done.5 = bf16[128,16]{0,1:T(8,128)(2,1)} collective-permute-done((bf16[128,16]{0,1:T(8,128)(2,1)S(1)}, bf16[128,16]{0,1:T(8,128)(2,1)}, u32[]{:S(2)}, u32[]{:S(2)}) %collective-permute-start.5) | collective-permute-done | bytes 4128 | tf_op jit(solution)/shard_map/ppermute | solution.py:65
  51.9 1.7 %multiply_reduce_fusion.2 = (f32[128]{0:T(128)S(1)}, f32[128,2688]{1,0:T(8,128)S(1)}) fusion(bf16[128,16]{0,1:T(8,128)(2,1)S(1)} %add_convert_fusion.3, bf16[16,2688]{1,0:T(8,128)(2,1)S(1)} %copy-done.17, bf16[128,2688]{1,0:T(8,128)(2,1)} %collective-permute-done.4, bf16[256,2688]{1,0:T(8,128)(2,1)S(1)} %convolution_convert_fusion.1, s32[]{:T(128)S(6)} %select_n.62), kind=kOutput, calls=%fused_computation.49 | convolution fusion | flops 13418368 | bytes 2843140 | tf_op jit(solution)/shard_map/dot_general | solution.py:33
  61.1 1.6 %convolution_bitcast_fusion = f32[2,256,1280]{1,2,0:T(8,128)S(1)} fusion(bf16[256,2,128]{0,2,1:T(8,128)(2,1)S(1)} %bitcast.96, bf16[1280,256]{0,1:T(8,128)(2,1)} %maximum_dynamic-update-slice_fusion), kind=kOutput, calls=%fused_computation.10 | convolution fusion | flops 167772160 | bytes 3080192 | tf_op jit(solution)/shard_map/thd,sd->hts/dot_general | solution.py:231
  67.3 10.4 %collective-permute-done.8 = bf16[512,256]{0,1:T(8,128)(2,1)S(1)} collective-permute-done((bf16[512,256]{0,1:T(8,128)(2,1)S(1)}, bf16[512,256]{0,1:T(8,128)(2,1)S(1)}, u32[]{:S(2)}, u32[]{:S(2)}) %collective-permute-start.8) | collective-permute-done | bytes 262176 | tf_op jit(solution)/shard_map/ppermute | solution.py:17
  79.2 1.5 %collective-permute-start.10 = (bf16[256,256]{0,1:T(8,128)(2,1)S(1)}, bf16[256,256]{0,1:T(8,128)(2,1)S(1)}, u32[]{:S(2)}, u32[]{:S(2)}) collective-permute-start(bf16[256,256]{0,1:T(8,128)(2,1)S(1)} %get-tuple-element.33), channel_id=1, source_target_pairs={{4,0},{6,2},{8,4},{10,6},{12,8},{14,10},{5,1},{7,3},{9,5},{11,7},{... | collective-permute-start | bytes 393224 | tf_op jit(solution)/shard_map/ppermute | solution.py:17
  80.8 4.2 %collective-permute-done.9 = bf16[256,256]{0,1:T(8,128)(2,1)S(1)} collective-permute-done((bf16[256,256]{0,1:T(8,128)(2,1)S(1)}, bf16[256,256]{0,1:T(8,128)(2,1)S(1)}, u32[]{:S(2)}, u32[]{:S(2)}) %collective-permute-start.9) | collective-permute-done | bytes 131104 | tf_op jit(solution)/shard_map/ppermute | solution.py:17
  85.0 2.5 %collective-permute-done.10 = bf16[256,256]{0,1:T(8,128)(2,1)S(1)} collective-permute-done((bf16[256,256]{0,1:T(8,128)(2,1)S(1)}, bf16[256,256]{0,1:T(8,128)(2,1)S(1)}, u32[]{:S(2)}, u32[]{:S(2)}) %collective-permute-start.10) | collective-permute-done | bytes 131104 | tf_op jit(solution)/shard_map/ppermute | solution.py:17
  92.0 1.7 %add_convert_fusion.2 = bf16[1344,48]{0,1:T(8,128)(2,1)} fusion(bf16[1344,48]{0,1:T(8,128)(2,1)} %collective-permute-done.12, bf16[2688,48]{0,1:T(8,128)(2,1)S(1)} %convolution_convert_fusion.2, s32[]{:T(128)S(6)} %select_n.69), kind=kLoop, calls=%fused_computation.104 | loop fusion | flops 258048 | bytes 387076 | tf_op jit(solution)/shard_map/convert.15
  100.4 3.2 %convolution_convert_fusion = bf16[256,2688]{1,0:T(8,128)(2,1)S(1)} fusion(bf16[256,560]{0,1:T(8,128)(2,1)} %copy-done.20, bf16[2688,48]{1,0:T(8,128)(2,1)S(1)} %copy-done.16, bf16[2688,128]{1,0:T(8,128)(2,1)} %param.30, bf16[2688,128]{1,0:T(8,128)(2,1)} %param.29, bf16[2688,256]{1,0:T(8,128)(2,1)} %param.28), kind=kOutput, calls=%fused_computation.1 | convolution fusion | flops 783433728 | bytes 4673536 | tf_op jit(solution)/shard_map/dot_general | solution.py:37
  103.6 2.9 %collective-permute-done.13 = bf16[98304]{0:T(1024)(128)(2,1)S(1)} collective-permute-done((bf16[98304]{0:T(1024)(128)(2,1)S(1)}, bf16[98304]{0:T(1024)(128)(2,1)S(1)}, u32[]{:S(2)}, u32[]{:S(2)}) %collective-permute-start.13) | collective-permute-done | bytes 196640 | tf_op jit(solution)/shard_map/ppermute | solution.py:87
  106.5 1.6 %collective-permute-start.14 = (bf16[98304]{0:T(1024)(128)(2,1)S(1)}, bf16[98304]{0:T(1024)(128)(2,1)S(1)}, u32[]{:S(2)}, u32[]{:S(2)}) collective-permute-start(bf16[98304]{0:T(1024)(128)(2,1)S(1)} %add_convert_fusion.1), channel_id=1, source_target_pairs={{0,4},{2,6},{4,0},{6,2},{8,12},{10,14},{12,8},{14,10},{1,5},{3,7},... | collective-permute-start | bytes 589832 | tf_op jit(solution)/shard_map/ppermute | solution.py:87
  108.3 4.8 %collective-permute-done.14 = bf16[98304]{0:T(1024)(128)(2,1)S(1)} collective-permute-done((bf16[98304]{0:T(1024)(128)(2,1)S(1)}, bf16[98304]{0:T(1024)(128)(2,1)S(1)}, u32[]{:S(2)}, u32[]{:S(2)}) %collective-permute-start.14) | collective-permute-done | bytes 196640 | tf_op jit(solution)/shard_map/ppermute | solution.py:87
  113.2 2.4 %collective-permute-start.15 = (bf16[98304]{0:T(1024)(128)(2,1)S(1)}, bf16[98304]{0:T(1024)(128)(2,1)S(1)}, u32[]{:S(2)}, u32[]{:S(2)}) collective-permute-start(bf16[98304]{0:T(1024)(128)(2,1)S(1)} %add_convert_fusion), channel_id=1, source_target_pairs={{0,8},{2,10},{4,12},{6,14},{8,0},{10,2},{12,4},{14,6},{1,9},{3,11}... | collective-permute-start | bytes 589832 | tf_op jit(solution)/shard_map/ppermute | solution.py:87
  117.4 6.6 %collective-permute-done.15 = bf16[98304]{0:T(1024)(128)(2,1)S(1)} collective-permute-done((bf16[98304]{0:T(1024)(128)(2,1)S(1)}, bf16[98304]{0:T(1024)(128)(2,1)S(1)}, u32[]{:S(2)}, u32[]{:S(2)}) %collective-permute-start.15) | collective-permute-done | bytes 196640 | tf_op jit(solution)/shard_map/ppermute | solution.py:87
  (205 shorter events, 45.5 us)
Async XLA Ops:
  0.6 46.8 %copy-start = (bf16[256,2688]{1,0:T(8,128)(2,1)S(1)}, bf16[256,2688]{1,0:T(8,128)(2,1)}, u32[]{:S(2)}) copy-start(bf16[256,2688]{1,0:T(8,128)(2,1)} %param.31) | copy-start | bytes 4128772
  3.5 3.5 %collective-permute-start = (bf16[128,2688]{1,0:T(8,128)(2,1)S(1)}, bf16[128,2688]{1,0:T(8,128)(2,1)S(1)}, u32[]{:S(2)}, u32[]{:S(2)}) collective-permute-start(bf16[128,2688]{1,0:T(8,128)(2,1)S(1)} %fusion.14), channel_id=1, source_target_pairs={{0,1},{1,0},{2,3},{3,2},{4,5},{5,4},{6,7},{7,6},{8,9},{9,8},{10,11... | collective-permute-start | bytes 2064392 | tf_op jit(solution)/shard_map/ppermute | solution.py:72
  6.9 38.9 %copy-start.40 = (f32[256]{0:T(256)}, f32[256]{0:T(256)S(1)}, u32[]{:S(2)}) copy-start(f32[256]{0:T(256)S(1)} %fusion.73) | copy-start | bytes 3076
  11.8 26.7 %copy-start.32 = (bf16[256,560]{0,1:T(8,128)(2,1)}, bf16[256,560]{0,1:T(8,128)(2,1)S(1)}, u32[]{:S(2)}) copy-start(bf16[256,560]{0,1:T(8,128)(2,1)S(1)} %get-tuple-element.50) | copy-start | bytes 860164
  13.9 28.1 %copy-start.38 = (f32[128]{0:T(128)S(1)}, f32[128]{0:T(128)}, u32[]{:S(2)}) copy-start(f32[128]{0:T(128)} %param.25) | copy-start | bytes 1540
  13.9 9.3 %collective-permute-start.1 = (bf16[272,256]{0,1:T(8,128)(2,1)S(1)}, bf16[272,256]{0,1:T(8,128)(2,1)S(1)}, u32[]{:S(2)}, u32[]{:S(2)}) collective-permute-start(bf16[272,256]{0,1:T(8,128)(2,1)S(1)} %pad_maximum_fusion.17), channel_id=1, source_target_pairs={{0,4},{2,6},{4,8},{6,10},{8,12},{10,14},{1,5},{3,7},{5,9},{7,11},{... | collective-permute-start | bytes 417800 | tf_op jit(solution)/shard_map/ppermute | solution.py:17
  18.5 27.3 %copy-start.24 = (f32[256,2]{0,1:T(2,128)}, f32[256,2]{0,1:T(2,128)S(1)}, u32[]{:S(2)}) copy-start(f32[256,2]{0,1:T(2,128)S(1)} %add_rsqrt_fusion) | copy-start | bytes 6148
  23.2 8.4 %collective-permute-start.2 = (bf16[272,256]{0,1:T(8,128)(2,1)S(1)}, bf16[272,256]{0,1:T(8,128)(2,1)S(1)}, u32[]{:S(2)}, u32[]{:S(2)}) collective-permute-start(bf16[272,256]{0,1:T(8,128)(2,1)S(1)} %collective-permute-done.1), channel_id=1, source_target_pairs={{0,4},{2,6},{4,8},{6,10},{8,12},{10,14},{1,5},{3,7},{5,9},{7,11},{... | collective-permute-start | bytes 417800 | tf_op jit(solution)/shard_map/ppermute | solution.py:17
  27.7 9.9 %collective-permute-start.3 = (bf16[544,256]{0,1:T(8,128)(2,1)S(1)}, bf16[544,256]{0,1:T(8,128)(2,1)S(1)}, u32[]{:S(2)}, u32[]{:S(2)}) collective-permute-start(bf16[544,256]{0,1:T(8,128)(2,1)S(1)} %pad_maximum_fusion.15), channel_id=1, source_target_pairs={{0,2},{2,4},{4,6},{6,8},{8,10},{10,12},{12,14},{1,3},{3,5},{5,7},{... | collective-permute-start | bytes 835592 | tf_op jit(solution)/shard_map/ppermute | solution.py:17
  48.9 3.0 %collective-permute-start.4 = (bf16[128,2688]{1,0:T(8,128)(2,1)}, bf16[128,2688]{1,0:T(8,128)(2,1)}, u32[]{:S(2)}, u32[]{:S(2)}) collective-permute-start(bf16[128,2688]{1,0:T(8,128)(2,1)} %constant_dynamic-slice_fusion.3), channel_id=1, source_target_pairs={{0,1},{1,0},{2,3},{3,2},{4,5},{5,4},{6,7},{7,6},{8,9},{9,8},{10,11... | collective-permute-start | bytes 2064392 | tf_op jit(solution)/shard_map/ppermute | solution.py:65
  49.1 2.1 %collective-permute-start.5 = (bf16[128,16]{0,1:T(8,128)(2,1)S(1)}, bf16[128,16]{0,1:T(8,128)(2,1)}, u32[]{:S(2)}, u32[]{:S(2)}) collective-permute-start(bf16[128,16]{0,1:T(8,128)(2,1)S(1)} %constant_dynamic-slice_fusion.2), channel_id=1, source_target_pairs={{0,1},{1,0},{2,3},{3,2},{4,5},{5,4},{6,7},{7,6},{8,9},{9,8},{10,11... | collective-permute-start | bytes 12296 | tf_op jit(solution)/shard_map/ppermute | solution.py:65
  55.5 1.2 collective-permute-start.7
  55.7 2.3 %collective-permute-start.6 = (bf16[128,2688]{1,0:T(8,128)(2,1)S(1)}, bf16[128,2688]{1,0:T(8,128)(2,1)}, u32[]{:S(2)}, u32[]{:S(2)}) collective-permute-start(bf16[128,2688]{1,0:T(8,128)(2,1)S(1)} %get-tuple-element.34), channel_id=1, source_target_pairs={{0,1},{1,0},{2,3},{3,2},{4,5},{5,4},{6,7},{7,6},{8,9},{9,8},{10,11... | collective-permute-start | bytes 2064392 | tf_op jit(solution)/shard_map/ppermute | solution.py:72
  64.6 13.1 %collective-permute-start.8 = (bf16[512,256]{0,1:T(8,128)(2,1)S(1)}, bf16[512,256]{0,1:T(8,128)(2,1)S(1)}, u32[]{:S(2)}, u32[]{:S(2)}) collective-permute-start(bf16[512,256]{0,1:T(8,128)(2,1)S(1)} %pad_maximum_fusion.16), channel_id=1, source_target_pairs={{4,0},{6,2},{8,4},{10,6},{12,8},{14,10},{5,1},{7,3},{9,5},{11,7},{... | collective-permute-start | bytes 786440 | tf_op jit(solution)/shard_map/ppermute | solution.py:17
  77.9 7.1 %collective-permute-start.9 = (bf16[256,256]{0,1:T(8,128)(2,1)S(1)}, bf16[256,256]{0,1:T(8,128)(2,1)S(1)}, u32[]{:S(2)}, u32[]{:S(2)}) collective-permute-start(bf16[256,256]{0,1:T(8,128)(2,1)S(1)} %get-tuple-element.32), channel_id=1, source_target_pairs={{2,0},{4,2},{6,4},{8,6},{10,8},{12,10},{14,12},{3,1},{5,3},{7,5},{... | collective-permute-start | bytes 393224 | tf_op jit(solution)/shard_map/ppermute | solution.py:17
  79.2 8.3 %collective-permute-start.10 = (bf16[256,256]{0,1:T(8,128)(2,1)S(1)}, bf16[256,256]{0,1:T(8,128)(2,1)S(1)}, u32[]{:S(2)}, u32[]{:S(2)}) collective-permute-start(bf16[256,256]{0,1:T(8,128)(2,1)S(1)} %get-tuple-element.33), channel_id=1, source_target_pairs={{4,0},{6,2},{8,4},{10,6},{12,8},{14,10},{5,1},{7,3},{9,5},{11,7},{... | collective-permute-start | bytes 393224 | tf_op jit(solution)/shard_map/ppermute | solution.py:17
  89.4 2.7 %collective-permute-start.12 = (bf16[1344,48]{0,1:T(8,128)(2,1)}, bf16[1344,48]{0,1:T(8,128)(2,1)}, u32[]{:S(2)}, u32[]{:S(2)}) collective-permute-start(bf16[1344,48]{0,1:T(8,128)(2,1)} %constant_dynamic-slice_fusion), channel_id=1, source_target_pairs={{0,1},{1,0},{2,3},{3,2},{4,5},{5,4},{6,7},{7,6},{8,9},{9,8},{10,11... | collective-permute-start | bytes 387080 | tf_op jit(solution)/shard_map/ppermute | solution.py:65
  89.8 10.6 %copy-start.16 = (bf16[2688,48]{1,0:T(8,128)(2,1)S(1)}, bf16[2688,48]{1,0:T(8,128)(2,1)}, u32[]{:S(2)}) copy-start(bf16[2688,48]{1,0:T(8,128)(2,1)} %copy.35) | copy-start | bytes 774148
  99.2 7.3 %collective-permute-start.13 = (bf16[98304]{0:T(1024)(128)(2,1)S(1)}, bf16[98304]{0:T(1024)(128)(2,1)S(1)}, u32[]{:S(2)}, u32[]{:S(2)}) collective-permute-start(bf16[98304]{0:T(1024)(128)(2,1)S(1)} %constant_dynamic-update-slice_fusion.12), channel_id=1, source_target_pairs={{0,2},{2,0},{4,6},{6,4},{8,10},{10,8},{12,14},{14,12},{1,3},{3,1},... | collective-permute-start | bytes 589832 | tf_op jit(solution)/shard_map/ppermute | solution.py:87
  103.5 12.1 %copy-start.19 = (f32[2688]{0:T(1024)S(1)}, f32[2688]{0:T(1024)}, u32[]{:S(2)}) copy-start(f32[2688]{0:T(1024)} %param.24) | copy-start | bytes 32260
  103.5 12.1 %copy-start.34 = (f32[128]{0:T(128)S(1)}, f32[128]{0:T(128)}, u32[]{:S(2)}) copy-start(f32[128]{0:T(128)} %copy-done.33) | copy-start | bytes 1540
  106.5 6.6 %collective-permute-start.14 = (bf16[98304]{0:T(1024)(128)(2,1)S(1)}, bf16[98304]{0:T(1024)(128)(2,1)S(1)}, u32[]{:S(2)}, u32[]{:S(2)}) collective-permute-start(bf16[98304]{0:T(1024)(128)(2,1)S(1)} %add_convert_fusion.1), channel_id=1, source_target_pairs={{0,4},{2,6},{4,0},{6,2},{8,12},{10,14},{12,8},{14,10},{1,5},{3,7},... | collective-permute-start | bytes 589832 | tf_op jit(solution)/shard_map/ppermute | solution.py:87
  108.2 7.4 %collective-permute-start.11 = (bf16[128,2688]{1,0:T(8,128)(2,1)S(1)}, bf16[128,2688]{1,0:T(8,128)(2,1)S(1)}, u32[]{:S(2)}, u32[]{:S(2)}) collective-permute-start(bf16[128,2688]{1,0:T(8,128)(2,1)S(1)} %constant_dynamic-slice_fusion.1), channel_id=1, source_target_pairs={{0,1},{1,0},{2,3},{3,2},{4,5},{5,4},{6,7},{7,6},{8,9},{9,8},{10,11... | collective-permute-start | bytes 2064392 | tf_op jit(solution)/shard_map/ppermute | solution.py:65
  113.2 10.8 %collective-permute-start.15 = (bf16[98304]{0:T(1024)(128)(2,1)S(1)}, bf16[98304]{0:T(1024)(128)(2,1)S(1)}, u32[]{:S(2)}, u32[]{:S(2)}) collective-permute-start(bf16[98304]{0:T(1024)(128)(2,1)S(1)} %add_convert_fusion), channel_id=1, source_target_pairs={{0,8},{2,10},{4,12},{6,14},{8,0},{10,2},{12,4},{14,6},{1,9},{3,11}... | collective-permute-start | bytes 589832 | tf_op jit(solution)/shard_map/ppermute | solution.py:87
  (36 other events, 120.2 us)

commit v13 on v11

--- a/solution.py
+++ b/solution.py
@@ -201,10 +201,12 @@
         .astype(jnp.bfloat16)
         .reshape(shard_len, heads_here * head_dim)
     )
-    part_out = matrix_product(attention_result, output_projection)
-    partial_middle = matrix_product(attention_result, adapter_output_down)
-    output_total = tp_sum_scatter(part_out.astype(jnp.bfloat16))
-    mid_sum = tp_sum_scatter(partial_middle.astype(jnp.bfloat16))
+    out_parts = matrix_product(
+        attention_result, jnp.concatenate([output_projection, adapter_output_down], axis=1)
+    )
+    summed_parts = tp_sum_scatter(out_parts.astype(jnp.bfloat16))
+    output_total = summed_parts[:, :model_width]
+    mid_sum = summed_parts[:, model_width:]
     middle_output = mid_sum.astype(jnp.bfloat16)
     apply_prenorm = output_total + adapter_scale * matrix_product(middle_output, adapter_output_up)
     layer_out = norm_rows(apply_prenorm, output_norm_gain).astype(jnp.bfloat16)

time: 124 us -> 128 us (1.032)
  local copies, waits for them, and re-layouts: 18 us -> 25.2 us
  waiting for transfers between devices: 45.6 us -> 41.3 us
  matrix products: 20.3 us -> 22.9 us
    unnamed x107 -> x110, local copies, waits for them, and re-layouts: 9.9 us -> 17.9 us
    ppermute x6, waiting for transfers between devices: 29 us -> 27 us  [passed_along(): lax.ppermute(value, axis, [(source, source + steps) for source in range(l...]
    dot_general x6, matrix products: 3.45 us -> 5.14 us  [transpose_multiply(): lax.dot_general(first_op, second_op, (((0,), (0,)), ((), ())), preferred_...]
    dot_general x7 -> x6, matrix products: 5.7 us -> 4.1 us  [matrix_product(): return jnp.dot(first_op, second_op, preferred_element_type=jnp.float32)]
    dot_general x7, matrix products: 4.63 us -> 6.19 us  [multiply_by_transpose(): lax.dot_general(first_op, second_op, (((1,), (1,)), ((), ())), preferred_...]
    another operation x2, other arithmetic: 1.74 us -> 0.18 us
    add x0 -> x1, other arithmetic: none -> 1.44 us  [tp_sum_scatter(): return mine.astype(jnp.float32) + received.astype(jnp.float32)]
    ppermute x4 -> x3, waiting for transfers between devices: 1.62 us -> 0.28 us  [tp_sum_scatter(): received = lax.ppermute(theirs, 'tp', [(0, 1), (1, 0)])]
  transfers between devices with their start and end apart: 16 -> 15, of which waited for: 11 -> 10; matrix products, arithmetic and copies ran while one was open for 10% -> 17% of each run, Pallas kernels for 0% -> 0%
where the time goes in v13:
time: 128 us; the launch traced here: 127 us
  waiting for transfers between devices  41.3 us (32%)
  local copies, waits for them, and re-layouts  25.2 us (20%)
  starting transfers between devices  23.2 us (18%)
  matrix products  22.9 us (18%)
  other arithmetic  12.3 us (10%)
  between operations  2.28 us (2%)
    ppermute x6, waiting for transfers between devices, passed_along(): lax.ppermute(value, axis, [(source, source + steps) for source in range(l...  27 us
    unnamed x110, local copies, waits for them, and re-layouts  17.9 us
    ppermute x6, starting transfers between devices, passed_along(): lax.ppermute(value, axis, [(source, source + steps) for source in range(l...  16.6 us
    ppermute x3, waiting for transfers between devices, ctx_sum(): received = lax.ppermute(sent, 'ctx', [(i, i ^ step) for i in range(count)])  14 us
    dot_general x7, matrix products, multiply_by_transpose(): lax.dot_general(first_op, second_op, (((1,), (1,)), ((), ())), preferred_...  6.19 us
    ppermute x3, starting transfers between devices, ctx_sum(): received = lax.ppermute(sent, 'ctx', [(i, i ^ step) for i in range(count)])  5.44 us
    dot_general x6, matrix products, transpose_multiply(): lax.dot_general(first_op, second_op, (((0,), (0,)), ((), ())), preferred_...  5.14 us
    dot_general x6, matrix products, matrix_product(): return jnp.dot(first_op, second_op, preferred_element_type=jnp.float32)  4.1 us
  transfers between devices with their start and end apart: 15, of which 10 were waited for; matrix products, arithmetic and copies ran while one was open for 17% of the time, Pallas kernels for 0%

profile of v13, /device:TPU:0, one launch (start us, length us, event | category | flops | bytes accessed | tf_op | source)
XLA Modules:
  0.0 127.2 jit_solution(15580056164679800005)
XLA Ops:
  0.7 1.5 %copy.42 = bf16[128,2688]{0,1:T(8,128)(2,1)S(1)} copy(bf16[128,2688]{1,0:T(8,128)(2,1)} %param.20) | data formatting | bytes 1376256 | tf_op args[0]
  11.6 4.5 %collective-permute-start.1 = (bf16[272,256]{0,1:T(8,128)(2,1)S(1)}, bf16[272,256]{0,1:T(8,128)(2,1)S(1)}, u32[]{:S(2)}, u32[]{:S(2)}) collective-permute-start(bf16[272,256]{0,1:T(8,128)(2,1)S(1)} %pad_maximum_fusion.17), channel_id=1, source_target_pairs={{0,4},{2,6},{4,8},{6,10},{8,12},{10,14},{1,5},{3,7},{5,9},{7,11},{... | collective-permute-start | bytes 417800 | tf_op jit(solution)/shard_map/ppermute | solution.py:17
  16.1 4.7 %collective-permute-done.1 = bf16[272,256]{0,1:T(8,128)(2,1)S(1)} collective-permute-done((bf16[272,256]{0,1:T(8,128)(2,1)S(1)}, bf16[272,256]{0,1:T(8,128)(2,1)S(1)}, u32[]{:S(2)}, u32[]{:S(2)}) %collective-permute-start.1) | collective-permute-done | bytes 139296 | tf_op jit(solution)/shard_map/ppermute | solution.py:17
  20.9 4.4 %collective-permute-start.2 = (bf16[272,256]{0,1:T(8,128)(2,1)S(1)}, bf16[272,256]{0,1:T(8,128)(2,1)S(1)}, u32[]{:S(2)}, u32[]{:S(2)}) collective-permute-start(bf16[272,256]{0,1:T(8,128)(2,1)S(1)} %collective-permute-done.1), channel_id=1, source_target_pairs={{0,4},{2,6},{4,8},{6,10},{8,12},{10,14},{1,5},{3,7},{5,9},{7,11},{... | collective-permute-start | bytes 417800 | tf_op jit(solution)/shard_map/ppermute | solution.py:17
  25.4 3.6 %collective-permute-start.3 = (bf16[544,256]{0,1:T(8,128)(2,1)S(1)}, bf16[544,256]{0,1:T(8,128)(2,1)S(1)}, u32[]{:S(2)}, u32[]{:S(2)}) collective-permute-start(bf16[544,256]{0,1:T(8,128)(2,1)S(1)} %pad_maximum_fusion.15), channel_id=1, source_target_pairs={{0,2},{2,4},{4,6},{6,8},{8,10},{10,12},{12,14},{1,3},{3,5},{5,7},{... | collective-permute-start | bytes 835592 | tf_op jit(solution)/shard_map/ppermute | solution.py:17
  30.1 5.2 %collective-permute-done.3 = bf16[544,256]{0,1:T(8,128)(2,1)S(1)} collective-permute-done((bf16[544,256]{0,1:T(8,128)(2,1)S(1)}, bf16[544,256]{0,1:T(8,128)(2,1)S(1)}, u32[]{:S(2)}, u32[]{:S(2)}) %collective-permute-start.3) | collective-permute-done | bytes 278560 | tf_op jit(solution)/shard_map/ppermute | solution.py:17
  39.7 2.1 %fusion.25 = f32[2,256,1280]{1,2,0:T(8,128)S(1)} fusion(pred[256,1280]{0,1:T(8,128)(4,1)} %fusion.29, bf16[1280,256]{0,1:T(8,128)(2,1)} %maximum_dynamic-update-slice_fusion, f32[256,256]{0,1:T(8,128)} %get-tuple-element.63, f32[128]{0:T(128)S(1)} %copy-done.35, f32[256,2]{0,1:T(2,128)S(1)} %add_rsqrt_fusion), kind=kOutput, calls=%fused_computation.57 | convolution fusion | flops 169936640 | bytes 3541504 | tf_op jit(solution)/shard_map/div | solution.py:194
  46.1 2.2 %copy.50 = bf16[128,2688]{0,1:T(8,128)(2,1)} copy(bf16[128,2688]{1,0:T(8,128)(2,1)} %param.21) | data formatting | bytes 1376256 | tf_op args[1]
  51.6 1.6 %multiply_convert_fusion = (bf16[128,2688]{0,1:T(8,128)(2,1)}, bf16[128,2688]{0,1:T(8,128)(2,1)}) fusion(bf16[128,2688]{0,1:T(8,128)(2,1)S(1)} %copy-done.1, f32[128,2688]{0,1:T(8,128)S(1)} %get-tuple-element.65, f32[128]{0:T(128)S(1)} %broadcast_multiply_fusion.3, f32[2688]{0:T(1024)S(1)} %copy-done.14, f32[128]{0:T(128)S(1)} %add_rsqrt_fusion.2), kind=kLoop, calls=%fused_computation.50 | loop fusion | flops 3096576 | bytes 3452416 | tf_op jit(solution)/shard_map/convert_element_type | solution.py:215
  55.6 2.2 %copy.59 = bf16[128,2688]{1,0:T(8,128)(2,1)} copy(bf16[128,2688]{0,1:T(8,128)(2,1)} %get-tuple-element.43) | data formatting | bytes 1376256
  58.5 1.7 %convolution_convert_fusion.3 = bf16[256,16]{0,1:T(8,128)(2,1)} fusion(bf16[256,256]{0,1:T(8,128)(2,1)} %bitcast.87, bf16[128,32]{0,1:T(8,128)(2,1)S(1)} %get-tuple-element.55, bf16[128,32]{0,1:T(8,128)(2,1)S(1)} %get-tuple-element.54), kind=kOutput, calls=%fused_computation.83 | convolution fusion | flops 2117632 | bytes 155648 | tf_op jit(solution)/shard_map/dot_general | solution.py:43
  61.7 1.6 %reshape.264 = bf16[4096]{0:T(1024)(128)(2,1)} reshape(bf16[256,16]{1,0:T(8,128)(2,1)} %copy.58) | data formatting | bytes 16384 | tf_op jit(solution)/shard_map/reshape | solution.py:83
  64.2 1.5 %broadcast_select_fusion.1 = (bf16[128,2688]{0,1:T(8,128)(2,1)S(1)}, bf16[128,2688]{0,1:T(8,128)(2,1)S(1)}) fusion(bf16[128,2688]{0,1:T(8,128)(2,1)} %get-tuple-element.42, bf16[128,2688]{0,1:T(8,128)(2,1)} %collective-permute-done.5, pred[]{:T(512)S(6)} %eq.29), kind=kLoop, calls=%fused_computation.98 | loop fusion | flops 688128 | bytes 2752513 | tf_op jit(solution)/shard_map/jit(_where)/select_n | solution.py:75
  67.0 1.5 %convolution_bitcast_fusion = f32[2,256,1280]{1,2,0:T(8,128)S(1)} fusion(bf16[256,2,128]{0,2,1:T(8,128)(2,1)S(1)} %bitcast.89, bf16[1280,256]{0,1:T(8,128)(2,1)} %maximum_dynamic-update-slice_fusion), kind=kOutput, calls=%fused_computation.10 | convolution fusion | flops 167772160 | bytes 3080192 | tf_op jit(solution)/shard_map/thd,sd->hts/dot_general | solution.py:233
  72.9 10.3 %collective-permute-done.7 = bf16[512,256]{0,1:T(8,128)(2,1)S(1)} collective-permute-done((bf16[512,256]{0,1:T(8,128)(2,1)S(1)}, bf16[512,256]{0,1:T(8,128)(2,1)S(1)}, u32[]{:S(2)}, u32[]{:S(2)}) %collective-permute-start.7) | collective-permute-done | bytes 262176 | tf_op jit(solution)/shard_map/ppermute | solution.py:17
  84.7 1.5 %collective-permute-start.9 = (bf16[256,256]{0,1:T(8,128)(2,1)S(1)}, bf16[256,256]{0,1:T(8,128)(2,1)S(1)}, u32[]{:S(2)}, u32[]{:S(2)}) collective-permute-start(bf16[256,256]{0,1:T(8,128)(2,1)S(1)} %get-tuple-element.41), channel_id=1, source_target_pairs={{4,0},{6,2},{8,4},{10,6},{12,8},{14,10},{5,1},{7,3},{9,5},{11,7},{... | collective-permute-start | bytes 393224 | tf_op jit(solution)/shard_map/ppermute | solution.py:17
  86.3 4.1 %collective-permute-done.8 = bf16[256,256]{0,1:T(8,128)(2,1)S(1)} collective-permute-done((bf16[256,256]{0,1:T(8,128)(2,1)S(1)}, bf16[256,256]{0,1:T(8,128)(2,1)S(1)}, u32[]{:S(2)}, u32[]{:S(2)}) %collective-permute-start.8) | collective-permute-done | bytes 131104 | tf_op jit(solution)/shard_map/ppermute | solution.py:17
  90.4 2.5 %collective-permute-done.9 = bf16[256,256]{0,1:T(8,128)(2,1)S(1)} collective-permute-done((bf16[256,256]{0,1:T(8,128)(2,1)S(1)}, bf16[256,256]{0,1:T(8,128)(2,1)S(1)}, u32[]{:S(2)}, u32[]{:S(2)}) %collective-permute-start.9) | collective-permute-done | bytes 131104 | tf_op jit(solution)/shard_map/ppermute | solution.py:17
  99.7 3.0 %convolution_convert_fusion = bf16[256,2688]{0,1:T(8,128)(2,1)S(1)} fusion(bf16[256,560]{0,1:T(8,128)(2,1)S(1)} %get-tuple-element.72, bf16[2688,48]{1,0:T(8,128)(2,1)S(1)} %copy-done.9, bf16[2688,128]{1,0:T(8,128)(2,1)} %param.30, bf16[2688,128]{1,0:T(8,128)(2,1)} %param.29, bf16[2688,256]{1,0:T(8,128)(2,1)} %param.28), kind=kOutput, calls=%fused_computation.1 | convolution fusion | flops 783433728 | bytes 4673536 | tf_op jit(solution)/shard_map/dot_general | solution.py:37
  102.7 3.0 %collective-permute-done.12 = bf16[98304]{0:T(1024)(128)(2,1)S(1)} collective-permute-done((bf16[98304]{0:T(1024)(128)(2,1)S(1)}, bf16[98304]{0:T(1024)(128)(2,1)S(1)}, u32[]{:S(2)}, u32[]{:S(2)}) %collective-permute-start.12) | collective-permute-done | bytes 196640 | tf_op jit(solution)/shard_map/ppermute | solution.py:87
  105.8 1.6 %collective-permute-start.13 = (bf16[98304]{0:T(1024)(128)(2,1)S(1)}, bf16[98304]{0:T(1024)(128)(2,1)S(1)}, u32[]{:S(2)}, u32[]{:S(2)}) collective-permute-start(bf16[98304]{0:T(1024)(128)(2,1)S(1)} %add_convert_fusion.1), channel_id=1, source_target_pairs={{0,4},{2,6},{4,0},{6,2},{8,12},{10,14},{12,8},{14,10},{1,5},{3,7},... | collective-permute-start | bytes 589832 | tf_op jit(solution)/shard_map/ppermute | solution.py:87
  107.5 4.8 %collective-permute-done.13 = bf16[98304]{0:T(1024)(128)(2,1)S(1)} collective-permute-done((bf16[98304]{0:T(1024)(128)(2,1)S(1)}, bf16[98304]{0:T(1024)(128)(2,1)S(1)}, u32[]{:S(2)}, u32[]{:S(2)}) %collective-permute-start.13) | collective-permute-done | bytes 196640 | tf_op jit(solution)/shard_map/ppermute | solution.py:87
  112.4 2.5 %collective-permute-start.14 = (bf16[98304]{0:T(1024)(128)(2,1)S(1)}, bf16[98304]{0:T(1024)(128)(2,1)S(1)}, u32[]{:S(2)}, u32[]{:S(2)}) collective-permute-start(bf16[98304]{0:T(1024)(128)(2,1)S(1)} %add_convert_fusion), channel_id=1, source_target_pairs={{0,8},{2,10},{4,12},{6,14},{8,0},{10,2},{12,4},{14,6},{1,9},{3,11}... | collective-permute-start | bytes 589832 | tf_op jit(solution)/shard_map/ppermute | solution.py:87
  117.1 6.2 %collective-permute-done.14 = bf16[98304]{0:T(1024)(128)(2,1)S(1)} collective-permute-done((bf16[98304]{0:T(1024)(128)(2,1)S(1)}, bf16[98304]{0:T(1024)(128)(2,1)S(1)}, u32[]{:S(2)}, u32[]{:S(2)}) %collective-permute-start.14) | collective-permute-done | bytes 196640 | tf_op jit(solution)/shard_map/ppermute | solution.py:87
  (207 shorter events, 47.1 us)
Async XLA Ops:
  0.6 49.4 %copy-start = (bf16[16,2688]{1,0:T(8,128)(2,1)S(1)}, bf16[16,2688]{1,0:T(8,128)(2,1)}, u32[]{:S(2)}) copy-start(bf16[16,2688]{1,0:T(8,128)(2,1)} %param.37) | copy-start | bytes 258052
  3.0 2.6 %collective-permute-start = (bf16[128,2688]{0,1:T(8,128)(2,1)S(1)}, bf16[128,2688]{0,1:T(8,128)(2,1)S(1)}, u32[]{:S(2)}, u32[]{:S(2)}) collective-permute-start(bf16[128,2688]{0,1:T(8,128)(2,1)S(1)} %fusion.17), channel_id=1, source_target_pairs={{0,1},{1,0},{2,3},{3,2},{4,5},{5,4},{6,7},{7,6},{8,9},{9,8},{10,11... | collective-permute-start | bytes 2064392 | tf_op jit(solution)/shard_map/ppermute | solution.py:72
  5.5 36.3 %copy-start.37 = (f32[256]{0:T(256)}, f32[256]{0:T(256)S(1)}, u32[]{:S(2)}) copy-start(f32[256]{0:T(256)S(1)} %fusion.78) | copy-start | bytes 3076
  9.4 26.7 %copy-start.29 = (bf16[256,560]{0,1:T(8,128)(2,1)}, bf16[256,560]{0,1:T(8,128)(2,1)S(1)}, u32[]{:S(2)}) copy-start(bf16[256,560]{0,1:T(8,128)(2,1)S(1)} %get-tuple-element.58) | copy-start | bytes 860164
  11.6 28.2 %copy-start.35 = (f32[128]{0:T(128)S(1)}, f32[128]{0:T(128)}, u32[]{:S(2)}) copy-start(f32[128]{0:T(128)} %param.25) | copy-start | bytes 1540
  11.6 9.3 %collective-permute-start.1 = (bf16[272,256]{0,1:T(8,128)(2,1)S(1)}, bf16[272,256]{0,1:T(8,128)(2,1)S(1)}, u32[]{:S(2)}, u32[]{:S(2)}) collective-permute-start(bf16[272,256]{0,1:T(8,128)(2,1)S(1)} %pad_maximum_fusion.17), channel_id=1, source_target_pairs={{0,4},{2,6},{4,8},{6,10},{8,12},{10,14},{1,5},{3,7},{5,9},{7,11},{... | collective-permute-start | bytes 417800 | tf_op jit(solution)/shard_map/ppermute | solution.py:17
  16.1 25.7 %copy-start.21 = (f32[256,2]{0,1:T(2,128)}, f32[256,2]{0,1:T(2,128)S(1)}, u32[]{:S(2)}) copy-start(f32[256,2]{0,1:T(2,128)S(1)} %add_rsqrt_fusion) | copy-start | bytes 6148
  20.9 8.4 %collective-permute-start.2 = (bf16[272,256]{0,1:T(8,128)(2,1)S(1)}, bf16[272,256]{0,1:T(8,128)(2,1)S(1)}, u32[]{:S(2)}, u32[]{:S(2)}) collective-permute-start(bf16[272,256]{0,1:T(8,128)(2,1)S(1)} %collective-permute-done.1), channel_id=1, source_target_pairs={{0,4},{2,6},{4,8},{6,10},{8,12},{10,14},{1,5},{3,7},{5,9},{7,11},{... | collective-permute-start | bytes 417800 | tf_op jit(solution)/shard_map/ppermute | solution.py:17
  25.4 9.9 %collective-permute-start.3 = (bf16[544,256]{0,1:T(8,128)(2,1)S(1)}, bf16[544,256]{0,1:T(8,128)(2,1)S(1)}, u32[]{:S(2)}, u32[]{:S(2)}) collective-permute-start(bf16[544,256]{0,1:T(8,128)(2,1)S(1)} %pad_maximum_fusion.15), channel_id=1, source_target_pairs={{0,2},{2,4},{4,6},{6,8},{8,10},{10,12},{12,14},{1,3},{3,5},{5,7},{... | collective-permute-start | bytes 835592 | tf_op jit(solution)/shard_map/ppermute | solution.py:17
  46.1 2.5 %collective-permute-start.4 = (bf16[128,2704]{0,1:T(8,128)(2,1)}, bf16[128,2704]{0,1:T(8,128)(2,1)}, u32[]{:S(2)}, u32[]{:S(2)}) collective-permute-start(bf16[128,2704]{0,1:T(8,128)(2,1)} %constant_dynamic-slice_fusion.2), channel_id=1, source_target_pairs={{0,1},{1,0},{2,3},{3,2},{4,5},{5,4},{6,7},{7,6},{8,9},{9,8},{10,11... | collective-permute-start | bytes 2076680 | tf_op jit(solution)/shard_map/ppermute | solution.py:65
  55.1 2.7 %collective-permute-start.6 = (bf16[128,32]{0,1:T(8,128)(2,1)S(1)}, bf16[128,32]{0,1:T(8,128)(2,1)}, u32[]{:S(2)}, u32[]{:S(2)}) collective-permute-start(bf16[128,32]{0,1:T(8,128)(2,1)S(1)} %pad_maximum_fusion.20), channel_id=1, source_target_pairs={{0,1},{1,0},{2,3},{3,2},{4,5},{5,4},{6,7},{7,6},{8,9},{9,8},{10,11... | collective-permute-start | bytes 24584 | tf_op jit(solution)/shard_map/ppermute | solution.py:72
  55.3 8.8 %collective-permute-start.5 = (bf16[128,2688]{0,1:T(8,128)(2,1)}, bf16[128,2688]{0,1:T(8,128)(2,1)}, u32[]{:S(2)}, u32[]{:S(2)}) collective-permute-start(bf16[128,2688]{0,1:T(8,128)(2,1)} %get-tuple-element.42), channel_id=1, source_target_pairs={{0,1},{1,0},{2,3},{3,2},{4,5},{5,4},{6,7},{7,6},{8,9},{9,8},{10,11... | collective-permute-start | bytes 2064392 | tf_op jit(solution)/shard_map/ppermute | solution.py:72
  70.3 13.0 %collective-permute-start.7 = (bf16[512,256]{0,1:T(8,128)(2,1)S(1)}, bf16[512,256]{0,1:T(8,128)(2,1)S(1)}, u32[]{:S(2)}, u32[]{:S(2)}) collective-permute-start(bf16[512,256]{0,1:T(8,128)(2,1)S(1)} %pad_maximum_fusion.16), channel_id=1, source_target_pairs={{4,0},{6,2},{8,4},{10,6},{12,8},{14,10},{5,1},{7,3},{9,5},{11,7},{... | collective-permute-start | bytes 786440 | tf_op jit(solution)/shard_map/ppermute | solution.py:17
  83.4 7.0 %collective-permute-start.8 = (bf16[256,256]{0,1:T(8,128)(2,1)S(1)}, bf16[256,256]{0,1:T(8,128)(2,1)S(1)}, u32[]{:S(2)}, u32[]{:S(2)}) collective-permute-start(bf16[256,256]{0,1:T(8,128)(2,1)S(1)} %get-tuple-element.40), channel_id=1, source_target_pairs={{2,0},{4,2},{6,4},{8,6},{10,8},{12,10},{14,12},{3,1},{5,3},{7,5},{... | collective-permute-start | bytes 393224 | tf_op jit(solution)/shard_map/ppermute | solution.py:17
  84.7 8.2 %collective-permute-start.9 = (bf16[256,256]{0,1:T(8,128)(2,1)S(1)}, bf16[256,256]{0,1:T(8,128)(2,1)S(1)}, u32[]{:S(2)}, u32[]{:S(2)}) collective-permute-start(bf16[256,256]{0,1:T(8,128)(2,1)S(1)} %get-tuple-element.41), channel_id=1, source_target_pairs={{4,0},{6,2},{8,4},{10,6},{12,8},{14,10},{5,1},{7,3},{9,5},{11,7},{... | collective-permute-start | bytes 393224 | tf_op jit(solution)/shard_map/ppermute | solution.py:17
  86.3 7.2 %copy-start.28 = (bf16[16,128]{1,0:T(8,128)(2,1)S(1)}, bf16[16,128]{1,0:T(8,128)(2,1)}, u32[]{:S(2)}) copy-start(bf16[16,128]{1,0:T(8,128)(2,1)} %param.35) | copy-start | bytes 12292
  86.3 7.3 %copy-start.5 = (bf16[128,2688]{0,1:T(8,128)(2,1)S(1)}, bf16[128,2688]{0,1:T(8,128)(2,1)}, u32[]{:S(2)}) copy-start(bf16[128,2688]{0,1:T(8,128)(2,1)} %copy-done.4) | copy-start | bytes 2064388
  86.3 7.3 %copy-start.7 = (bf16[128,2688]{0,1:T(8,128)(2,1)S(1)}, bf16[128,2688]{0,1:T(8,128)(2,1)}, u32[]{:S(2)}) copy-start(bf16[128,2688]{0,1:T(8,128)(2,1)} %copy-done.6) | copy-start | bytes 2064388
  94.3 1.5 %collective-permute-start.11 = (bf16[1344,48]{0,1:T(8,128)(2,1)S(1)}, bf16[1344,48]{0,1:T(8,128)(2,1)S(1)}, u32[]{:S(2)}, u32[]{:S(2)}) collective-permute-start(bf16[1344,48]{0,1:T(8,128)(2,1)S(1)} %constant_dynamic-slice_fusion), channel_id=1, source_target_pairs={{0,1},{1,0},{2,3},{3,2},{4,5},{5,4},{6,7},{7,6},{8,9},{9,8},{10,11... | collective-permute-start | bytes 387080 | tf_op jit(solution)/shard_map/ppermute | solution.py:65
  98.4 7.4 %collective-permute-start.12 = (bf16[98304]{0:T(1024)(128)(2,1)S(1)}, bf16[98304]{0:T(1024)(128)(2,1)S(1)}, u32[]{:S(2)}, u32[]{:S(2)}) collective-permute-start(bf16[98304]{0:T(1024)(128)(2,1)S(1)} %constant_dynamic-update-slice_fusion.12), channel_id=1, source_target_pairs={{0,2},{2,0},{4,6},{6,4},{8,10},{10,8},{12,14},{14,12},{1,3},{3,1},... | collective-permute-start | bytes 589832 | tf_op jit(solution)/shard_map/ppermute | solution.py:87
  102.7 12.2 %copy-start.31 = (f32[128]{0:T(128)S(1)}, f32[128]{0:T(128)}, u32[]{:S(2)}) copy-start(f32[128]{0:T(128)} %copy-done.30) | copy-start | bytes 1540
  105.8 6.6 %collective-permute-start.13 = (bf16[98304]{0:T(1024)(128)(2,1)S(1)}, bf16[98304]{0:T(1024)(128)(2,1)S(1)}, u32[]{:S(2)}, u32[]{:S(2)}) collective-permute-start(bf16[98304]{0:T(1024)(128)(2,1)S(1)} %add_convert_fusion.1), channel_id=1, source_target_pairs={{0,4},{2,6},{4,0},{6,2},{8,12},{10,14},{12,8},{14,10},{1,5},{3,7},... | collective-permute-start | bytes 589832 | tf_op jit(solution)/shard_map/ppermute | solution.py:87
  107.4 7.5 %collective-permute-start.10 = (bf16[128,2688]{0,1:T(8,128)(2,1)S(1)}, bf16[128,2688]{0,1:T(8,128)(2,1)S(1)}, u32[]{:S(2)}, u32[]{:S(2)}) collective-permute-start(bf16[128,2688]{0,1:T(8,128)(2,1)S(1)} %constant_dynamic-slice_fusion.1), channel_id=1, source_target_pairs={{0,1},{1,0},{2,3},{3,2},{4,5},{5,4},{6,7},{7,6},{8,9},{9,8},{10,11... | collective-permute-start | bytes 2064392 | tf_op jit(solution)/shard_map/ppermute | solution.py:65
  112.4 10.8 %collective-permute-start.14 = (bf16[98304]{0:T(1024)(128)(2,1)S(1)}, bf16[98304]{0:T(1024)(128)(2,1)S(1)}, u32[]{:S(2)}, u32[]{:S(2)}) collective-permute-start(bf16[98304]{0:T(1024)(128)(2,1)S(1)} %add_convert_fusion), channel_id=1, source_target_pairs={{0,8},{2,10},{4,12},{6,14},{8,0},{10,2},{12,4},{14,6},{1,9},{3,11}... | collective-permute-start | bytes 589832 | tf_op jit(solution)/shard_map/ppermute | solution.py:87
  (35 other events, 90.3 us)

commit v14 on v11

--- a/solution.py
+++ b/solution.py
@@ -252,15 +252,15 @@
         return grad_pairs[first_row : first_row + shard_len]
 
     if send_count == 4:
-        far = passed_along(
-            jnp.concatenate([hop_block(3), hop_block(4)], axis=0).astype(jnp.bfloat16), "ctx", -2
+        one_down = passed_along(
+            jnp.concatenate([hop_block(1), hop_block(3)], axis=0).astype(jnp.bfloat16), "ctx", -1
         ).astype(jnp.float32)
-        near_sum = hop_block(1) + far[:shard_len]
-        next_sum = hop_block(2) + far[shard_len:]
+        two_down = passed_along(hop_block(4).astype(jnp.bfloat16), "ctx", -2).astype(jnp.float32)
+        pending = hop_block(2) + one_down[shard_len:] + two_down
         own_grads = (
             own_grads
-            + passed_along(near_sum.astype(jnp.bfloat16), "ctx", -1).astype(jnp.float32)
-            + passed_along(next_sum.astype(jnp.bfloat16), "ctx", -2).astype(jnp.float32)
+            + one_down[:shard_len]
+            + passed_along(pending.astype(jnp.bfloat16), "ctx", -2).astype(jnp.float32)
         )
     else:
         for hop_index in range(1, send_count + 1):

time: 124 us -> 124 us (level)
  no operation moved by 1% of the time
where the time goes in v14:
time: 124 us; the launch traced here: 123 us
  waiting for transfers between devices  46.8 us (38%)
  starting transfers between devices  22.4 us (18%)
  matrix products  20.3 us (16%)
  local copies, waits for them, and re-layouts  18 us (15%)
  other arithmetic  13.2 us (11%)
  between operations  2.29 us (2%)
    ppermute x6, waiting for transfers between devices, passed_along(): lax.ppermute(value, axis, [(source, source + steps) for source in range(l...  29.3 us
    ppermute x6, starting transfers between devices, passed_along(): lax.ppermute(value, axis, [(source, source + steps) for source in range(l...  16.4 us
    ppermute x3, waiting for transfers between devices, ctx_sum(): received = lax.ppermute(sent, 'ctx', [(i, i ^ step) for i in range(count)])  15.3 us
    unnamed x107, local copies, waits for them, and re-layouts  9.89 us
    dot_general x7, matrix products, matrix_product(): return jnp.dot(first_op, second_op, preferred_element_type=jnp.float32)  5.69 us
    dot_general x7, matrix products, multiply_by_transpose(): lax.dot_general(first_op, second_op, (((1,), (1,)), ((), ())), preferred_...  4.63 us
    ppermute x3, starting transfers between devices, ctx_sum(): received = lax.ppermute(sent, 'ctx', [(i, i ^ step) for i in range(count)])  4.29 us
    dot_general x6, matrix products, transpose_multiply(): lax.dot_general(first_op, second_op, (((0,), (0,)), ((), ())), preferred_...  3.45 us
  transfers between devices with their start and end apart: 16, of which 11 were waited for; matrix products, arithmetic and copies ran while one was open for 10% of the time, Pallas kernels for 0%

profile of v14, /device:TPU:0, one launch (start us, length us, event | category | flops | bytes accessed | tf_op | source)
XLA Modules:
  0.0 123.0 jit_solution(3287998647358371320)
XLA Ops:
  0.7 1.4 %fusion.19 = f32[128]{0:T(128)S(1)} fusion(bf16[128,2688]{1,0:T(8,128)(2,1)} %param.20), kind=kLoop, calls=%fused_computation.40 | loop fusion | flops 1032064 | bytes 688640 | tf_op jit(solution)/shard_map/reduce_sum | solution.py:21
  2.1 1.4 %fusion.14 = bf16[128,2688]{1,0:T(8,128)(2,1)S(1)} fusion(bf16[128,2688]{1,0:T(8,128)(2,1)} %param.20, f32[2688]{0:T(1024)} %param.24, f32[128]{0:T(128)S(1)} %add_rsqrt_fusion.3), kind=kLoop, calls=%fused_computation.35 | loop fusion | flops 1376256 | bytes 1387520 | tf_op jit(solution)/shard_map/convert_element_type | solution.py:128
  4.8 2.1 %copy.35 = bf16[2688,48]{1,0:T(8,128)(2,1)} copy(bf16[2688,48]{0,1:T(8,128)(2,1)} %param.32) | data formatting | bytes 516096 | tf_op args[12]
  9.2 2.6 %fusion.86 = (bf16[256,560]{0,1:T(8,128)(2,1)S(1)}, f32[256,560]{0,1:T(8,128)S(1)}) fusion(bf16[2688,48]{1,0:T(8,128)(2,1)S(1)} %copy-done.16, bf16[2688,128]{1,0:T(8,128)(2,1)S(1)} %copy-done.44, bf16[2688,128]{1,0:T(8,128)(2,1)} %param.29, bf16[2688,256]{1,0:T(8,128)(2,1)S(1)} %copy-done.43, bf16[128,2688]{1,0:T(8,128)(2,1)S(1)} %get-tuple-element.37, ...), kind=kOutput, calls=%fused_computation.201 | convolution fusion | flops 785641472 | bytes 5246976 | tf_op jit(solution)/shard_map/dot_general | solution.py:33
  13.1 4.5 %collective-permute-start.1 = (bf16[272,256]{0,1:T(8,128)(2,1)S(1)}, bf16[272,256]{0,1:T(8,128)(2,1)S(1)}, u32[]{:S(2)}, u32[]{:S(2)}) collective-permute-start(bf16[272,256]{0,1:T(8,128)(2,1)S(1)} %pad_maximum_fusion.17), channel_id=1, source_target_pairs={{0,4},{2,6},{4,8},{6,10},{8,12},{10,14},{1,5},{3,7},{5,9},{7,11},{... | collective-permute-start | bytes 417800 | tf_op jit(solution)/shard_map/ppermute | solution.py:17
  17.6 4.8 %collective-permute-done.1 = bf16[272,256]{0,1:T(8,128)(2,1)S(1)} collective-permute-done((bf16[272,256]{0,1:T(8,128)(2,1)S(1)}, bf16[272,256]{0,1:T(8,128)(2,1)S(1)}, u32[]{:S(2)}, u32[]{:S(2)}) %collective-permute-start.1) | collective-permute-done | bytes 139296 | tf_op jit(solution)/shard_map/ppermute | solution.py:17
  22.4 4.4 %collective-permute-start.2 = (bf16[272,256]{0,1:T(8,128)(2,1)S(1)}, bf16[272,256]{0,1:T(8,128)(2,1)S(1)}, u32[]{:S(2)}, u32[]{:S(2)}) collective-permute-start(bf16[272,256]{0,1:T(8,128)(2,1)S(1)} %collective-permute-done.1), channel_id=1, source_target_pairs={{0,4},{2,6},{4,8},{6,10},{8,12},{10,14},{1,5},{3,7},{5,9},{7,11},{... | collective-permute-start | bytes 417800 | tf_op jit(solution)/shard_map/ppermute | solution.py:17
  26.9 3.4 %collective-permute-start.3 = (bf16[544,256]{0,1:T(8,128)(2,1)S(1)}, bf16[544,256]{0,1:T(8,128)(2,1)S(1)}, u32[]{:S(2)}, u32[]{:S(2)}) collective-permute-start(bf16[544,256]{0,1:T(8,128)(2,1)S(1)} %pad_maximum_fusion.15), channel_id=1, source_target_pairs={{0,2},{2,4},{4,6},{6,8},{8,10},{10,12},{12,14},{1,3},{3,5},{5,7},{... | collective-permute-start | bytes 835592 | tf_op jit(solution)/shard_map/ppermute | solution.py:17
  30.9 5.9 %collective-permute-done.3 = bf16[544,256]{0,1:T(8,128)(2,1)S(1)} collective-permute-done((bf16[544,256]{0,1:T(8,128)(2,1)S(1)}, bf16[544,256]{0,1:T(8,128)(2,1)S(1)}, u32[]{:S(2)}, u32[]{:S(2)}) %collective-permute-start.3) | collective-permute-done | bytes 278560 | tf_op jit(solution)/shard_map/ppermute | solution.py:17
  37.9 2.4 %fusion.22 = f32[2,256,1280]{1,2,0:T(8,128)} fusion(pred[256,1280]{0,1:T(8,128)(4,1)S(1)} %fusion.26, bf16[1280,256]{0,1:T(8,128)(2,1)S(1)} %maximum_dynamic-update-slice_fusion, f32[256,256]{0,1:T(8,128)S(1)} %get-tuple-element.54, f32[128]{0:T(128)S(1)} %copy-done.39, f32[256,2]{0,1:T(2,128)S(1)} %add_rsqrt_fusion), kind=kOutput, calls=%fused_computation.51 | convolution fusion | flops 169936640 | bytes 3541504 | tf_op jit(solution)/shard_map/div | solution.py:194
  40.3 2.1 %fusion.32 = bf16[128,2,256]{2,0,1:T(8,128)(2,1)S(1)} fusion(f32[2,256,1280]{1,2,0:T(8,128)} %fusion.22, bf16[1280,256]{0,1:T(8,128)(2,1)S(1)} %maximum_dynamic-update-slice_fusion, f32[256]{0:T(256)S(1)} %fusion.73), kind=kOutput, calls=%fused_computation.65 | convolution fusion | flops 168558592 | bytes 3081216 | tf_op jit(solution)/shard_map/hts,sd->thd/dot_general | solution.py:196
  44.6 1.6 %collective-permute-done.5 = bf16[128,16]{0,1:T(8,128)(2,1)} collective-permute-done((bf16[128,16]{0,1:T(8,128)(2,1)S(1)}, bf16[128,16]{0,1:T(8,128)(2,1)}, u32[]{:S(2)}, u32[]{:S(2)}) %collective-permute-start.5) | collective-permute-done | bytes 4128 | tf_op jit(solution)/shard_map/ppermute | solution.py:65
  46.9 1.7 %multiply_reduce_fusion.2 = (f32[128]{0:T(128)S(1)}, f32[128,2688]{1,0:T(8,128)S(1)}) fusion(bf16[128,16]{0,1:T(8,128)(2,1)S(1)} %add_convert_fusion.3, bf16[16,2688]{1,0:T(8,128)(2,1)S(1)} %copy-done.18, bf16[128,2688]{1,0:T(8,128)(2,1)} %collective-permute-done.4, bf16[256,2688]{1,0:T(8,128)(2,1)S(1)} %convolution_convert_fusion.1, s32[]{:T(128)S(6)} %select_n.62), kind=kOutput, calls=%fused_computation.47 | convolution fusion | flops 13418368 | bytes 2843140 | tf_op jit(solution)/shard_map/dot_general | solution.py:33
  62.3 8.2 %collective-permute-done.8 = bf16[512,256]{0,1:T(8,128)(2,1)S(1)} collective-permute-done((bf16[512,256]{0,1:T(8,128)(2,1)S(1)}, bf16[512,256]{0,1:T(8,128)(2,1)S(1)}, u32[]{:S(2)}, u32[]{:S(2)}) %collective-permute-start.8) | collective-permute-done | bytes 262176 | tf_op jit(solution)/shard_map/ppermute | solution.py:17
  70.6 4.6 %collective-permute-done.9 = bf16[256,256]{0,1:T(8,128)(2,1)S(1)} collective-permute-done((bf16[256,256]{0,1:T(8,128)(2,1)S(1)}, bf16[256,256]{0,1:T(8,128)(2,1)S(1)}, u32[]{:S(2)}, u32[]{:S(2)}) %collective-permute-start.9) | collective-permute-done | bytes 131104 | tf_op jit(solution)/shard_map/ppermute | solution.py:17
  75.3 1.5 %collective-permute-start.10 = (bf16[256,256]{0,1:T(8,128)(2,1)S(1)}, bf16[256,256]{0,1:T(8,128)(2,1)S(1)}, u32[]{:S(2)}, u32[]{:S(2)}) collective-permute-start(bf16[256,256]{0,1:T(8,128)(2,1)S(1)} %fusion.57), channel_id=1, source_target_pairs={{4,0},{6,2},{8,4},{10,6},{12,8},{14,10},{5,1},{7,3},{9,5},{11,7},{... | collective-permute-start | bytes 393224 | tf_op jit(solution)/shard_map/ppermute | solution.py:17
  76.9 5.5 %collective-permute-done.10 = bf16[256,256]{0,1:T(8,128)(2,1)S(1)} collective-permute-done((bf16[256,256]{0,1:T(8,128)(2,1)S(1)}, bf16[256,256]{0,1:T(8,128)(2,1)S(1)}, u32[]{:S(2)}, u32[]{:S(2)}) %collective-permute-start.10) | collective-permute-done | bytes 131104 | tf_op jit(solution)/shard_map/ppermute | solution.py:17
  87.0 1.7 %add_convert_fusion.2 = bf16[1344,48]{0,1:T(8,128)(2,1)} fusion(bf16[1344,48]{0,1:T(8,128)(2,1)} %collective-permute-done.12, bf16[2688,48]{0,1:T(8,128)(2,1)S(1)} %convolution_convert_fusion.2, s32[]{:T(128)S(6)} %select_n.69), kind=kLoop, calls=%fused_computation.104 | loop fusion | flops 258048 | bytes 387076 | tf_op jit(solution)/shard_map/convert.15
  94.2 3.2 %convolution_convert_fusion = bf16[256,2688]{1,0:T(8,128)(2,1)S(1)} fusion(bf16[256,560]{0,1:T(8,128)(2,1)} %copy-done.21, bf16[2688,48]{1,0:T(8,128)(2,1)S(1)} %copy-done.17, bf16[2688,128]{1,0:T(8,128)(2,1)} %param.30, bf16[2688,128]{1,0:T(8,128)(2,1)} %param.29, bf16[2688,256]{1,0:T(8,128)(2,1)} %param.28), kind=kOutput, calls=%fused_computation.1 | convolution fusion | flops 783433728 | bytes 4673536 | tf_op jit(solution)/shard_map/dot_general | solution.py:37
  97.4 4.1 %collective-permute-done.13 = bf16[98304]{0:T(1024)(128)(2,1)S(1)} collective-permute-done((bf16[98304]{0:T(1024)(128)(2,1)S(1)}, bf16[98304]{0:T(1024)(128)(2,1)S(1)}, u32[]{:S(2)}, u32[]{:S(2)}) %collective-permute-start.13) | collective-permute-done | bytes 196640 | tf_op jit(solution)/shard_map/ppermute | solution.py:87
  101.5 1.6 %collective-permute-start.14 = (bf16[98304]{0:T(1024)(128)(2,1)S(1)}, bf16[98304]{0:T(1024)(128)(2,1)S(1)}, u32[]{:S(2)}, u32[]{:S(2)}) collective-permute-start(bf16[98304]{0:T(1024)(128)(2,1)S(1)} %add_convert_fusion.1), channel_id=1, source_target_pairs={{0,4},{2,6},{4,0},{6,2},{8,12},{10,14},{12,8},{14,10},{1,5},{3,7},... | collective-permute-start | bytes 589832 | tf_op jit(solution)/shard_map/ppermute | solution.py:87
  103.3 4.8 %collective-permute-done.14 = bf16[98304]{0:T(1024)(128)(2,1)S(1)} collective-permute-done((bf16[98304]{0:T(1024)(128)(2,1)S(1)}, bf16[98304]{0:T(1024)(128)(2,1)S(1)}, u32[]{:S(2)}, u32[]{:S(2)}) %collective-permute-start.14) | collective-permute-done | bytes 196640 | tf_op jit(solution)/shard_map/ppermute | solution.py:87
  108.2 2.6 %collective-permute-start.15 = (bf16[98304]{0:T(1024)(128)(2,1)S(1)}, bf16[98304]{0:T(1024)(128)(2,1)S(1)}, u32[]{:S(2)}, u32[]{:S(2)}) collective-permute-start(bf16[98304]{0:T(1024)(128)(2,1)S(1)} %add_convert_fusion), channel_id=1, source_target_pairs={{0,8},{2,10},{4,12},{6,14},{8,0},{10,2},{12,4},{14,6},{1,9},{3,11}... | collective-permute-start | bytes 589832 | tf_op jit(solution)/shard_map/ppermute | solution.py:87
  112.7 6.3 %collective-permute-done.15 = bf16[98304]{0:T(1024)(128)(2,1)S(1)} collective-permute-done((bf16[98304]{0:T(1024)(128)(2,1)S(1)}, bf16[98304]{0:T(1024)(128)(2,1)S(1)}, u32[]{:S(2)}, u32[]{:S(2)}) %collective-permute-start.15) | collective-permute-done | bytes 196640 | tf_op jit(solution)/shard_map/ppermute | solution.py:87
  (207 shorter events, 38.2 us)
Async XLA Ops:
  0.6 41.8 %copy-start = (bf16[256,2688]{1,0:T(8,128)(2,1)S(1)}, bf16[256,2688]{1,0:T(8,128)(2,1)}, u32[]{:S(2)}) copy-start(bf16[256,2688]{1,0:T(8,128)(2,1)} %param.31) | copy-start | bytes 4128772
  3.5 3.5 %collective-permute-start = (bf16[128,2688]{1,0:T(8,128)(2,1)S(1)}, bf16[128,2688]{1,0:T(8,128)(2,1)S(1)}, u32[]{:S(2)}, u32[]{:S(2)}) collective-permute-start(bf16[128,2688]{1,0:T(8,128)(2,1)S(1)} %fusion.14), channel_id=1, source_target_pairs={{0,1},{1,0},{2,3},{3,2},{4,5},{5,4},{6,7},{7,6},{8,9},{9,8},{10,11... | collective-permute-start | bytes 2064392 | tf_op jit(solution)/shard_map/ppermute | solution.py:72
  6.9 33.4 %copy-start.41 = (f32[256]{0:T(256)}, f32[256]{0:T(256)S(1)}, u32[]{:S(2)}) copy-start(f32[256]{0:T(256)S(1)} %fusion.73) | copy-start | bytes 3076
  12.6 25.3 %copy-start.3 = (f32[256,256]{0,1:T(8,128)}, f32[256,256]{0,1:T(8,128)S(1)}, u32[]{:S(2)}) copy-start(f32[256,256]{0,1:T(8,128)S(1)} %get-tuple-element.54) | copy-start | bytes 786436
  12.6 18.3 %copy-start.27 = (f32[256]{0:T(256)}, f32[256]{0:T(256)S(1)}, u32[]{:S(2)}) copy-start(f32[256]{0:T(256)S(1)} %add_rsqrt_fusion.1) | copy-start | bytes 3076
  13.1 24.8 %copy-start.39 = (f32[128]{0:T(128)S(1)}, f32[128]{0:T(128)}, u32[]{:S(2)}) copy-start(f32[128]{0:T(128)} %param.25) | copy-start | bytes 1540
  13.1 9.3 %collective-permute-start.1 = (bf16[272,256]{0,1:T(8,128)(2,1)S(1)}, bf16[272,256]{0,1:T(8,128)(2,1)S(1)}, u32[]{:S(2)}, u32[]{:S(2)}) collective-permute-start(bf16[272,256]{0,1:T(8,128)(2,1)S(1)} %pad_maximum_fusion.17), channel_id=1, source_target_pairs={{0,4},{2,6},{4,8},{6,10},{8,12},{10,14},{1,5},{3,7},{5,9},{7,11},{... | collective-permute-start | bytes 417800 | tf_op jit(solution)/shard_map/ppermute | solution.py:17
  17.6 22.7 %copy-start.25 = (f32[256,2]{0,1:T(2,128)}, f32[256,2]{0,1:T(2,128)S(1)}, u32[]{:S(2)}) copy-start(f32[256,2]{0,1:T(2,128)S(1)} %add_rsqrt_fusion) | copy-start | bytes 6148
  22.4 8.4 %collective-permute-start.2 = (bf16[272,256]{0,1:T(8,128)(2,1)S(1)}, bf16[272,256]{0,1:T(8,128)(2,1)S(1)}, u32[]{:S(2)}, u32[]{:S(2)}) collective-permute-start(bf16[272,256]{0,1:T(8,128)(2,1)S(1)} %collective-permute-done.1), channel_id=1, source_target_pairs={{0,4},{2,6},{4,8},{6,10},{8,12},{10,14},{1,5},{3,7},{5,9},{7,11},{... | collective-permute-start | bytes 417800 | tf_op jit(solution)/shard_map/ppermute | solution.py:17
  26.9 9.9 %collective-permute-start.3 = (bf16[544,256]{0,1:T(8,128)(2,1)S(1)}, bf16[544,256]{0,1:T(8,128)(2,1)S(1)}, u32[]{:S(2)}, u32[]{:S(2)}) collective-permute-start(bf16[544,256]{0,1:T(8,128)(2,1)S(1)} %pad_maximum_fusion.15), channel_id=1, source_target_pairs={{0,2},{2,4},{4,6},{6,8},{8,10},{10,12},{12,14},{1,3},{3,5},{5,7},{... | collective-permute-start | bytes 835592 | tf_op jit(solution)/shard_map/ppermute | solution.py:17
  43.9 3.0 %collective-permute-start.4 = (bf16[128,2688]{1,0:T(8,128)(2,1)}, bf16[128,2688]{1,0:T(8,128)(2,1)}, u32[]{:S(2)}, u32[]{:S(2)}) collective-permute-start(bf16[128,2688]{1,0:T(8,128)(2,1)} %constant_dynamic-slice_fusion.3), channel_id=1, source_target_pairs={{0,1},{1,0},{2,3},{3,2},{4,5},{5,4},{6,7},{7,6},{8,9},{9,8},{10,11... | collective-permute-start | bytes 2064392 | tf_op jit(solution)/shard_map/ppermute | solution.py:65
  44.1 2.1 %collective-permute-start.5 = (bf16[128,16]{0,1:T(8,128)(2,1)S(1)}, bf16[128,16]{0,1:T(8,128)(2,1)}, u32[]{:S(2)}, u32[]{:S(2)}) collective-permute-start(bf16[128,16]{0,1:T(8,128)(2,1)S(1)} %constant_dynamic-slice_fusion.2), channel_id=1, source_target_pairs={{0,1},{1,0},{2,3},{3,2},{4,5},{5,4},{6,7},{7,6},{8,9},{9,8},{10,11... | collective-permute-start | bytes 12296 | tf_op jit(solution)/shard_map/ppermute | solution.py:65
  50.5 1.2 %collective-permute-start.7 = (bf16[128,32]{0,1:T(8,128)(2,1)S(1)}, bf16[128,32]{0,1:T(8,128)(2,1)S(1)}, u32[]{:S(2)}, u32[]{:S(2)}) collective-permute-start(bf16[128,32]{0,1:T(8,128)(2,1)S(1)} %pad_maximum_fusion.20), channel_id=1, source_target_pairs={{0,1},{1,0},{2,3},{3,2},{4,5},{5,4},{6,7},{7,6},{8,9},{9,8},{10,11... | collective-permute-start | bytes 24584 | tf_op jit(solution)/shard_map/ppermute | solution.py:72
  50.7 2.3 %collective-permute-start.6 = (bf16[128,2688]{1,0:T(8,128)(2,1)S(1)}, bf16[128,2688]{1,0:T(8,128)(2,1)}, u32[]{:S(2)}, u32[]{:S(2)}) collective-permute-start(bf16[128,2688]{1,0:T(8,128)(2,1)S(1)} %get-tuple-element.32), channel_id=1, source_target_pairs={{0,1},{1,0},{2,3},{3,2},{4,5},{5,4},{6,7},{7,6},{8,9},{9,8},{10,11... | collective-permute-start | bytes 2064392 | tf_op jit(solution)/shard_map/ppermute | solution.py:72
  59.4 11.2 %collective-permute-start.8 = (bf16[512,256]{0,1:T(8,128)(2,1)S(1)}, bf16[512,256]{0,1:T(8,128)(2,1)S(1)}, u32[]{:S(2)}, u32[]{:S(2)}) collective-permute-start(bf16[512,256]{0,1:T(8,128)(2,1)S(1)} %pad_maximum_fusion.16), channel_id=1, source_target_pairs={{2,0},{4,2},{6,4},{8,6},{10,8},{12,10},{14,12},{3,1},{5,3},{7,5},{... | collective-permute-start | bytes 786440 | tf_op jit(solution)/shard_map/ppermute | solution.py:17
  61.0 14.2 %collective-permute-start.9 = (bf16[256,256]{0,1:T(8,128)(2,1)S(1)}, bf16[256,256]{0,1:T(8,128)(2,1)S(1)}, u32[]{:S(2)}, u32[]{:S(2)}) collective-permute-start(bf16[256,256]{0,1:T(8,128)(2,1)S(1)} %get-tuple-element.38), channel_id=1, source_target_pairs={{4,0},{6,2},{8,4},{10,6},{12,8},{14,10},{5,1},{7,3},{9,5},{11,7},{... | collective-permute-start | bytes 393224 | tf_op jit(solution)/shard_map/ppermute | solution.py:17
  75.3 7.1 %collective-permute-start.10 = (bf16[256,256]{0,1:T(8,128)(2,1)S(1)}, bf16[256,256]{0,1:T(8,128)(2,1)S(1)}, u32[]{:S(2)}, u32[]{:S(2)}) collective-permute-start(bf16[256,256]{0,1:T(8,128)(2,1)S(1)} %fusion.57), channel_id=1, source_target_pairs={{4,0},{6,2},{8,4},{10,6},{12,8},{14,10},{5,1},{7,3},{9,5},{11,7},{... | collective-permute-start | bytes 393224 | tf_op jit(solution)/shard_map/ppermute | solution.py:17
  84.4 2.7 %collective-permute-start.12 = (bf16[1344,48]{0,1:T(8,128)(2,1)}, bf16[1344,48]{0,1:T(8,128)(2,1)}, u32[]{:S(2)}, u32[]{:S(2)}) collective-permute-start(bf16[1344,48]{0,1:T(8,128)(2,1)} %constant_dynamic-slice_fusion), channel_id=1, source_target_pairs={{0,1},{1,0},{2,3},{3,2},{4,5},{5,4},{6,7},{7,6},{8,9},{9,8},{10,11... | collective-permute-start | bytes 387080 | tf_op jit(solution)/shard_map/ppermute | solution.py:65
  94.2 7.3 %collective-permute-start.13 = (bf16[98304]{0:T(1024)(128)(2,1)S(1)}, bf16[98304]{0:T(1024)(128)(2,1)S(1)}, u32[]{:S(2)}, u32[]{:S(2)}) collective-permute-start(bf16[98304]{0:T(1024)(128)(2,1)S(1)} %constant_dynamic-update-slice_fusion.12), channel_id=1, source_target_pairs={{0,2},{2,0},{4,6},{6,4},{8,10},{10,8},{12,14},{14,12},{1,3},{3,1},... | collective-permute-start | bytes 589832 | tf_op jit(solution)/shard_map/ppermute | solution.py:87
  97.3 13.5 %copy-start.20 = (f32[2688]{0:T(1024)S(1)}, f32[2688]{0:T(1024)}, u32[]{:S(2)}) copy-start(f32[2688]{0:T(1024)} %param.24) | copy-start | bytes 32260
  97.4 13.5 %copy-start.35 = (f32[128]{0:T(128)S(1)}, f32[128]{0:T(128)}, u32[]{:S(2)}) copy-start(f32[128]{0:T(128)} %copy-done.34) | copy-start | bytes 1540
  101.5 6.6 %collective-permute-start.14 = (bf16[98304]{0:T(1024)(128)(2,1)S(1)}, bf16[98304]{0:T(1024)(128)(2,1)S(1)}, u32[]{:S(2)}, u32[]{:S(2)}) collective-permute-start(bf16[98304]{0:T(1024)(128)(2,1)S(1)} %add_convert_fusion.1), channel_id=1, source_target_pairs={{0,4},{2,6},{4,0},{6,2},{8,12},{10,14},{12,8},{14,10},{1,5},{3,7},... | collective-permute-start | bytes 589832 | tf_op jit(solution)/shard_map/ppermute | solution.py:87
  103.2 7.6 %collective-permute-start.11 = (bf16[128,2688]{1,0:T(8,128)(2,1)S(1)}, bf16[128,2688]{1,0:T(8,128)(2,1)S(1)}, u32[]{:S(2)}, u32[]{:S(2)}) collective-permute-start(bf16[128,2688]{1,0:T(8,128)(2,1)S(1)} %constant_dynamic-slice_fusion.1), channel_id=1, source_target_pairs={{0,1},{1,0},{2,3},{3,2},{4,5},{5,4},{6,7},{7,6},{8,9},{9,8},{10,11... | collective-permute-start | bytes 2064392 | tf_op jit(solution)/shard_map/ppermute | solution.py:65
  108.2 10.8 %collective-permute-start.15 = (bf16[98304]{0:T(1024)(128)(2,1)S(1)}, bf16[98304]{0:T(1024)(128)(2,1)S(1)}, u32[]{:S(2)}, u32[]{:S(2)}) collective-permute-start(bf16[98304]{0:T(1024)(128)(2,1)S(1)} %add_convert_fusion), channel_id=1, source_target_pairs={{0,8},{2,10},{4,12},{6,14},{8,0},{10,2},{12,4},{14,6},{1,9},{3,11}... | collective-permute-start | bytes 589832 | tf_op jit(solution)/shard_map/ppermute | solution.py:87
  (37 other events, 122.2 us)

commit v15 on v11

--- a/solution.py
+++ b/solution.py
@@ -81,12 +81,12 @@
     if count & (count - 1):
         return [lax.psum(p.astype(jnp.bfloat16), "ctx").astype(jnp.float32) for p in parts]
     flat = jnp.concatenate([p.astype(jnp.float32).reshape(-1) for p in parts])
-    step = 1
-    while step < count:
+    step = count // 2
+    while step >= 1:
         sent = flat.astype(jnp.bfloat16)
         received = lax.ppermute(sent, "ctx", [(i, i ^ step) for i in range(count)])
         flat = sent.astype(jnp.float32) + received.astype(jnp.float32)
-        step *= 2
+        step //= 2
     results, offset = [], 0
     for p in parts:
         results.append(flat[offset : offset + p.size].reshape(p.shape))

time: 124 us -> 124 us (level)
  waiting for transfers between devices: 45.6 us -> 47.4 us
  starting transfers between devices: 23.3 us -> 21.6 us
    ppermute x3, waiting for transfers between devices: 14.3 us -> 16.1 us  [ctx_sum(): received = lax.ppermute(sent, 'ctx', [(i, i ^ step) for i in range(count)])]
    ppermute x3, starting transfers between devices: 5.28 us -> 3.49 us  [ctx_sum(): received = lax.ppermute(sent, 'ctx', [(i, i ^ step) for i in range(count)])]
where the time goes in v15:
time: 124 us; the launch traced here: 123 us
  waiting for transfers between devices  47.4 us (38%)
  starting transfers between devices  21.6 us (17%)
  matrix products  20.3 us (16%)
  local copies, waits for them, and re-layouts  18 us (15%)
  other arithmetic  13.2 us (11%)
  between operations  2.3 us (2%)
    ppermute x6, waiting for transfers between devices, passed_along(): lax.ppermute(value, axis, [(source, source + steps) for source in range(l...  29 us
    ppermute x6, starting transfers between devices, passed_along(): lax.ppermute(value, axis, [(source, source + steps) for source in range(l...  16.4 us
    ppermute x3, waiting for transfers between devices, ctx_sum(): received = lax.ppermute(sent, 'ctx', [(i, i ^ step) for i in range(count)])  16.1 us
    unnamed x107, local copies, waits for them, and re-layouts  9.9 us
    dot_general x7, matrix products, matrix_product(): return jnp.dot(first_op, second_op, preferred_element_type=jnp.float32)  5.7 us
    dot_general x7, matrix products, multiply_by_transpose(): lax.dot_general(first_op, second_op, (((1,), (1,)), ((), ())), preferred_...  4.63 us
    ppermute x3, starting transfers between devices, ctx_sum(): received = lax.ppermute(sent, 'ctx', [(i, i ^ step) for i in range(count)])  3.49 us
    dot_general x6, matrix products, transpose_multiply(): lax.dot_general(first_op, second_op, (((0,), (0,)), ((), ())), preferred_...  3.45 us
  transfers between devices with their start and end apart: 16, of which 11 were waited for; matrix products, arithmetic and copies ran while one was open for 10% of the time, Pallas kernels for 0%

profile of v15, /device:TPU:0, one launch (start us, length us, event | category | flops | bytes accessed | tf_op | source)
XLA Modules:
  0.0 122.8 jit_solution(3318447812254212216)
XLA Ops:
  0.7 1.4 %fusion.19 = f32[128]{0:T(128)S(1)} fusion(bf16[128,2688]{1,0:T(8,128)(2,1)} %param.20), kind=kLoop, calls=%fused_computation.42 | loop fusion | flops 1032064 | bytes 688640 | tf_op jit(solution)/shard_map/reduce_sum | solution.py:21
  2.1 1.4 %fusion.14 = bf16[128,2688]{1,0:T(8,128)(2,1)S(1)} fusion(bf16[128,2688]{1,0:T(8,128)(2,1)} %param.20, f32[2688]{0:T(1024)} %param.24, f32[128]{0:T(128)S(1)} %add_rsqrt_fusion.3), kind=kLoop, calls=%fused_computation.37 | loop fusion | flops 1376256 | bytes 1387520 | tf_op jit(solution)/shard_map/convert_element_type | solution.py:128
  4.8 2.1 %copy.35 = bf16[2688,48]{1,0:T(8,128)(2,1)} copy(bf16[2688,48]{0,1:T(8,128)(2,1)} %param.32) | data formatting | bytes 516096 | tf_op args[12]
  9.2 2.6 %fusion.88 = (bf16[256,560]{0,1:T(8,128)(2,1)S(1)}, f32[256,560]{0,1:T(8,128)S(1)}) fusion(bf16[2688,48]{1,0:T(8,128)(2,1)S(1)} %copy-done.16, bf16[2688,128]{1,0:T(8,128)(2,1)S(1)} %copy-done.44, bf16[2688,128]{1,0:T(8,128)(2,1)} %param.29, bf16[2688,256]{1,0:T(8,128)(2,1)S(1)} %copy-done.43, bf16[128,2688]{1,0:T(8,128)(2,1)S(1)} %get-tuple-element.39, ...), kind=kOutput, calls=%fused_computation.205 | convolution fusion | flops 785641472 | bytes 5246976 | tf_op jit(solution)/shard_map/dot_general | solution.py:33
  13.1 4.5 %collective-permute-start.1 = (bf16[272,256]{0,1:T(8,128)(2,1)S(1)}, bf16[272,256]{0,1:T(8,128)(2,1)S(1)}, u32[]{:S(2)}, u32[]{:S(2)}) collective-permute-start(bf16[272,256]{0,1:T(8,128)(2,1)S(1)} %pad_maximum_fusion.17), channel_id=1, source_target_pairs={{0,4},{2,6},{4,8},{6,10},{8,12},{10,14},{1,5},{3,7},{5,9},{7,11},{... | collective-permute-start | bytes 417800 | tf_op jit(solution)/shard_map/ppermute | solution.py:17
  17.6 4.8 %collective-permute-done.1 = bf16[272,256]{0,1:T(8,128)(2,1)S(1)} collective-permute-done((bf16[272,256]{0,1:T(8,128)(2,1)S(1)}, bf16[272,256]{0,1:T(8,128)(2,1)S(1)}, u32[]{:S(2)}, u32[]{:S(2)}) %collective-permute-start.1) | collective-permute-done | bytes 139296 | tf_op jit(solution)/shard_map/ppermute | solution.py:17
  22.4 4.4 %collective-permute-start.2 = (bf16[272,256]{0,1:T(8,128)(2,1)S(1)}, bf16[272,256]{0,1:T(8,128)(2,1)S(1)}, u32[]{:S(2)}, u32[]{:S(2)}) collective-permute-start(bf16[272,256]{0,1:T(8,128)(2,1)S(1)} %collective-permute-done.1), channel_id=1, source_target_pairs={{0,4},{2,6},{4,8},{6,10},{8,12},{10,14},{1,5},{3,7},{5,9},{7,11},{... | collective-permute-start | bytes 417800 | tf_op jit(solution)/shard_map/ppermute | solution.py:17
  26.9 3.4 %collective-permute-start.3 = (bf16[544,256]{0,1:T(8,128)(2,1)S(1)}, bf16[544,256]{0,1:T(8,128)(2,1)S(1)}, u32[]{:S(2)}, u32[]{:S(2)}) collective-permute-start(bf16[544,256]{0,1:T(8,128)(2,1)S(1)} %pad_maximum_fusion.15), channel_id=1, source_target_pairs={{0,2},{2,4},{4,6},{6,8},{8,10},{10,12},{12,14},{1,3},{3,5},{5,7},{... | collective-permute-start | bytes 835592 | tf_op jit(solution)/shard_map/ppermute | solution.py:17
  30.9 5.9 %collective-permute-done.3 = bf16[544,256]{0,1:T(8,128)(2,1)S(1)} collective-permute-done((bf16[544,256]{0,1:T(8,128)(2,1)S(1)}, bf16[544,256]{0,1:T(8,128)(2,1)S(1)}, u32[]{:S(2)}, u32[]{:S(2)}) %collective-permute-start.3) | collective-permute-done | bytes 278560 | tf_op jit(solution)/shard_map/ppermute | solution.py:17
  37.9 2.4 %fusion.22 = f32[2,256,1280]{1,2,0:T(8,128)} fusion(pred[256,1280]{0,1:T(8,128)(4,1)S(1)} %fusion.26, bf16[1280,256]{0,1:T(8,128)(2,1)S(1)} %maximum_dynamic-update-slice_fusion, f32[256,256]{0,1:T(8,128)S(1)} %get-tuple-element.55, f32[128]{0:T(128)S(1)} %copy-done.39, f32[256,2]{0,1:T(2,128)S(1)} %add_rsqrt_fusion), kind=kOutput, calls=%fused_computation.53 | convolution fusion | flops 169936640 | bytes 3541504 | tf_op jit(solution)/shard_map/div | solution.py:194
  40.3 2.1 %fusion.32 = bf16[128,2,256]{2,0,1:T(8,128)(2,1)S(1)} fusion(f32[2,256,1280]{1,2,0:T(8,128)} %fusion.22, bf16[1280,256]{0,1:T(8,128)(2,1)S(1)} %maximum_dynamic-update-slice_fusion, f32[256]{0:T(256)S(1)} %fusion.75), kind=kOutput, calls=%fused_computation.67 | convolution fusion | flops 168558592 | bytes 3081216 | tf_op jit(solution)/shard_map/hts,sd->thd/dot_general | solution.py:196
  44.6 1.6 %collective-permute-done.5 = bf16[128,16]{0,1:T(8,128)(2,1)} collective-permute-done((bf16[128,16]{0,1:T(8,128)(2,1)S(1)}, bf16[128,16]{0,1:T(8,128)(2,1)}, u32[]{:S(2)}, u32[]{:S(2)}) %collective-permute-start.5) | collective-permute-done | bytes 4128 | tf_op jit(solution)/shard_map/ppermute | solution.py:65
  46.9 1.7 %multiply_reduce_fusion.2 = (f32[128]{0:T(128)S(1)}, f32[128,2688]{1,0:T(8,128)S(1)}) fusion(bf16[128,16]{0,1:T(8,128)(2,1)S(1)} %add_convert_fusion.3, bf16[16,2688]{1,0:T(8,128)(2,1)S(1)} %copy-done.18, bf16[128,2688]{1,0:T(8,128)(2,1)} %collective-permute-done.4, bf16[256,2688]{1,0:T(8,128)(2,1)S(1)} %convolution_convert_fusion.1, s32[]{:T(128)S(6)} %select_n.62), kind=kOutput, calls=%fused_computation.49 | convolution fusion | flops 13418368 | bytes 2843140 | tf_op jit(solution)/shard_map/dot_general | solution.py:33
  61.0 11.4 %collective-permute-done.8 = bf16[512,256]{0,1:T(8,128)(2,1)S(1)} collective-permute-done((bf16[512,256]{0,1:T(8,128)(2,1)S(1)}, bf16[512,256]{0,1:T(8,128)(2,1)S(1)}, u32[]{:S(2)}, u32[]{:S(2)}) %collective-permute-start.8) | collective-permute-done | bytes 262176 | tf_op jit(solution)/shard_map/ppermute | solution.py:17
  73.9 1.5 %collective-permute-start.10 = (bf16[256,256]{0,1:T(8,128)(2,1)S(1)}, bf16[256,256]{0,1:T(8,128)(2,1)S(1)}, u32[]{:S(2)}, u32[]{:S(2)}) collective-permute-start(bf16[256,256]{0,1:T(8,128)(2,1)S(1)} %get-tuple-element.33), channel_id=1, source_target_pairs={{4,0},{6,2},{8,4},{10,6},{12,8},{14,10},{5,1},{7,3},{9,5},{11,7},{... | collective-permute-start | bytes 393224 | tf_op jit(solution)/shard_map/ppermute | solution.py:17
  75.5 4.2 %collective-permute-done.9 = bf16[256,256]{0,1:T(8,128)(2,1)S(1)} collective-permute-done((bf16[256,256]{0,1:T(8,128)(2,1)S(1)}, bf16[256,256]{0,1:T(8,128)(2,1)S(1)}, u32[]{:S(2)}, u32[]{:S(2)}) %collective-permute-start.9) | collective-permute-done | bytes 131104 | tf_op jit(solution)/shard_map/ppermute | solution.py:17
  79.7 2.5 %collective-permute-done.10 = bf16[256,256]{0,1:T(8,128)(2,1)S(1)} collective-permute-done((bf16[256,256]{0,1:T(8,128)(2,1)S(1)}, bf16[256,256]{0,1:T(8,128)(2,1)S(1)}, u32[]{:S(2)}, u32[]{:S(2)}) %collective-permute-start.10) | collective-permute-done | bytes 131104 | tf_op jit(solution)/shard_map/ppermute | solution.py:17
  86.7 1.7 %add_convert_fusion.2 = bf16[1344,48]{0,1:T(8,128)(2,1)} fusion(bf16[1344,48]{0,1:T(8,128)(2,1)} %collective-permute-done.12, bf16[2688,48]{0,1:T(8,128)(2,1)S(1)} %convolution_convert_fusion.2, s32[]{:T(128)S(6)} %select_n.69), kind=kLoop, calls=%fused_computation.106 | loop fusion | flops 258048 | bytes 387076 | tf_op jit(solution)/shard_map/convert.15
  93.9 1.9 %collective-permute-start.13 = (bf16[98304]{0:T(1024)(128)(2,1)S(1)}, bf16[98304]{0:T(1024)(128)(2,1)S(1)}, u32[]{:S(2)}, u32[]{:S(2)}) collective-permute-start(bf16[98304]{0:T(1024)(128)(2,1)S(1)} %constant_dynamic-update-slice_fusion.12), channel_id=1, source_target_pairs={{0,8},{2,10},{4,12},{6,14},{8,0},{10,2},{12,4},{14,6},{1,9},{3,11}... | collective-permute-start | bytes 589832 | tf_op jit(solution)/shard_map/ppermute | solution.py:87
  95.8 3.2 %convolution_convert_fusion = bf16[256,2688]{1,0:T(8,128)(2,1)S(1)} fusion(bf16[256,560]{0,1:T(8,128)(2,1)} %copy-done.21, bf16[2688,48]{1,0:T(8,128)(2,1)S(1)} %copy-done.17, bf16[2688,128]{1,0:T(8,128)(2,1)} %param.30, bf16[2688,128]{1,0:T(8,128)(2,1)} %param.29, bf16[2688,256]{1,0:T(8,128)(2,1)} %param.28), kind=kOutput, calls=%fused_computation.1 | convolution fusion | flops 783433728 | bytes 4673536 | tf_op jit(solution)/shard_map/dot_general | solution.py:37
  99.0 7.3 %collective-permute-done.13 = bf16[98304]{0:T(1024)(128)(2,1)S(1)} collective-permute-done((bf16[98304]{0:T(1024)(128)(2,1)S(1)}, bf16[98304]{0:T(1024)(128)(2,1)S(1)}, u32[]{:S(2)}, u32[]{:S(2)}) %collective-permute-start.13) | collective-permute-done | bytes 196640 | tf_op jit(solution)/shard_map/ppermute | solution.py:87
  106.6 6.4 %collective-permute-done.14 = bf16[98304]{0:T(1024)(128)(2,1)S(1)} collective-permute-done((bf16[98304]{0:T(1024)(128)(2,1)S(1)}, bf16[98304]{0:T(1024)(128)(2,1)S(1)}, u32[]{:S(2)}, u32[]{:S(2)}) %collective-permute-start.14) | collective-permute-done | bytes 196640 | tf_op jit(solution)/shard_map/ppermute | solution.py:87
  113.0 1.5 %collective-permute-start.15 = (bf16[98304]{0:T(1024)(128)(2,1)S(1)}, bf16[98304]{0:T(1024)(128)(2,1)S(1)}, u32[]{:S(2)}, u32[]{:S(2)}) collective-permute-start(bf16[98304]{0:T(1024)(128)(2,1)S(1)} %add_convert_fusion), channel_id=1, source_target_pairs={{0,2},{2,0},{4,6},{6,4},{8,10},{10,8},{12,14},{14,12},{1,3},{3,1},... | collective-permute-start | bytes 589832 | tf_op jit(solution)/shard_map/ppermute | solution.py:87
  116.3 2.4 %collective-permute-done.15 = bf16[98304]{0:T(1024)(128)(2,1)S(1)} collective-permute-done((bf16[98304]{0:T(1024)(128)(2,1)S(1)}, bf16[98304]{0:T(1024)(128)(2,1)S(1)}, u32[]{:S(2)}, u32[]{:S(2)}) %collective-permute-start.15) | collective-permute-done | bytes 196640 | tf_op jit(solution)/shard_map/ppermute | solution.py:87
  (207 shorter events, 38.3 us)
Async XLA Ops:
  0.6 41.8 %copy-start = (bf16[256,2688]{1,0:T(8,128)(2,1)S(1)}, bf16[256,2688]{1,0:T(8,128)(2,1)}, u32[]{:S(2)}) copy-start(bf16[256,2688]{1,0:T(8,128)(2,1)} %param.31) | copy-start | bytes 4128772
  3.5 3.5 %collective-permute-start = (bf16[128,2688]{1,0:T(8,128)(2,1)S(1)}, bf16[128,2688]{1,0:T(8,128)(2,1)S(1)}, u32[]{:S(2)}, u32[]{:S(2)}) collective-permute-start(bf16[128,2688]{1,0:T(8,128)(2,1)S(1)} %fusion.14), channel_id=1, source_target_pairs={{0,1},{1,0},{2,3},{3,2},{4,5},{5,4},{6,7},{7,6},{8,9},{9,8},{10,11... | collective-permute-start | bytes 2064392 | tf_op jit(solution)/shard_map/ppermute | solution.py:72
  6.9 33.4 %copy-start.41 = (f32[256]{0:T(256)}, f32[256]{0:T(256)S(1)}, u32[]{:S(2)}) copy-start(f32[256]{0:T(256)S(1)} %fusion.75) | copy-start | bytes 3076
  12.6 25.3 %copy-start.3 = (f32[256,256]{0,1:T(8,128)}, f32[256,256]{0,1:T(8,128)S(1)}, u32[]{:S(2)}) copy-start(f32[256,256]{0,1:T(8,128)S(1)} %get-tuple-element.55) | copy-start | bytes 786436
  12.6 18.3 %copy-start.27 = (f32[256]{0:T(256)}, f32[256]{0:T(256)S(1)}, u32[]{:S(2)}) copy-start(f32[256]{0:T(256)S(1)} %add_rsqrt_fusion.1) | copy-start | bytes 3076
  13.1 24.8 %copy-start.39 = (f32[128]{0:T(128)S(1)}, f32[128]{0:T(128)}, u32[]{:S(2)}) copy-start(f32[128]{0:T(128)} %param.25) | copy-start | bytes 1540
  13.1 9.3 %collective-permute-start.1 = (bf16[272,256]{0,1:T(8,128)(2,1)S(1)}, bf16[272,256]{0,1:T(8,128)(2,1)S(1)}, u32[]{:S(2)}, u32[]{:S(2)}) collective-permute-start(bf16[272,256]{0,1:T(8,128)(2,1)S(1)} %pad_maximum_fusion.17), channel_id=1, source_target_pairs={{0,4},{2,6},{4,8},{6,10},{8,12},{10,14},{1,5},{3,7},{5,9},{7,11},{... | collective-permute-start | bytes 417800 | tf_op jit(solution)/shard_map/ppermute | solution.py:17
  17.6 22.7 %copy-start.25 = (f32[256,2]{0,1:T(2,128)}, f32[256,2]{0,1:T(2,128)S(1)}, u32[]{:S(2)}) copy-start(f32[256,2]{0,1:T(2,128)S(1)} %add_rsqrt_fusion) | copy-start | bytes 6148
  22.4 8.4 %collective-permute-start.2 = (bf16[272,256]{0,1:T(8,128)(2,1)S(1)}, bf16[272,256]{0,1:T(8,128)(2,1)S(1)}, u32[]{:S(2)}, u32[]{:S(2)}) collective-permute-start(bf16[272,256]{0,1:T(8,128)(2,1)S(1)} %collective-permute-done.1), channel_id=1, source_target_pairs={{0,4},{2,6},{4,8},{6,10},{8,12},{10,14},{1,5},{3,7},{5,9},{7,11},{... | collective-permute-start | bytes 417800 | tf_op jit(solution)/shard_map/ppermute | solution.py:17
  26.9 9.9 %collective-permute-start.3 = (bf16[544,256]{0,1:T(8,128)(2,1)S(1)}, bf16[544,256]{0,1:T(8,128)(2,1)S(1)}, u32[]{:S(2)}, u32[]{:S(2)}) collective-permute-start(bf16[544,256]{0,1:T(8,128)(2,1)S(1)} %pad_maximum_fusion.15), channel_id=1, source_target_pairs={{0,2},{2,4},{4,6},{6,8},{8,10},{10,12},{12,14},{1,3},{3,5},{5,7},{... | collective-permute-start | bytes 835592 | tf_op jit(solution)/shard_map/ppermute | solution.py:17
  43.9 3.0 %collective-permute-start.4 = (bf16[128,2688]{1,0:T(8,128)(2,1)}, bf16[128,2688]{1,0:T(8,128)(2,1)}, u32[]{:S(2)}, u32[]{:S(2)}) collective-permute-start(bf16[128,2688]{1,0:T(8,128)(2,1)} %constant_dynamic-slice_fusion.3), channel_id=1, source_target_pairs={{0,1},{1,0},{2,3},{3,2},{4,5},{5,4},{6,7},{7,6},{8,9},{9,8},{10,11... | collective-permute-start | bytes 2064392 | tf_op jit(solution)/shard_map/ppermute | solution.py:65
  44.1 2.1 %collective-permute-start.5 = (bf16[128,16]{0,1:T(8,128)(2,1)S(1)}, bf16[128,16]{0,1:T(8,128)(2,1)}, u32[]{:S(2)}, u32[]{:S(2)}) collective-permute-start(bf16[128,16]{0,1:T(8,128)(2,1)S(1)} %constant_dynamic-slice_fusion.2), channel_id=1, source_target_pairs={{0,1},{1,0},{2,3},{3,2},{4,5},{5,4},{6,7},{7,6},{8,9},{9,8},{10,11... | collective-permute-start | bytes 12296 | tf_op jit(solution)/shard_map/ppermute | solution.py:65
  50.5 1.2 %collective-permute-start.7 = (bf16[128,32]{0,1:T(8,128)(2,1)S(1)}, bf16[128,32]{0,1:T(8,128)(2,1)S(1)}, u32[]{:S(2)}, u32[]{:S(2)}) collective-permute-start(bf16[128,32]{0,1:T(8,128)(2,1)S(1)} %pad_maximum_fusion.20), channel_id=1, source_target_pairs={{0,1},{1,0},{2,3},{3,2},{4,5},{5,4},{6,7},{7,6},{8,9},{9,8},{10,11... | collective-permute-start | bytes 24584 | tf_op jit(solution)/shard_map/ppermute | solution.py:72
  50.7 2.3 %collective-permute-start.6 = (bf16[128,2688]{1,0:T(8,128)(2,1)S(1)}, bf16[128,2688]{1,0:T(8,128)(2,1)}, u32[]{:S(2)}, u32[]{:S(2)}) collective-permute-start(bf16[128,2688]{1,0:T(8,128)(2,1)S(1)} %get-tuple-element.34), channel_id=1, source_target_pairs={{0,1},{1,0},{2,3},{3,2},{4,5},{5,4},{6,7},{7,6},{8,9},{9,8},{10,11... | collective-permute-start | bytes 2064392 | tf_op jit(solution)/shard_map/ppermute | solution.py:72
  59.4 13.0 %collective-permute-start.8 = (bf16[512,256]{0,1:T(8,128)(2,1)S(1)}, bf16[512,256]{0,1:T(8,128)(2,1)S(1)}, u32[]{:S(2)}, u32[]{:S(2)}) collective-permute-start(bf16[512,256]{0,1:T(8,128)(2,1)S(1)} %pad_maximum_fusion.16), channel_id=1, source_target_pairs={{4,0},{6,2},{8,4},{10,6},{12,8},{14,10},{5,1},{7,3},{9,5},{11,7},{... | collective-permute-start | bytes 786440 | tf_op jit(solution)/shard_map/ppermute | solution.py:17
  72.6 7.1 %collective-permute-start.9 = (bf16[256,256]{0,1:T(8,128)(2,1)S(1)}, bf16[256,256]{0,1:T(8,128)(2,1)S(1)}, u32[]{:S(2)}, u32[]{:S(2)}) collective-permute-start(bf16[256,256]{0,1:T(8,128)(2,1)S(1)} %get-tuple-element.32), channel_id=1, source_target_pairs={{2,0},{4,2},{6,4},{8,6},{10,8},{12,10},{14,12},{3,1},{5,3},{7,5},{... | collective-permute-start | bytes 393224 | tf_op jit(solution)/shard_map/ppermute | solution.py:17
  73.9 8.3 %collective-permute-start.10 = (bf16[256,256]{0,1:T(8,128)(2,1)S(1)}, bf16[256,256]{0,1:T(8,128)(2,1)S(1)}, u32[]{:S(2)}, u32[]{:S(2)}) collective-permute-start(bf16[256,256]{0,1:T(8,128)(2,1)S(1)} %get-tuple-element.33), channel_id=1, source_target_pairs={{4,0},{6,2},{8,4},{10,6},{12,8},{14,10},{5,1},{7,3},{9,5},{11,7},{... | collective-permute-start | bytes 393224 | tf_op jit(solution)/shard_map/ppermute | solution.py:17
  84.1 2.7 %collective-permute-start.12 = (bf16[1344,48]{0,1:T(8,128)(2,1)}, bf16[1344,48]{0,1:T(8,128)(2,1)}, u32[]{:S(2)}, u32[]{:S(2)}) collective-permute-start(bf16[1344,48]{0,1:T(8,128)(2,1)} %constant_dynamic-slice_fusion), channel_id=1, source_target_pairs={{0,1},{1,0},{2,3},{3,2},{4,5},{5,4},{6,7},{7,6},{8,9},{9,8},{10,11... | collective-permute-start | bytes 387080 | tf_op jit(solution)/shard_map/ppermute | solution.py:65
  93.9 12.4 %collective-permute-start.13 = (bf16[98304]{0:T(1024)(128)(2,1)S(1)}, bf16[98304]{0:T(1024)(128)(2,1)S(1)}, u32[]{:S(2)}, u32[]{:S(2)}) collective-permute-start(bf16[98304]{0:T(1024)(128)(2,1)S(1)} %constant_dynamic-update-slice_fusion.12), channel_id=1, source_target_pairs={{0,8},{2,10},{4,12},{6,14},{8,0},{10,2},{12,4},{14,6},{1,9},{3,11}... | collective-permute-start | bytes 589832 | tf_op jit(solution)/shard_map/ppermute | solution.py:87
  99.0 15.5 %copy-start.20 = (f32[2688]{0:T(1024)S(1)}, f32[2688]{0:T(1024)}, u32[]{:S(2)}) copy-start(f32[2688]{0:T(1024)} %param.24) | copy-start | bytes 32260
  99.0 15.5 %copy-start.35 = (f32[128]{0:T(128)S(1)}, f32[128]{0:T(128)}, u32[]{:S(2)}) copy-start(f32[128]{0:T(128)} %copy-done.34) | copy-start | bytes 1540
  106.3 6.6 %collective-permute-start.14 = (bf16[98304]{0:T(1024)(128)(2,1)S(1)}, bf16[98304]{0:T(1024)(128)(2,1)S(1)}, u32[]{:S(2)}, u32[]{:S(2)}) collective-permute-start(bf16[98304]{0:T(1024)(128)(2,1)S(1)} %add_convert_fusion.1), channel_id=1, source_target_pairs={{0,4},{2,6},{4,0},{6,2},{8,12},{10,14},{12,8},{14,10},{1,5},{3,7},... | collective-permute-start | bytes 589832 | tf_op jit(solution)/shard_map/ppermute | solution.py:87
  106.5 8.0 %collective-permute-start.11 = (bf16[128,2688]{1,0:T(8,128)(2,1)S(1)}, bf16[128,2688]{1,0:T(8,128)(2,1)S(1)}, u32[]{:S(2)}, u32[]{:S(2)}) collective-permute-start(bf16[128,2688]{1,0:T(8,128)(2,1)S(1)} %constant_dynamic-slice_fusion.1), channel_id=1, source_target_pairs={{0,1},{1,0},{2,3},{3,2},{4,5},{5,4},{6,7},{7,6},{8,9},{9,8},{10,11... | collective-permute-start | bytes 2064392 | tf_op jit(solution)/shard_map/ppermute | solution.py:65
  113.0 5.7 %collective-permute-start.15 = (bf16[98304]{0:T(1024)(128)(2,1)S(1)}, bf16[98304]{0:T(1024)(128)(2,1)S(1)}, u32[]{:S(2)}, u32[]{:S(2)}) collective-permute-start(bf16[98304]{0:T(1024)(128)(2,1)S(1)} %add_convert_fusion), channel_id=1, source_target_pairs={{0,2},{2,0},{4,6},{6,4},{8,10},{10,8},{12,14},{14,12},{1,3},{3,1},... | collective-permute-start | bytes 589832 | tf_op jit(solution)/shard_map/ppermute | solution.py:87
  (37 other events, 132.3 us)

commit v16 on v11

--- a/solution.py
+++ b/solution.py
@@ -214,17 +214,44 @@
     middle_output_gradient = (
         adapter_scale * multiply_by_transpose(prenorm_gradient, adapter_output_up)
     ).astype(jnp.bfloat16)
-    complete_gradient = tp_gather(prenorm_gradient)
     middle_pair = tp_gather(jnp.concatenate([middle_output_gradient, middle_output], axis=1))
     middle_complete_gradient = middle_pair[:, :adapter_product]
     middle_complete = middle_pair[:, adapter_product:]
-    gradient_portion = lax.dynamic_slice_in_dim(
-        complete_gradient, tp_index * slice_width, slice_width, 1
-    )
-    output_up_contribution = adapter_scale * transpose_multiply(middle_complete, gradient_portion)
-    attention_gradient = multiply_by_transpose(
-        complete_gradient, output_projection
-    ) + multiply_by_transpose(middle_complete_gradient, adapter_output_down)
+    middle_part = multiply_by_transpose(middle_complete_gradient, adapter_output_down)
+    if lax.axis_size("tp") == 2:
+        partner_gradient = lax.ppermute(prenorm_gradient, "tp", [(0, 1), (1, 0)])
+        partner_middle = lax.ppermute(middle_output, "tp", [(0, 1), (1, 0)])
+        own_portion = lax.dynamic_slice_in_dim(
+            prenorm_gradient, tp_index * slice_width, slice_width, 1
+        )
+        partner_portion = lax.dynamic_slice_in_dim(
+            partner_gradient, tp_index * slice_width, slice_width, 1
+        )
+        output_up_contribution = adapter_scale * (
+            transpose_multiply(middle_output, own_portion)
+            + transpose_multiply(partner_middle, partner_portion)
+        )
+        own_rows = multiply_by_transpose(prenorm_gradient, output_projection)
+        partner_rows = multiply_by_transpose(partner_gradient, output_projection)
+        first = tp_index == 0
+        attention_gradient = (
+            jnp.concatenate(
+                [jnp.where(first, own_rows, partner_rows), jnp.where(first, partner_rows, own_rows)],
+                axis=0,
+            )
+            + middle_part
+        )
+    else:
+        complete_gradient = tp_gather(prenorm_gradient)
+        gradient_portion = lax.dynamic_slice_in_dim(
+            complete_gradient, tp_index * slice_width, slice_width, 1
+        )
+        output_up_contribution = adapter_scale * transpose_multiply(
+            middle_complete, gradient_portion
+        )
+        attention_gradient = (
+            multiply_by_transpose(complete_gradient, output_projection) + middle_part
+        )
     attention_gradient = (attention_gradient * valid_rows[:, None]).astype(jnp.bfloat16)
     down_out_term = transpose_multiply(attention_result, middle_complete_gradient)
     grad_heads = attention_gradient.reshape(shard_len, heads_here, head_dim)

time: 124 us -> 126 us (1.016)
  matrix products: 20.3 us -> 27.2 us
  waiting for transfers between devices: 45.6 us -> 43 us
  other arithmetic: 13.2 us -> 11.3 us
    dot_general x7 -> x8, matrix products: 4.63 us -> 8.44 us  [multiply_by_transpose(): lax.dot_general(first_op, second_op, (((1,), (1,)), ((), ())), preferred_...]
    dot_general x1, matrix products: 0.55 us -> 2.37 us  [on_device(): jnp.einsum('hts,thd->sd', probs_cast, grad_heads, preferred_element_type=...]
    reshape x0 -> x1, local copies, waits for them, and re-layouts: none -> 1.66 us  [on_device(): grad_heads = attention_gradient.reshape(shard_len, heads_here, head_dim)]
    dot_general x6 -> x7, matrix products: 3.45 us -> 4.91 us  [transpose_multiply(): lax.dot_general(first_op, second_op, (((0,), (0,)), ((), ())), preferred_...]
    ppermute x3, waiting for transfers between devices: 14.3 us -> 12.8 us  [ctx_sum(): received = lax.ppermute(sent, 'ctx', [(i, i ^ step) for i in range(count)])]
    unnamed x107 -> x111, local copies, waits for them, and re-layouts: 9.9 us -> 8.75 us
  transfers between devices with their start and end apart: 16 -> 17, of which waited for: 11 -> 12; matrix products, arithmetic and copies ran while one was open for 10% -> 22% of each run, Pallas kernels for 0% -> 0%
where the time goes in v16:
time: 126 us; the launch traced here: 125 us
  waiting for transfers between devices  43 us (34%)
  matrix products  27.2 us (22%)
  starting transfers between devices  24.2 us (19%)
  local copies, waits for them, and re-layouts  16.9 us (13%)
  other arithmetic  11.3 us (9%)
  between operations  2.28 us (2%)
    ppermute x6, waiting for transfers between devices, passed_along(): lax.ppermute(value, axis, [(source, source + steps) for source in range(l...  28.3 us
    ppermute x6, starting transfers between devices, passed_along(): lax.ppermute(value, axis, [(source, source + steps) for source in range(l...  16.5 us
    ppermute x3, waiting for transfers between devices, ctx_sum(): received = lax.ppermute(sent, 'ctx', [(i, i ^ step) for i in range(count)])  12.8 us
    unnamed x111, local copies, waits for them, and re-layouts  8.75 us
    dot_general x8, matrix products, multiply_by_transpose(): lax.dot_general(first_op, second_op, (((1,), (1,)), ((), ())), preferred_...  8.44 us
    ppermute x3, starting transfers between devices, ctx_sum(): received = lax.ppermute(sent, 'ctx', [(i, i ^ step) for i in range(count)])  5.71 us
    dot_general x7, matrix products, matrix_product(): return jnp.dot(first_op, second_op, preferred_element_type=jnp.float32)  5.57 us
    dot_general x7, matrix products, transpose_multiply(): lax.dot_general(first_op, second_op, (((0,), (0,)), ((), ())), preferred_...  4.91 us
  transfers between devices with their start and end apart: 17, of which 12 were waited for; matrix products, arithmetic and copies ran while one was open for 22% of the time, Pallas kernels for 0%

profile of v16, /device:TPU:0, one launch (start us, length us, event | category | flops | bytes accessed | tf_op | source)
XLA Modules:
  0.0 124.9 jit_solution(11889026236980523482)
XLA Ops:
  4.8 2.1 %copy.37 = bf16[2688,48]{1,0:T(8,128)(2,1)} copy(bf16[2688,48]{0,1:T(8,128)(2,1)} %param.32) | data formatting | bytes 516096 | tf_op args[12]
  9.2 2.6 %fusion.84 = (bf16[256,560]{0,1:T(8,128)(2,1)S(1)}, f32[256,560]{0,1:T(8,128)S(1)}) fusion(bf16[2688,48]{1,0:T(8,128)(2,1)S(1)} %copy-done.19, bf16[2688,128]{1,0:T(8,128)(2,1)S(1)} %copy-done.46, bf16[2688,128]{1,0:T(8,128)(2,1)} %param.29, bf16[2688,256]{1,0:T(8,128)(2,1)S(1)} %copy-done.45, bf16[128,2688]{1,0:T(8,128)(2,1)S(1)} %get-tuple-element.37, ...), kind=kOutput, calls=%fused_computation.200 | convolution fusion | flops 785641472 | bytes 5246976 | tf_op jit(solution)/shard_map/dot_general | solution.py:33
  13.1 4.5 %collective-permute-start.1 = (bf16[272,256]{0,1:T(8,128)(2,1)S(1)}, bf16[272,256]{0,1:T(8,128)(2,1)S(1)}, u32[]{:S(2)}, u32[]{:S(2)}) collective-permute-start(bf16[272,256]{0,1:T(8,128)(2,1)S(1)} %pad_maximum_fusion.9), channel_id=1, source_target_pairs={{0,4},{2,6},{4,8},{6,10},{8,12},{10,14},{1,5},{3,7},{5,9},{7,11},{... | collective-permute-start | bytes 417800 | tf_op jit(solution)/shard_map/ppermute | solution.py:17
  17.6 4.8 %collective-permute-done.1 = bf16[272,256]{0,1:T(8,128)(2,1)S(1)} collective-permute-done((bf16[272,256]{0,1:T(8,128)(2,1)S(1)}, bf16[272,256]{0,1:T(8,128)(2,1)S(1)}, u32[]{:S(2)}, u32[]{:S(2)}) %collective-permute-start.1) | collective-permute-done | bytes 139296 | tf_op jit(solution)/shard_map/ppermute | solution.py:17
  22.4 4.4 %collective-permute-start.2 = (bf16[272,256]{0,1:T(8,128)(2,1)S(1)}, bf16[272,256]{0,1:T(8,128)(2,1)S(1)}, u32[]{:S(2)}, u32[]{:S(2)}) collective-permute-start(bf16[272,256]{0,1:T(8,128)(2,1)S(1)} %collective-permute-done.1), channel_id=1, source_target_pairs={{0,4},{2,6},{4,8},{6,10},{8,12},{10,14},{1,5},{3,7},{5,9},{7,11},{... | collective-permute-start | bytes 417800 | tf_op jit(solution)/shard_map/ppermute | solution.py:17
  26.9 3.4 %collective-permute-start.3 = (bf16[544,256]{0,1:T(8,128)(2,1)S(1)}, bf16[544,256]{0,1:T(8,128)(2,1)S(1)}, u32[]{:S(2)}, u32[]{:S(2)}) collective-permute-start(bf16[544,256]{0,1:T(8,128)(2,1)S(1)} %pad_maximum_fusion.7), channel_id=1, source_target_pairs={{0,2},{2,4},{4,6},{6,8},{8,10},{10,12},{12,14},{1,3},{3,5},{5,7},{... | collective-permute-start | bytes 835592 | tf_op jit(solution)/shard_map/ppermute | solution.py:17
  30.9 5.9 %collective-permute-done.3 = bf16[544,256]{0,1:T(8,128)(2,1)S(1)} collective-permute-done((bf16[544,256]{0,1:T(8,128)(2,1)S(1)}, bf16[544,256]{0,1:T(8,128)(2,1)S(1)}, u32[]{:S(2)}, u32[]{:S(2)}) %collective-permute-start.3) | collective-permute-done | bytes 278560 | tf_op jit(solution)/shard_map/ppermute | solution.py:17
  37.9 2.4 %fusion.22 = f32[2,256,1280]{1,2,0:T(8,128)} fusion(pred[256,1280]{0,1:T(8,128)(4,1)S(1)} %fusion.26, bf16[1280,256]{0,1:T(8,128)(2,1)S(1)} %maximum_dynamic-update-slice_fusion, f32[256,256]{0,1:T(8,128)S(1)} %get-tuple-element.55, f32[128]{0:T(128)S(1)} %copy-done.43, f32[256,2]{0,1:T(2,128)S(1)} %add_rsqrt_fusion), kind=kOutput, calls=%fused_computation.50 | convolution fusion | flops 169936640 | bytes 3541504 | tf_op jit(solution)/shard_map/div | solution.py:194
  40.3 2.1 %fusion.32 = bf16[128,2,256]{2,0,1:T(8,128)(2,1)S(1)} fusion(f32[2,256,1280]{1,2,0:T(8,128)} %fusion.22, bf16[1280,256]{0,1:T(8,128)(2,1)S(1)} %maximum_dynamic-update-slice_fusion, f32[256]{0:T(256)S(1)} %fusion.74), kind=kOutput, calls=%fused_computation.65 | convolution fusion | flops 168558592 | bytes 3081216 | tf_op jit(solution)/shard_map/hts,sd->thd/dot_general | solution.py:196
  47.2 1.6 %multiply_reduce_fusion.2 = (f32[128]{0:T(128)S(1)}, f32[128,2688]{1,0:T(8,128)S(1)}) fusion(bf16[128,16]{0,1:T(8,128)(2,1)S(1)} %add_convert_fusion.3, bf16[16,2688]{1,0:T(8,128)(2,1)S(1)} %copy-done.20, bf16[128,2688]{1,0:T(8,128)(2,1)} %collective-permute-done.4, bf16[256,2688]{1,0:T(8,128)(2,1)S(1)} %convolution_convert_fusion.1, s32[]{:T(128)S(6)} %select_n.67), kind=kOutput, calls=%fused_computation.46 | convolution fusion | flops 13418368 | bytes 2843140 | tf_op jit(solution)/shard_map/dot_general | solution.py:33
  55.3 1.6 %broadcast_select_fusion.3 = (f32[128,256]{1,0:T(8,128)S(1)}, f32[128,256]{1,0:T(8,128)S(1)}) fusion(f32[128,256]{1,0:T(8,128)} %fusion.85, pred[]{:T(512)S(6)} %eq.29, bf16[128,2688]{1,0:T(8,128)(2,1)S(1)} %collective-permute-done.6, bf16[256,2688]{1,0:T(8,128)(2,1)S(1)} %copy-done), kind=kOutput, calls=%fused_computation.139 | convolution fusion | flops 176226304 | bytes 2457601 | tf_op jit(solution)/shard_map/dot_general | solution.py:37
  57.0 1.6 %fusion.31 = bf16[256,256]{1,0:T(8,128)(2,1)} fusion(bf16[256,16]{0,1:T(8,128)(2,1)} %param.36, f32[128,256]{1,0:T(8,128)S(1)} %get-tuple-element.45, f32[128,256]{1,0:T(8,128)S(1)} %get-tuple-element.44, f32[256]{0:T(256)S(1)} %copy-done.40, bf16[128,32]{0,1:T(8,128)(2,1)S(1)} %get-tuple-element.47, bf16[128,32]{0,1:T(8,128)(2,1)S(1)} %get-tuple-element.46), kind=kOutput, calls=%fused_computation.64 | convolution fusion | flops 2375680 | bytes 418816 | tf_op jit(solution)/shard_map/dot_general | solution.py:37
  58.5 1.7 %copy.63 = bf16[256,256]{0,1:T(8,128)(2,1)} copy(bf16[256,256]{1,0:T(8,128)(2,1)} %fusion.31) | data formatting | bytes 262144 | tf_op jit(solution)/shard_map/reshape | solution.py:257
  60.2 2.4 %convolution_bitcast_fusion.1 = f32[1280,128]{0,1:T(8,128)S(1)} fusion(bf16[256,2,128]{0,2,1:T(8,128)(2,1)} %bitcast.98, f32[2,256,1280]{1,2,0:T(8,128)} %fusion.22), kind=kOutput, calls=%fused_computation.15 | convolution fusion | flops 168427520 | bytes 3407872 | tf_op jit(solution)/shard_map/hts,thd->sd/dot_general | solution.py:271
  67.7 11.6 %collective-permute-done.8 = bf16[512,256]{0,1:T(8,128)(2,1)S(1)} collective-permute-done((bf16[512,256]{0,1:T(8,128)(2,1)S(1)}, bf16[512,256]{0,1:T(8,128)(2,1)S(1)}, u32[]{:S(2)}, u32[]{:S(2)}) %collective-permute-start.8) | collective-permute-done | bytes 262176 | tf_op jit(solution)/shard_map/ppermute | solution.py:17
  80.9 1.5 %collective-permute-start.10 = (bf16[256,256]{0,1:T(8,128)(2,1)S(1)}, bf16[256,256]{0,1:T(8,128)(2,1)S(1)}, u32[]{:S(2)}, u32[]{:S(2)}) collective-permute-start(bf16[256,256]{0,1:T(8,128)(2,1)S(1)} %get-tuple-element.33), channel_id=1, source_target_pairs={{4,0},{6,2},{8,4},{10,6},{12,8},{14,10},{5,1},{7,3},{9,5},{11,7},{... | collective-permute-start | bytes 393224 | tf_op jit(solution)/shard_map/ppermute | solution.py:17
  83.4 3.2 %collective-permute-done.9 = bf16[256,256]{0,1:T(8,128)(2,1)S(1)} collective-permute-done((bf16[256,256]{0,1:T(8,128)(2,1)S(1)}, bf16[256,256]{0,1:T(8,128)(2,1)S(1)}, u32[]{:S(2)}, u32[]{:S(2)}) %collective-permute-start.9) | collective-permute-done | bytes 131104 | tf_op jit(solution)/shard_map/ppermute | solution.py:17
  86.6 2.5 %collective-permute-done.10 = bf16[256,256]{0,1:T(8,128)(2,1)S(1)} collective-permute-done((bf16[256,256]{0,1:T(8,128)(2,1)S(1)}, bf16[256,256]{0,1:T(8,128)(2,1)S(1)}, u32[]{:S(2)}, u32[]{:S(2)}) %collective-permute-start.10) | collective-permute-done | bytes 131104 | tf_op jit(solution)/shard_map/ppermute | solution.py:17
  98.2 3.4 %convolution_convert_fusion = bf16[256,2688]{1,0:T(8,128)(2,1)S(1)} fusion(bf16[256,560]{0,1:T(8,128)(2,1)} %copy-done.22, bf16[2688,48]{1,0:T(8,128)(2,1)} %copy.37, bf16[2688,128]{1,0:T(8,128)(2,1)} %param.30, bf16[2688,128]{1,0:T(8,128)(2,1)} %param.29, bf16[2688,256]{1,0:T(8,128)(2,1)} %param.28), kind=kOutput, calls=%fused_computation.1 | convolution fusion | flops 783433728 | bytes 4673536 | tf_op jit(solution)/shard_map/dot_general | solution.py:37
  101.6 2.3 %collective-permute-done.14 = bf16[98304]{0:T(1024)(128)(2,1)S(1)} collective-permute-done((bf16[98304]{0:T(1024)(128)(2,1)S(1)}, bf16[98304]{0:T(1024)(128)(2,1)S(1)}, u32[]{:S(2)}, u32[]{:S(2)}) %collective-permute-start.14) | collective-permute-done | bytes 196640 | tf_op jit(solution)/shard_map/ppermute | solution.py:87
  103.9 1.7 %collective-permute-start.15 = (bf16[98304]{0:T(1024)(128)(2,1)S(1)}, bf16[98304]{0:T(1024)(128)(2,1)S(1)}, u32[]{:S(2)}, u32[]{:S(2)}) collective-permute-start(bf16[98304]{0:T(1024)(128)(2,1)S(1)} %add_convert_fusion.1), channel_id=1, source_target_pairs={{0,4},{2,6},{4,0},{6,2},{8,12},{10,14},{12,8},{14,10},{1,5},{3,7},... | collective-permute-start | bytes 589832 | tf_op jit(solution)/shard_map/ppermute | solution.py:87
  105.7 4.4 %collective-permute-done.15 = bf16[98304]{0:T(1024)(128)(2,1)S(1)} collective-permute-done((bf16[98304]{0:T(1024)(128)(2,1)S(1)}, bf16[98304]{0:T(1024)(128)(2,1)S(1)}, u32[]{:S(2)}, u32[]{:S(2)}) %collective-permute-start.15) | collective-permute-done | bytes 196640 | tf_op jit(solution)/shard_map/ppermute | solution.py:87
  110.2 2.7 %collective-permute-start.16 = (bf16[98304]{0:T(1024)(128)(2,1)S(1)}, bf16[98304]{0:T(1024)(128)(2,1)S(1)}, u32[]{:S(2)}, u32[]{:S(2)}) collective-permute-start(bf16[98304]{0:T(1024)(128)(2,1)S(1)} %add_convert_fusion), channel_id=1, source_target_pairs={{0,8},{2,10},{4,12},{6,14},{8,0},{10,2},{12,4},{14,6},{1,9},{3,11}... | collective-permute-start | bytes 589832 | tf_op jit(solution)/shard_map/ppermute | solution.py:87
  114.7 6.2 %collective-permute-done.16 = bf16[98304]{0:T(1024)(128)(2,1)S(1)} collective-permute-done((bf16[98304]{0:T(1024)(128)(2,1)S(1)}, bf16[98304]{0:T(1024)(128)(2,1)S(1)}, u32[]{:S(2)}, u32[]{:S(2)}) %collective-permute-start.16) | collective-permute-done | bytes 196640 | tf_op jit(solution)/shard_map/ppermute | solution.py:87
  (215 shorter events, 42.4 us)
Async XLA Ops:
  0.6 41.8 %copy-start = (bf16[256,2688]{1,0:T(8,128)(2,1)S(1)}, bf16[256,2688]{1,0:T(8,128)(2,1)}, u32[]{:S(2)}) copy-start(bf16[256,2688]{1,0:T(8,128)(2,1)} %param.31) | copy-start | bytes 4128772
  3.5 3.5 %collective-permute-start = (bf16[128,2688]{1,0:T(8,128)(2,1)S(1)}, bf16[128,2688]{1,0:T(8,128)(2,1)S(1)}, u32[]{:S(2)}, u32[]{:S(2)}) collective-permute-start(bf16[128,2688]{1,0:T(8,128)(2,1)S(1)} %fusion.14), channel_id=1, source_target_pairs={{0,1},{1,0},{2,3},{3,2},{4,5},{5,4},{6,7},{7,6},{8,9},{9,8},{10,11... | collective-permute-start | bytes 2064392 | tf_op jit(solution)/shard_map/ppermute | solution.py:72
  6.9 33.3 %copy-start.39 = (f32[256]{0:T(256)}, f32[256]{0:T(256)S(1)}, u32[]{:S(2)}) copy-start(f32[256]{0:T(256)S(1)} %fusion.74) | copy-start | bytes 3076
  12.5 25.3 %copy-start.3 = (f32[256,256]{0,1:T(8,128)}, f32[256,256]{0,1:T(8,128)S(1)}, u32[]{:S(2)}) copy-start(f32[256,256]{0,1:T(8,128)S(1)} %get-tuple-element.55) | copy-start | bytes 786436
  12.6 24.4 %copy-start.28 = (f32[256]{0:T(256)}, f32[256]{0:T(256)S(1)}, u32[]{:S(2)}) copy-start(f32[256]{0:T(256)S(1)} %add_rsqrt_fusion.1) | copy-start | bytes 3076
  13.0 24.2 %copy-start.42 = (s32[256]{0:T(256)S(1)}, s32[256]{0:T(256)}, u32[]{:S(2)}) copy-start(s32[256]{0:T(256)} %param.22) | copy-start | bytes 3076
  13.1 24.8 %copy-start.43 = (f32[128]{0:T(128)S(1)}, f32[128]{0:T(128)}, u32[]{:S(2)}) copy-start(f32[128]{0:T(128)} %param.25) | copy-start | bytes 1540
  13.1 9.3 %collective-permute-start.1 = (bf16[272,256]{0,1:T(8,128)(2,1)S(1)}, bf16[272,256]{0,1:T(8,128)(2,1)S(1)}, u32[]{:S(2)}, u32[]{:S(2)}) collective-permute-start(bf16[272,256]{0,1:T(8,128)(2,1)S(1)} %pad_maximum_fusion.9), channel_id=1, source_target_pairs={{0,4},{2,6},{4,8},{6,10},{8,12},{10,14},{1,5},{3,7},{5,9},{7,11},{... | collective-permute-start | bytes 417800 | tf_op jit(solution)/shard_map/ppermute | solution.py:17
  22.4 8.4 %collective-permute-start.2 = (bf16[272,256]{0,1:T(8,128)(2,1)S(1)}, bf16[272,256]{0,1:T(8,128)(2,1)S(1)}, u32[]{:S(2)}, u32[]{:S(2)}) collective-permute-start(bf16[272,256]{0,1:T(8,128)(2,1)S(1)} %collective-permute-done.1), channel_id=1, source_target_pairs={{0,4},{2,6},{4,8},{6,10},{8,12},{10,14},{1,5},{3,7},{5,9},{7,11},{... | collective-permute-start | bytes 417800 | tf_op jit(solution)/shard_map/ppermute | solution.py:17
  26.9 9.9 %collective-permute-start.3 = (bf16[544,256]{0,1:T(8,128)(2,1)S(1)}, bf16[544,256]{0,1:T(8,128)(2,1)S(1)}, u32[]{:S(2)}, u32[]{:S(2)}) collective-permute-start(bf16[544,256]{0,1:T(8,128)(2,1)S(1)} %pad_maximum_fusion.7), channel_id=1, source_target_pairs={{0,2},{2,4},{4,6},{6,8},{8,10},{10,12},{12,14},{1,3},{3,5},{5,7},{... | collective-permute-start | bytes 835592 | tf_op jit(solution)/shard_map/ppermute | solution.py:17
  43.9 3.3 %collective-permute-start.4 = (bf16[128,2688]{1,0:T(8,128)(2,1)}, bf16[128,2688]{1,0:T(8,128)(2,1)}, u32[]{:S(2)}, u32[]{:S(2)}) collective-permute-start(bf16[128,2688]{1,0:T(8,128)(2,1)} %constant_dynamic-slice_fusion.3), channel_id=1, source_target_pairs={{0,1},{1,0},{2,3},{3,2},{4,5},{5,4},{6,7},{7,6},{8,9},{9,8},{10,11... | collective-permute-start | bytes 2064392 | tf_op jit(solution)/shard_map/ppermute | solution.py:65
  44.7 1.5 %collective-permute-start.5 = (bf16[128,16]{0,1:T(8,128)(2,1)S(1)}, bf16[128,16]{0,1:T(8,128)(2,1)}, u32[]{:S(2)}, u32[]{:S(2)}) collective-permute-start(bf16[128,16]{0,1:T(8,128)(2,1)S(1)} %constant_dynamic-slice_fusion.2), channel_id=1, source_target_pairs={{0,1},{1,0},{2,3},{3,2},{4,5},{5,4},{6,7},{7,6},{8,9},{9,8},{10,11... | collective-permute-start | bytes 12296 | tf_op jit(solution)/shard_map/ppermute | solution.py:65
  46.9 35.5 %collective-permute-start.13 = (bf16[128,16]{0,1:T(8,128)(2,1)S(1)}, bf16[128,16]{0,1:T(8,128)(2,1)}, u32[]{:S(2)}, u32[]{:S(2)}) collective-permute-start(bf16[128,16]{0,1:T(8,128)(2,1)S(1)} %add_convert_fusion.3), channel_id=1, source_target_pairs={{0,1},{1,0},{2,3},{3,2},{4,5},{5,4},{6,7},{7,6},{8,9},{9,8},{10,11... | collective-permute-start | bytes 12296 | tf_op jit(solution)/shard_map/ppermute | solution.py:223
  50.8 4.6 %collective-permute-start.6 = (bf16[128,2688]{1,0:T(8,128)(2,1)S(1)}, bf16[128,2688]{1,0:T(8,128)(2,1)S(1)}, u32[]{:S(2)}, u32[]{:S(2)}) collective-permute-start(bf16[128,2688]{1,0:T(8,128)(2,1)S(1)} %get-tuple-element.34), channel_id=1, source_target_pairs={{0,1},{1,0},{2,3},{3,2},{4,5},{5,4},{6,7},{7,6},{8,9},{9,8},{10,11... | collective-permute-start | bytes 2064392 | tf_op jit(solution)/shard_map/ppermute | solution.py:222
  51.1 1.9 %collective-permute-start.7 = (bf16[128,32]{0,1:T(8,128)(2,1)S(1)}, bf16[128,32]{0,1:T(8,128)(2,1)S(1)}, u32[]{:S(2)}, u32[]{:S(2)}) collective-permute-start(bf16[128,32]{0,1:T(8,128)(2,1)S(1)} %pad_maximum_fusion.11), channel_id=1, source_target_pairs={{0,1},{1,0},{2,3},{3,2},{4,5},{5,4},{6,7},{7,6},{8,9},{9,8},{10,11... | collective-permute-start | bytes 24584 | tf_op jit(solution)/shard_map/ppermute | solution.py:72
  66.4 13.0 %collective-permute-start.8 = (bf16[512,256]{0,1:T(8,128)(2,1)S(1)}, bf16[512,256]{0,1:T(8,128)(2,1)S(1)}, u32[]{:S(2)}, u32[]{:S(2)}) collective-permute-start(bf16[512,256]{0,1:T(8,128)(2,1)S(1)} %pad_maximum_fusion.8), channel_id=1, source_target_pairs={{4,0},{6,2},{8,4},{10,6},{12,8},{14,10},{5,1},{7,3},{9,5},{11,7},{... | collective-permute-start | bytes 786440 | tf_op jit(solution)/shard_map/ppermute | solution.py:17
  67.7 14.7 %copy-start.13 = (bf16[128,2688]{1,0:T(8,128)(2,1)S(1)}, bf16[128,2688]{1,0:T(8,128)(2,1)}, u32[]{:S(2)}) copy-start(bf16[128,2688]{1,0:T(8,128)(2,1)} %copy-done.12) | copy-start | bytes 2064388
  79.5 7.1 %collective-permute-start.9 = (bf16[256,256]{0,1:T(8,128)(2,1)S(1)}, bf16[256,256]{0,1:T(8,128)(2,1)S(1)}, u32[]{:S(2)}, u32[]{:S(2)}) collective-permute-start(bf16[256,256]{0,1:T(8,128)(2,1)S(1)} %get-tuple-element.32), channel_id=1, source_target_pairs={{2,0},{4,2},{6,4},{8,6},{10,8},{12,10},{14,12},{3,1},{5,3},{7,5},{... | collective-permute-start | bytes 393224 | tf_op jit(solution)/shard_map/ppermute | solution.py:17
  80.9 8.2 %collective-permute-start.10 = (bf16[256,256]{0,1:T(8,128)(2,1)S(1)}, bf16[256,256]{0,1:T(8,128)(2,1)S(1)}, u32[]{:S(2)}, u32[]{:S(2)}) collective-permute-start(bf16[256,256]{0,1:T(8,128)(2,1)S(1)} %get-tuple-element.33), channel_id=1, source_target_pairs={{4,0},{6,2},{8,4},{10,6},{12,8},{14,10},{5,1},{7,3},{9,5},{11,7},{... | collective-permute-start | bytes 393224 | tf_op jit(solution)/shard_map/ppermute | solution.py:17
  91.7 1.7 %collective-permute-start.12 = (bf16[1344,48]{0,1:T(8,128)(2,1)}, bf16[1344,48]{0,1:T(8,128)(2,1)}, u32[]{:S(2)}, u32[]{:S(2)}) collective-permute-start(bf16[1344,48]{0,1:T(8,128)(2,1)} %constant_dynamic-slice_fusion), channel_id=1, source_target_pairs={{0,1},{1,0},{2,3},{3,2},{4,5},{5,4},{6,7},{7,6},{8,9},{9,8},{10,11... | collective-permute-start | bytes 387080 | tf_op jit(solution)/shard_map/ppermute | solution.py:65
  96.9 7.0 %collective-permute-start.14 = (bf16[98304]{0:T(1024)(128)(2,1)S(1)}, bf16[98304]{0:T(1024)(128)(2,1)S(1)}, u32[]{:S(2)}, u32[]{:S(2)}) collective-permute-start(bf16[98304]{0:T(1024)(128)(2,1)S(1)} %constant_dynamic-update-slice_fusion.12), channel_id=1, source_target_pairs={{0,2},{2,0},{4,6},{6,4},{8,10},{10,8},{12,14},{14,12},{1,3},{3,1},... | collective-permute-start | bytes 589832 | tf_op jit(solution)/shard_map/ppermute | solution.py:87
  103.9 6.2 %collective-permute-start.15 = (bf16[98304]{0:T(1024)(128)(2,1)S(1)}, bf16[98304]{0:T(1024)(128)(2,1)S(1)}, u32[]{:S(2)}, u32[]{:S(2)}) collective-permute-start(bf16[98304]{0:T(1024)(128)(2,1)S(1)} %add_convert_fusion.1), channel_id=1, source_target_pairs={{0,4},{2,6},{4,0},{6,2},{8,12},{10,14},{12,8},{14,10},{1,5},{3,7},... | collective-permute-start | bytes 589832 | tf_op jit(solution)/shard_map/ppermute | solution.py:87
  105.7 7.2 %collective-permute-start.11 = (bf16[128,2688]{1,0:T(8,128)(2,1)S(1)}, bf16[128,2688]{1,0:T(8,128)(2,1)S(1)}, u32[]{:S(2)}, u32[]{:S(2)}) collective-permute-start(bf16[128,2688]{1,0:T(8,128)(2,1)S(1)} %constant_dynamic-slice_fusion.1), channel_id=1, source_target_pairs={{0,1},{1,0},{2,3},{3,2},{4,5},{5,4},{6,7},{7,6},{8,9},{9,8},{10,11... | collective-permute-start | bytes 2064392 | tf_op jit(solution)/shard_map/ppermute | solution.py:65
  110.2 10.7 %collective-permute-start.16 = (bf16[98304]{0:T(1024)(128)(2,1)S(1)}, bf16[98304]{0:T(1024)(128)(2,1)S(1)}, u32[]{:S(2)}, u32[]{:S(2)}) collective-permute-start(bf16[98304]{0:T(1024)(128)(2,1)S(1)} %add_convert_fusion), channel_id=1, source_target_pairs={{0,8},{2,10},{4,12},{6,14},{8,0},{10,2},{12,4},{14,6},{1,9},{3,11}... | collective-permute-start | bytes 589832 | tf_op jit(solution)/shard_map/ppermute | solution.py:87
  (40 other events, 153.1 us)

commit v17 on v11

--- a/solution.py
+++ b/solution.py
@@ -252,11 +252,12 @@
         return grad_pairs[first_row : first_row + shard_len]
 
     if send_count == 4:
+        far_start = (reach_shards - 4) * shard_len
         far = passed_along(
-            jnp.concatenate([hop_block(3), hop_block(4)], axis=0).astype(jnp.bfloat16), "ctx", -2
+            grad_pairs[far_start : far_start + 2 * shard_len].astype(jnp.bfloat16), "ctx", -2
         ).astype(jnp.float32)
-        near_sum = hop_block(1) + far[:shard_len]
-        next_sum = hop_block(2) + far[shard_len:]
+        near_sum = hop_block(1) + far[shard_len:]
+        next_sum = hop_block(2) + far[:shard_len]
         own_grads = (
             own_grads
             + passed_along(near_sum.astype(jnp.bfloat16), "ctx", -1).astype(jnp.float32)

time: 124 us -> 124 us (level)
  no operation moved by 1% of the time
where the time goes in v17:
time: 124 us; the launch traced here: 123 us
  waiting for transfers between devices  45.6 us (37%)
  starting transfers between devices  23.3 us (19%)
  matrix products  20.3 us (16%)
  local copies, waits for them, and re-layouts  18 us (15%)
  other arithmetic  13.1 us (11%)
  between operations  2.27 us (2%)
    ppermute x6, waiting for transfers between devices, passed_along(): lax.ppermute(value, axis, [(source, source + steps) for source in range(l...  29.1 us
    ppermute x6, starting transfers between devices, passed_along(): lax.ppermute(value, axis, [(source, source + steps) for source in range(l...  16.4 us
    ppermute x3, waiting for transfers between devices, ctx_sum(): received = lax.ppermute(sent, 'ctx', [(i, i ^ step) for i in range(count)])  14.3 us
    unnamed x107, local copies, waits for them, and re-layouts  9.89 us
    dot_general x7, matrix products, matrix_product(): return jnp.dot(first_op, second_op, preferred_element_type=jnp.float32)  5.69 us
    ppermute x3, starting transfers between devices, ctx_sum(): received = lax.ppermute(sent, 'ctx', [(i, i ^ step) for i in range(count)])  5.27 us
    dot_general x7, matrix products, multiply_by_transpose(): lax.dot_general(first_op, second_op, (((1,), (1,)), ((), ())), preferred_...  4.63 us
    dot_general x6, matrix products, transpose_multiply(): lax.dot_general(first_op, second_op, (((0,), (0,)), ((), ())), preferred_...  3.45 us
  transfers between devices with their start and end apart: 16, of which 11 were waited for; matrix products, arithmetic and copies ran while one was open for 10% of the time, Pallas kernels for 0%

profile of v17, /device:TPU:0, one launch (start us, length us, event | category | flops | bytes accessed | tf_op | source)
XLA Modules:
  0.0 122.6 jit_solution(10701273763485070997)
XLA Ops:
  0.7 1.4 %fusion.19 = f32[128]{0:T(128)S(1)} fusion(bf16[128,2688]{1,0:T(8,128)(2,1)} %param.20), kind=kLoop, calls=%fused_computation.41 | loop fusion | flops 1032064 | bytes 688640 | tf_op jit(solution)/shard_map/reduce_sum | solution.py:21
  2.1 1.4 %fusion.14 = bf16[128,2688]{1,0:T(8,128)(2,1)S(1)} fusion(bf16[128,2688]{1,0:T(8,128)(2,1)} %param.20, f32[2688]{0:T(1024)} %param.24, f32[128]{0:T(128)S(1)} %add_rsqrt_fusion.3), kind=kLoop, calls=%fused_computation.36 | loop fusion | flops 1376256 | bytes 1387520 | tf_op jit(solution)/shard_map/convert_element_type | solution.py:128
  4.8 2.1 %copy.35 = bf16[2688,48]{1,0:T(8,128)(2,1)} copy(bf16[2688,48]{0,1:T(8,128)(2,1)} %param.32) | data formatting | bytes 516096 | tf_op args[12]
  9.2 2.6 %fusion.86 = (bf16[256,560]{0,1:T(8,128)(2,1)S(1)}, f32[256,560]{0,1:T(8,128)S(1)}) fusion(bf16[2688,48]{1,0:T(8,128)(2,1)S(1)} %copy-done.16, bf16[2688,128]{1,0:T(8,128)(2,1)S(1)} %copy-done.44, bf16[2688,128]{1,0:T(8,128)(2,1)} %param.29, bf16[2688,256]{1,0:T(8,128)(2,1)S(1)} %copy-done.43, bf16[128,2688]{1,0:T(8,128)(2,1)S(1)} %get-tuple-element.39, ...), kind=kOutput, calls=%fused_computation.203 | convolution fusion | flops 785641472 | bytes 5246976 | tf_op jit(solution)/shard_map/dot_general | solution.py:33
  13.1 4.5 %collective-permute-start.1 = (bf16[272,256]{0,1:T(8,128)(2,1)S(1)}, bf16[272,256]{0,1:T(8,128)(2,1)S(1)}, u32[]{:S(2)}, u32[]{:S(2)}) collective-permute-start(bf16[272,256]{0,1:T(8,128)(2,1)S(1)} %pad_maximum_fusion.16), channel_id=1, source_target_pairs={{0,4},{2,6},{4,8},{6,10},{8,12},{10,14},{1,5},{3,7},{5,9},{7,11},{... | collective-permute-start | bytes 417800 | tf_op jit(solution)/shard_map/ppermute | solution.py:17
  17.6 4.8 %collective-permute-done.1 = bf16[272,256]{0,1:T(8,128)(2,1)S(1)} collective-permute-done((bf16[272,256]{0,1:T(8,128)(2,1)S(1)}, bf16[272,256]{0,1:T(8,128)(2,1)S(1)}, u32[]{:S(2)}, u32[]{:S(2)}) %collective-permute-start.1) | collective-permute-done | bytes 139296 | tf_op jit(solution)/shard_map/ppermute | solution.py:17
  22.4 4.4 %collective-permute-start.2 = (bf16[272,256]{0,1:T(8,128)(2,1)S(1)}, bf16[272,256]{0,1:T(8,128)(2,1)S(1)}, u32[]{:S(2)}, u32[]{:S(2)}) collective-permute-start(bf16[272,256]{0,1:T(8,128)(2,1)S(1)} %collective-permute-done.1), channel_id=1, source_target_pairs={{0,4},{2,6},{4,8},{6,10},{8,12},{10,14},{1,5},{3,7},{5,9},{7,11},{... | collective-permute-start | bytes 417800 | tf_op jit(solution)/shard_map/ppermute | solution.py:17
  26.9 3.4 %collective-permute-start.3 = (bf16[544,256]{0,1:T(8,128)(2,1)S(1)}, bf16[544,256]{0,1:T(8,128)(2,1)S(1)}, u32[]{:S(2)}, u32[]{:S(2)}) collective-permute-start(bf16[544,256]{0,1:T(8,128)(2,1)S(1)} %pad_maximum_fusion.14), channel_id=1, source_target_pairs={{0,2},{2,4},{4,6},{6,8},{8,10},{10,12},{12,14},{1,3},{3,5},{5,7},{... | collective-permute-start | bytes 835592 | tf_op jit(solution)/shard_map/ppermute | solution.py:17
  30.9 5.9 %collective-permute-done.3 = bf16[544,256]{0,1:T(8,128)(2,1)S(1)} collective-permute-done((bf16[544,256]{0,1:T(8,128)(2,1)S(1)}, bf16[544,256]{0,1:T(8,128)(2,1)S(1)}, u32[]{:S(2)}, u32[]{:S(2)}) %collective-permute-start.3) | collective-permute-done | bytes 278560 | tf_op jit(solution)/shard_map/ppermute | solution.py:17
  37.9 2.4 %fusion.21 = f32[2,256,1280]{1,2,0:T(8,128)} fusion(pred[256,1280]{0,1:T(8,128)(4,1)S(1)} %fusion.25, bf16[1280,256]{0,1:T(8,128)(2,1)S(1)} %maximum_dynamic-update-slice_fusion, f32[256,256]{0,1:T(8,128)S(1)} %get-tuple-element.53, f32[128]{0:T(128)S(1)} %copy-done.39, f32[256,2]{0,1:T(2,128)S(1)} %add_rsqrt_fusion), kind=kOutput, calls=%fused_computation.51 | convolution fusion | flops 169936640 | bytes 3541504 | tf_op jit(solution)/shard_map/div | solution.py:194
  40.3 2.1 %fusion.31 = bf16[128,2,256]{2,0,1:T(8,128)(2,1)S(1)} fusion(f32[2,256,1280]{1,2,0:T(8,128)} %fusion.21, bf16[1280,256]{0,1:T(8,128)(2,1)S(1)} %maximum_dynamic-update-slice_fusion, f32[256]{0:T(256)S(1)} %fusion.74), kind=kOutput, calls=%fused_computation.65 | convolution fusion | flops 168558592 | bytes 3081216 | tf_op jit(solution)/shard_map/hts,sd->thd/dot_general | solution.py:196
  44.6 1.6 %collective-permute-done.5 = bf16[128,16]{0,1:T(8,128)(2,1)} collective-permute-done((bf16[128,16]{0,1:T(8,128)(2,1)S(1)}, bf16[128,16]{0,1:T(8,128)(2,1)}, u32[]{:S(2)}, u32[]{:S(2)}) %collective-permute-start.5) | collective-permute-done | bytes 4128 | tf_op jit(solution)/shard_map/ppermute | solution.py:65
  46.9 1.7 %multiply_reduce_fusion.2 = (f32[128]{0:T(128)S(1)}, f32[128,2688]{1,0:T(8,128)S(1)}) fusion(bf16[128,16]{0,1:T(8,128)(2,1)S(1)} %add_convert_fusion.3, bf16[16,2688]{1,0:T(8,128)(2,1)S(1)} %copy-done.18, bf16[128,2688]{1,0:T(8,128)(2,1)} %collective-permute-done.4, bf16[256,2688]{1,0:T(8,128)(2,1)S(1)} %convolution_convert_fusion.1, s32[]{:T(128)S(6)} %select_n.62), kind=kOutput, calls=%fused_computation.48 | convolution fusion | flops 13418368 | bytes 2843140 | tf_op jit(solution)/shard_map/dot_general | solution.py:33
  60.9 11.4 %collective-permute-done.8 = bf16[512,256]{0,1:T(8,128)(2,1)S(1)} collective-permute-done((bf16[512,256]{0,1:T(8,128)(2,1)S(1)}, bf16[512,256]{0,1:T(8,128)(2,1)S(1)}, u32[]{:S(2)}, u32[]{:S(2)}) %collective-permute-start.8) | collective-permute-done | bytes 262176 | tf_op jit(solution)/shard_map/ppermute | solution.py:17
  73.8 1.5 %collective-permute-start.10 = (bf16[256,256]{0,1:T(8,128)(2,1)S(1)}, bf16[256,256]{0,1:T(8,128)(2,1)S(1)}, u32[]{:S(2)}, u32[]{:S(2)}) collective-permute-start(bf16[256,256]{0,1:T(8,128)(2,1)S(1)} %get-tuple-element.33), channel_id=1, source_target_pairs={{4,0},{6,2},{8,4},{10,6},{12,8},{14,10},{5,1},{7,3},{9,5},{11,7},{... | collective-permute-start | bytes 393224 | tf_op jit(solution)/shard_map/ppermute | solution.py:17
  75.4 4.2 %collective-permute-done.9 = bf16[256,256]{0,1:T(8,128)(2,1)S(1)} collective-permute-done((bf16[256,256]{0,1:T(8,128)(2,1)S(1)}, bf16[256,256]{0,1:T(8,128)(2,1)S(1)}, u32[]{:S(2)}, u32[]{:S(2)}) %collective-permute-start.9) | collective-permute-done | bytes 131104 | tf_op jit(solution)/shard_map/ppermute | solution.py:17
  79.6 2.5 %collective-permute-done.10 = bf16[256,256]{0,1:T(8,128)(2,1)S(1)} collective-permute-done((bf16[256,256]{0,1:T(8,128)(2,1)S(1)}, bf16[256,256]{0,1:T(8,128)(2,1)S(1)}, u32[]{:S(2)}, u32[]{:S(2)}) %collective-permute-start.10) | collective-permute-done | bytes 131104 | tf_op jit(solution)/shard_map/ppermute | solution.py:17
  86.6 1.7 %add_convert_fusion.2 = bf16[1344,48]{0,1:T(8,128)(2,1)} fusion(bf16[1344,48]{0,1:T(8,128)(2,1)} %collective-permute-done.12, bf16[2688,48]{0,1:T(8,128)(2,1)S(1)} %convolution_convert_fusion.2, s32[]{:T(128)S(6)} %select_n.69), kind=kLoop, calls=%fused_computation.106 | loop fusion | flops 258048 | bytes 387076 | tf_op jit(solution)/shard_map/convert.15
  95.0 3.2 %convolution_convert_fusion = bf16[256,2688]{1,0:T(8,128)(2,1)S(1)} fusion(bf16[256,560]{0,1:T(8,128)(2,1)} %copy-done.21, bf16[2688,48]{1,0:T(8,128)(2,1)S(1)} %copy-done.17, bf16[2688,128]{1,0:T(8,128)(2,1)} %param.30, bf16[2688,128]{1,0:T(8,128)(2,1)} %param.29, bf16[2688,256]{1,0:T(8,128)(2,1)} %param.28), kind=kOutput, calls=%fused_computation.1 | convolution fusion | flops 783433728 | bytes 4673536 | tf_op jit(solution)/shard_map/dot_general | solution.py:37
  98.2 2.9 %collective-permute-done.13 = bf16[98304]{0:T(1024)(128)(2,1)S(1)} collective-permute-done((bf16[98304]{0:T(1024)(128)(2,1)S(1)}, bf16[98304]{0:T(1024)(128)(2,1)S(1)}, u32[]{:S(2)}, u32[]{:S(2)}) %collective-permute-start.13) | collective-permute-done | bytes 196640 | tf_op jit(solution)/shard_map/ppermute | solution.py:87
  101.1 1.6 %collective-permute-start.14 = (bf16[98304]{0:T(1024)(128)(2,1)S(1)}, bf16[98304]{0:T(1024)(128)(2,1)S(1)}, u32[]{:S(2)}, u32[]{:S(2)}) collective-permute-start(bf16[98304]{0:T(1024)(128)(2,1)S(1)} %add_convert_fusion.1), channel_id=1, source_target_pairs={{0,4},{2,6},{4,0},{6,2},{8,12},{10,14},{12,8},{14,10},{1,5},{3,7},... | collective-permute-start | bytes 589832 | tf_op jit(solution)/shard_map/ppermute | solution.py:87
  102.9 4.8 %collective-permute-done.14 = bf16[98304]{0:T(1024)(128)(2,1)S(1)} collective-permute-done((bf16[98304]{0:T(1024)(128)(2,1)S(1)}, bf16[98304]{0:T(1024)(128)(2,1)S(1)}, u32[]{:S(2)}, u32[]{:S(2)}) %collective-permute-start.14) | collective-permute-done | bytes 196640 | tf_op jit(solution)/shard_map/ppermute | solution.py:87
  107.8 2.4 %collective-permute-start.15 = (bf16[98304]{0:T(1024)(128)(2,1)S(1)}, bf16[98304]{0:T(1024)(128)(2,1)S(1)}, u32[]{:S(2)}, u32[]{:S(2)}) collective-permute-start(bf16[98304]{0:T(1024)(128)(2,1)S(1)} %add_convert_fusion), channel_id=1, source_target_pairs={{0,8},{2,10},{4,12},{6,14},{8,0},{10,2},{12,4},{14,6},{1,9},{3,11}... | collective-permute-start | bytes 589832 | tf_op jit(solution)/shard_map/ppermute | solution.py:87
  112.1 6.5 %collective-permute-done.15 = bf16[98304]{0:T(1024)(128)(2,1)S(1)} collective-permute-done((bf16[98304]{0:T(1024)(128)(2,1)S(1)}, bf16[98304]{0:T(1024)(128)(2,1)S(1)}, u32[]{:S(2)}, u32[]{:S(2)}) %collective-permute-start.15) | collective-permute-done | bytes 196640 | tf_op jit(solution)/shard_map/ppermute | solution.py:87
  (205 shorter events, 39.3 us)
Async XLA Ops:
  0.6 41.8 %copy-start = (bf16[256,2688]{1,0:T(8,128)(2,1)S(1)}, bf16[256,2688]{1,0:T(8,128)(2,1)}, u32[]{:S(2)}) copy-start(bf16[256,2688]{1,0:T(8,128)(2,1)} %param.31) | copy-start | bytes 4128772
  3.5 3.5 %collective-permute-start = (bf16[128,2688]{1,0:T(8,128)(2,1)S(1)}, bf16[128,2688]{1,0:T(8,128)(2,1)S(1)}, u32[]{:S(2)}, u32[]{:S(2)}) collective-permute-start(bf16[128,2688]{1,0:T(8,128)(2,1)S(1)} %fusion.14), channel_id=1, source_target_pairs={{0,1},{1,0},{2,3},{3,2},{4,5},{5,4},{6,7},{7,6},{8,9},{9,8},{10,11... | collective-permute-start | bytes 2064392 | tf_op jit(solution)/shard_map/ppermute | solution.py:72
  6.9 33.4 %copy-start.41 = (f32[256]{0:T(256)}, f32[256]{0:T(256)S(1)}, u32[]{:S(2)}) copy-start(f32[256]{0:T(256)S(1)} %fusion.74) | copy-start | bytes 3076
  12.6 25.3 %copy-start.3 = (f32[256,256]{0,1:T(8,128)}, f32[256,256]{0,1:T(8,128)S(1)}, u32[]{:S(2)}) copy-start(f32[256,256]{0,1:T(8,128)S(1)} %get-tuple-element.53) | copy-start | bytes 786436
  12.6 18.3 %copy-start.27 = (f32[256]{0:T(256)}, f32[256]{0:T(256)S(1)}, u32[]{:S(2)}) copy-start(f32[256]{0:T(256)S(1)} %add_rsqrt_fusion.1) | copy-start | bytes 3076
  13.1 24.8 %copy-start.39 = (f32[128]{0:T(128)S(1)}, f32[128]{0:T(128)}, u32[]{:S(2)}) copy-start(f32[128]{0:T(128)} %param.25) | copy-start | bytes 1540
  13.1 9.3 %collective-permute-start.1 = (bf16[272,256]{0,1:T(8,128)(2,1)S(1)}, bf16[272,256]{0,1:T(8,128)(2,1)S(1)}, u32[]{:S(2)}, u32[]{:S(2)}) collective-permute-start(bf16[272,256]{0,1:T(8,128)(2,1)S(1)} %pad_maximum_fusion.16), channel_id=1, source_target_pairs={{0,4},{2,6},{4,8},{6,10},{8,12},{10,14},{1,5},{3,7},{5,9},{7,11},{... | collective-permute-start | bytes 417800 | tf_op jit(solution)/shard_map/ppermute | solution.py:17
  17.6 22.7 %copy-start.25 = (f32[256,2]{0,1:T(2,128)}, f32[256,2]{0,1:T(2,128)S(1)}, u32[]{:S(2)}) copy-start(f32[256,2]{0,1:T(2,128)S(1)} %add_rsqrt_fusion) | copy-start | bytes 6148
  22.4 8.4 %collective-permute-start.2 = (bf16[272,256]{0,1:T(8,128)(2,1)S(1)}, bf16[272,256]{0,1:T(8,128)(2,1)S(1)}, u32[]{:S(2)}, u32[]{:S(2)}) collective-permute-start(bf16[272,256]{0,1:T(8,128)(2,1)S(1)} %collective-permute-done.1), channel_id=1, source_target_pairs={{0,4},{2,6},{4,8},{6,10},{8,12},{10,14},{1,5},{3,7},{5,9},{7,11},{... | collective-permute-start | bytes 417800 | tf_op jit(solution)/shard_map/ppermute | solution.py:17
  26.9 9.9 %collective-permute-start.3 = (bf16[544,256]{0,1:T(8,128)(2,1)S(1)}, bf16[544,256]{0,1:T(8,128)(2,1)S(1)}, u32[]{:S(2)}, u32[]{:S(2)}) collective-permute-start(bf16[544,256]{0,1:T(8,128)(2,1)S(1)} %pad_maximum_fusion.14), channel_id=1, source_target_pairs={{0,2},{2,4},{4,6},{6,8},{8,10},{10,12},{12,14},{1,3},{3,5},{5,7},{... | collective-permute-start | bytes 835592 | tf_op jit(solution)/shard_map/ppermute | solution.py:17
  43.9 3.0 %collective-permute-start.4 = (bf16[128,2688]{1,0:T(8,128)(2,1)}, bf16[128,2688]{1,0:T(8,128)(2,1)}, u32[]{:S(2)}, u32[]{:S(2)}) collective-permute-start(bf16[128,2688]{1,0:T(8,128)(2,1)} %constant_dynamic-slice_fusion.3), channel_id=1, source_target_pairs={{0,1},{1,0},{2,3},{3,2},{4,5},{5,4},{6,7},{7,6},{8,9},{9,8},{10,11... | collective-permute-start | bytes 2064392 | tf_op jit(solution)/shard_map/ppermute | solution.py:65
  44.1 2.1 %collective-permute-start.5 = (bf16[128,16]{0,1:T(8,128)(2,1)S(1)}, bf16[128,16]{0,1:T(8,128)(2,1)}, u32[]{:S(2)}, u32[]{:S(2)}) collective-permute-start(bf16[128,16]{0,1:T(8,128)(2,1)S(1)} %constant_dynamic-slice_fusion.2), channel_id=1, source_target_pairs={{0,1},{1,0},{2,3},{3,2},{4,5},{5,4},{6,7},{7,6},{8,9},{9,8},{10,11... | collective-permute-start | bytes 12296 | tf_op jit(solution)/shard_map/ppermute | solution.py:65
  50.5 1.2 %collective-permute-start.7 = (bf16[128,32]{0,1:T(8,128)(2,1)S(1)}, bf16[128,32]{0,1:T(8,128)(2,1)S(1)}, u32[]{:S(2)}, u32[]{:S(2)}) collective-permute-start(bf16[128,32]{0,1:T(8,128)(2,1)S(1)} %pad_maximum_fusion.19), channel_id=1, source_target_pairs={{0,1},{1,0},{2,3},{3,2},{4,5},{5,4},{6,7},{7,6},{8,9},{9,8},{10,11... | collective-permute-start | bytes 24584 | tf_op jit(solution)/shard_map/ppermute | solution.py:72
  50.7 2.3 %collective-permute-start.6 = (bf16[128,2688]{1,0:T(8,128)(2,1)S(1)}, bf16[128,2688]{1,0:T(8,128)(2,1)}, u32[]{:S(2)}, u32[]{:S(2)}) collective-permute-start(bf16[128,2688]{1,0:T(8,128)(2,1)S(1)} %get-tuple-element.34), channel_id=1, source_target_pairs={{0,1},{1,0},{2,3},{3,2},{4,5},{5,4},{6,7},{7,6},{8,9},{9,8},{10,11... | collective-permute-start | bytes 2064392 | tf_op jit(solution)/shard_map/ppermute | solution.py:72
  59.3 13.1 %collective-permute-start.8 = (bf16[512,256]{0,1:T(8,128)(2,1)S(1)}, bf16[512,256]{0,1:T(8,128)(2,1)S(1)}, u32[]{:S(2)}, u32[]{:S(2)}) collective-permute-start(bf16[512,256]{0,1:T(8,128)(2,1)S(1)} %fusion.51), channel_id=1, source_target_pairs={{4,0},{6,2},{8,4},{10,6},{12,8},{14,10},{5,1},{7,3},{9,5},{11,7},{... | collective-permute-start | bytes 786440 | tf_op jit(solution)/shard_map/ppermute | solution.py:17
  72.5 7.1 %collective-permute-start.9 = (bf16[256,256]{0,1:T(8,128)(2,1)S(1)}, bf16[256,256]{0,1:T(8,128)(2,1)S(1)}, u32[]{:S(2)}, u32[]{:S(2)}) collective-permute-start(bf16[256,256]{0,1:T(8,128)(2,1)S(1)} %get-tuple-element.32), channel_id=1, source_target_pairs={{2,0},{4,2},{6,4},{8,6},{10,8},{12,10},{14,12},{3,1},{5,3},{7,5},{... | collective-permute-start | bytes 393224 | tf_op jit(solution)/shard_map/ppermute | solution.py:17
  73.8 8.3 %collective-permute-start.10 = (bf16[256,256]{0,1:T(8,128)(2,1)S(1)}, bf16[256,256]{0,1:T(8,128)(2,1)S(1)}, u32[]{:S(2)}, u32[]{:S(2)}) collective-permute-start(bf16[256,256]{0,1:T(8,128)(2,1)S(1)} %get-tuple-element.33), channel_id=1, source_target_pairs={{4,0},{6,2},{8,4},{10,6},{12,8},{14,10},{5,1},{7,3},{9,5},{11,7},{... | collective-permute-start | bytes 393224 | tf_op jit(solution)/shard_map/ppermute | solution.py:17
  84.0 2.7 %collective-permute-start.12 = (bf16[1344,48]{0,1:T(8,128)(2,1)}, bf16[1344,48]{0,1:T(8,128)(2,1)}, u32[]{:S(2)}, u32[]{:S(2)}) collective-permute-start(bf16[1344,48]{0,1:T(8,128)(2,1)} %constant_dynamic-slice_fusion), channel_id=1, source_target_pairs={{0,1},{1,0},{2,3},{3,2},{4,5},{5,4},{6,7},{7,6},{8,9},{9,8},{10,11... | collective-permute-start | bytes 387080 | tf_op jit(solution)/shard_map/ppermute | solution.py:65
  93.8 7.3 %collective-permute-start.13 = (bf16[98304]{0:T(1024)(128)(2,1)S(1)}, bf16[98304]{0:T(1024)(128)(2,1)S(1)}, u32[]{:S(2)}, u32[]{:S(2)}) collective-permute-start(bf16[98304]{0:T(1024)(128)(2,1)S(1)} %constant_dynamic-update-slice_fusion.12), channel_id=1, source_target_pairs={{0,2},{2,0},{4,6},{6,4},{8,10},{10,8},{12,14},{14,12},{1,3},{3,1},... | collective-permute-start | bytes 589832 | tf_op jit(solution)/shard_map/ppermute | solution.py:87
  98.1 12.1 %copy-start.20 = (f32[2688]{0:T(1024)S(1)}, f32[2688]{0:T(1024)}, u32[]{:S(2)}) copy-start(f32[2688]{0:T(1024)} %param.24) | copy-start | bytes 32260
  98.2 12.1 %copy-start.35 = (f32[128]{0:T(128)S(1)}, f32[128]{0:T(128)}, u32[]{:S(2)}) copy-start(f32[128]{0:T(128)} %copy-done.34) | copy-start | bytes 1540
  101.1 6.6 %collective-permute-start.14 = (bf16[98304]{0:T(1024)(128)(2,1)S(1)}, bf16[98304]{0:T(1024)(128)(2,1)S(1)}, u32[]{:S(2)}, u32[]{:S(2)}) collective-permute-start(bf16[98304]{0:T(1024)(128)(2,1)S(1)} %add_convert_fusion.1), channel_id=1, source_target_pairs={{0,4},{2,6},{4,0},{6,2},{8,12},{10,14},{12,8},{14,10},{1,5},{3,7},... | collective-permute-start | bytes 589832 | tf_op jit(solution)/shard_map/ppermute | solution.py:87
  102.8 7.4 %collective-permute-start.11 = (bf16[128,2688]{1,0:T(8,128)(2,1)S(1)}, bf16[128,2688]{1,0:T(8,128)(2,1)S(1)}, u32[]{:S(2)}, u32[]{:S(2)}) collective-permute-start(bf16[128,2688]{1,0:T(8,128)(2,1)S(1)} %constant_dynamic-slice_fusion.1), channel_id=1, source_target_pairs={{0,1},{1,0},{2,3},{3,2},{4,5},{5,4},{6,7},{7,6},{8,9},{9,8},{10,11... | collective-permute-start | bytes 2064392 | tf_op jit(solution)/shard_map/ppermute | solution.py:65
  107.8 10.8 %collective-permute-start.15 = (bf16[98304]{0:T(1024)(128)(2,1)S(1)}, bf16[98304]{0:T(1024)(128)(2,1)S(1)}, u32[]{:S(2)}, u32[]{:S(2)}) collective-permute-start(bf16[98304]{0:T(1024)(128)(2,1)S(1)} %add_convert_fusion), channel_id=1, source_target_pairs={{0,8},{2,10},{4,12},{6,14},{8,0},{10,2},{12,4},{14,6},{1,9},{3,11}... | collective-permute-start | bytes 589832 | tf_op jit(solution)/shard_map/ppermute | solution.py:87
  (37 other events, 131.5 us)

commit v18 on v11

--- a/solution.py
+++ b/solution.py
@@ -70,9 +70,9 @@
     if lax.axis_size("tp") != 2:
         return lax.all_gather(value, "tp", axis=0, tiled=True)
     received = lax.ppermute(value, "tp", [(0, 1), (1, 0)])
-    first = lax.axis_index("tp") == 0
-    return jnp.concatenate(
-        [jnp.where(first, value, received), jnp.where(first, received, value)], axis=0
+    both = jnp.concatenate([received, received], axis=0)
+    return lax.dynamic_update_slice_in_dim(
+        both, value, lax.axis_index("tp") * value.shape[0], 0
     )
 
 

time: 124 us -> 122 us (0.984)
    dot_general x7, matrix products: 5.7 us -> 3.39 us  [matrix_product(): return jnp.dot(first_op, second_op, preferred_element_type=jnp.float32)]
    select_n x3 -> x0, other arithmetic: 1.67 us -> none  [the longest x2 1.66 us: tp_gather(): jnp.where(first, value, received)]
    concatenate x0 -> x3, other arithmetic: none -> 1.5 us  [tp_gather(): both = jnp.concatenate([received, received], axis=0)]
    unnamed x107 -> x77, local copies, waits for them, and re-layouts: 9.9 us -> 9.61 us
  transfers between devices with their start and end apart: 16 -> 16, of which waited for: 11 -> 12; matrix products, arithmetic and copies ran while one was open for 10% -> 10% of each run, Pallas kernels for 0% -> 0%
where the time goes in v18:
time: 122 us; the launch traced here: 121 us
  waiting for transfers between devices  46.3 us (38%)
  starting transfers between devices  22.9 us (19%)
  matrix products  19.6 us (16%)
  local copies, waits for them, and re-layouts  17 us (14%)
  other arithmetic  13.3 us (11%)
  between operations  2.11 us (2%)
    ppermute x6, waiting for transfers between devices, passed_along(): lax.ppermute(value, axis, [(source, source + steps) for source in range(l...  29.2 us
    ppermute x6, starting transfers between devices, passed_along(): lax.ppermute(value, axis, [(source, source + steps) for source in range(l...  16.4 us
    ppermute x3, waiting for transfers between devices, ctx_sum(): received = lax.ppermute(sent, 'ctx', [(i, i ^ step) for i in range(count)])  14.4 us
    unnamed x77, local copies, waits for them, and re-layouts  9.61 us
    ppermute x3, starting transfers between devices, ctx_sum(): received = lax.ppermute(sent, 'ctx', [(i, i ^ step) for i in range(count)])  5.28 us
    dot_general x7, matrix products, multiply_by_transpose(): lax.dot_general(first_op, second_op, (((1,), (1,)), ((), ())), preferred_...  4.64 us
    dot_general x6, matrix products, transpose_multiply(): lax.dot_general(first_op, second_op, (((0,), (0,)), ((), ())), preferred_...  4.05 us
    div x1, matrix products, on_device(): attn_probs = weights / jnp.sum(weights, axis=-1, keepdims=True)  3.42 us
  transfers between devices with their start and end apart: 16, of which 12 were waited for; matrix products, arithmetic and copies ran while one was open for 10% of the time, Pallas kernels for 0%

profile of v18, /device:TPU:0, one launch (start us, length us, event | category | flops | bytes accessed | tf_op | source)
XLA Modules:
  0.0 121.2 jit_solution(9236740145773045569)
XLA Ops:
  0.7 1.4 %fusion.18 = f32[128]{0:T(128)S(1)} fusion(bf16[128,2688]{1,0:T(8,128)(2,1)} %param.20), kind=kLoop, calls=%fused_computation.38 | loop fusion | flops 1032064 | bytes 688640 | tf_op jit(solution)/shard_map/reduce_sum | solution.py:21
  4.8 2.1 %copy.35 = bf16[2688,48]{1,0:T(8,128)(2,1)} copy(bf16[2688,48]{0,1:T(8,128)(2,1)} %param.32) | data formatting | bytes 516096 | tf_op args[12]
  8.9 1.5 %fusion.82 = (bf16[256,560]{0,1:T(8,128)(2,1)S(1)}, f32[256,560]{0,1:T(8,128)S(1)}) fusion(bf16[256,2688]{1,0:T(8,128)(2,1)S(1)} %constant_dynamic-update-slice_fusion.17, bf16[2688,48]{1,0:T(8,128)(2,1)S(1)} %copy-done.8, bf16[2688,128]{1,0:T(8,128)(2,1)S(1)} %copy-done.28, bf16[2688,128]{1,0:T(8,128)(2,1)S(1)} %copy-done.29, ...), kind=kOutput, calls=%fused_computation.196 | convolution fusion | flops 782888960 | bytes 5246976 | tf_op jit(solution)/shard_map/dot_general | solution.py:33
  11.3 4.5 %collective-permute-start.1 = (bf16[272,256]{0,1:T(8,128)(2,1)S(1)}, bf16[272,256]{0,1:T(8,128)(2,1)S(1)}, u32[]{:S(2)}, u32[]{:S(2)}) collective-permute-start(bf16[272,256]{0,1:T(8,128)(2,1)S(1)} %pad_maximum_fusion.8), channel_id=1, source_target_pairs={{0,4},{2,6},{4,8},{6,10},{8,12},{10,14},{1,5},{3,7},{5,9},{7,11},{... | collective-permute-start | bytes 417800 | tf_op jit(solution)/shard_map/ppermute | solution.py:17
  15.8 4.8 %collective-permute-done.1 = bf16[272,256]{0,1:T(8,128)(2,1)S(1)} collective-permute-done((bf16[272,256]{0,1:T(8,128)(2,1)S(1)}, bf16[272,256]{0,1:T(8,128)(2,1)S(1)}, u32[]{:S(2)}, u32[]{:S(2)}) %collective-permute-start.1) | collective-permute-done | bytes 139296 | tf_op jit(solution)/shard_map/ppermute | solution.py:17
  20.6 4.4 %collective-permute-start.2 = (bf16[272,256]{0,1:T(8,128)(2,1)S(1)}, bf16[272,256]{0,1:T(8,128)(2,1)S(1)}, u32[]{:S(2)}, u32[]{:S(2)}) collective-permute-start(bf16[272,256]{0,1:T(8,128)(2,1)S(1)} %collective-permute-done.1), channel_id=1, source_target_pairs={{0,4},{2,6},{4,8},{6,10},{8,12},{10,14},{1,5},{3,7},{5,9},{7,11},{... | collective-permute-start | bytes 417800 | tf_op jit(solution)/shard_map/ppermute | solution.py:17
  25.1 3.4 %collective-permute-start.3 = (bf16[544,256]{0,1:T(8,128)(2,1)S(1)}, bf16[544,256]{0,1:T(8,128)(2,1)S(1)}, u32[]{:S(2)}, u32[]{:S(2)}) collective-permute-start(bf16[544,256]{0,1:T(8,128)(2,1)S(1)} %pad_maximum_fusion.6), channel_id=1, source_target_pairs={{0,2},{2,4},{4,6},{6,8},{8,10},{10,12},{12,14},{1,3},{3,5},{5,7},{... | collective-permute-start | bytes 835592 | tf_op jit(solution)/shard_map/ppermute | solution.py:17
  29.2 5.9 %collective-permute-done.3 = bf16[544,256]{0,1:T(8,128)(2,1)S(1)} collective-permute-done((bf16[544,256]{0,1:T(8,128)(2,1)S(1)}, bf16[544,256]{0,1:T(8,128)(2,1)S(1)}, u32[]{:S(2)}, u32[]{:S(2)}) %collective-permute-start.3) | collective-permute-done | bytes 278560 | tf_op jit(solution)/shard_map/ppermute | solution.py:17
  36.8 3.4 %fusion.21 = f32[2,256,1280]{1,2,0:T(8,128)} fusion(pred[256,1280]{0,1:T(8,128)(4,1)} %fusion.25, bf16[1280,256]{0,1:T(8,128)(2,1)S(1)} %maximum_dynamic-update-slice_fusion, f32[256,256]{0,1:T(8,128)S(1)} %get-tuple-element.49, f32[128]{0:T(128)S(1)} %copy-done.25, f32[256,2]{0,1:T(2,128)S(1)} %add_rsqrt_fusion), kind=kOutput, calls=%fused_computation.50 | convolution fusion | flops 169936640 | bytes 3541504 | tf_op jit(solution)/shard_map/div | solution.py:194
  40.2 2.1 %fusion.31 = bf16[128,2,256]{2,0,1:T(8,128)(2,1)S(1)} fusion(f32[2,256,1280]{1,2,0:T(8,128)} %fusion.21, bf16[1280,256]{0,1:T(8,128)(2,1)S(1)} %maximum_dynamic-update-slice_fusion, f32[256]{0:T(256)S(1)} %fusion.74), kind=kOutput, calls=%fused_computation.65 | convolution fusion | flops 168558592 | bytes 3081216 | tf_op jit(solution)/shard_map/hts,sd->thd/dot_general | solution.py:196
  43.8 1.5 %collective-permute-done.5 = bf16[128,16]{0,1:T(8,128)(2,1)S(1)} collective-permute-done((bf16[128,16]{0,1:T(8,128)(2,1)S(1)}, bf16[128,16]{0,1:T(8,128)(2,1)S(1)}, u32[]{:S(2)}, u32[]{:S(2)}) %collective-permute-start.5) | collective-permute-done | bytes 4128 | tf_op jit(solution)/shard_map/ppermute | solution.py:65
  50.7 1.4 %pad_maximum_fusion.3 = bf16[256,2688]{1,0:T(8,128)(2,1)S(1)} fusion(bf16[128,2688]{1,0:T(8,128)(2,1)} %collective-permute-done.6), kind=kLoop, calls=%fused_computation.40 | loop fusion | flops 2752512 | bytes 2064384 | tf_op jit(solution)/shard_map/concatenate | solution.py:73
  58.9 11.4 %collective-permute-done.8 = bf16[512,256]{0,1:T(8,128)(2,1)S(1)} collective-permute-done((bf16[512,256]{0,1:T(8,128)(2,1)S(1)}, bf16[512,256]{0,1:T(8,128)(2,1)S(1)}, u32[]{:S(2)}, u32[]{:S(2)}) %collective-permute-start.8) | collective-permute-done | bytes 262176 | tf_op jit(solution)/shard_map/ppermute | solution.py:17
  71.8 1.5 %collective-permute-start.10 = (bf16[256,256]{0,1:T(8,128)(2,1)S(1)}, bf16[256,256]{0,1:T(8,128)(2,1)S(1)}, u32[]{:S(2)}, u32[]{:S(2)}) collective-permute-start(bf16[256,256]{0,1:T(8,128)(2,1)S(1)} %get-tuple-element.33), channel_id=1, source_target_pairs={{4,0},{6,2},{8,4},{10,6},{12,8},{14,10},{5,1},{7,3},{9,5},{11,7},{... | collective-permute-start | bytes 393224 | tf_op jit(solution)/shard_map/ppermute | solution.py:17
  73.3 4.2 %collective-permute-done.9 = bf16[256,256]{0,1:T(8,128)(2,1)S(1)} collective-permute-done((bf16[256,256]{0,1:T(8,128)(2,1)S(1)}, bf16[256,256]{0,1:T(8,128)(2,1)S(1)}, u32[]{:S(2)}, u32[]{:S(2)}) %collective-permute-start.9) | collective-permute-done | bytes 131104 | tf_op jit(solution)/shard_map/ppermute | solution.py:17
  77.5 2.6 %collective-permute-done.10 = bf16[256,256]{0,1:T(8,128)(2,1)S(1)} collective-permute-done((bf16[256,256]{0,1:T(8,128)(2,1)S(1)}, bf16[256,256]{0,1:T(8,128)(2,1)S(1)}, u32[]{:S(2)}, u32[]{:S(2)}) %collective-permute-start.10) | collective-permute-done | bytes 131104 | tf_op jit(solution)/shard_map/ppermute | solution.py:17
  83.3 1.5 %reshape.265 = bf16[21504]{0:T(1024)(128)(2,1)} reshape(bf16[16,1344]{1,0:T(8,128)(2,1)} %fusion.9) | data formatting | bytes 86016 | tf_op jit(solution)/shard_map/reshape | solution.py:83
  85.7 1.7 %add_convert_fusion.2 = bf16[1344,48]{0,1:T(8,128)(2,1)} fusion(bf16[1344,48]{0,1:T(8,128)(2,1)} %collective-permute-done.12, bf16[2688,48]{0,1:T(8,128)(2,1)S(1)} %convolution_convert_fusion.2, s32[]{:T(128)S(6)} %select_n.32), kind=kLoop, calls=%fused_computation.99 | loop fusion | flops 258048 | bytes 387076 | tf_op jit(solution)/shard_map/convert.15
  93.5 3.2 %convolution_convert_fusion = bf16[256,2688]{1,0:T(8,128)(2,1)S(1)} fusion(bf16[256,560]{0,1:T(8,128)(2,1)} %copy-done.13, bf16[2688,48]{1,0:T(8,128)(2,1)S(1)} %copy-done.9, bf16[2688,128]{1,0:T(8,128)(2,1)} %param.30, bf16[2688,128]{1,0:T(8,128)(2,1)} %param.29, bf16[2688,256]{1,0:T(8,128)(2,1)} %param.28), kind=kOutput, calls=%fused_computation.1 | convolution fusion | flops 783433728 | bytes 4673536 | tf_op jit(solution)/shard_map/dot_general | solution.py:37
  96.7 3.0 %collective-permute-done.13 = bf16[98304]{0:T(1024)(128)(2,1)S(1)} collective-permute-done((bf16[98304]{0:T(1024)(128)(2,1)S(1)}, bf16[98304]{0:T(1024)(128)(2,1)S(1)}, u32[]{:S(2)}, u32[]{:S(2)}) %collective-permute-start.13) | collective-permute-done | bytes 196640 | tf_op jit(solution)/shard_map/ppermute | solution.py:87
  99.7 1.7 %collective-permute-start.14 = (bf16[98304]{0:T(1024)(128)(2,1)S(1)}, bf16[98304]{0:T(1024)(128)(2,1)S(1)}, u32[]{:S(2)}, u32[]{:S(2)}) collective-permute-start(bf16[98304]{0:T(1024)(128)(2,1)S(1)} %add_convert_fusion.1), channel_id=1, source_target_pairs={{0,4},{2,6},{4,0},{6,2},{8,12},{10,14},{12,8},{14,10},{1,5},{3,7},... | collective-permute-start | bytes 589832 | tf_op jit(solution)/shard_map/ppermute | solution.py:87
  101.5 4.8 %collective-permute-done.14 = bf16[98304]{0:T(1024)(128)(2,1)S(1)} collective-permute-done((bf16[98304]{0:T(1024)(128)(2,1)S(1)}, bf16[98304]{0:T(1024)(128)(2,1)S(1)}, u32[]{:S(2)}, u32[]{:S(2)}) %collective-permute-start.14) | collective-permute-done | bytes 196640 | tf_op jit(solution)/shard_map/ppermute | solution.py:87
  106.4 2.4 %collective-permute-start.15 = (bf16[98304]{0:T(1024)(128)(2,1)S(1)}, bf16[98304]{0:T(1024)(128)(2,1)S(1)}, u32[]{:S(2)}, u32[]{:S(2)}) collective-permute-start(bf16[98304]{0:T(1024)(128)(2,1)S(1)} %add_convert_fusion), channel_id=1, source_target_pairs={{0,8},{2,10},{4,12},{6,14},{8,0},{10,2},{12,4},{14,6},{1,9},{3,11}... | collective-permute-start | bytes 589832 | tf_op jit(solution)/shard_map/ppermute | solution.py:87
  110.6 6.6 %collective-permute-done.15 = bf16[98304]{0:T(1024)(128)(2,1)S(1)} collective-permute-done((bf16[98304]{0:T(1024)(128)(2,1)S(1)}, bf16[98304]{0:T(1024)(128)(2,1)S(1)}, u32[]{:S(2)}, u32[]{:S(2)}) %collective-permute-start.15) | collective-permute-done | bytes 196640 | tf_op jit(solution)/shard_map/ppermute | solution.py:87
  (180 shorter events, 38.2 us)
Async XLA Ops:
  0.6 41.7 %copy-start = (bf16[256,2688]{1,0:T(8,128)(2,1)S(1)}, bf16[256,2688]{1,0:T(8,128)(2,1)}, u32[]{:S(2)}) copy-start(bf16[256,2688]{1,0:T(8,128)(2,1)} %param.31) | copy-start | bytes 4128772
  3.4 3.6 %collective-permute-start = (bf16[128,2688]{1,0:T(8,128)(2,1)S(1)}, bf16[128,2688]{1,0:T(8,128)(2,1)S(1)}, u32[]{:S(2)}, u32[]{:S(2)}) collective-permute-start(bf16[128,2688]{1,0:T(8,128)(2,1)S(1)} %fusion.13), channel_id=1, source_target_pairs={{0,1},{1,0},{2,3},{3,2},{4,5},{5,4},{6,7},{7,6},{8,9},{9,8},{10,11... | collective-permute-start | bytes 2064392 | tf_op jit(solution)/shard_map/ppermute | solution.py:72
  10.4 24.8 %copy-start.19 = (bf16[256,560]{0,1:T(8,128)(2,1)}, bf16[256,560]{0,1:T(8,128)(2,1)S(1)}, u32[]{:S(2)}) copy-start(bf16[256,560]{0,1:T(8,128)(2,1)S(1)} %get-tuple-element.44) | copy-start | bytes 860164
  10.4 18.7 %copy-start.20 = (s32[1280]{0:T(1024)S(1)}, s32[1280]{0:T(1024)}, u32[]{:S(2)}) copy-start(s32[1280]{0:T(1024)} %custom-call.2) | copy-start | bytes 15364
  11.3 24.2 %copy-start.24 = (s32[256]{0:T(256)S(1)}, s32[256]{0:T(256)}, u32[]{:S(2)}) copy-start(s32[256]{0:T(256)} %param.22) | copy-start | bytes 3076
  11.3 25.5 %copy-start.25 = (f32[128]{0:T(128)S(1)}, f32[128]{0:T(128)}, u32[]{:S(2)}) copy-start(f32[128]{0:T(128)} %param.25) | copy-start | bytes 1540
  11.3 9.3 %collective-permute-start.1 = (bf16[272,256]{0,1:T(8,128)(2,1)S(1)}, bf16[272,256]{0,1:T(8,128)(2,1)S(1)}, u32[]{:S(2)}, u32[]{:S(2)}) collective-permute-start(bf16[272,256]{0,1:T(8,128)(2,1)S(1)} %pad_maximum_fusion.8), channel_id=1, source_target_pairs={{0,4},{2,6},{4,8},{6,10},{8,12},{10,14},{1,5},{3,7},{5,9},{7,11},{... | collective-permute-start | bytes 417800 | tf_op jit(solution)/shard_map/ppermute | solution.py:17
  20.6 8.4 %collective-permute-start.2 = (bf16[272,256]{0,1:T(8,128)(2,1)S(1)}, bf16[272,256]{0,1:T(8,128)(2,1)S(1)}, u32[]{:S(2)}, u32[]{:S(2)}) collective-permute-start(bf16[272,256]{0,1:T(8,128)(2,1)S(1)} %collective-permute-done.1), channel_id=1, source_target_pairs={{0,4},{2,6},{4,8},{6,10},{8,12},{10,14},{1,5},{3,7},{5,9},{7,11},{... | collective-permute-start | bytes 417800 | tf_op jit(solution)/shard_map/ppermute | solution.py:17
  25.1 9.9 %collective-permute-start.3 = (bf16[544,256]{0,1:T(8,128)(2,1)S(1)}, bf16[544,256]{0,1:T(8,128)(2,1)S(1)}, u32[]{:S(2)}, u32[]{:S(2)}) collective-permute-start(bf16[544,256]{0,1:T(8,128)(2,1)S(1)} %pad_maximum_fusion.6), channel_id=1, source_target_pairs={{0,2},{2,4},{4,6},{6,8},{8,10},{10,12},{12,14},{1,3},{3,5},{5,7},{... | collective-permute-start | bytes 835592 | tf_op jit(solution)/shard_map/ppermute | solution.py:17
  43.0 2.2 %collective-permute-start.4 = (bf16[128,2688]{1,0:T(8,128)(2,1)S(1)}, bf16[128,2688]{1,0:T(8,128)(2,1)S(1)}, u32[]{:S(2)}, u32[]{:S(2)}) collective-permute-start(bf16[128,2688]{1,0:T(8,128)(2,1)S(1)} %constant_dynamic-slice_fusion.3), channel_id=1, source_target_pairs={{0,1},{1,0},{2,3},{3,2},{4,5},{5,4},{6,7},{7,6},{8,9},{9,8},{10,11... | collective-permute-start | bytes 2064392 | tf_op jit(solution)/shard_map/ppermute | solution.py:65
  43.8 1.5 %collective-permute-start.5 = (bf16[128,16]{0,1:T(8,128)(2,1)S(1)}, bf16[128,16]{0,1:T(8,128)(2,1)S(1)}, u32[]{:S(2)}, u32[]{:S(2)}) collective-permute-start(bf16[128,16]{0,1:T(8,128)(2,1)S(1)} %constant_dynamic-slice_fusion.2), channel_id=1, source_target_pairs={{0,1},{1,0},{2,3},{3,2},{4,5},{5,4},{6,7},{7,6},{8,9},{9,8},{10,11... | collective-permute-start | bytes 12296 | tf_op jit(solution)/shard_map/ppermute | solution.py:65
  48.2 1.2 %collective-permute-start.7 = (bf16[128,32]{0,1:T(8,128)(2,1)S(1)}, bf16[128,32]{0,1:T(8,128)(2,1)S(1)}, u32[]{:S(2)}, u32[]{:S(2)}) collective-permute-start(bf16[128,32]{0,1:T(8,128)(2,1)S(1)} %pad_maximum_fusion.10), channel_id=1, source_target_pairs={{0,1},{1,0},{2,3},{3,2},{4,5},{5,4},{6,7},{7,6},{8,9},{9,8},{10,11... | collective-permute-start | bytes 24584 | tf_op jit(solution)/shard_map/ppermute | solution.py:72
  48.4 2.3 %collective-permute-start.6 = (bf16[128,2688]{1,0:T(8,128)(2,1)S(1)}, bf16[128,2688]{1,0:T(8,128)(2,1)}, u32[]{:S(2)}, u32[]{:S(2)}) collective-permute-start(bf16[128,2688]{1,0:T(8,128)(2,1)S(1)} %get-tuple-element.34), channel_id=1, source_target_pairs={{0,1},{1,0},{2,3},{3,2},{4,5},{5,4},{6,7},{7,6},{8,9},{9,8},{10,11... | collective-permute-start | bytes 2064392 | tf_op jit(solution)/shard_map/ppermute | solution.py:72
  57.2 13.1 %collective-permute-start.8 = (bf16[512,256]{0,1:T(8,128)(2,1)S(1)}, bf16[512,256]{0,1:T(8,128)(2,1)S(1)}, u32[]{:S(2)}, u32[]{:S(2)}) collective-permute-start(bf16[512,256]{0,1:T(8,128)(2,1)S(1)} %pad_maximum_fusion.7), channel_id=1, source_target_pairs={{4,0},{6,2},{8,4},{10,6},{12,8},{14,10},{5,1},{7,3},{9,5},{11,7},{... | collective-permute-start | bytes 786440 | tf_op jit(solution)/shard_map/ppermute | solution.py:17
  70.5 7.1 %collective-permute-start.9 = (bf16[256,256]{0,1:T(8,128)(2,1)S(1)}, bf16[256,256]{0,1:T(8,128)(2,1)S(1)}, u32[]{:S(2)}, u32[]{:S(2)}) collective-permute-start(bf16[256,256]{0,1:T(8,128)(2,1)S(1)} %get-tuple-element.32), channel_id=1, source_target_pairs={{2,0},{4,2},{6,4},{8,6},{10,8},{12,10},{14,12},{3,1},{5,3},{7,5},{... | collective-permute-start | bytes 393224 | tf_op jit(solution)/shard_map/ppermute | solution.py:17
  71.8 8.4 %collective-permute-start.10 = (bf16[256,256]{0,1:T(8,128)(2,1)S(1)}, bf16[256,256]{0,1:T(8,128)(2,1)S(1)}, u32[]{:S(2)}, u32[]{:S(2)}) collective-permute-start(bf16[256,256]{0,1:T(8,128)(2,1)S(1)} %get-tuple-element.33), channel_id=1, source_target_pairs={{4,0},{6,2},{8,4},{10,6},{12,8},{14,10},{5,1},{7,3},{9,5},{11,7},{... | collective-permute-start | bytes 393224 | tf_op jit(solution)/shard_map/ppermute | solution.py:17
  73.2 6.9 %copy-start.22 = (f32[128]{0:T(128)S(1)}, f32[128]{0:T(128)}, u32[]{:S(2)}) copy-start(f32[128]{0:T(128)} %param.26) | copy-start | bytes 1540
  73.3 7.5 %copy-start.4 = (bf16[256,2688]{1,0:T(8,128)(2,1)S(1)}, bf16[256,2688]{1,0:T(8,128)(2,1)}, u32[]{:S(2)}) copy-start(bf16[256,2688]{1,0:T(8,128)(2,1)} %copy-done.3) | copy-start | bytes 4128772
  82.3 11.2 %copy-start.9 = (bf16[2688,48]{1,0:T(8,128)(2,1)S(1)}, bf16[2688,48]{1,0:T(8,128)(2,1)}, u32[]{:S(2)}) copy-start(bf16[2688,48]{1,0:T(8,128)(2,1)} %copy.35) | copy-start | bytes 774148
  82.3 3.4 %collective-permute-start.12 = (bf16[1344,48]{0,1:T(8,128)(2,1)}, bf16[1344,48]{0,1:T(8,128)(2,1)}, u32[]{:S(2)}, u32[]{:S(2)}) collective-permute-start(bf16[1344,48]{0,1:T(8,128)(2,1)} %constant_dynamic-slice_fusion), channel_id=1, source_target_pairs={{0,1},{1,0},{2,3},{3,2},{4,5},{5,4},{6,7},{7,6},{8,9},{9,8},{10,11... | collective-permute-start | bytes 387080 | tf_op jit(solution)/shard_map/ppermute | solution.py:65
  92.3 7.4 %collective-permute-start.13 = (bf16[98304]{0:T(1024)(128)(2,1)S(1)}, bf16[98304]{0:T(1024)(128)(2,1)S(1)}, u32[]{:S(2)}, u32[]{:S(2)}) collective-permute-start(bf16[98304]{0:T(1024)(128)(2,1)S(1)} %constant_dynamic-update-slice_fusion.12), channel_id=1, source_target_pairs={{0,2},{2,0},{4,6},{6,4},{8,10},{10,8},{12,14},{14,12},{1,3},{3,1},... | collective-permute-start | bytes 589832 | tf_op jit(solution)/shard_map/ppermute | solution.py:87
  99.7 6.6 %collective-permute-start.14 = (bf16[98304]{0:T(1024)(128)(2,1)S(1)}, bf16[98304]{0:T(1024)(128)(2,1)S(1)}, u32[]{:S(2)}, u32[]{:S(2)}) collective-permute-start(bf16[98304]{0:T(1024)(128)(2,1)S(1)} %add_convert_fusion.1), channel_id=1, source_target_pairs={{0,4},{2,6},{4,0},{6,2},{8,12},{10,14},{12,8},{14,10},{1,5},{3,7},... | collective-permute-start | bytes 589832 | tf_op jit(solution)/shard_map/ppermute | solution.py:87
  101.4 7.4 %collective-permute-start.11 = (bf16[128,2688]{1,0:T(8,128)(2,1)S(1)}, bf16[128,2688]{1,0:T(8,128)(2,1)S(1)}, u32[]{:S(2)}, u32[]{:S(2)}) collective-permute-start(bf16[128,2688]{1,0:T(8,128)(2,1)S(1)} %constant_dynamic-slice_fusion.1), channel_id=1, source_target_pairs={{0,1},{1,0},{2,3},{3,2},{4,5},{5,4},{6,7},{7,6},{8,9},{9,8},{10,11... | collective-permute-start | bytes 2064392 | tf_op jit(solution)/shard_map/ppermute | solution.py:65
  106.4 10.8 %collective-permute-start.15 = (bf16[98304]{0:T(1024)(128)(2,1)S(1)}, bf16[98304]{0:T(1024)(128)(2,1)S(1)}, u32[]{:S(2)}, u32[]{:S(2)}) collective-permute-start(bf16[98304]{0:T(1024)(128)(2,1)S(1)} %add_convert_fusion), channel_id=1, source_target_pairs={{0,8},{2,10},{4,12},{6,14},{8,0},{10,2},{12,4},{14,6},{1,9},{3,11}... | collective-permute-start | bytes 589832 | tf_op jit(solution)/shard_map/ppermute | solution.py:87
  (22 other events, 43.6 us)
